TPU v7x, 512 devices: a whole 4x8x8 slice. The times are simulated.
512 devices in a mesh: sec: 4 (over x), lat: 8 (over z), lon: 16 (over y, core).
Axes of the slice: x: 4, y: 8, z: 8, core: 2. Of those that a mesh axis runs over, the one named last changes fastest.
Arguments:
- state: float32 [4, 75, 32, 2048], P('sec', None, 'lat', 'lon'), may hold values from -6 to 6
- mixing: bfloat16 [4, 75, 32, 2048], P('sec', None, 'lat', 'lon'), may hold values from 0.05 to 50
- eastward: bfloat16 [4, 75, 32, 2048], P('sec', None, 'lat', 'lon'), may hold values from -0.44921875 to 0.44921875
- northward: bfloat16 [4, 75, 32, 2048], P('sec', None, 'lat', 'lon'), may hold values from -0.44921875 to 0.44921875
- sea_mask: int32 [32, 2048], P('lat', 'lon'), may hold values 0 or 1
- weights: bfloat16 [4, 8, 16, 16, 16, 512], P('sec', 'lat', 'lon'), may hold values from -1.5 to 1.5
- source_block: int32 [4, 8, 16, 128, 4], P('sec', 'lat', 'lon'), may hold values from 0 to 31
- dest_block: int32 [4, 8, 16, 128, 4], P('sec', 'lat', 'lon'), may hold values from 0 to 31
- record_counts: int32 [4, 8, 16, 128], P('sec', 'lat', 'lon'), may hold values from 0 to 4, as said below
Outputs:
- adjoint: float32 [4, 75, 32, 2048], P('sec', None, 'lat', 'lon')
Inputs may be any that keep to these rules, and one draw needn't show every extreme that they name: `record_counts`: in every section some receiving device has 4 live slots from every sending device.
All inputs are finite; a program needn't handle non-finite values. No bound on the sum of `sea_mask` on one device may be relied on, other than what follows from the above.
Results may differ from a plain program's by a relative error of at most 0.0003.
Values sent between devices are 32-bit elements; how exact they have to be, the bound alone decides.
No kernel may reach another device: no remote copies, remote signals or barrier semaphores. Data moves between devices by JAX's collectives and lax.ppermute only.
A program may use at most 64 MiB of HBM per device.

v0:
```python
import jax
import jax.numpy as jnp
from jax import lax
from jax.sharding import PartitionSpec as P

NCPL = 4
NSUB = 2


def extended(block, sides, width, periodic):
    for axis, dim in sides:
        count = lax.axis_size(axis)
        forward = [(i, i + 1) for i in range(count - 1)]
        if periodic:
            forward.append((count - 1, 0))
        backward = [(target, source) for source, target in forward]
        low = lax.ppermute(
            lax.slice_in_dim(block, block.shape[dim] - width, None, axis=dim), axis, forward
        )
        high = lax.ppermute(lax.slice_in_dim(block, 0, width, axis=dim), axis, backward)
        block = jnp.concatenate([low, block, high], axis=dim)
    return block


def column_solve(right, coeff):
    zero_row = jnp.zeros_like(coeff[:1])
    lower_band = jnp.concatenate([zero_row, coeff[1:]], axis=0)
    upper_band = jnp.concatenate([coeff[1:], zero_row], axis=0)
    centre = 1.0 + lower_band + upper_band

    def sweep_down(carried, entries):
        prior_c, prior_z = carried
        centre_k, beneath, overhead, right_k = entries
        pivot_value = centre_k + beneath * prior_c
        factor = -overhead / pivot_value
        partial_value = (right_k + beneath * prior_z) / pivot_value
        return ((factor, partial_value), (factor, partial_value))

    start_pair = (jnp.zeros_like(right[0]), jnp.zeros_like(right[0]))
    _, (factors, partials) = lax.scan(
        sweep_down, start_pair, (centre, lower_band, upper_band, right)
    )

    def sweep_up(carried, entries):
        factor, partial_value = entries
        solved_k = partial_value - factor * carried
        return (solved_k, solved_k)

    _, solved = lax.scan(sweep_up, jnp.zeros_like(right[0]), (factors, partials), reverse=True)
    return solved


def advect(mixed_adj, east_speed, north_speed):
    east_flux = east_speed.astype(jnp.float32) * mixed_adj
    north_flux = north_speed.astype(jnp.float32) * mixed_adj
    east_rim = extended(east_flux, (("lon", 2),), 1, True)
    north_rim = extended(north_flux, (("lat", 1),), 1, False)
    east_diff = east_rim[:, :, 2:] - east_rim[:, :, :-2]
    north_diff = north_rim[:, 2:, :] - north_rim[:, :-2, :]
    return mixed_adj + 0.5 * (east_diff + north_diff)


def couple(field_part, weights, source_block, dest_block, record_counts, air_factor):
    block_cells = weights.shape[3]
    capacity = source_block.shape[-1]
    peer_count = record_counts.shape[-1]
    surface = field_part[-1].reshape(-1, block_cells)
    block_count = surface.shape[0]
    gathered = jnp.take(surface, source_block.reshape(-1), axis=0)
    weight_table = weights[0, 0, 0].astype(jnp.float32)
    contribution = jnp.einsum("diz,zi->dz", weight_table, gathered, precision=lax.Precision.HIGHEST)
    received = lax.all_to_all(
        contribution.reshape(block_cells, peer_count, capacity),
        ("lat", "lon"),
        split_axis=1,
        concat_axis=1,
        tiled=True,
    )
    arrived = received.reshape(block_cells, peer_count * capacity)
    live_slot = (
        jnp.arange(capacity, dtype=jnp.int32)[None, :] < record_counts[0, 0, 0][:, None]
    ).reshape(-1)
    matches = dest_block.reshape(-1)[:, None] == jnp.arange(block_count, dtype=jnp.int32)[None, :]
    one_hot = jnp.logical_and(matches, live_slot[:, None]).astype(jnp.float32)
    accumulated = jnp.dot(
        arrived, one_hot, precision=lax.Precision.HIGHEST, preferred_element_type=jnp.float32
    )
    summed = lax.psum(accumulated * air_factor, "sec")
    return summed.T.reshape(field_part.shape[1], field_part.shape[2])


def local(
    state, mixing, eastward, northward, sea_mask, weights, source_block, dest_block, record_counts
):
    section = lax.axis_index("sec")
    section_count = lax.axis_size("sec")
    is_ocean = section == section_count - 1
    air_factor = jnp.where(is_ocean, 0.0, 1.0).astype(jnp.float32)
    ocean_keep = sea_mask.astype(jnp.float32)
    keep_factor = jnp.where(is_ocean, ocean_keep, jnp.ones_like(ocean_keep))
    field_part = state[0]
    mix_part = mixing[0]
    east_part = eastward[0]
    north_part = northward[0]
    for coupling in range(NCPL):
        for repeat in range(NSUB):
            mixed_adj = column_solve(field_part, mix_part.astype(jnp.float32))
            field_part = advect(mixed_adj, east_part, north_part) * keep_factor
        forcing = couple(field_part, weights, source_block, dest_block, record_counts, air_factor)
        field_part = field_part.at[0].add(
            jnp.where(is_ocean, forcing * ocean_keep, jnp.zeros_like(forcing))
        )
    return field_part[None]


def solution(mesh):
    in_specs = (
        P("sec", None, "lat", "lon"),
        P("sec", None, "lat", "lon"),
        P("sec", None, "lat", "lon"),
        P("sec", None, "lat", "lon"),
        P("lat", "lon"),
        P("sec", "lat", "lon", None, None, None),
        P("sec", "lat", "lon", None, None),
        P("sec", "lat", "lon", None, None),
        P("sec", "lat", "lon", None),
    )
    out_specs = P("sec", None, "lat", "lon")
    return jax.shard_map(local, mesh=mesh, in_specs=in_specs, out_specs=out_specs, check_vma=False)
```

profile of v0, /device:TPU:6, one launch (start us, length us, event | category | flops | bytes accessed | tf_op | source)
XLA Modules:
  0.0 361.2 jit_solution(979839688588339115)
XLA Ops:
  1.1 52.6 %while.276 = (s32[]{:T(128)}, f32[4,128]{1,0:T(4,128)S(1)}, f32[4,128]{1,0:T(4,128)S(1)}, f32[75,4,128]{2,1,0:T(4,128)S(1)}, f32[75,4,128]{2,1,0:T(4,128)S(1)}, ...) while((s32[]{:T(128)}, f32[4,128]{1,0:T(4,128)S(1)}, ...), condition=%wide.region_1.2_spmd.clone, body=%wide.region_0.1_spmd.clone.sunk | while | flops 4611 | bytes 20603 | solution.py:40
  53.7 2.7 while.277
  57.6 2.9 collective-permute-start
  61.9 4.9 %collective-permute-start.3 = (f32[75,1,128]{2,1,0:T(1,128)S(1)}, f32[75,1,128]{2,1,0:T(1,128)S(1)}, u32[]{:S(2)}, u32[]{:S(2)}) collective-permute-start(f32[75,1,128]{2,1,0:T(1,128)S(1)} %get-tuple-element.2005), channel_id=1, source_target_pairs={{0,16},{16,32},{32,48},{48,64},{64,80},{80,96},{96,112},{1,17},{17... | collective-permute-start | bytes 115208 | tf_op jit(solution)/shard_map/ppermute | solution.py:17
  68.9 3.2 while.278
  72.1 2.7 while.279
  79.8 4.9 %collective-permute-start.7 = (f32[75,1,128]{2,1,0:T(1,128)}, f32[75,1,128]{2,1,0:T(1,128)S(1)}, u32[]{:S(2)}, u32[]{:S(2)}) collective-permute-start(f32[75,1,128]{2,1,0:T(1,128)} %get-tuple-element.1999), channel_id=1, source_target_pairs={{0,16},{16,32},{32,48},{48,64},{64,80},{80,96},{96,112},{1,17},{17... | collective-permute-start | bytes 115208 | tf_op jit(solution)/shard_map/ppermute | solution.py:17
  89.5 2.6 fusion.127
  92.1 16.9 %all-to-all-start = ((f32[16,128,4]{0,2,1:T(4,128)}), f32[16,128,4]{0,2,1:T(4,128)S(1)}, u32[]{:S(2)}, u32[]{:S(2)}) async-start(f32[16,128,4]{0,2,1:T(4,128)} %bitcast.13), calls=%async_computation | async-start | bytes 524288 | tf_op jit(solution)/shard_map/all_to_all | solution.py:72
  109.5 14.2 %all-to-all-done = f32[16,128,4]{0,2,1:T(4,128)S(1)} async-done(((f32[16,128,4]{0,2,1:T(4,128)}), f32[16,128,4]{0,2,1:T(4,128)S(1)}, u32[]{:S(2)}, u32[]{:S(2)}) %all-to-all-start) | async-done | bytes 32800 | tf_op jit(solution)/shard_map/all_to_all | solution.py:72
  124.4 7.5 %psum.28 = f32[4,128]{1,0:T(4,128)S(1)} all-reduce(f32[4,128]{1,0:T(4,128)S(1)} %reshape.204), channel_id=1, replica_groups=mesh['sec'=4,'lat'=8,'lon'=16] {'sec'}, use_global_device_ids=true, to_apply=%region_8.10 | all-reduce | flops 512 | bytes 4096 | tf_op jit(solution)/shard_map/psum | solution.py:88
  132.0 3.2 while.280
  135.2 2.7 while.281
  140.0 5.2 %collective-permute-start.11 = (f32[75,1,128]{2,1,0:T(1,128)}, f32[75,1,128]{2,1,0:T(1,128)}, u32[]{:S(2)}, u32[]{:S(2)}) collective-permute-start(f32[75,1,128]{2,1,0:T(1,128)} %get-tuple-element.1993), channel_id=1, source_target_pairs={{0,16},{16,32},{32,48},{48,64},{64,80},{80,96},{96,112},{1,17},{17... | collective-permute-start | bytes 115208 | tf_op jit(solution)/shard_map/ppermute | solution.py:17
  149.0 3.0 collective-permute-done.9
  154.1 3.0 while.282
  157.1 2.7 while.283
  161.3 4.7 %collective-permute-start.15 = (f32[75,1,128]{2,1,0:T(1,128)S(1)}, f32[75,1,128]{2,1,0:T(1,128)S(1)}, u32[]{:S(2)}, u32[]{:S(2)}) collective-permute-start(f32[75,1,128]{2,1,0:T(1,128)S(1)} %get-tuple-element.1987), channel_id=1, source_target_pairs={{0,16},{16,32},{32,48},{48,64},{64,80},{80,96},{96,112},{1,17},{17... | collective-permute-start | bytes 115208 | tf_op jit(solution)/shard_map/ppermute | solution.py:17
  169.0 3.1 collective-permute-done.13
  173.7 2.6 fusion.128
  176.4 7.4 %all-to-all-start.1 = ((f32[16,128,4]{0,2,1:T(4,128)}), f32[16,128,4]{0,2,1:T(4,128)S(1)}, u32[]{:S(2)}, u32[]{:S(2)}) async-start(f32[16,128,4]{0,2,1:T(4,128)} %bitcast.23), calls=%async_computation.1 | async-start | bytes 524288 | tf_op jit(solution)/shard_map/all_to_all | solution.py:72
  183.7 14.7 %all-to-all-done.1 = f32[16,128,4]{0,2,1:T(4,128)S(1)} async-done(((f32[16,128,4]{0,2,1:T(4,128)}), f32[16,128,4]{0,2,1:T(4,128)S(1)}, u32[]{:S(2)}, u32[]{:S(2)}) %all-to-all-start.1) | async-done | bytes 32800 | tf_op jit(solution)/shard_map/all_to_all | solution.py:72
  199.1 10.0 %psum.29 = f32[4,128]{1,0:T(4,128)S(1)} all-reduce(f32[4,128]{1,0:T(4,128)S(1)} %reshape.208), channel_id=1, replica_groups=mesh['sec'=4,'lat'=8,'lon'=16] {'sec'}, use_global_device_ids=true, to_apply=%region_17.19 | all-reduce | flops 512 | bytes 4096 | tf_op jit(solution)/shard_map/psum | solution.py:88
  209.2 3.2 while.284
  212.4 2.7 while.285
  217.2 5.2 %collective-permute-start.19 = (f32[75,1,128]{2,1,0:T(1,128)}, f32[75,1,128]{2,1,0:T(1,128)}, u32[]{:S(2)}, u32[]{:S(2)}) collective-permute-start(f32[75,1,128]{2,1,0:T(1,128)} %get-tuple-element.1981), channel_id=1, source_target_pairs={{0,16},{16,32},{32,48},{48,64},{64,80},{80,96},{96,112},{1,17},{17... | collective-permute-start | bytes 115208 | tf_op jit(solution)/shard_map/ppermute | solution.py:17
  223.7 2.5 collective-permute-done.16
  226.2 3.0 collective-permute-done.17
  231.3 3.0 while.286
  234.3 2.7 while.287
  238.5 4.5 %collective-permute-start.23 = (f32[75,1,128]{2,1,0:T(1,128)S(1)}, f32[75,1,128]{2,1,0:T(1,128)S(1)}, u32[]{:S(2)}, u32[]{:S(2)}) collective-permute-start(f32[75,1,128]{2,1,0:T(1,128)S(1)} %get-tuple-element.1975), channel_id=1, source_target_pairs={{0,16},{16,32},{32,48},{48,64},{64,80},{80,96},{96,112},{1,17},{17... | collective-permute-start | bytes 115208 | tf_op jit(solution)/shard_map/ppermute | solution.py:17
  246.0 3.1 collective-permute-done.21
  250.8 2.6 fusion.129
  253.4 7.4 %all-to-all-start.2 = ((f32[16,128,4]{0,2,1:T(4,128)}), f32[16,128,4]{0,2,1:T(4,128)S(1)}, u32[]{:S(2)}, u32[]{:S(2)}) async-start(f32[16,128,4]{0,2,1:T(4,128)} %bitcast.32), calls=%async_computation.2 | async-start | bytes 524288 | tf_op jit(solution)/shard_map/all_to_all | solution.py:72
  260.8 14.7 %all-to-all-done.2 = f32[16,128,4]{0,2,1:T(4,128)S(1)} async-done(((f32[16,128,4]{0,2,1:T(4,128)}), f32[16,128,4]{0,2,1:T(4,128)S(1)}, u32[]{:S(2)}, u32[]{:S(2)}) %all-to-all-start.2) | async-done | bytes 32800 | tf_op jit(solution)/shard_map/all_to_all | solution.py:72
  276.1 7.7 %psum.30 = f32[4,128]{1,0:T(4,128)S(1)} all-reduce(f32[4,128]{1,0:T(4,128)S(1)} %reshape.212), channel_id=1, replica_groups=mesh['sec'=4,'lat'=8,'lon'=16] {'sec'}, use_global_device_ids=true, to_apply=%region_26.28 | all-reduce | flops 512 | bytes 4096 | tf_op jit(solution)/shard_map/psum | solution.py:88
  283.9 3.2 while.288
  287.2 2.7 while.289
  292.0 5.2 %collective-permute-start.27 = (f32[75,1,128]{2,1,0:T(1,128)}, f32[75,1,128]{2,1,0:T(1,128)}, u32[]{:S(2)}, u32[]{:S(2)}) collective-permute-start(f32[75,1,128]{2,1,0:T(1,128)} %get-tuple-element.1969), channel_id=1, source_target_pairs={{0,16},{16,32},{32,48},{48,64},{64,80},{80,96},{96,112},{1,17},{17... | collective-permute-start | bytes 115208 | tf_op jit(solution)/shard_map/ppermute | solution.py:17
  301.0 3.0 collective-permute-done.25
  306.0 3.0 while.290
  309.1 2.7 while.291
  313.3 4.5 %collective-permute-start.31 = (f32[75,1,128]{2,1,0:T(1,128)S(1)}, f32[75,1,128]{2,1,0:T(1,128)S(1)}, u32[]{:S(2)}, u32[]{:S(2)}) collective-permute-start(f32[75,1,128]{2,1,0:T(1,128)S(1)} %get-tuple-element.1963), channel_id=1, source_target_pairs={{0,16},{16,32},{32,48},{48,64},{64,80},{80,96},{96,112},{1,17},{17... | collective-permute-start | bytes 115208 | tf_op jit(solution)/shard_map/ppermute | solution.py:17
  320.7 3.1 collective-permute-done.29
  325.5 2.6 fusion.130
  328.1 7.4 %all-to-all-start.3 = ((f32[16,128,4]{0,2,1:T(4,128)}), f32[16,128,4]{0,2,1:T(4,128)S(1)}, u32[]{:S(2)}, u32[]{:S(2)}) async-start(f32[16,128,4]{0,2,1:T(4,128)} %bitcast.42), calls=%async_computation.3 | async-start | bytes 524288 | tf_op jit(solution)/shard_map/all_to_all | solution.py:72
  336.1 14.0 %all-to-all-done.3 = f32[16,128,4]{0,2,1:T(4,128)S(1)} async-done(((f32[16,128,4]{0,2,1:T(4,128)}), f32[16,128,4]{0,2,1:T(4,128)S(1)}, u32[]{:S(2)}, u32[]{:S(2)}) %all-to-all-start.3) | async-done | bytes 32800 | tf_op jit(solution)/shard_map/all_to_all | solution.py:72
  350.9 9.7 %psum.31 = f32[4,128]{1,0:T(4,128)S(1)} all-reduce(f32[4,128]{1,0:T(4,128)S(1)} %reshape.216), channel_id=1, replica_groups=mesh['sec'=4,'lat'=8,'lon'=16] {'sec'}, use_global_device_ids=true, to_apply=%region_35.37 | all-reduce | flops 512 | bytes 4096 | tf_op jit(solution)/shard_map/psum | solution.py:88
  (1398 shorter events, 133.6 us)
Async XLA Ops:
  0.0 66.8 %copy-start.9 = (s32[1,1,1,128,4]{3,4,2,1,0:T(4,128)S(1)}, s32[1,1,1,128,4]{3,4,2,1,0:T(4,128)}, u32[]{:S(2)}) copy-start(s32[1,1,1,128,4]{3,4,2,1,0:T(4,128)} %param.57) | copy-start | bytes 6148
  0.0 67.1 %copy-start.6 = (s32[4,128]{1,0:T(4,128)S(1)}, s32[4,128]{1,0:T(4,128)}, u32[]{:S(2)}) copy-start(s32[4,128]{1,0:T(4,128)} %param.55) | copy-start | bytes 6148
  1.1 73.8 %copy-start = (bf16[1,75,4,128]{3,2,1,0:T(4,128)(2,1)S(1)}, bf16[1,75,4,128]{3,2,1,0:T(4,128)(2,1)}, u32[]{:S(2)}) copy-start(bf16[1,75,4,128]{3,2,1,0:T(4,128)(2,1)} %param.53) | copy-start | bytes 230404
  1.1 73.8 %copy-start.1 = (bf16[1,75,4,128]{3,2,1,0:T(4,128)(2,1)S(1)}, bf16[1,75,4,128]{3,2,1,0:T(4,128)(2,1)}, u32[]{:S(2)}) copy-start(bf16[1,75,4,128]{3,2,1,0:T(4,128)(2,1)} %param.54) | copy-start | bytes 230404
  57.4 27.3 %copy-start.2 = (bf16[1,1,1,16,16,512]{5,4,3,2,1,0:T(8,128)(2,1)S(1)}, bf16[1,1,1,16,16,512]{5,4,3,2,1,0:T(8,128)(2,1)}, u32[]{:S(2)}) copy-start(bf16[1,1,1,16,16,512]{5,4,3,2,1,0:T(8,128)(2,1)} %param.56) | copy-start | bytes 786436
  57.6 9.5 %collective-permute-start = (f32[75,4,1]{2,1,0:T(4,128)S(1)}, f32[75,4,1]{2,1,0:T(4,128)S(1)}, u32[]{:S(2)}, u32[]{:S(2)}) collective-permute-start(f32[75,4,1]{2,1,0:T(4,128)S(1)} %get-tuple-element.2000), channel_id=1, source_target_pairs={{1,0},{2,1},{3,2},{4,3},{5,4},{6,5},{7,6},{8,7},{9,8},{10,9},{11,1... | collective-permute-start | bytes 3608 | tf_op jit(solution)/shard_map/ppermute | solution.py:20
  60.5 6.6 %collective-permute-start.1 = (f32[75,4,1]{2,1,0:T(4,128)S(1)}, f32[75,4,1]{2,1,0:T(4,128)S(1)}, u32[]{:S(2)}, u32[]{:S(2)}) collective-permute-start(f32[75,4,1]{2,1,0:T(4,128)S(1)} %get-tuple-element.2001), channel_id=1, source_target_pairs={{0,1},{1,2},{2,3},{3,4},{4,5},{5,6},{6,7},{7,8},{8,9},{9,10},{10,1... | collective-permute-start | bytes 3608 | tf_op jit(solution)/shard_map/ppermute | solution.py:17
  60.6 6.6 %collective-permute-start.2 = (f32[75,1,128]{2,1,0:T(1,128)S(1)}, f32[75,1,128]{2,1,0:T(1,128)S(1)}, u32[]{:S(2)}, u32[]{:S(2)}) collective-permute-start(f32[75,1,128]{2,1,0:T(1,128)S(1)} %get-tuple-element.2004), channel_id=1, source_target_pairs={{16,0},{32,16},{48,32},{64,48},{80,64},{96,80},{112,96},{17,1},{33... | collective-permute-start | bytes 115208 | tf_op jit(solution)/shard_map/ppermute | solution.py:20
  61.9 6.5 %collective-permute-start.3 = (f32[75,1,128]{2,1,0:T(1,128)S(1)}, f32[75,1,128]{2,1,0:T(1,128)S(1)}, u32[]{:S(2)}, u32[]{:S(2)}) collective-permute-start(f32[75,1,128]{2,1,0:T(1,128)S(1)} %get-tuple-element.2005), channel_id=1, source_target_pairs={{0,16},{16,32},{32,48},{48,64},{64,80},{80,96},{96,112},{1,17},{17... | collective-permute-start | bytes 115208 | tf_op jit(solution)/shard_map/ppermute | solution.py:17
  67.1 22.3 %copy-start.7 = (pred[512]{0:T(512)(128)(4,1)}, pred[512]{0:T(512)(128)(4,1)S(1)}, u32[]{:S(2)}) copy-start(pred[512]{0:T(512)(128)(4,1)S(1)} %compare_and_fusion) | copy-start | bytes 1540
  75.8 11.1 %collective-permute-start.4 = (f32[75,4,1]{2,1,0:T(4,128)}, f32[75,4,1]{2,1,0:T(4,128)}, u32[]{:S(2)}, u32[]{:S(2)}) collective-permute-start(f32[75,4,1]{2,1,0:T(4,128)} %get-tuple-element.1994), channel_id=1, source_target_pairs={{1,0},{2,1},{3,2},{4,3},{5,4},{6,5},{7,6},{8,7},{9,8},{10,9},{11,1... | collective-permute-start | bytes 3608 | tf_op jit(solution)/shard_map/ppermute | solution.py:20
  77.9 9.0 %collective-permute-start.5 = (f32[75,4,1]{2,1,0:T(4,128)}, f32[75,4,1]{2,1,0:T(4,128)}, u32[]{:S(2)}, u32[]{:S(2)}) collective-permute-start(f32[75,4,1]{2,1,0:T(4,128)} %get-tuple-element.1995), channel_id=1, source_target_pairs={{0,1},{1,2},{2,3},{3,4},{4,5},{5,6},{6,7},{7,8},{8,9},{9,10},{10,1... | collective-permute-start | bytes 3608 | tf_op jit(solution)/shard_map/ppermute | solution.py:17
  78.6 8.3 %collective-permute-start.6 = (f32[75,1,128]{2,1,0:T(1,128)}, f32[75,1,128]{2,1,0:T(1,128)S(1)}, u32[]{:S(2)}, u32[]{:S(2)}) collective-permute-start(f32[75,1,128]{2,1,0:T(1,128)} %get-tuple-element.1998), channel_id=1, source_target_pairs={{16,0},{32,16},{48,32},{64,48},{80,64},{96,80},{112,96},{17,1},{33... | collective-permute-start | bytes 115208 | tf_op jit(solution)/shard_map/ppermute | solution.py:20
  79.8 7.0 %collective-permute-start.7 = (f32[75,1,128]{2,1,0:T(1,128)}, f32[75,1,128]{2,1,0:T(1,128)S(1)}, u32[]{:S(2)}, u32[]{:S(2)}) collective-permute-start(f32[75,1,128]{2,1,0:T(1,128)} %get-tuple-element.1999), channel_id=1, source_target_pairs={{0,16},{16,32},{32,48},{48,64},{64,80},{80,96},{96,112},{1,17},{17... | collective-permute-start | bytes 115208 | tf_op jit(solution)/shard_map/ppermute | solution.py:17
  89.4 19.7 %copy-start.11 = (s32[1,1,1,128]{3,2,1,0:T(1,128)S(1)}, s32[1,1,1,128]{3,2,1,0:T(1,128)}, u32[]{:S(2)}) copy-start(s32[1,1,1,128]{3,2,1,0:T(1,128)} %param.59) | copy-start | bytes 1540
  89.4 19.8 %copy-start.10 = (s32[1,1,1,128,4]{3,4,2,1,0:T(4,128)S(1)}, s32[1,1,1,128,4]{3,4,2,1,0:T(4,128)}, u32[]{:S(2)}) copy-start(s32[1,1,1,128,4]{3,4,2,1,0:T(4,128)} %param.58) | copy-start | bytes 6148
  92.1 31.6 %all-to-all-start = ((f32[16,128,4]{0,2,1:T(4,128)}), f32[16,128,4]{0,2,1:T(4,128)S(1)}, u32[]{:S(2)}, u32[]{:S(2)}) async-start(f32[16,128,4]{0,2,1:T(4,128)} %bitcast.13), calls=%async_computation | async-start | bytes 524288 | tf_op jit(solution)/shard_map/all_to_all | solution.py:72
  138.7 13.3 %collective-permute-start.10 = (f32[75,1,128]{2,1,0:T(1,128)}, f32[75,1,128]{2,1,0:T(1,128)}, u32[]{:S(2)}, u32[]{:S(2)}) collective-permute-start(f32[75,1,128]{2,1,0:T(1,128)} %get-tuple-element.1992), channel_id=1, source_target_pairs={{16,0},{32,16},{48,32},{64,48},{80,64},{96,80},{112,96},{17,1},{33... | collective-permute-start | bytes 115208 | tf_op jit(solution)/shard_map/ppermute | solution.py:20
  140.0 12.7 %collective-permute-start.11 = (f32[75,1,128]{2,1,0:T(1,128)}, f32[75,1,128]{2,1,0:T(1,128)}, u32[]{:S(2)}, u32[]{:S(2)}) collective-permute-start(f32[75,1,128]{2,1,0:T(1,128)} %get-tuple-element.1993), channel_id=1, source_target_pairs={{0,16},{16,32},{32,48},{48,64},{64,80},{80,96},{96,112},{1,17},{17... | collective-permute-start | bytes 115208 | tf_op jit(solution)/shard_map/ppermute | solution.py:17
  146.0 3.1 collective-permute-start.8
  146.0 6.1 %collective-permute-start.9 = (f32[75,4,1]{2,1,0:T(4,128)}, f32[75,4,1]{2,1,0:T(4,128)S(1)}, u32[]{:S(2)}, u32[]{:S(2)}) collective-permute-start(f32[75,4,1]{2,1,0:T(4,128)} %get-tuple-element.1989), channel_id=1, source_target_pairs={{0,1},{1,2},{2,3},{3,4},{4,5},{5,6},{6,7},{7,8},{8,9},{9,10},{10,1... | collective-permute-start | bytes 3608 | tf_op jit(solution)/shard_map/ppermute | solution.py:17
  152.0 0.7 copy-start.3
  159.9 13.7 %copy-start.8 = (pred[512]{0:T(512)(128)(4,1)S(1)}, pred[512]{0:T(512)(128)(4,1)}, u32[]{:S(2)}) copy-start(pred[512]{0:T(512)(128)(4,1)} %copy-done.7) | copy-start | bytes 1540
  160.0 12.1 %collective-permute-start.14 = (f32[75,1,128]{2,1,0:T(1,128)S(1)}, f32[75,1,128]{2,1,0:T(1,128)S(1)}, u32[]{:S(2)}, u32[]{:S(2)}) collective-permute-start(f32[75,1,128]{2,1,0:T(1,128)S(1)} %get-tuple-element.1986), channel_id=1, source_target_pairs={{16,0},{32,16},{48,32},{64,48},{80,64},{96,80},{112,96},{17,1},{33... | collective-permute-start | bytes 115208 | tf_op jit(solution)/shard_map/ppermute | solution.py:20
  161.3 10.8 %collective-permute-start.15 = (f32[75,1,128]{2,1,0:T(1,128)S(1)}, f32[75,1,128]{2,1,0:T(1,128)S(1)}, u32[]{:S(2)}, u32[]{:S(2)}) collective-permute-start(f32[75,1,128]{2,1,0:T(1,128)S(1)} %get-tuple-element.1987), channel_id=1, source_target_pairs={{0,16},{16,32},{32,48},{48,64},{64,80},{80,96},{96,112},{1,17},{17... | collective-permute-start | bytes 115208 | tf_op jit(solution)/shard_map/ppermute | solution.py:17
  166.2 2.8 collective-permute-start.12
  166.2 5.9 %collective-permute-start.13 = (f32[75,4,1]{2,1,0:T(4,128)S(1)}, f32[75,4,1]{2,1,0:T(4,128)S(1)}, u32[]{:S(2)}, u32[]{:S(2)}) collective-permute-start(f32[75,4,1]{2,1,0:T(4,128)S(1)} %get-tuple-element.1983), channel_id=1, source_target_pairs={{0,1},{1,2},{2,3},{3,4},{4,5},{5,6},{6,7},{7,8},{8,9},{9,10},{10,1... | collective-permute-start | bytes 3608 | tf_op jit(solution)/shard_map/ppermute | solution.py:17
  176.4 22.1 %all-to-all-start.1 = ((f32[16,128,4]{0,2,1:T(4,128)}), f32[16,128,4]{0,2,1:T(4,128)S(1)}, u32[]{:S(2)}, u32[]{:S(2)}) async-start(f32[16,128,4]{0,2,1:T(4,128)} %bitcast.23), calls=%async_computation.1 | async-start | bytes 524288 | tf_op jit(solution)/shard_map/all_to_all | solution.py:72
  215.9 13.3 %collective-permute-start.18 = (f32[75,1,128]{2,1,0:T(1,128)}, f32[75,1,128]{2,1,0:T(1,128)}, u32[]{:S(2)}, u32[]{:S(2)}) collective-permute-start(f32[75,1,128]{2,1,0:T(1,128)} %get-tuple-element.1980), channel_id=1, source_target_pairs={{16,0},{32,16},{48,32},{64,48},{80,64},{96,80},{112,96},{17,1},{33... | collective-permute-start | bytes 115208 | tf_op jit(solution)/shard_map/ppermute | solution.py:20
  217.2 12.7 %collective-permute-start.19 = (f32[75,1,128]{2,1,0:T(1,128)}, f32[75,1,128]{2,1,0:T(1,128)}, u32[]{:S(2)}, u32[]{:S(2)}) collective-permute-start(f32[75,1,128]{2,1,0:T(1,128)} %get-tuple-element.1981), channel_id=1, source_target_pairs={{0,16},{16,32},{32,48},{48,64},{64,80},{80,96},{96,112},{1,17},{17... | collective-permute-start | bytes 115208 | tf_op jit(solution)/shard_map/ppermute | solution.py:17
  223.2 3.1 collective-permute-start.16
  223.2 6.1 %collective-permute-start.17 = (f32[75,4,1]{2,1,0:T(4,128)}, f32[75,4,1]{2,1,0:T(4,128)S(1)}, u32[]{:S(2)}, u32[]{:S(2)}) collective-permute-start(f32[75,4,1]{2,1,0:T(4,128)} %get-tuple-element.1977), channel_id=1, source_target_pairs={{0,1},{1,2},{2,3},{3,4},{4,5},{5,6},{6,7},{7,8},{8,9},{9,10},{10,1... | collective-permute-start | bytes 3608 | tf_op jit(solution)/shard_map/ppermute | solution.py:17
  229.2 0.7 copy-start.4
  237.2 11.9 %collective-permute-start.22 = (f32[75,1,128]{2,1,0:T(1,128)S(1)}, f32[75,1,128]{2,1,0:T(1,128)S(1)}, u32[]{:S(2)}, u32[]{:S(2)}) collective-permute-start(f32[75,1,128]{2,1,0:T(1,128)S(1)} %get-tuple-element.1974), channel_id=1, source_target_pairs={{16,0},{32,16},{48,32},{64,48},{80,64},{96,80},{112,96},{17,1},{33... | collective-permute-start | bytes 115208 | tf_op jit(solution)/shard_map/ppermute | solution.py:20
  238.5 10.6 %collective-permute-start.23 = (f32[75,1,128]{2,1,0:T(1,128)S(1)}, f32[75,1,128]{2,1,0:T(1,128)S(1)}, u32[]{:S(2)}, u32[]{:S(2)}) collective-permute-start(f32[75,1,128]{2,1,0:T(1,128)S(1)} %get-tuple-element.1975), channel_id=1, source_target_pairs={{0,16},{16,32},{32,48},{48,64},{64,80},{80,96},{96,112},{1,17},{17... | collective-permute-start | bytes 115208 | tf_op jit(solution)/shard_map/ppermute | solution.py:17
  243.2 2.8 collective-permute-start.20
  243.3 5.9 %collective-permute-start.21 = (f32[75,4,1]{2,1,0:T(4,128)S(1)}, f32[75,4,1]{2,1,0:T(4,128)S(1)}, u32[]{:S(2)}, u32[]{:S(2)}) collective-permute-start(f32[75,4,1]{2,1,0:T(4,128)S(1)} %get-tuple-element.1971), channel_id=1, source_target_pairs={{0,1},{1,2},{2,3},{3,4},{4,5},{5,6},{6,7},{7,8},{8,9},{9,10},{10,1... | collective-permute-start | bytes 3608 | tf_op jit(solution)/shard_map/ppermute | solution.py:17
  253.4 22.1 %all-to-all-start.2 = ((f32[16,128,4]{0,2,1:T(4,128)}), f32[16,128,4]{0,2,1:T(4,128)S(1)}, u32[]{:S(2)}, u32[]{:S(2)}) async-start(f32[16,128,4]{0,2,1:T(4,128)} %bitcast.32), calls=%async_computation.2 | async-start | bytes 524288 | tf_op jit(solution)/shard_map/all_to_all | solution.py:72
  290.7 13.3 %collective-permute-start.26 = (f32[75,1,128]{2,1,0:T(1,128)}, f32[75,1,128]{2,1,0:T(1,128)}, u32[]{:S(2)}, u32[]{:S(2)}) collective-permute-start(f32[75,1,128]{2,1,0:T(1,128)} %get-tuple-element.1968), channel_id=1, source_target_pairs={{16,0},{32,16},{48,32},{64,48},{80,64},{96,80},{112,96},{17,1},{33... | collective-permute-start | bytes 115208 | tf_op jit(solution)/shard_map/ppermute | solution.py:20
  292.0 12.7 %collective-permute-start.27 = (f32[75,1,128]{2,1,0:T(1,128)}, f32[75,1,128]{2,1,0:T(1,128)}, u32[]{:S(2)}, u32[]{:S(2)}) collective-permute-start(f32[75,1,128]{2,1,0:T(1,128)} %get-tuple-element.1969), channel_id=1, source_target_pairs={{0,16},{16,32},{32,48},{48,64},{64,80},{80,96},{96,112},{1,17},{17... | collective-permute-start | bytes 115208 | tf_op jit(solution)/shard_map/ppermute | solution.py:17
  297.9 3.1 collective-permute-start.24
  297.9 6.1 %collective-permute-start.25 = (f32[75,4,1]{2,1,0:T(4,128)}, f32[75,4,1]{2,1,0:T(4,128)S(1)}, u32[]{:S(2)}, u32[]{:S(2)}) collective-permute-start(f32[75,4,1]{2,1,0:T(4,128)} %get-tuple-element.1965), channel_id=1, source_target_pairs={{0,1},{1,2},{2,3},{3,4},{4,5},{5,6},{6,7},{7,8},{8,9},{9,10},{10,1... | collective-permute-start | bytes 3608 | tf_op jit(solution)/shard_map/ppermute | solution.py:17
  304.0 0.7 copy-start.5
  312.0 11.9 %collective-permute-start.30 = (f32[75,1,128]{2,1,0:T(1,128)S(1)}, f32[75,1,128]{2,1,0:T(1,128)S(1)}, u32[]{:S(2)}, u32[]{:S(2)}) collective-permute-start(f32[75,1,128]{2,1,0:T(1,128)S(1)} %get-tuple-element.1962), channel_id=1, source_target_pairs={{16,0},{32,16},{48,32},{64,48},{80,64},{96,80},{112,96},{17,1},{33... | collective-permute-start | bytes 115208 | tf_op jit(solution)/shard_map/ppermute | solution.py:20
  313.3 10.6 %collective-permute-start.31 = (f32[75,1,128]{2,1,0:T(1,128)S(1)}, f32[75,1,128]{2,1,0:T(1,128)S(1)}, u32[]{:S(2)}, u32[]{:S(2)}) collective-permute-start(f32[75,1,128]{2,1,0:T(1,128)S(1)} %get-tuple-element.1963), channel_id=1, source_target_pairs={{0,16},{16,32},{32,48},{48,64},{64,80},{80,96},{96,112},{1,17},{17... | collective-permute-start | bytes 115208 | tf_op jit(solution)/shard_map/ppermute | solution.py:17
  318.0 2.8 collective-permute-start.28
  318.0 5.9 %collective-permute-start.29 = (f32[75,4,1]{2,1,0:T(4,128)S(1)}, f32[75,4,1]{2,1,0:T(4,128)S(1)}, u32[]{:S(2)}, u32[]{:S(2)}) collective-permute-start(f32[75,4,1]{2,1,0:T(4,128)S(1)} %get-tuple-element.1959), channel_id=1, source_target_pairs={{0,1},{1,2},{2,3},{3,4},{4,5},{5,6},{6,7},{7,8},{8,9},{9,10},{10,1... | collective-permute-start | bytes 3608 | tf_op jit(solution)/shard_map/ppermute | solution.py:17
  328.1 22.1 %all-to-all-start.3 = ((f32[16,128,4]{0,2,1:T(4,128)}), f32[16,128,4]{0,2,1:T(4,128)S(1)}, u32[]{:S(2)}, u32[]{:S(2)}) async-start(f32[16,128,4]{0,2,1:T(4,128)} %bitcast.42), calls=%async_computation.3 | async-start | bytes 524288 | tf_op jit(solution)/shard_map/all_to_all | solution.py:72
where the time goes:
time: 365 us; the launch traced here: 361 us
  starting transfers between devices  96.5 us (26%)
  waiting for transfers between devices  91.7 us (25%)
  other arithmetic  85.1 us (23%)
  blocking collectives  34.9 us (10%)
  loops' own time  21.6 us (6%)
  local copies, waits for them, and re-layouts  17.9 us (5%)
  matrix products  12.5 us (3%)
    dynamic_update_slice x1200, other arithmetic, column_solve(): lax.scan(sweep_down, start_pair, (centre, lower_band, upper_band, right))  74.6 us
    all_to_all x4, waiting for transfers between devices, couple(): lax.all_to_all(contribution.reshape(block_cells, peer_count, capacity), (...  57.7 us
    ppermute x16, starting transfers between devices, extended(): lax.ppermute(lax.slice_in_dim(block, block.shape[dim] - width, None, axis...  42.1 us
    all_to_all x4, starting transfers between devices, couple(): lax.all_to_all(contribution.reshape(block_cells, peer_count, capacity), (...  39 us
    psum x4, blocking collectives, couple(): summed = lax.psum(accumulated * air_factor, 'sec')  34.9 us
    ppermute x16, waiting for transfers between devices, extended(): lax.ppermute(lax.slice_in_dim(block, block.shape[dim] - width, None, axis...  19.7 us
    ppermute x16, starting transfers between devices, extended(): lax.ppermute(lax.slice_in_dim(block, 0, width, axis=dim), axis, backward)  15.4 us
    ppermute x16, waiting for transfers between devices, extended(): lax.ppermute(lax.slice_in_dim(block, 0, width, axis=dim), axis, backward)  14.3 us
  transfers between devices with their start and end apart: 36, of which 17 were waited for; matrix products, arithmetic and copies ran while one was open for 2% of the time, Pallas kernels for 0%

commit v1 on v0

v1 whole, which is shorter than its diff:
```python
import jax
import jax.numpy as jnp
from jax import lax
from jax.experimental import pallas as pl
from jax.experimental.pallas import tpu as pltpu
from jax.sharding import PartitionSpec as P

NCPL = 4
NSUB = 2
SKEW = 2


def extended(block, sides, width, periodic):
    for axis, dim in sides:
        count = lax.axis_size(axis)
        forward = [(i, i + 1) for i in range(count - 1)]
        if periodic:
            forward.append((count - 1, 0))
        backward = [(target, source) for source, target in forward]
        low = lax.ppermute(
            lax.slice_in_dim(block, block.shape[dim] - width, None, axis=dim), axis, forward
        )
        high = lax.ppermute(lax.slice_in_dim(block, 0, width, axis=dim), axis, backward)
        block = jnp.concatenate([low, block, high], axis=dim)
    return block


def _factor_kernel(a_ref, inv_ref, b_ref, c_ref):
    lev = a_ref.shape[0]
    prior_c = jnp.zeros(a_ref.shape[1:], jnp.float32)
    zero = jnp.zeros(a_ref.shape[1:], jnp.float32)
    for k in range(lev):
        lower = a_ref[k] if k >= 1 else zero
        upper = a_ref[k + 1] if k + 1 < lev else zero
        centre = 1.0 + lower + upper
        pivot = centre + lower * prior_c
        inv = 1.0 / pivot
        factor = -upper / pivot
        inv_ref[k] = inv
        b_ref[k] = lower * inv
        c_ref[k] = factor
        prior_c = factor


def _solve_kernel(x_ref, inv_ref, b_ref, c_ref, o_ref):
    lev = x_ref.shape[0]

    def down(k, z):
        z = x_ref[k] * inv_ref[k] + b_ref[k] * z
        o_ref[k] = z
        return z

    def up(i, x):
        k = lev - 1 - i
        x = o_ref[k] - c_ref[k] * x
        o_ref[k] = x
        return x

    zero = jnp.zeros(x_ref.shape[1:], jnp.float32)
    lax.fori_loop(0, lev, down, zero, unroll=5)
    lax.fori_loop(0, lev, up, zero, unroll=5)


def factorise(coeff):
    shape = jax.ShapeDtypeStruct(coeff.shape, jnp.float32)
    size = coeff.size
    return pl.pallas_call(
        _factor_kernel,
        out_shape=(shape, shape, shape),
        cost_estimate=pl.CostEstimate(flops=8 * size, bytes_accessed=16 * size, transcendentals=0),
    )(coeff)


def column_solve(right, inv, lower, factor):
    size = right.size
    return pl.pallas_call(
        _solve_kernel,
        out_shape=jax.ShapeDtypeStruct(right.shape, jnp.float32),
        cost_estimate=pl.CostEstimate(flops=6 * size, bytes_accessed=20 * size, transcendentals=0),
    )(right, inv, lower, factor)


def advect(mixed_adj, east_speed, north_speed):
    east_flux = east_speed * mixed_adj
    north_flux = north_speed * mixed_adj
    east_rim = extended(east_flux, (("lon", 2),), 1, True)
    north_rim = extended(north_flux, (("lat", 1),), 1, False)
    east_diff = east_rim[:, :, 2:] - east_rim[:, :, :-2]
    north_diff = north_rim[:, 2:, :] - north_rim[:, :-2, :]
    return mixed_adj + 0.5 * (east_diff + north_diff)


def couple(field_part, weight_table, source_block, peer_count):
    block_cells = weight_table.shape[0]
    capacity = source_block.shape[-1]
    surface = field_part[-1].reshape(-1, block_cells)
    gathered = jnp.take(surface, source_block.reshape(-1), axis=0)
    contribution = jnp.einsum("diz,zi->dz", weight_table, gathered, precision=lax.Precision.HIGHEST)
    return lax.all_to_all(
        contribution.reshape(block_cells, peer_count, capacity),
        ("lat", "lon"),
        split_axis=1,
        concat_axis=1,
        tiled=True,
    )


def reduce_forcing(received, one_hot):
    block_cells = received.shape[0]
    arrived = received.reshape(block_cells, -1)
    accumulated = jnp.dot(
        arrived, one_hot, precision=lax.Precision.HIGHEST, preferred_element_type=jnp.float32
    )
    section_count = lax.axis_size("sec")
    return [lax.ppermute(accumulated, "sec", [(s, section_count - 1)]) for s in range(section_count - 1)]


def forcing_field(parts, shape):
    total = parts[0]
    for part in parts[1:]:
        total = total + part
    return total.T.reshape(shape)


def local(
    state, mixing, eastward, northward, sea_mask, weights, source_block, dest_block, record_counts
):
    section = lax.axis_index("sec")
    section_count = lax.axis_size("sec")
    is_ocean = section == section_count - 1
    ocean_keep = sea_mask.astype(jnp.float32)
    keep_factor = jnp.where(is_ocean, ocean_keep, jnp.ones_like(ocean_keep))
    field_part = state[0]
    inv, lower, factor = factorise(mixing[0].astype(jnp.float32))
    east_part = eastward[0].astype(jnp.float32)
    north_part = northward[0].astype(jnp.float32)

    weight_table = weights[0, 0, 0].astype(jnp.float32)
    block_count = field_part.shape[1] * field_part.shape[2] // weight_table.shape[0]
    capacity = source_block.shape[-1]
    live_slot = (
        jnp.arange(capacity, dtype=jnp.int32)[None, :] < record_counts[0, 0, 0][:, None]
    ).reshape(-1)
    matches = dest_block.reshape(-1)[:, None] == jnp.arange(block_count, dtype=jnp.int32)[None, :]
    one_hot = jnp.logical_and(matches, live_slot[:, None]).astype(jnp.float32)

    def substep(x):
        mixed_adj = column_solve(x, inv, lower, factor)
        return advect(mixed_adj, east_part, north_part) * keep_factor

    total_steps = NCPL * NSUB
    peer_count = record_counts.shape[-1]
    plane = field_part.shape[1:]
    in_flight = {}
    saved = None
    for step in range(total_steps + SKEW):
        advanced = substep(field_part)
        if step < SKEW:
            field_part = jnp.where(is_ocean, field_part, advanced)
        else:
            field_part = advanced
        for c, (stage, value) in list(in_flight.items()):
            if stage == 0:
                value, _ = lax.optimization_barrier((value, field_part))
                in_flight[c] = (1, reduce_forcing(value, one_hot))
        air_done = step + 1
        if air_done <= total_steps and air_done % NSUB == 0:
            in_flight[air_done // NSUB - 1] = (
                0, couple(field_part, weight_table, source_block, peer_count))
        if step == total_steps - 1:
            saved = field_part
        ocean_done = step - SKEW + 1
        if ocean_done >= 1 and ocean_done % NSUB == 0:
            stage, parts = in_flight.pop(ocean_done // NSUB - 1)
            forcing = forcing_field(parts, plane)
            field_part = field_part.at[0].add(
                jnp.where(is_ocean, forcing * ocean_keep, jnp.zeros_like(forcing))
            )
    field_part = jnp.where(is_ocean, field_part, saved)
    return field_part[None]


def solution(mesh):
    in_specs = (
        P("sec", None, "lat", "lon"),
        P("sec", None, "lat", "lon"),
        P("sec", None, "lat", "lon"),
        P("sec", None, "lat", "lon"),
        P("lat", "lon"),
        P("sec", "lat", "lon", None, None, None),
        P("sec", "lat", "lon", None, None),
        P("sec", "lat", "lon", None, None),
        P("sec", "lat", "lon", None),
    )
    out_specs = P("sec", None, "lat", "lon")
    return jax.shard_map(local, mesh=mesh, in_specs=in_specs, out_specs=out_specs, check_vma=False)
```

time: 365 us -> 283 us (0.78)
  other arithmetic: 85.1 us -> 25.6 us
  starting transfers between devices: 96.5 us -> 141 us
  blocking collectives: 34.9 us -> 0 us
  waiting for transfers between devices: 91.7 us -> 58.4 us
  Pallas kernels: 0 us -> 24.7 us
  loops' own time: 21.6 us -> 0 us
    dynamic_update_slice x1200 -> x0, other arithmetic: 74.6 us -> none  [column_solve(): lax.scan(sweep_down, start_pair, (centre, lower_band, upper_band, right))]
    psum x4 -> x0, blocking collectives: 34.9 us -> none  [couple(): summed = lax.psum(accumulated * air_factor, 'sec')]
    all_to_all x4, waiting for transfers between devices: 57.7 us -> 28.3 us  [couple(): lax.all_to_all(contribution.reshape(block_cells, peer_count, capacity), (...]
    pallas_call x0 -> x11, Pallas kernels: none -> 24.7 us  [the longest x10 22.4 us: column_solve(): pl.pallas_call(_solve_kernel, out_shape=jax.ShapeDtypeStruct(right.shape,...]
    another operation x16 -> x0, loops' own time: 21.6 us -> none  [the longest x8 11.4 us: column_solve(): lax.scan(sweep_up, jnp.zeros_like(right[0]), (factors, partials), reverse...]
    ppermute x0 -> x12, waiting for transfers between devices: none -> 20.4 us  [reduce_forcing(): lax.ppermute(accumulated, 'sec', [(s, section_count - 1)])]
    all_to_all x4, starting transfers between devices: 39 us -> 58.6 us  [couple(): lax.all_to_all(contribution.reshape(block_cells, peer_count, capacity), (...]
    ppermute x0 -> x12, starting transfers between devices: none -> 15.8 us  [reduce_forcing(): lax.ppermute(accumulated, 'sec', [(s, section_count - 1)])]
  transfers between devices with their start and end apart: 36 -> 56, of which waited for: 17 -> 22; matrix products, arithmetic and copies ran while one was open for 2% -> 11% of each run, Pallas kernels for 0% -> 3%
where the time goes in v1:
time: 283 us; the launch traced here: 279 us
  starting transfers between devices  141 us (50%)
  waiting for transfers between devices  58.4 us (21%)
  other arithmetic  25.6 us (9%)
  Pallas kernels  24.7 us (9%)
  local copies, waits for them, and re-layouts  15.8 us (6%)
  matrix products  12.6 us (4%)
    all_to_all x4, starting transfers between devices, couple(): lax.all_to_all(contribution.reshape(block_cells, peer_count, capacity), (...  58.6 us
    ppermute x20, starting transfers between devices, extended(): lax.ppermute(lax.slice_in_dim(block, block.shape[dim] - width, None, axis...  35.8 us
    ppermute x20, starting transfers between devices, extended(): lax.ppermute(lax.slice_in_dim(block, 0, width, axis=dim), axis, backward)  31 us
    all_to_all x4, waiting for transfers between devices, couple(): lax.all_to_all(contribution.reshape(block_cells, peer_count, capacity), (...  28.3 us
    pallas_call x10, Pallas kernels, column_solve(): pl.pallas_call(_solve_kernel, out_shape=jax.ShapeDtypeStruct(right.shape,...  22.4 us
    ppermute x12, waiting for transfers between devices, reduce_forcing(): lax.ppermute(accumulated, 'sec', [(s, section_count - 1)])  20.4 us
    ppermute x12, starting transfers between devices, reduce_forcing(): lax.ppermute(accumulated, 'sec', [(s, section_count - 1)])  15.8 us
    dot_general x4, matrix products, couple(): jnp.einsum('diz,zi->dz', weight_table, gathered, precision=lax.Precision....  10.5 us
  transfers between devices with their start and end apart: 56, of which 22 were waited for; matrix products, arithmetic and copies ran while one was open for 11% of the time, Pallas kernels for 3%

profile of v1, /device:TPU:6, one launch (start us, length us, event | category | flops | bytes accessed | tf_op | source)
XLA Modules:
  0.0 279.2 jit_solution(11503272042722470061)
XLA Ops:
  0.0 1.6 bitcast_convert_fusion.a_ref
  1.6 2.4 shard_map.91
  4.0 2.3 shard_map.92
  7.4 4.4 %collective-permute-start.3 = (f32[75,1,128]{2,1,0:T(1,128)S(1)}, f32[75,1,128]{2,1,0:T(1,128)S(1)}, u32[]{:S(2)}, u32[]{:S(2)}) collective-permute-start(f32[75,1,128]{2,1,0:T(1,128)S(1)} %get-tuple-element.133), channel_id=1, source_target_pairs={{0,16},{16,32},{32,48},{48,64},{64,80},{80,96},{96,112},{1,17},{17... | collective-permute-start | bytes 115208 | tf_op jit(solution)/shard_map/ppermute | solution.py:20
  13.3 2.9 %collective-permute-start = (f32[75,4,1]{2,1,0:T(4,128)S(1)}, f32[75,4,1]{2,1,0:T(4,128)S(1)}, u32[]{:S(2)}, u32[]{:S(2)}) collective-permute-start(f32[75,4,1]{2,1,0:T(4,128)S(1)} %get-tuple-element.128), channel_id=1, source_target_pairs={{1,0},{2,1},{3,2},{4,3},{5,4},{6,5},{7,6},{8,7},{9,8},{10,9},{11,1... | collective-permute-start | bytes 3608 | tf_op jit(solution)/shard_map/ppermute | solution.py:23
  16.6 2.5 collective-permute-done.1
  19.2 1.9 fusion.69.x_ref
  21.1 2.3 shard_map.93
  25.1 4.9 %collective-permute-start.7 = (f32[75,1,128]{2,1,0:T(1,128)}, f32[75,1,128]{2,1,0:T(1,128)S(1)}, u32[]{:S(2)}, u32[]{:S(2)}) collective-permute-start(f32[75,1,128]{2,1,0:T(1,128)} %get-tuple-element.127), channel_id=1, source_target_pairs={{0,16},{16,32},{32,48},{48,64},{64,80},{80,96},{96,112},{1,17},{17... | collective-permute-start | bytes 115208 | tf_op jit(solution)/shard_map/ppermute | solution.py:20
  32.3 2.8 collective-permute-start.4
  35.1 2.1 copy.21
  38.2 1.8 fusion.62.x_ref
  40.1 2.2 shard_map.94
  43.4 4.9 %collective-permute-start.11 = (f32[75,1,128]{2,1,0:T(1,128)S(1)}, f32[75,1,128]{2,1,0:T(1,128)S(1)}, u32[]{:S(2)}, u32[]{:S(2)}) collective-permute-start(f32[75,1,128]{2,1,0:T(1,128)S(1)} %get-tuple-element.121), channel_id=1, source_target_pairs={{0,16},{16,32},{32,48},{48,64},{64,80},{80,96},{96,112},{1,17},{17... | collective-permute-start | bytes 115208 | tf_op jit(solution)/shard_map/ppermute | solution.py:20
  50.5 3.0 %collective-permute-start.8 = (f32[75,4,1]{2,1,0:T(4,128)S(1)}, f32[75,4,1]{2,1,0:T(4,128)S(1)}, u32[]{:S(2)}, u32[]{:S(2)}) collective-permute-start(f32[75,4,1]{2,1,0:T(4,128)S(1)} %get-tuple-element.116), channel_id=1, source_target_pairs={{1,0},{2,1},{3,2},{4,3},{5,4},{6,5},{7,6},{8,7},{9,8},{10,9},{11,1... | collective-permute-start | bytes 3608 | tf_op jit(solution)/shard_map/ppermute | solution.py:23
  54.7 2.6 fusion.106
  58.3 21.0 %all-to-all-start = ((f32[16,128,4]{0,2,1:T(4,128)}), f32[16,128,4]{0,2,1:T(4,128)S(1)}, u32[]{:S(2)}, u32[]{:S(2)}) async-start(f32[16,128,4]{0,2,1:T(4,128)} %bitcast.12), calls=%async_computation | async-start | bytes 524288 | tf_op jit(solution)/shard_map/all_to_all | solution.py:99
  79.3 2.2 shard_map.95
  82.6 3.0 %collective-permute-start.15 = (f32[75,1,128]{2,1,0:T(1,128)S(1)}, f32[75,1,128]{2,1,0:T(1,128)S(1)}, u32[]{:S(2)}, u32[]{:S(2)}) collective-permute-start(f32[75,1,128]{2,1,0:T(1,128)S(1)} %get-tuple-element.115), channel_id=1, source_target_pairs={{0,16},{16,32},{32,48},{48,64},{64,80},{80,96},{96,112},{1,17},{17... | collective-permute-start | bytes 115208 | tf_op jit(solution)/shard_map/ppermute | solution.py:20
  86.9 7.1 %all-to-all-done = f32[16,128,4]{0,2,1:T(4,128)S(1)} async-done(((f32[16,128,4]{0,2,1:T(4,128)}), f32[16,128,4]{0,2,1:T(4,128)S(1)}, u32[]{:S(2)}, u32[]{:S(2)}) %all-to-all-start) | async-done | bytes 32800 | tf_op jit(solution)/shard_map/all_to_all | solution.py:99
  100.1 2.5 collective-permute-done.16
  107.9 2.2 shard_map.96
  111.2 2.6 collective-permute-start.22
  116.5 2.5 collective-permute-start.19
  120.3 2.6 fusion.107
  123.9 12.6 %all-to-all-start.1 = ((f32[16,128,4]{0,2,1:T(4,128)}), f32[16,128,4]{0,2,1:T(4,128)S(1)}, u32[]{:S(2)}, u32[]{:S(2)}) async-start(f32[16,128,4]{0,2,1:T(4,128)} %bitcast.22), calls=%async_computation.1 | async-start | bytes 524288 | tf_op jit(solution)/shard_map/all_to_all | solution.py:99
  136.5 2.2 shard_map.97
  139.8 3.0 %collective-permute-start.26 = (f32[75,1,128]{2,1,0:T(1,128)S(1)}, f32[75,1,128]{2,1,0:T(1,128)S(1)}, u32[]{:S(2)}, u32[]{:S(2)}) collective-permute-start(f32[75,1,128]{2,1,0:T(1,128)S(1)} %get-tuple-element.103), channel_id=1, source_target_pairs={{0,16},{16,32},{32,48},{48,64},{64,80},{80,96},{96,112},{1,17},{17... | collective-permute-start | bytes 115208 | tf_op jit(solution)/shard_map/ppermute | solution.py:20
  144.1 7.1 %all-to-all-done.1 = f32[16,128,4]{0,2,1:T(4,128)S(1)} async-done(((f32[16,128,4]{0,2,1:T(4,128)}), f32[16,128,4]{0,2,1:T(4,128)S(1)}, u32[]{:S(2)}, u32[]{:S(2)}) %all-to-all-start.1) | async-done | bytes 32800 | tf_op jit(solution)/shard_map/all_to_all | solution.py:99
  157.3 2.5 collective-permute-done.27
  165.1 2.2 shard_map.98
  168.4 2.6 collective-permute-start.33
  173.5 2.5 collective-permute-start.30
  177.3 2.6 fusion.108
  181.0 12.5 %all-to-all-start.2 = ((f32[16,128,4]{0,2,1:T(4,128)}), f32[16,128,4]{0,2,1:T(4,128)S(1)}, u32[]{:S(2)}, u32[]{:S(2)}) async-start(f32[16,128,4]{0,2,1:T(4,128)} %bitcast.31), calls=%async_computation.2 | async-start | bytes 524288 | tf_op jit(solution)/shard_map/all_to_all | solution.py:99
  193.5 2.2 shard_map.99
  196.8 3.0 %collective-permute-start.37 = (f32[75,1,128]{2,1,0:T(1,128)S(1)}, f32[75,1,128]{2,1,0:T(1,128)S(1)}, u32[]{:S(2)}, u32[]{:S(2)}) collective-permute-start(f32[75,1,128]{2,1,0:T(1,128)S(1)} %get-tuple-element.89), channel_id=1, source_target_pairs={{0,16},{16,32},{32,48},{48,64},{64,80},{80,96},{96,112},{1,17},{17... | collective-permute-start | bytes 115208 | tf_op jit(solution)/shard_map/ppermute | solution.py:20
  201.2 7.1 %all-to-all-done.2 = f32[16,128,4]{0,2,1:T(4,128)S(1)} async-done(((f32[16,128,4]{0,2,1:T(4,128)}), f32[16,128,4]{0,2,1:T(4,128)S(1)}, u32[]{:S(2)}, u32[]{:S(2)}) %all-to-all-start.2) | async-done | bytes 32800 | tf_op jit(solution)/shard_map/all_to_all | solution.py:99
  214.3 2.5 collective-permute-done.38
  222.1 2.2 shard_map.100
  225.4 2.6 collective-permute-start.44
  230.6 2.5 collective-permute-start.41
  234.3 2.6 fusion.109
  238.0 12.5 %all-to-all-start.3 = ((f32[16,128,4]{0,2,1:T(4,128)}), f32[16,128,4]{0,2,1:T(4,128)S(1)}, u32[]{:S(2)}, u32[]{:S(2)}) async-start(f32[16,128,4]{0,2,1:T(4,128)} %bitcast.40), calls=%async_computation.3 | async-start | bytes 524288 | tf_op jit(solution)/shard_map/all_to_all | solution.py:99
  250.5 2.2 shard_map.101
  253.8 3.0 %collective-permute-start.48 = (f32[75,1,128]{2,1,0:T(1,128)S(1)}, f32[75,1,128]{2,1,0:T(1,128)S(1)}, u32[]{:S(2)}, u32[]{:S(2)}) collective-permute-start(f32[75,1,128]{2,1,0:T(1,128)S(1)} %get-tuple-element.75), channel_id=1, source_target_pairs={{0,16},{16,32},{32,48},{48,64},{64,80},{80,96},{96,112},{1,17},{17... | collective-permute-start | bytes 115208 | tf_op jit(solution)/shard_map/ppermute | solution.py:20
  258.2 7.1 %all-to-all-done.3 = f32[16,128,4]{0,2,1:T(4,128)S(1)} async-done(((f32[16,128,4]{0,2,1:T(4,128)}), f32[16,128,4]{0,2,1:T(4,128)S(1)}, u32[]{:S(2)}, u32[]{:S(2)}) %all-to-all-start.3) | async-done | bytes 32800 | tf_op jit(solution)/shard_map/all_to_all | solution.py:99
  271.3 2.5 collective-permute-done.49
  (201 shorter events, 85.9 us)
Async XLA Ops:
  7.4 11.7 %collective-permute-start.3 = (f32[75,1,128]{2,1,0:T(1,128)S(1)}, f32[75,1,128]{2,1,0:T(1,128)S(1)}, u32[]{:S(2)}, u32[]{:S(2)}) collective-permute-start(f32[75,1,128]{2,1,0:T(1,128)S(1)} %get-tuple-element.133), channel_id=1, source_target_pairs={{0,16},{16,32},{32,48},{48,64},{64,80},{80,96},{96,112},{1,17},{17... | collective-permute-start | bytes 115208 | tf_op jit(solution)/shard_map/ppermute | solution.py:20
  11.8 7.3 %collective-permute-start.2 = (f32[75,1,128]{2,1,0:T(1,128)S(1)}, f32[75,1,128]{2,1,0:T(1,128)S(1)}, u32[]{:S(2)}, u32[]{:S(2)}) collective-permute-start(f32[75,1,128]{2,1,0:T(1,128)S(1)} %get-tuple-element.132), channel_id=1, source_target_pairs={{16,0},{32,16},{48,32},{64,48},{80,64},{96,80},{112,96},{17,1},{33... | collective-permute-start | bytes 115208 | tf_op jit(solution)/shard_map/ppermute | solution.py:23
  13.3 5.9 %collective-permute-start.1 = (f32[75,4,1]{2,1,0:T(4,128)S(1)}, f32[75,4,1]{2,1,0:T(4,128)S(1)}, u32[]{:S(2)}, u32[]{:S(2)}) collective-permute-start(f32[75,4,1]{2,1,0:T(4,128)S(1)} %get-tuple-element.129), channel_id=1, source_target_pairs={{0,1},{1,2},{2,3},{3,4},{4,5},{5,6},{6,7},{7,8},{8,9},{9,10},{10,1... | collective-permute-start | bytes 3608 | tf_op jit(solution)/shard_map/ppermute | solution.py:20
  13.3 5.8 %collective-permute-start = (f32[75,4,1]{2,1,0:T(4,128)S(1)}, f32[75,4,1]{2,1,0:T(4,128)S(1)}, u32[]{:S(2)}, u32[]{:S(2)}) collective-permute-start(f32[75,4,1]{2,1,0:T(4,128)S(1)} %get-tuple-element.128), channel_id=1, source_target_pairs={{1,0},{2,1},{3,2},{4,3},{5,4},{6,5},{7,6},{8,7},{9,8},{10,9},{11,1... | collective-permute-start | bytes 3608 | tf_op jit(solution)/shard_map/ppermute | solution.py:23
  25.1 13.1 %collective-permute-start.7 = (f32[75,1,128]{2,1,0:T(1,128)}, f32[75,1,128]{2,1,0:T(1,128)S(1)}, u32[]{:S(2)}, u32[]{:S(2)}) collective-permute-start(f32[75,1,128]{2,1,0:T(1,128)} %get-tuple-element.127), channel_id=1, source_target_pairs={{0,16},{16,32},{32,48},{48,64},{64,80},{80,96},{96,112},{1,17},{17... | collective-permute-start | bytes 115208 | tf_op jit(solution)/shard_map/ppermute | solution.py:20
  30.0 8.2 %collective-permute-start.6 = (f32[75,1,128]{2,1,0:T(1,128)}, f32[75,1,128]{2,1,0:T(1,128)}, u32[]{:S(2)}, u32[]{:S(2)}) collective-permute-start(f32[75,1,128]{2,1,0:T(1,128)} %get-tuple-element.126), channel_id=1, source_target_pairs={{16,0},{32,16},{48,32},{64,48},{80,64},{96,80},{112,96},{17,1},{33... | collective-permute-start | bytes 115208 | tf_op jit(solution)/shard_map/ppermute | solution.py:23
  32.1 6.1 %collective-permute-start.5 = (f32[75,4,1]{2,1,0:T(4,128)}, f32[75,4,1]{2,1,0:T(4,128)S(1)}, u32[]{:S(2)}, u32[]{:S(2)}) collective-permute-start(f32[75,4,1]{2,1,0:T(4,128)} %get-tuple-element.123), channel_id=1, source_target_pairs={{0,1},{1,2},{2,3},{3,4},{4,5},{5,6},{6,7},{7,8},{8,9},{9,10},{10,1... | collective-permute-start | bytes 3608 | tf_op jit(solution)/shard_map/ppermute | solution.py:20
  32.3 5.9 %collective-permute-start.4 = (f32[75,4,1]{2,1,0:T(4,128)}, f32[75,4,1]{2,1,0:T(4,128)S(1)}, u32[]{:S(2)}, u32[]{:S(2)}) collective-permute-start(f32[75,4,1]{2,1,0:T(4,128)} %get-tuple-element.122), channel_id=1, source_target_pairs={{1,0},{2,1},{3,2},{4,3},{5,4},{6,5},{7,6},{8,7},{9,8},{10,9},{11,1... | collective-permute-start | bytes 3608 | tf_op jit(solution)/shard_map/ppermute | solution.py:23
  43.4 13.9 %collective-permute-start.11 = (f32[75,1,128]{2,1,0:T(1,128)S(1)}, f32[75,1,128]{2,1,0:T(1,128)S(1)}, u32[]{:S(2)}, u32[]{:S(2)}) collective-permute-start(f32[75,1,128]{2,1,0:T(1,128)S(1)} %get-tuple-element.121), channel_id=1, source_target_pairs={{0,16},{16,32},{32,48},{48,64},{64,80},{80,96},{96,112},{1,17},{17... | collective-permute-start | bytes 115208 | tf_op jit(solution)/shard_map/ppermute | solution.py:20
  48.3 9.0 %collective-permute-start.10 = (f32[75,1,128]{2,1,0:T(1,128)S(1)}, f32[75,1,128]{2,1,0:T(1,128)S(1)}, u32[]{:S(2)}, u32[]{:S(2)}) collective-permute-start(f32[75,1,128]{2,1,0:T(1,128)S(1)} %get-tuple-element.120), channel_id=1, source_target_pairs={{16,0},{32,16},{48,32},{64,48},{80,64},{96,80},{112,96},{17,1},{33... | collective-permute-start | bytes 115208 | tf_op jit(solution)/shard_map/ppermute | solution.py:23
  50.5 6.9 %collective-permute-start.9 = (f32[75,4,1]{2,1,0:T(4,128)}, f32[75,4,1]{2,1,0:T(4,128)S(1)}, u32[]{:S(2)}, u32[]{:S(2)}) collective-permute-start(f32[75,4,1]{2,1,0:T(4,128)} %get-tuple-element.117), channel_id=1, source_target_pairs={{0,1},{1,2},{2,3},{3,4},{4,5},{5,6},{6,7},{7,8},{8,9},{9,10},{10,1... | collective-permute-start | bytes 3608 | tf_op jit(solution)/shard_map/ppermute | solution.py:20
  50.5 6.9 %collective-permute-start.8 = (f32[75,4,1]{2,1,0:T(4,128)S(1)}, f32[75,4,1]{2,1,0:T(4,128)S(1)}, u32[]{:S(2)}, u32[]{:S(2)}) collective-permute-start(f32[75,4,1]{2,1,0:T(4,128)S(1)} %get-tuple-element.116), channel_id=1, source_target_pairs={{1,0},{2,1},{3,2},{4,3},{5,4},{6,5},{7,6},{8,7},{9,8},{10,9},{11,1... | collective-permute-start | bytes 3608 | tf_op jit(solution)/shard_map/ppermute | solution.py:23
  58.3 35.7 %all-to-all-start = ((f32[16,128,4]{0,2,1:T(4,128)}), f32[16,128,4]{0,2,1:T(4,128)S(1)}, u32[]{:S(2)}, u32[]{:S(2)}) async-start(f32[16,128,4]{0,2,1:T(4,128)} %bitcast.12), calls=%async_computation | async-start | bytes 524288 | tf_op jit(solution)/shard_map/all_to_all | solution.py:99
  82.6 23.4 %collective-permute-start.15 = (f32[75,1,128]{2,1,0:T(1,128)S(1)}, f32[75,1,128]{2,1,0:T(1,128)S(1)}, u32[]{:S(2)}, u32[]{:S(2)}) collective-permute-start(f32[75,1,128]{2,1,0:T(1,128)S(1)} %get-tuple-element.115), channel_id=1, source_target_pairs={{0,16},{16,32},{32,48},{48,64},{64,80},{80,96},{96,112},{1,17},{17... | collective-permute-start | bytes 115208 | tf_op jit(solution)/shard_map/ppermute | solution.py:20
  85.6 20.3 %collective-permute-start.14 = (f32[75,1,128]{2,1,0:T(1,128)S(1)}, f32[75,1,128]{2,1,0:T(1,128)S(1)}, u32[]{:S(2)}, u32[]{:S(2)}) collective-permute-start(f32[75,1,128]{2,1,0:T(1,128)S(1)} %get-tuple-element.114), channel_id=1, source_target_pairs={{16,0},{32,16},{48,32},{64,48},{80,64},{96,80},{112,96},{17,1},{33... | collective-permute-start | bytes 115208 | tf_op jit(solution)/shard_map/ppermute | solution.py:23
  95.8 6.8 %collective-permute-start.16 = (f32[16,32]{1,0:T(8,128)S(1)}, f32[16,32]{1,0:T(8,128)S(1)}, u32[]{:S(2)}, u32[]{:S(2)}) collective-permute-start(f32[16,32]{1,0:T(8,128)S(1)} %fusion.7), channel_id=1, source_target_pairs={{0,384},{1,385},{2,386},{3,387},{4,388},{5,389},{6,390},{7,391},{8... | collective-permute-start | bytes 6152 | tf_op jit(solution)/shard_map/ppermute | solution.py:115
  97.1 7.0 %collective-permute-start.17 = (f32[16,32]{1,0:T(8,128)S(1)}, f32[16,32]{1,0:T(8,128)S(1)}, u32[]{:S(2)}, u32[]{:S(2)}) collective-permute-start(f32[16,32]{1,0:T(8,128)S(1)} %fusion.7), channel_id=1, source_target_pairs={{128,384},{129,385},{130,386},{131,387},{132,388},{133,389},{134,3... | collective-permute-start | bytes 6152 | tf_op jit(solution)/shard_map/ppermute | solution.py:115
  100.1 5.8 %collective-permute-start.13 = (f32[75,4,1]{2,1,0:T(4,128)S(1)}, f32[75,4,1]{2,1,0:T(4,128)S(1)}, u32[]{:S(2)}, u32[]{:S(2)}) collective-permute-start(f32[75,4,1]{2,1,0:T(4,128)S(1)} %get-tuple-element.111), channel_id=1, source_target_pairs={{0,1},{1,2},{2,3},{3,4},{4,5},{5,6},{6,7},{7,8},{8,9},{9,10},{10,1... | collective-permute-start | bytes 3608 | tf_op jit(solution)/shard_map/ppermute | solution.py:20
  111.2 11.8 %collective-permute-start.22 = (f32[75,1,128]{2,1,0:T(1,128)S(1)}, f32[75,1,128]{2,1,0:T(1,128)S(1)}, u32[]{:S(2)}, u32[]{:S(2)}) collective-permute-start(f32[75,1,128]{2,1,0:T(1,128)S(1)} %get-tuple-element.109), channel_id=1, source_target_pairs={{0,16},{16,32},{32,48},{48,64},{64,80},{80,96},{96,112},{1,17},{17... | collective-permute-start | bytes 115208 | tf_op jit(solution)/shard_map/ppermute | solution.py:20
  113.8 9.2 %collective-permute-start.21 = (f32[75,1,128]{2,1,0:T(1,128)S(1)}, f32[75,1,128]{2,1,0:T(1,128)S(1)}, u32[]{:S(2)}, u32[]{:S(2)}) collective-permute-start(f32[75,1,128]{2,1,0:T(1,128)S(1)} %get-tuple-element.108), channel_id=1, source_target_pairs={{16,0},{32,16},{48,32},{64,48},{80,64},{96,80},{112,96},{17,1},{33... | collective-permute-start | bytes 115208 | tf_op jit(solution)/shard_map/ppermute | solution.py:23
  116.1 6.9 %collective-permute-start.20 = (f32[75,4,1]{2,1,0:T(4,128)}, f32[75,4,1]{2,1,0:T(4,128)S(1)}, u32[]{:S(2)}, u32[]{:S(2)}) collective-permute-start(f32[75,4,1]{2,1,0:T(4,128)} %get-tuple-element.105), channel_id=1, source_target_pairs={{0,1},{1,2},{2,3},{3,4},{4,5},{5,6},{6,7},{7,8},{8,9},{9,10},{10,1... | collective-permute-start | bytes 3608 | tf_op jit(solution)/shard_map/ppermute | solution.py:20
  116.5 6.4 %collective-permute-start.19 = (f32[75,4,1]{2,1,0:T(4,128)S(1)}, f32[75,4,1]{2,1,0:T(4,128)S(1)}, u32[]{:S(2)}, u32[]{:S(2)}) collective-permute-start(f32[75,4,1]{2,1,0:T(4,128)S(1)} %get-tuple-element.104), channel_id=1, source_target_pairs={{1,0},{2,1},{3,2},{4,3},{5,4},{6,5},{7,6},{8,7},{9,8},{10,9},{11,1... | collective-permute-start | bytes 3608 | tf_op jit(solution)/shard_map/ppermute | solution.py:23
  123.9 27.3 %all-to-all-start.1 = ((f32[16,128,4]{0,2,1:T(4,128)}), f32[16,128,4]{0,2,1:T(4,128)S(1)}, u32[]{:S(2)}, u32[]{:S(2)}) async-start(f32[16,128,4]{0,2,1:T(4,128)} %bitcast.22), calls=%async_computation.1 | async-start | bytes 524288 | tf_op jit(solution)/shard_map/all_to_all | solution.py:99
  139.8 23.4 %collective-permute-start.26 = (f32[75,1,128]{2,1,0:T(1,128)S(1)}, f32[75,1,128]{2,1,0:T(1,128)S(1)}, u32[]{:S(2)}, u32[]{:S(2)}) collective-permute-start(f32[75,1,128]{2,1,0:T(1,128)S(1)} %get-tuple-element.103), channel_id=1, source_target_pairs={{0,16},{16,32},{32,48},{48,64},{64,80},{80,96},{96,112},{1,17},{17... | collective-permute-start | bytes 115208 | tf_op jit(solution)/shard_map/ppermute | solution.py:20
  142.8 20.3 %collective-permute-start.25 = (f32[75,1,128]{2,1,0:T(1,128)S(1)}, f32[75,1,128]{2,1,0:T(1,128)S(1)}, u32[]{:S(2)}, u32[]{:S(2)}) collective-permute-start(f32[75,1,128]{2,1,0:T(1,128)S(1)} %get-tuple-element.102), channel_id=1, source_target_pairs={{16,0},{32,16},{48,32},{64,48},{80,64},{96,80},{112,96},{17,1},{33... | collective-permute-start | bytes 115208 | tf_op jit(solution)/shard_map/ppermute | solution.py:23
  153.0 6.8 %collective-permute-start.27 = (f32[16,32]{1,0:T(8,128)S(1)}, f32[16,32]{1,0:T(8,128)S(1)}, u32[]{:S(2)}, u32[]{:S(2)}) collective-permute-start(f32[16,32]{1,0:T(8,128)S(1)} %fusion.5), channel_id=1, source_target_pairs={{0,384},{1,385},{2,386},{3,387},{4,388},{5,389},{6,390},{7,391},{8... | collective-permute-start | bytes 6152 | tf_op jit(solution)/shard_map/ppermute | solution.py:115
  154.3 7.0 %collective-permute-start.28 = (f32[16,32]{1,0:T(8,128)S(1)}, f32[16,32]{1,0:T(8,128)S(1)}, u32[]{:S(2)}, u32[]{:S(2)}) collective-permute-start(f32[16,32]{1,0:T(8,128)S(1)} %fusion.5), channel_id=1, source_target_pairs={{128,384},{129,385},{130,386},{131,387},{132,388},{133,389},{134,3... | collective-permute-start | bytes 6152 | tf_op jit(solution)/shard_map/ppermute | solution.py:115
  157.3 5.8 %collective-permute-start.24 = (f32[75,4,1]{2,1,0:T(4,128)S(1)}, f32[75,4,1]{2,1,0:T(4,128)S(1)}, u32[]{:S(2)}, u32[]{:S(2)}) collective-permute-start(f32[75,4,1]{2,1,0:T(4,128)S(1)} %get-tuple-element.99), channel_id=1, source_target_pairs={{0,1},{1,2},{2,3},{3,4},{4,5},{5,6},{6,7},{7,8},{8,9},{9,10},{10,1... | collective-permute-start | bytes 3608 | tf_op jit(solution)/shard_map/ppermute | solution.py:20
  168.4 11.6 %collective-permute-start.33 = (f32[75,1,128]{2,1,0:T(1,128)S(1)}, f32[75,1,128]{2,1,0:T(1,128)S(1)}, u32[]{:S(2)}, u32[]{:S(2)}) collective-permute-start(f32[75,1,128]{2,1,0:T(1,128)S(1)} %get-tuple-element.95), channel_id=1, source_target_pairs={{0,16},{16,32},{32,48},{48,64},{64,80},{80,96},{96,112},{1,17},{17... | collective-permute-start | bytes 115208 | tf_op jit(solution)/shard_map/ppermute | solution.py:20
  171.0 9.0 %collective-permute-start.32 = (f32[75,1,128]{2,1,0:T(1,128)S(1)}, f32[75,1,128]{2,1,0:T(1,128)S(1)}, u32[]{:S(2)}, u32[]{:S(2)}) collective-permute-start(f32[75,1,128]{2,1,0:T(1,128)S(1)} %get-tuple-element.94), channel_id=1, source_target_pairs={{16,0},{32,16},{48,32},{64,48},{80,64},{96,80},{112,96},{17,1},{33... | collective-permute-start | bytes 115208 | tf_op jit(solution)/shard_map/ppermute | solution.py:23
  173.1 6.9 %collective-permute-start.31 = (f32[75,4,1]{2,1,0:T(4,128)}, f32[75,4,1]{2,1,0:T(4,128)S(1)}, u32[]{:S(2)}, u32[]{:S(2)}) collective-permute-start(f32[75,4,1]{2,1,0:T(4,128)} %get-tuple-element.91), channel_id=1, source_target_pairs={{0,1},{1,2},{2,3},{3,4},{4,5},{5,6},{6,7},{7,8},{8,9},{9,10},{10,1... | collective-permute-start | bytes 3608 | tf_op jit(solution)/shard_map/ppermute | solution.py:20
  173.5 6.4 %collective-permute-start.30 = (f32[75,4,1]{2,1,0:T(4,128)S(1)}, f32[75,4,1]{2,1,0:T(4,128)S(1)}, u32[]{:S(2)}, u32[]{:S(2)}) collective-permute-start(f32[75,4,1]{2,1,0:T(4,128)S(1)} %get-tuple-element.90), channel_id=1, source_target_pairs={{1,0},{2,1},{3,2},{4,3},{5,4},{6,5},{7,6},{8,7},{9,8},{10,9},{11,1... | collective-permute-start | bytes 3608 | tf_op jit(solution)/shard_map/ppermute | solution.py:23
  181.0 27.3 %all-to-all-start.2 = ((f32[16,128,4]{0,2,1:T(4,128)}), f32[16,128,4]{0,2,1:T(4,128)S(1)}, u32[]{:S(2)}, u32[]{:S(2)}) async-start(f32[16,128,4]{0,2,1:T(4,128)} %bitcast.31), calls=%async_computation.2 | async-start | bytes 524288 | tf_op jit(solution)/shard_map/all_to_all | solution.py:99
  196.8 23.4 %collective-permute-start.37 = (f32[75,1,128]{2,1,0:T(1,128)S(1)}, f32[75,1,128]{2,1,0:T(1,128)S(1)}, u32[]{:S(2)}, u32[]{:S(2)}) collective-permute-start(f32[75,1,128]{2,1,0:T(1,128)S(1)} %get-tuple-element.89), channel_id=1, source_target_pairs={{0,16},{16,32},{32,48},{48,64},{64,80},{80,96},{96,112},{1,17},{17... | collective-permute-start | bytes 115208 | tf_op jit(solution)/shard_map/ppermute | solution.py:20
  199.9 20.3 %collective-permute-start.36 = (f32[75,1,128]{2,1,0:T(1,128)S(1)}, f32[75,1,128]{2,1,0:T(1,128)S(1)}, u32[]{:S(2)}, u32[]{:S(2)}) collective-permute-start(f32[75,1,128]{2,1,0:T(1,128)S(1)} %get-tuple-element.88), channel_id=1, source_target_pairs={{16,0},{32,16},{48,32},{64,48},{80,64},{96,80},{112,96},{17,1},{33... | collective-permute-start | bytes 115208 | tf_op jit(solution)/shard_map/ppermute | solution.py:23
  210.1 6.8 %collective-permute-start.38 = (f32[16,32]{1,0:T(8,128)S(1)}, f32[16,32]{1,0:T(8,128)S(1)}, u32[]{:S(2)}, u32[]{:S(2)}) collective-permute-start(f32[16,32]{1,0:T(8,128)S(1)} %fusion.3), channel_id=1, source_target_pairs={{0,384},{1,385},{2,386},{3,387},{4,388},{5,389},{6,390},{7,391},{8... | collective-permute-start | bytes 6152 | tf_op jit(solution)/shard_map/ppermute | solution.py:115
  211.4 7.0 %collective-permute-start.39 = (f32[16,32]{1,0:T(8,128)S(1)}, f32[16,32]{1,0:T(8,128)S(1)}, u32[]{:S(2)}, u32[]{:S(2)}) collective-permute-start(f32[16,32]{1,0:T(8,128)S(1)} %fusion.3), channel_id=1, source_target_pairs={{128,384},{129,385},{130,386},{131,387},{132,388},{133,389},{134,3... | collective-permute-start | bytes 6152 | tf_op jit(solution)/shard_map/ppermute | solution.py:115
  214.3 5.8 %collective-permute-start.35 = (f32[75,4,1]{2,1,0:T(4,128)S(1)}, f32[75,4,1]{2,1,0:T(4,128)S(1)}, u32[]{:S(2)}, u32[]{:S(2)}) collective-permute-start(f32[75,4,1]{2,1,0:T(4,128)S(1)} %get-tuple-element.85), channel_id=1, source_target_pairs={{0,1},{1,2},{2,3},{3,4},{4,5},{5,6},{6,7},{7,8},{8,9},{9,10},{10,1... | collective-permute-start | bytes 3608 | tf_op jit(solution)/shard_map/ppermute | solution.py:20
  225.4 11.6 %collective-permute-start.44 = (f32[75,1,128]{2,1,0:T(1,128)S(1)}, f32[75,1,128]{2,1,0:T(1,128)S(1)}, u32[]{:S(2)}, u32[]{:S(2)}) collective-permute-start(f32[75,1,128]{2,1,0:T(1,128)S(1)} %get-tuple-element.81), channel_id=1, source_target_pairs={{0,16},{16,32},{32,48},{48,64},{64,80},{80,96},{96,112},{1,17},{17... | collective-permute-start | bytes 115208 | tf_op jit(solution)/shard_map/ppermute | solution.py:20
  228.0 9.0 %collective-permute-start.43 = (f32[75,1,128]{2,1,0:T(1,128)S(1)}, f32[75,1,128]{2,1,0:T(1,128)S(1)}, u32[]{:S(2)}, u32[]{:S(2)}) collective-permute-start(f32[75,1,128]{2,1,0:T(1,128)S(1)} %get-tuple-element.80), channel_id=1, source_target_pairs={{16,0},{32,16},{48,32},{64,48},{80,64},{96,80},{112,96},{17,1},{33... | collective-permute-start | bytes 115208 | tf_op jit(solution)/shard_map/ppermute | solution.py:23
  230.1 6.9 %collective-permute-start.42 = (f32[75,4,1]{2,1,0:T(4,128)}, f32[75,4,1]{2,1,0:T(4,128)S(1)}, u32[]{:S(2)}, u32[]{:S(2)}) collective-permute-start(f32[75,4,1]{2,1,0:T(4,128)} %get-tuple-element.77), channel_id=1, source_target_pairs={{0,1},{1,2},{2,3},{3,4},{4,5},{5,6},{6,7},{7,8},{8,9},{9,10},{10,1... | collective-permute-start | bytes 3608 | tf_op jit(solution)/shard_map/ppermute | solution.py:20
  230.6 6.4 %collective-permute-start.41 = (f32[75,4,1]{2,1,0:T(4,128)}, f32[75,4,1]{2,1,0:T(4,128)S(1)}, u32[]{:S(2)}, u32[]{:S(2)}) collective-permute-start(f32[75,4,1]{2,1,0:T(4,128)} %get-tuple-element.76), channel_id=1, source_target_pairs={{1,0},{2,1},{3,2},{4,3},{5,4},{6,5},{7,6},{8,7},{9,8},{10,9},{11,1... | collective-permute-start | bytes 3608 | tf_op jit(solution)/shard_map/ppermute | solution.py:23
  238.0 27.3 %all-to-all-start.3 = ((f32[16,128,4]{0,2,1:T(4,128)}), f32[16,128,4]{0,2,1:T(4,128)S(1)}, u32[]{:S(2)}, u32[]{:S(2)}) async-start(f32[16,128,4]{0,2,1:T(4,128)} %bitcast.40), calls=%async_computation.3 | async-start | bytes 524288 | tf_op jit(solution)/shard_map/all_to_all | solution.py:99
  253.8 23.4 %collective-permute-start.48 = (f32[75,1,128]{2,1,0:T(1,128)S(1)}, f32[75,1,128]{2,1,0:T(1,128)S(1)}, u32[]{:S(2)}, u32[]{:S(2)}) collective-permute-start(f32[75,1,128]{2,1,0:T(1,128)S(1)} %get-tuple-element.75), channel_id=1, source_target_pairs={{0,16},{16,32},{32,48},{48,64},{64,80},{80,96},{96,112},{1,17},{17... | collective-permute-start | bytes 115208 | tf_op jit(solution)/shard_map/ppermute | solution.py:20
  256.9 20.3 %collective-permute-start.47 = (f32[75,1,128]{2,1,0:T(1,128)S(1)}, f32[75,1,128]{2,1,0:T(1,128)S(1)}, u32[]{:S(2)}, u32[]{:S(2)}) collective-permute-start(f32[75,1,128]{2,1,0:T(1,128)S(1)} %get-tuple-element.74), channel_id=1, source_target_pairs={{16,0},{32,16},{48,32},{64,48},{80,64},{96,80},{112,96},{17,1},{33... | collective-permute-start | bytes 115208 | tf_op jit(solution)/shard_map/ppermute | solution.py:23
  267.1 6.8 %collective-permute-start.49 = (f32[16,32]{1,0:T(8,128)S(1)}, f32[16,32]{1,0:T(8,128)S(1)}, u32[]{:S(2)}, u32[]{:S(2)}) collective-permute-start(f32[16,32]{1,0:T(8,128)S(1)} %fusion.1), channel_id=1, source_target_pairs={{0,384},{1,385},{2,386},{3,387},{4,388},{5,389},{6,390},{7,391},{8... | collective-permute-start | bytes 6152 | tf_op jit(solution)/shard_map/ppermute | solution.py:115
  268.4 7.0 %collective-permute-start.50 = (f32[16,32]{1,0:T(8,128)S(1)}, f32[16,32]{1,0:T(8,128)S(1)}, u32[]{:S(2)}, u32[]{:S(2)}) collective-permute-start(f32[16,32]{1,0:T(8,128)S(1)} %fusion.1), channel_id=1, source_target_pairs={{128,384},{129,385},{130,386},{131,387},{132,388},{133,389},{134,3... | collective-permute-start | bytes 6152 | tf_op jit(solution)/shard_map/ppermute | solution.py:115
  271.3 5.8 %collective-permute-start.46 = (f32[75,4,1]{2,1,0:T(4,128)S(1)}, f32[75,4,1]{2,1,0:T(4,128)S(1)}, u32[]{:S(2)}, u32[]{:S(2)}) collective-permute-start(f32[75,4,1]{2,1,0:T(4,128)S(1)} %get-tuple-element.71), channel_id=1, source_target_pairs={{0,1},{1,2},{2,3},{3,4},{4,5},{5,6},{6,7},{7,8},{8,9},{9,10},{10,1... | collective-permute-start | bytes 3608 | tf_op jit(solution)/shard_map/ppermute | solution.py:20
  (26 other events, 242.9 us)

commit v2 on v1

--- a/solution.py
+++ b/solution.py
@@ -90,24 +90,30 @@
     return mixed_adj + 0.5 * (east_diff + north_diff)
 
 
-def couple(field_part, weight_table, source_block, peer_count):
-    block_cells = weight_table.shape[0]
-    capacity = source_block.shape[-1]
+def redistribute(weights, source_block, block_count):
+    block_cells = weights.shape[3]
+    peer_count, capacity = source_block.shape[-2:]
+    table = weights[0, 0, 0].astype(jnp.float32).reshape(block_cells * block_cells, peer_count, capacity)
+    sources = source_block[0, 0, 0].astype(jnp.float32)[None]
+    packed = lax.all_to_all(
+        jnp.concatenate([table, sources], axis=0), ("lat", "lon"), split_axis=1, concat_axis=1, tiled=True
+    )
+    weight_in = packed[:-1].reshape(block_cells, block_cells, peer_count * capacity)
+    sender = jnp.arange(peer_count, dtype=jnp.int32)[:, None] * block_count
+    rows = (packed[-1].astype(jnp.int32) + sender).reshape(-1)
+    return weight_in, rows
+
+
+def couple(field_part, block_cells):
     surface = field_part[-1].reshape(-1, block_cells)
-    gathered = jnp.take(surface, source_block.reshape(-1), axis=0)
-    contribution = jnp.einsum("diz,zi->dz", weight_table, gathered, precision=lax.Precision.HIGHEST)
-    return lax.all_to_all(
-        contribution.reshape(block_cells, peer_count, capacity),
-        ("lat", "lon"),
-        split_axis=1,
-        concat_axis=1,
-        tiled=True,
-    )
-
-
-def reduce_forcing(received, one_hot):
-    block_cells = received.shape[0]
-    arrived = received.reshape(block_cells, -1)
+    return lax.all_gather(surface, ("lat", "lon"))
+
+
+def reduce_forcing(gathered_surfaces, weight_in, rows, one_hot):
+    block_cells = weight_in.shape[0]
+    table = gathered_surfaces.reshape(-1, block_cells)
+    picked = jnp.take(table, rows, axis=0)
+    arrived = jnp.einsum("diz,zi->dz", weight_in, picked, precision=lax.Precision.HIGHEST)
     accumulated = jnp.dot(
         arrived, one_hot, precision=lax.Precision.HIGHEST, preferred_element_type=jnp.float32
     )
@@ -135,8 +141,9 @@
     east_part = eastward[0].astype(jnp.float32)
     north_part = northward[0].astype(jnp.float32)
 
-    weight_table = weights[0, 0, 0].astype(jnp.float32)
-    block_count = field_part.shape[1] * field_part.shape[2] // weight_table.shape[0]
+    block_cells = weights.shape[3]
+    block_count = field_part.shape[1] * field_part.shape[2] // block_cells
+    weight_in, rows = redistribute(weights, source_block, block_count)
     capacity = source_block.shape[-1]
     live_slot = (
         jnp.arange(capacity, dtype=jnp.int32)[None, :] < record_counts[0, 0, 0][:, None]
@@ -149,7 +156,6 @@
         return advect(mixed_adj, east_part, north_part) * keep_factor
 
     total_steps = NCPL * NSUB
-    peer_count = record_counts.shape[-1]
     plane = field_part.shape[1:]
     in_flight = {}
     saved = None
@@ -162,11 +168,11 @@
         for c, (stage, value) in list(in_flight.items()):
             if stage == 0:
                 value, _ = lax.optimization_barrier((value, field_part))
-                in_flight[c] = (1, reduce_forcing(value, one_hot))
+                in_flight[c] = (1, reduce_forcing(value, weight_in, rows, one_hot))
         air_done = step + 1
         if air_done <= total_steps and air_done % NSUB == 0:
             in_flight[air_done // NSUB - 1] = (
-                0, couple(field_part, weight_table, source_block, peer_count))
+                0, couple(field_part, block_cells))
         if step == total_steps - 1:
             saved = field_part
         ocean_done = step - SKEW + 1

time: 283 us -> 480 us (1.70)
  the two profiles are of different devices: /device:TPU:6 before, /device:TPU:64 now
where the time goes in v2:
time: 480 us; the launch traced here: 470 us
  blocking collectives  201 us (42%)
  starting transfers between devices  114 us (24%)
  waiting for transfers between devices  39.9 us (8%)
  matrix products  35.5 us (7%)
  other arithmetic  28 us (6%)
  local copies, waits for them, and re-layouts  26.6 us (6%)
  Pallas kernels  24.7 us (5%)
    all_gather x4, blocking collectives, couple(): return lax.all_gather(surface, ('lat', 'lon'))  201 us
    ppermute x20, starting transfers between devices, extended(): lax.ppermute(lax.slice_in_dim(block, 0, width, axis=dim), axis, backward)  46.3 us
    dot_general x4, matrix products, reduce_forcing(): jnp.einsum('diz,zi->dz', weight_in, picked, precision=lax.Precision.HIGHEST)  33.5 us
    ppermute x20, starting transfers between devices, extended(): lax.ppermute(lax.slice_in_dim(block, block.shape[dim] - width, None, axis...  31.1 us
    ppermute x12, starting transfers between devices, reduce_forcing(): lax.ppermute(accumulated, 'sec', [(s, section_count - 1)])  22.7 us
    pallas_call x10, Pallas kernels, column_solve(): pl.pallas_call(_solve_kernel, out_shape=jax.ShapeDtypeStruct(right.shape,...  22.3 us
    ppermute x20, waiting for transfers between devices, extended(): lax.ppermute(lax.slice_in_dim(block, block.shape[dim] - width, None, axis...  21.8 us
    ppermute x20, waiting for transfers between devices, extended(): lax.ppermute(lax.slice_in_dim(block, 0, width, axis=dim), axis, backward)  18.1 us
  transfers between devices with their start and end apart: 53, of which 14 were waited for; matrix products, arithmetic and copies ran while one was open for 8% of the time, Pallas kernels for 1%

profile of v2, /device:TPU:64, one launch (start us, length us, event | category | flops | bytes accessed | tf_op | source)
XLA Modules:
  0.0 470.5 jit_solution(9852988825880505372)
XLA Ops:
  1.6 2.4 shard_map.91
  7.4 6.9 %collective-permute-start.2 = (f32[75,1,128]{2,1,0:T(1,128)S(1)}, f32[75,1,128]{2,1,0:T(1,128)S(1)}, u32[]{:S(2)}, u32[]{:S(2)}) collective-permute-start(f32[75,1,128]{2,1,0:T(1,128)S(1)} %get-tuple-element.134), channel_id=1, source_target_pairs={{16,0},{32,16},{48,32},{64,48},{80,64},{96,80},{112,96},{17,1},{33... | collective-permute-start | bytes 115208 | tf_op jit(solution)/shard_map/ppermute | solution.py:23
  18.4 3.8 copy.29
  23.3 3.6 reshape.215
  27.0 2.2 shard_map.93
  30.3 3.9 collective-permute-start.6
  36.6 2.2 collective-permute-start.4
  40.0 13.6 %all-to-all-start = ((f32[257,128,4]{0,2,1:T(4,128)}), f32[257,128,4]{0,2,1:T(4,128)}, u32[]{:S(2)}, u32[]{:S(2)}) async-start(f32[257,128,4]{0,2,1:T(4,128)} %pad_maximum_fusion), calls=%async_computation | async-start | bytes 1572864 | tf_op jit(solution)/shard_map/all_to_all | solution.py:98
  58.1 2.9 collective-permute-start.10
  60.9 3.0 collective-permute-start.11
  68.0 3.6 collective-permute-done.8
  71.6 3.0 collective-permute-done.9
  76.5 50.1 %all_gather.12 = f32[128,32,16]{1,2,0:T(8,128)S(1)} all-gather(f32[1,32,16]{1,2,0:T(8,128)S(1)} %copy.31), channel_id=1, replica_groups=mesh['sec'=4,'lat'=8,'lon'=16] {'lat','lon'}, dimensions={0}, use_global_device_ids=true | all-gather | bytes 264192 | tf_op jit(solution)/shard_map/all_gather | solution.py:109
  130.5 3.1 collective-permute-start.14
  133.6 3.0 collective-permute-start.15
  139.1 3.2 fusion
  143.5 2.7 reshape.200
  147.4 8.4 %fusion.107 = f32[512,1,16]{2,1,0:T(1,128)S(1)} fusion(f32[512,16,1]{1,2,0:T(1,128)S(1)} %bitcast.99, f32[16,16,512]{1,0,2:T(8,128)} %reshape.200), kind=kOutput, calls=%fused_computation.191 | convolution fusion | flops 1572864 | bytes 589824 | tf_op jit(solution)/shard_map/diz,zi->dz/dot_general | solution.py:116
  157.7 5.9 %collective-permute-start.16 = (f32[16,32]{1,0:T(8,128)S(1)}, f32[16,32]{1,0:T(8,128)S(1)}, u32[]{:S(2)}, u32[]{:S(2)}) collective-permute-start(f32[16,32]{1,0:T(8,128)S(1)} %fusion.8), channel_id=1, source_target_pairs={{0,384},{1,385},{2,386},{3,387},{4,388},{5,389},{6,390},{7,391},{8... | collective-permute-start | bytes 6152 | tf_op jit(solution)/shard_map/ppermute | solution.py:121
  169.2 3.1 collective-permute-start.21
  172.3 2.7 collective-permute-start.22
  177.5 2.6 collective-permute-done.19
  180.0 3.1 collective-permute-done.20
  185.1 50.6 %all_gather.13 = f32[128,32,16]{1,2,0:T(8,128)S(1)} all-gather(f32[1,32,16]{1,2,0:T(8,128)S(1)} %copy.35), channel_id=1, replica_groups=mesh['sec'=4,'lat'=8,'lon'=16] {'lat','lon'}, dimensions={0}, use_global_device_ids=true | all-gather | bytes 264192 | tf_op jit(solution)/shard_map/all_gather | solution.py:109
  239.7 8.4 %fusion.108 = f32[512,1,16]{2,1,0:T(1,128)S(1)} fusion(f32[512,16,1]{1,2,0:T(1,128)S(1)} %bitcast.100, f32[16,16,512]{1,0,2:T(8,128)} %reshape.200), kind=kOutput, calls=%fused_computation.192 | convolution fusion | flops 1572864 | bytes 589824 | tf_op jit(solution)/shard_map/diz,zi->dz/dot_general | solution.py:116
  250.0 5.7 %collective-permute-start.27 = (f32[16,32]{1,0:T(8,128)S(1)}, f32[16,32]{1,0:T(8,128)S(1)}, u32[]{:S(2)}, u32[]{:S(2)}) collective-permute-start(f32[16,32]{1,0:T(8,128)S(1)} %fusion.6), channel_id=1, source_target_pairs={{0,384},{1,385},{2,386},{3,387},{4,388},{5,389},{6,390},{7,391},{8... | collective-permute-start | bytes 6152 | tf_op jit(solution)/shard_map/ppermute | solution.py:121
  255.9 3.6 collective-permute-start.25
  259.6 3.1 collective-permute-start.26
  264.2 2.6 collective-permute-done.23
  266.7 3.1 collective-permute-done.24
  276.4 3.6 collective-permute-start.33
  282.9 3.1 collective-permute-done.31
  288.0 50.1 %all_gather.14 = f32[128,32,16]{1,2,0:T(8,128)S(1)} all-gather(f32[1,32,16]{1,2,0:T(8,128)S(1)} %copy.38), channel_id=1, replica_groups=mesh['sec'=4,'lat'=8,'lon'=16] {'lat','lon'}, dimensions={0}, use_global_device_ids=true | all-gather | bytes 264192 | tf_op jit(solution)/shard_map/all_gather | solution.py:109
  342.1 8.4 %fusion.109 = f32[512,1,16]{2,1,0:T(1,128)S(1)} fusion(f32[512,16,1]{1,2,0:T(1,128)S(1)} %bitcast.101, f32[16,16,512]{1,0,2:T(8,128)} %reshape.200), kind=kOutput, calls=%fused_computation.193 | convolution fusion | flops 1572864 | bytes 589824 | tf_op jit(solution)/shard_map/diz,zi->dz/dot_general | solution.py:116
  352.4 2.8 collective-permute-start.38
  355.4 3.8 collective-permute-start.36
  359.2 3.1 collective-permute-start.37
  363.8 2.6 collective-permute-done.34
  366.4 3.1 collective-permute-done.35
  376.0 3.6 collective-permute-start.44
  382.6 3.1 collective-permute-done.42
  387.6 50.1 %all_gather.15 = f32[128,32,16]{1,2,0:T(8,128)S(1)} all-gather(f32[1,32,16]{1,2,0:T(8,128)S(1)} %copy.41), channel_id=1, replica_groups=mesh['sec'=4,'lat'=8,'lon'=16] {'lat','lon'}, dimensions={0}, use_global_device_ids=true | all-gather | bytes 264192 | tf_op jit(solution)/shard_map/all_gather | solution.py:109
  441.8 8.4 %fusion.110 = f32[512,1,16]{2,1,0:T(1,128)S(1)} fusion(f32[512,16,1]{1,2,0:T(1,128)S(1)} %bitcast.98, f32[16,16,512]{1,0,2:T(8,128)} %reshape.200), kind=kOutput, calls=%fused_computation.194 | convolution fusion | flops 1572864 | bytes 589824 | tf_op jit(solution)/shard_map/diz,zi->dz/dot_general | solution.py:116
  452.0 2.8 collective-permute-start.49
  455.0 3.8 collective-permute-start.47
  458.9 3.1 collective-permute-start.48
  463.5 2.6 collective-permute-done.45
  466.0 3.1 collective-permute-done.46
  (224 shorter events, 91.5 us)
Async XLA Ops:
  7.4 14.9 %collective-permute-start.2 = (f32[75,1,128]{2,1,0:T(1,128)S(1)}, f32[75,1,128]{2,1,0:T(1,128)S(1)}, u32[]{:S(2)}, u32[]{:S(2)}) collective-permute-start(f32[75,1,128]{2,1,0:T(1,128)S(1)} %get-tuple-element.134), channel_id=1, source_target_pairs={{16,0},{32,16},{48,32},{64,48},{80,64},{96,80},{112,96},{17,1},{33... | collective-permute-start | bytes 115208 | tf_op jit(solution)/shard_map/ppermute | solution.py:23
  14.3 8.0 %collective-permute-start.3 = (f32[75,1,128]{2,1,0:T(1,128)S(1)}, f32[75,1,128]{2,1,0:T(1,128)S(1)}, u32[]{:S(2)}, u32[]{:S(2)}) collective-permute-start(f32[75,1,128]{2,1,0:T(1,128)S(1)} %get-tuple-element.135), channel_id=1, source_target_pairs={{0,16},{16,32},{32,48},{48,64},{64,80},{80,96},{96,112},{1,17},{17... | collective-permute-start | bytes 115208 | tf_op jit(solution)/shard_map/ppermute | solution.py:20
  16.4 5.9 %collective-permute-start = (f32[75,4,1]{2,1,0:T(4,128)S(1)}, f32[75,4,1]{2,1,0:T(4,128)S(1)}, u32[]{:S(2)}, u32[]{:S(2)}) collective-permute-start(f32[75,4,1]{2,1,0:T(4,128)S(1)} %get-tuple-element.130), channel_id=1, source_target_pairs={{1,0},{2,1},{3,2},{4,3},{5,4},{6,5},{7,6},{8,7},{9,8},{10,9},{11,1... | collective-permute-start | bytes 3608 | tf_op jit(solution)/shard_map/ppermute | solution.py:23
  16.4 5.9 %collective-permute-start.1 = (f32[75,4,1]{2,1,0:T(4,128)S(1)}, f32[75,4,1]{2,1,0:T(4,128)S(1)}, u32[]{:S(2)}, u32[]{:S(2)}) collective-permute-start(f32[75,4,1]{2,1,0:T(4,128)S(1)} %get-tuple-element.131), channel_id=1, source_target_pairs={{0,1},{1,2},{2,3},{3,4},{4,5},{5,6},{6,7},{7,8},{8,9},{9,10},{10,1... | collective-permute-start | bytes 3608 | tf_op jit(solution)/shard_map/ppermute | solution.py:20
  30.3 23.3 %collective-permute-start.6 = (f32[75,1,128]{2,1,0:T(1,128)S(1)}, f32[75,1,128]{2,1,0:T(1,128)S(1)}, u32[]{:S(2)}, u32[]{:S(2)}) collective-permute-start(f32[75,1,128]{2,1,0:T(1,128)S(1)} %get-tuple-element.128), channel_id=1, source_target_pairs={{16,0},{32,16},{48,32},{64,48},{80,64},{96,80},{112,96},{17,1},{33... | collective-permute-start | bytes 115208 | tf_op jit(solution)/shard_map/ppermute | solution.py:23
  34.3 19.4 %collective-permute-start.7 = (f32[75,1,128]{2,1,0:T(1,128)S(1)}, f32[75,1,128]{2,1,0:T(1,128)S(1)}, u32[]{:S(2)}, u32[]{:S(2)}) collective-permute-start(f32[75,1,128]{2,1,0:T(1,128)S(1)} %get-tuple-element.129), channel_id=1, source_target_pairs={{0,16},{16,32},{32,48},{48,64},{64,80},{80,96},{96,112},{1,17},{17... | collective-permute-start | bytes 115208 | tf_op jit(solution)/shard_map/ppermute | solution.py:20
  36.6 17.0 %collective-permute-start.4 = (f32[75,4,1]{2,1,0:T(4,128)S(1)}, f32[75,4,1]{2,1,0:T(4,128)S(1)}, u32[]{:S(2)}, u32[]{:S(2)}) collective-permute-start(f32[75,4,1]{2,1,0:T(4,128)S(1)} %get-tuple-element.124), channel_id=1, source_target_pairs={{1,0},{2,1},{3,2},{4,3},{5,4},{6,5},{7,6},{8,7},{9,8},{10,9},{11,1... | collective-permute-start | bytes 3608 | tf_op jit(solution)/shard_map/ppermute | solution.py:23
  38.9 14.7 %collective-permute-start.5 = (f32[75,4,1]{2,1,0:T(4,128)S(1)}, f32[75,4,1]{2,1,0:T(4,128)S(1)}, u32[]{:S(2)}, u32[]{:S(2)}) collective-permute-start(f32[75,4,1]{2,1,0:T(4,128)S(1)} %get-tuple-element.125), channel_id=1, source_target_pairs={{0,1},{1,2},{2,3},{3,4},{4,5},{5,6},{6,7},{7,8},{8,9},{9,10},{10,1... | collective-permute-start | bytes 3608 | tf_op jit(solution)/shard_map/ppermute | solution.py:20
  40.0 99.1 %all-to-all-start = ((f32[257,128,4]{0,2,1:T(4,128)}), f32[257,128,4]{0,2,1:T(4,128)}, u32[]{:S(2)}, u32[]{:S(2)}) async-start(f32[257,128,4]{0,2,1:T(4,128)} %pad_maximum_fusion), calls=%async_computation | async-start | bytes 1572864 | tf_op jit(solution)/shard_map/all_to_all | solution.py:98
  58.1 16.5 %collective-permute-start.10 = (f32[75,1,128]{2,1,0:T(1,128)S(1)}, f32[75,1,128]{2,1,0:T(1,128)S(1)}, u32[]{:S(2)}, u32[]{:S(2)}) collective-permute-start(f32[75,1,128]{2,1,0:T(1,128)S(1)} %get-tuple-element.122), channel_id=1, source_target_pairs={{16,0},{32,16},{48,32},{64,48},{80,64},{96,80},{112,96},{17,1},{33... | collective-permute-start | bytes 115208 | tf_op jit(solution)/shard_map/ppermute | solution.py:23
  60.9 13.7 %collective-permute-start.11 = (f32[75,1,128]{2,1,0:T(1,128)S(1)}, f32[75,1,128]{2,1,0:T(1,128)S(1)}, u32[]{:S(2)}, u32[]{:S(2)}) collective-permute-start(f32[75,1,128]{2,1,0:T(1,128)S(1)} %get-tuple-element.123), channel_id=1, source_target_pairs={{0,16},{16,32},{32,48},{48,64},{64,80},{80,96},{96,112},{1,17},{17... | collective-permute-start | bytes 115208 | tf_op jit(solution)/shard_map/ppermute | solution.py:20
  64.1 7.5 %collective-permute-start.8 = (f32[75,4,1]{2,1,0:T(4,128)S(1)}, f32[75,4,1]{2,1,0:T(4,128)S(1)}, u32[]{:S(2)}, u32[]{:S(2)}) collective-permute-start(f32[75,4,1]{2,1,0:T(4,128)S(1)} %get-tuple-element.118), channel_id=1, source_target_pairs={{1,0},{2,1},{3,2},{4,3},{5,4},{6,5},{7,6},{8,7},{9,8},{10,9},{11,1... | collective-permute-start | bytes 3608 | tf_op jit(solution)/shard_map/ppermute | solution.py:23
  66.0 8.6 %collective-permute-start.9 = (f32[75,4,1]{2,1,0:T(4,128)S(1)}, f32[75,4,1]{2,1,0:T(4,128)S(1)}, u32[]{:S(2)}, u32[]{:S(2)}) collective-permute-start(f32[75,4,1]{2,1,0:T(4,128)S(1)} %get-tuple-element.119), channel_id=1, source_target_pairs={{0,1},{1,2},{2,3},{3,4},{4,5},{5,6},{6,7},{7,8},{8,9},{9,10},{10,1... | collective-permute-start | bytes 3608 | tf_op jit(solution)/shard_map/ppermute | solution.py:20
  130.5 33.1 %collective-permute-start.14 = (f32[75,1,128]{2,1,0:T(1,128)}, f32[75,1,128]{2,1,0:T(1,128)S(1)}, u32[]{:S(2)}, u32[]{:S(2)}) collective-permute-start(f32[75,1,128]{2,1,0:T(1,128)} %get-tuple-element.116), channel_id=1, source_target_pairs={{16,0},{32,16},{48,32},{64,48},{80,64},{96,80},{112,96},{17,1},{33... | collective-permute-start | bytes 115208 | tf_op jit(solution)/shard_map/ppermute | solution.py:23
  133.6 30.1 %collective-permute-start.15 = (f32[75,1,128]{2,1,0:T(1,128)}, f32[75,1,128]{2,1,0:T(1,128)S(1)}, u32[]{:S(2)}, u32[]{:S(2)}) collective-permute-start(f32[75,1,128]{2,1,0:T(1,128)} %get-tuple-element.117), channel_id=1, source_target_pairs={{0,16},{16,32},{32,48},{48,64},{64,80},{80,96},{96,112},{1,17},{17... | collective-permute-start | bytes 115208 | tf_op jit(solution)/shard_map/ppermute | solution.py:20
  137.5 19.5 %collective-permute-start.12 = (f32[75,4,1]{2,1,0:T(4,128)}, f32[75,4,1]{2,1,0:T(4,128)}, u32[]{:S(2)}, u32[]{:S(2)}) collective-permute-start(f32[75,4,1]{2,1,0:T(4,128)} %get-tuple-element.112), channel_id=1, source_target_pairs={{1,0},{2,1},{3,2},{4,3},{5,4},{6,5},{7,6},{8,7},{9,8},{10,9},{11,1... | collective-permute-start | bytes 3608 | tf_op jit(solution)/shard_map/ppermute | solution.py:23
  138.4 19.3 %collective-permute-start.13 = (f32[75,4,1]{2,1,0:T(4,128)}, f32[75,4,1]{2,1,0:T(4,128)}, u32[]{:S(2)}, u32[]{:S(2)}) collective-permute-start(f32[75,4,1]{2,1,0:T(4,128)} %get-tuple-element.113), channel_id=1, source_target_pairs={{0,1},{1,2},{2,3},{3,4},{4,5},{5,6},{6,7},{7,8},{8,9},{9,10},{10,1... | collective-permute-start | bytes 3608 | tf_op jit(solution)/shard_map/ppermute | solution.py:20
  156.3 8.7 %collective-permute-start.18 = (f32[16,32]{1,0:T(8,128)S(1)}, f32[16,32]{1,0:T(8,128)S(1)}, u32[]{:S(2)}, u32[]{:S(2)}) collective-permute-start(f32[16,32]{1,0:T(8,128)S(1)} %fusion.8), channel_id=1, source_target_pairs={{256,384},{257,385},{258,386},{259,387},{260,388},{261,389},{262,3... | collective-permute-start | bytes 6152 | tf_op jit(solution)/shard_map/ppermute | solution.py:121
  157.0 8.0 %collective-permute-start.17 = (f32[16,32]{1,0:T(8,128)S(1)}, f32[16,32]{1,0:T(8,128)S(1)}, u32[]{:S(2)}, u32[]{:S(2)}) collective-permute-start(f32[16,32]{1,0:T(8,128)S(1)} %fusion.8), channel_id=1, source_target_pairs={{128,384},{129,385},{130,386},{131,387},{132,388},{133,389},{134,3... | collective-permute-start | bytes 6152 | tf_op jit(solution)/shard_map/ppermute | solution.py:121
  157.7 7.3 %collective-permute-start.16 = (f32[16,32]{1,0:T(8,128)S(1)}, f32[16,32]{1,0:T(8,128)S(1)}, u32[]{:S(2)}, u32[]{:S(2)}) collective-permute-start(f32[16,32]{1,0:T(8,128)S(1)} %fusion.8), channel_id=1, source_target_pairs={{0,384},{1,385},{2,386},{3,387},{4,388},{5,389},{6,390},{7,391},{8... | collective-permute-start | bytes 6152 | tf_op jit(solution)/shard_map/ppermute | solution.py:121
  169.2 14.0 %collective-permute-start.21 = (f32[75,1,128]{2,1,0:T(1,128)S(1)}, f32[75,1,128]{2,1,0:T(1,128)S(1)}, u32[]{:S(2)}, u32[]{:S(2)}) collective-permute-start(f32[75,1,128]{2,1,0:T(1,128)S(1)} %get-tuple-element.110), channel_id=1, source_target_pairs={{16,0},{32,16},{48,32},{64,48},{80,64},{96,80},{112,96},{17,1},{33... | collective-permute-start | bytes 115208 | tf_op jit(solution)/shard_map/ppermute | solution.py:23
  172.3 10.9 %collective-permute-start.22 = (f32[75,1,128]{2,1,0:T(1,128)S(1)}, f32[75,1,128]{2,1,0:T(1,128)S(1)}, u32[]{:S(2)}, u32[]{:S(2)}) collective-permute-start(f32[75,1,128]{2,1,0:T(1,128)S(1)} %get-tuple-element.111), channel_id=1, source_target_pairs={{0,16},{16,32},{32,48},{48,64},{64,80},{80,96},{96,112},{1,17},{17... | collective-permute-start | bytes 115208 | tf_op jit(solution)/shard_map/ppermute | solution.py:20
  175.2 4.9 %collective-permute-start.19 = (f32[75,4,1]{2,1,0:T(4,128)S(1)}, f32[75,4,1]{2,1,0:T(4,128)S(1)}, u32[]{:S(2)}, u32[]{:S(2)}) collective-permute-start(f32[75,4,1]{2,1,0:T(4,128)S(1)} %get-tuple-element.106), channel_id=1, source_target_pairs={{1,0},{2,1},{3,2},{4,3},{5,4},{6,5},{7,6},{8,7},{9,8},{10,9},{11,1... | collective-permute-start | bytes 3608 | tf_op jit(solution)/shard_map/ppermute | solution.py:23
  177.3 5.8 %collective-permute-start.20 = (f32[75,4,1]{2,1,0:T(4,128)S(1)}, f32[75,4,1]{2,1,0:T(4,128)S(1)}, u32[]{:S(2)}, u32[]{:S(2)}) collective-permute-start(f32[75,4,1]{2,1,0:T(4,128)S(1)} %get-tuple-element.107), channel_id=1, source_target_pairs={{0,1},{1,2},{2,3},{3,4},{4,5},{5,6},{6,7},{7,8},{8,9},{9,10},{10,1... | collective-permute-start | bytes 3608 | tf_op jit(solution)/shard_map/ppermute | solution.py:20
  248.7 14.2 %collective-permute-start.29 = (f32[16,32]{1,0:T(8,128)S(1)}, f32[16,32]{1,0:T(8,128)S(1)}, u32[]{:S(2)}, u32[]{:S(2)}) collective-permute-start(f32[16,32]{1,0:T(8,128)S(1)} %fusion.6), channel_id=1, source_target_pairs={{256,384},{257,385},{258,386},{259,387},{260,388},{261,389},{262,3... | collective-permute-start | bytes 6152 | tf_op jit(solution)/shard_map/ppermute | solution.py:121
  249.3 14.7 %collective-permute-start.28 = (f32[16,32]{1,0:T(8,128)S(1)}, f32[16,32]{1,0:T(8,128)S(1)}, u32[]{:S(2)}, u32[]{:S(2)}) collective-permute-start(f32[16,32]{1,0:T(8,128)S(1)} %fusion.6), channel_id=1, source_target_pairs={{128,384},{129,385},{130,386},{131,387},{132,388},{133,389},{134,3... | collective-permute-start | bytes 6152 | tf_op jit(solution)/shard_map/ppermute | solution.py:121
  250.0 14.0 %collective-permute-start.27 = (f32[16,32]{1,0:T(8,128)S(1)}, f32[16,32]{1,0:T(8,128)S(1)}, u32[]{:S(2)}, u32[]{:S(2)}) collective-permute-start(f32[16,32]{1,0:T(8,128)S(1)} %fusion.6), channel_id=1, source_target_pairs={{0,384},{1,385},{2,386},{3,387},{4,388},{5,389},{6,390},{7,391},{8... | collective-permute-start | bytes 6152 | tf_op jit(solution)/shard_map/ppermute | solution.py:121
  255.9 13.9 %collective-permute-start.25 = (f32[75,1,128]{2,1,0:T(1,128)S(1)}, f32[75,1,128]{2,1,0:T(1,128)S(1)}, u32[]{:S(2)}, u32[]{:S(2)}) collective-permute-start(f32[75,1,128]{2,1,0:T(1,128)S(1)} %get-tuple-element.104), channel_id=1, source_target_pairs={{16,0},{32,16},{48,32},{64,48},{80,64},{96,80},{112,96},{17,1},{33... | collective-permute-start | bytes 115208 | tf_op jit(solution)/shard_map/ppermute | solution.py:23
  259.6 10.3 %collective-permute-start.26 = (f32[75,1,128]{2,1,0:T(1,128)S(1)}, f32[75,1,128]{2,1,0:T(1,128)S(1)}, u32[]{:S(2)}, u32[]{:S(2)}) collective-permute-start(f32[75,1,128]{2,1,0:T(1,128)S(1)} %get-tuple-element.105), channel_id=1, source_target_pairs={{0,16},{16,32},{32,48},{48,64},{64,80},{80,96},{96,112},{1,17},{17... | collective-permute-start | bytes 115208 | tf_op jit(solution)/shard_map/ppermute | solution.py:20
  264.0 5.8 %collective-permute-start.24 = (f32[75,4,1]{2,1,0:T(4,128)S(1)}, f32[75,4,1]{2,1,0:T(4,128)S(1)}, u32[]{:S(2)}, u32[]{:S(2)}) collective-permute-start(f32[75,4,1]{2,1,0:T(4,128)S(1)} %get-tuple-element.101), channel_id=1, source_target_pairs={{0,1},{1,2},{2,3},{3,4},{4,5},{5,6},{6,7},{7,8},{8,9},{9,10},{10,1... | collective-permute-start | bytes 3608 | tf_op jit(solution)/shard_map/ppermute | solution.py:20
  274.2 11.9 %collective-permute-start.32 = (f32[75,1,128]{2,1,0:T(1,128)S(1)}, f32[75,1,128]{2,1,0:T(1,128)S(1)}, u32[]{:S(2)}, u32[]{:S(2)}) collective-permute-start(f32[75,1,128]{2,1,0:T(1,128)S(1)} %get-tuple-element.96), channel_id=1, source_target_pairs={{16,0},{32,16},{48,32},{64,48},{80,64},{96,80},{112,96},{17,1},{33... | collective-permute-start | bytes 115208 | tf_op jit(solution)/shard_map/ppermute | solution.py:23
  276.4 9.7 %collective-permute-start.33 = (f32[75,1,128]{2,1,0:T(1,128)S(1)}, f32[75,1,128]{2,1,0:T(1,128)S(1)}, u32[]{:S(2)}, u32[]{:S(2)}) collective-permute-start(f32[75,1,128]{2,1,0:T(1,128)S(1)} %get-tuple-element.97), channel_id=1, source_target_pairs={{0,16},{16,32},{32,48},{48,64},{64,80},{80,96},{96,112},{1,17},{17... | collective-permute-start | bytes 115208 | tf_op jit(solution)/shard_map/ppermute | solution.py:20
  280.2 5.9 %collective-permute-start.31 = (f32[75,4,1]{2,1,0:T(4,128)S(1)}, f32[75,4,1]{2,1,0:T(4,128)S(1)}, u32[]{:S(2)}, u32[]{:S(2)}) collective-permute-start(f32[75,4,1]{2,1,0:T(4,128)S(1)} %get-tuple-element.93), channel_id=1, source_target_pairs={{0,1},{1,2},{2,3},{3,4},{4,5},{5,6},{6,7},{7,8},{8,9},{9,10},{10,1... | collective-permute-start | bytes 3608 | tf_op jit(solution)/shard_map/ppermute | solution.py:20
  351.0 11.5 %collective-permute-start.40 = (f32[16,32]{1,0:T(8,128)S(1)}, f32[16,32]{1,0:T(8,128)S(1)}, u32[]{:S(2)}, u32[]{:S(2)}) collective-permute-start(f32[16,32]{1,0:T(8,128)S(1)} %fusion.4), channel_id=1, source_target_pairs={{256,384},{257,385},{258,386},{259,387},{260,388},{261,389},{262,3... | collective-permute-start | bytes 6152 | tf_op jit(solution)/shard_map/ppermute | solution.py:121
  351.7 11.9 %collective-permute-start.39 = (f32[16,32]{1,0:T(8,128)S(1)}, f32[16,32]{1,0:T(8,128)S(1)}, u32[]{:S(2)}, u32[]{:S(2)}) collective-permute-start(f32[16,32]{1,0:T(8,128)S(1)} %fusion.4), channel_id=1, source_target_pairs={{128,384},{129,385},{130,386},{131,387},{132,388},{133,389},{134,3... | collective-permute-start | bytes 6152 | tf_op jit(solution)/shard_map/ppermute | solution.py:121
  352.4 11.3 %collective-permute-start.38 = (f32[16,32]{1,0:T(8,128)S(1)}, f32[16,32]{1,0:T(8,128)S(1)}, u32[]{:S(2)}, u32[]{:S(2)}) collective-permute-start(f32[16,32]{1,0:T(8,128)S(1)} %fusion.4), channel_id=1, source_target_pairs={{0,384},{1,385},{2,386},{3,387},{4,388},{5,389},{6,390},{7,391},{8... | collective-permute-start | bytes 6152 | tf_op jit(solution)/shard_map/ppermute | solution.py:121
  355.4 14.1 %collective-permute-start.36 = (f32[75,1,128]{2,1,0:T(1,128)S(1)}, f32[75,1,128]{2,1,0:T(1,128)S(1)}, u32[]{:S(2)}, u32[]{:S(2)}) collective-permute-start(f32[75,1,128]{2,1,0:T(1,128)S(1)} %get-tuple-element.90), channel_id=1, source_target_pairs={{16,0},{32,16},{48,32},{64,48},{80,64},{96,80},{112,96},{17,1},{33... | collective-permute-start | bytes 115208 | tf_op jit(solution)/shard_map/ppermute | solution.py:23
  359.2 10.3 %collective-permute-start.37 = (f32[75,1,128]{2,1,0:T(1,128)S(1)}, f32[75,1,128]{2,1,0:T(1,128)S(1)}, u32[]{:S(2)}, u32[]{:S(2)}) collective-permute-start(f32[75,1,128]{2,1,0:T(1,128)S(1)} %get-tuple-element.91), channel_id=1, source_target_pairs={{0,16},{16,32},{32,48},{48,64},{64,80},{80,96},{96,112},{1,17},{17... | collective-permute-start | bytes 115208 | tf_op jit(solution)/shard_map/ppermute | solution.py:20
  363.6 5.8 %collective-permute-start.35 = (f32[75,4,1]{2,1,0:T(4,128)S(1)}, f32[75,4,1]{2,1,0:T(4,128)S(1)}, u32[]{:S(2)}, u32[]{:S(2)}) collective-permute-start(f32[75,4,1]{2,1,0:T(4,128)S(1)} %get-tuple-element.87), channel_id=1, source_target_pairs={{0,1},{1,2},{2,3},{3,4},{4,5},{5,6},{6,7},{7,8},{8,9},{9,10},{10,1... | collective-permute-start | bytes 3608 | tf_op jit(solution)/shard_map/ppermute | solution.py:20
  373.8 11.9 %collective-permute-start.43 = (f32[75,1,128]{2,1,0:T(1,128)S(1)}, f32[75,1,128]{2,1,0:T(1,128)S(1)}, u32[]{:S(2)}, u32[]{:S(2)}) collective-permute-start(f32[75,1,128]{2,1,0:T(1,128)S(1)} %get-tuple-element.82), channel_id=1, source_target_pairs={{16,0},{32,16},{48,32},{64,48},{80,64},{96,80},{112,96},{17,1},{33... | collective-permute-start | bytes 115208 | tf_op jit(solution)/shard_map/ppermute | solution.py:23
  376.0 9.7 %collective-permute-start.44 = (f32[75,1,128]{2,1,0:T(1,128)S(1)}, f32[75,1,128]{2,1,0:T(1,128)S(1)}, u32[]{:S(2)}, u32[]{:S(2)}) collective-permute-start(f32[75,1,128]{2,1,0:T(1,128)S(1)} %get-tuple-element.83), channel_id=1, source_target_pairs={{0,16},{16,32},{32,48},{48,64},{64,80},{80,96},{96,112},{1,17},{17... | collective-permute-start | bytes 115208 | tf_op jit(solution)/shard_map/ppermute | solution.py:20
  379.9 5.9 %collective-permute-start.42 = (f32[75,4,1]{2,1,0:T(4,128)S(1)}, f32[75,4,1]{2,1,0:T(4,128)S(1)}, u32[]{:S(2)}, u32[]{:S(2)}) collective-permute-start(f32[75,4,1]{2,1,0:T(4,128)S(1)} %get-tuple-element.79), channel_id=1, source_target_pairs={{0,1},{1,2},{2,3},{3,4},{4,5},{5,6},{6,7},{7,8},{8,9},{9,10},{10,1... | collective-permute-start | bytes 3608 | tf_op jit(solution)/shard_map/ppermute | solution.py:20
  450.7 11.5 %collective-permute-start.51 = (f32[16,32]{1,0:T(8,128)S(1)}, f32[16,32]{1,0:T(8,128)S(1)}, u32[]{:S(2)}, u32[]{:S(2)}) collective-permute-start(f32[16,32]{1,0:T(8,128)S(1)} %fusion.2), channel_id=1, source_target_pairs={{256,384},{257,385},{258,386},{259,387},{260,388},{261,389},{262,3... | collective-permute-start | bytes 6152 | tf_op jit(solution)/shard_map/ppermute | solution.py:121
  451.4 11.9 %collective-permute-start.50 = (f32[16,32]{1,0:T(8,128)S(1)}, f32[16,32]{1,0:T(8,128)S(1)}, u32[]{:S(2)}, u32[]{:S(2)}) collective-permute-start(f32[16,32]{1,0:T(8,128)S(1)} %fusion.2), channel_id=1, source_target_pairs={{128,384},{129,385},{130,386},{131,387},{132,388},{133,389},{134,3... | collective-permute-start | bytes 6152 | tf_op jit(solution)/shard_map/ppermute | solution.py:121
  452.0 11.3 %collective-permute-start.49 = (f32[16,32]{1,0:T(8,128)S(1)}, f32[16,32]{1,0:T(8,128)S(1)}, u32[]{:S(2)}, u32[]{:S(2)}) collective-permute-start(f32[16,32]{1,0:T(8,128)S(1)} %fusion.2), channel_id=1, source_target_pairs={{0,384},{1,385},{2,386},{3,387},{4,388},{5,389},{6,390},{7,391},{8... | collective-permute-start | bytes 6152 | tf_op jit(solution)/shard_map/ppermute | solution.py:121
  455.0 14.1 %collective-permute-start.47 = (f32[75,1,128]{2,1,0:T(1,128)S(1)}, f32[75,1,128]{2,1,0:T(1,128)S(1)}, u32[]{:S(2)}, u32[]{:S(2)}) collective-permute-start(f32[75,1,128]{2,1,0:T(1,128)S(1)} %get-tuple-element.76), channel_id=1, source_target_pairs={{16,0},{32,16},{48,32},{64,48},{80,64},{96,80},{112,96},{17,1},{33... | collective-permute-start | bytes 115208 | tf_op jit(solution)/shard_map/ppermute | solution.py:23
  458.9 10.3 %collective-permute-start.48 = (f32[75,1,128]{2,1,0:T(1,128)S(1)}, f32[75,1,128]{2,1,0:T(1,128)S(1)}, u32[]{:S(2)}, u32[]{:S(2)}) collective-permute-start(f32[75,1,128]{2,1,0:T(1,128)S(1)} %get-tuple-element.77), channel_id=1, source_target_pairs={{0,16},{16,32},{32,48},{48,64},{64,80},{80,96},{96,112},{1,17},{17... | collective-permute-start | bytes 115208 | tf_op jit(solution)/shard_map/ppermute | solution.py:20
  463.3 5.8 %collective-permute-start.46 = (f32[75,4,1]{2,1,0:T(4,128)S(1)}, f32[75,4,1]{2,1,0:T(4,128)S(1)}, u32[]{:S(2)}, u32[]{:S(2)}) collective-permute-start(f32[75,4,1]{2,1,0:T(4,128)S(1)} %get-tuple-element.73), channel_id=1, source_target_pairs={{0,1},{1,2},{2,3},{3,4},{4,5},{5,6},{6,7},{7,8},{8,9},{9,10},{10,1... | collective-permute-start | bytes 3608 | tf_op jit(solution)/shard_map/ppermute | solution.py:20
  (27 other events, 388.5 us)

commit v3 on v1

--- a/solution.py
+++ b/solution.py
@@ -96,13 +96,11 @@
     surface = field_part[-1].reshape(-1, block_cells)
     gathered = jnp.take(surface, source_block.reshape(-1), axis=0)
     contribution = jnp.einsum("diz,zi->dz", weight_table, gathered, precision=lax.Precision.HIGHEST)
-    return lax.all_to_all(
-        contribution.reshape(block_cells, peer_count, capacity),
-        ("lat", "lon"),
-        split_axis=1,
-        concat_axis=1,
-        tiled=True,
-    )
+    lat_count, lon_count = lax.axis_size("lat"), lax.axis_size("lon")
+    staged = contribution.reshape(block_cells, lat_count, lon_count, capacity)
+    staged = lax.all_to_all(staged, "lon", split_axis=2, concat_axis=2, tiled=True)
+    staged = lax.all_to_all(staged, "lat", split_axis=1, concat_axis=1, tiled=True)
+    return staged.reshape(block_cells, peer_count, capacity)
 
 
 def reduce_forcing(received, one_hot):

time: 283 us -> 270 us (0.954)
  waiting for transfers between devices: 58.4 us -> 26.6 us
  local copies, waits for them, and re-layouts: 15.8 us -> 27.5 us
  other arithmetic: 25.6 us -> 33.4 us
  starting transfers between devices: 141 us -> 145 us
  matrix products: 12.6 us -> 9.65 us
    all_to_all x4 -> x8, waiting for transfers between devices: 28.3 us -> 11.8 us  [the longest x4 8.4 us: couple(): lax.all_to_all(staged, 'lat', split_axis=1, concat_axis=1, tiled=True)]
    ppermute x20, starting transfers between devices: 35.8 us -> 48.5 us  [extended(): lax.ppermute(lax.slice_in_dim(block, block.shape[dim] - width, None, axis...]
    all_to_all x4 -> x8, starting transfers between devices: 58.6 us -> 48.8 us  [the longest x4 31.2 us: couple(): lax.all_to_all(staged, 'lat', split_axis=1, concat_axis=1, tiled=True)]
    ppermute x20, waiting for transfers between devices: 9.65 us -> 1.27 us  [extended(): lax.ppermute(lax.slice_in_dim(block, block.shape[dim] - width, None, axis...]
    unnamed x37 -> x69, local copies, waits for them, and re-layouts: 2.27 us -> 9.47 us
    ppermute x12, waiting for transfers between devices: 20.4 us -> 13.4 us  [reduce_forcing(): lax.ppermute(accumulated, 'sec', [(s, section_count - 1)])]
    all_to_all x0 -> x8, other arithmetic: none -> 6.1 us  [the longest x4 3.05 us: couple(): lax.all_to_all(staged, 'lon', split_axis=2, concat_axis=2, tiled=True)]
    dot_general x4, matrix products: 10.5 us -> 7.59 us  [couple(): jnp.einsum('diz,zi->dz', weight_table, gathered, precision=lax.Precision....]
  transfers between devices with their start and end apart: 56 -> 60, of which waited for: 22 -> 17; matrix products, arithmetic and copies ran while one was open for 11% -> 16% of each run, Pallas kernels for 3% -> 3%
where the time goes in v3:
time: 270 us; the launch traced here: 268 us
  starting transfers between devices  145 us (54%)
  other arithmetic  33.4 us (12%)
  local copies, waits for them, and re-layouts  27.5 us (10%)
  waiting for transfers between devices  26.6 us (10%)
  Pallas kernels  24.8 us (9%)
  matrix products  9.65 us (4%)
    ppermute x20, starting transfers between devices, extended(): lax.ppermute(lax.slice_in_dim(block, block.shape[dim] - width, None, axis...  48.5 us
    ppermute x20, starting transfers between devices, extended(): lax.ppermute(lax.slice_in_dim(block, 0, width, axis=dim), axis, backward)  32 us
    all_to_all x4, starting transfers between devices, couple(): lax.all_to_all(staged, 'lat', split_axis=1, concat_axis=1, tiled=True)  31.2 us
    pallas_call x10, Pallas kernels, column_solve(): pl.pallas_call(_solve_kernel, out_shape=jax.ShapeDtypeStruct(right.shape,...  22.5 us
    all_to_all x4, starting transfers between devices, couple(): lax.all_to_all(staged, 'lon', split_axis=2, concat_axis=2, tiled=True)  17.6 us
    ppermute x12, starting transfers between devices, reduce_forcing(): lax.ppermute(accumulated, 'sec', [(s, section_count - 1)])  15.6 us
    ppermute x12, waiting for transfers between devices, reduce_forcing(): lax.ppermute(accumulated, 'sec', [(s, section_count - 1)])  13.4 us
    mul x8, other arithmetic, substep(): return advect(mixed_adj, east_part, north_part) * keep_factor  10.9 us
  transfers between devices with their start and end apart: 60, of which 17 were waited for; matrix products, arithmetic and copies ran while one was open for 16% of the time, Pallas kernels for 3%

profile of v3, /device:TPU:6, one launch (start us, length us, event | category | flops | bytes accessed | tf_op | source)
XLA Modules:
  0.0 268.2 jit_solution(8337746160494547188)
XLA Ops:
  1.6 2.3 shard_map.91
  4.0 2.3 shard_map.92
  7.5 2.9 %collective-permute-start = (f32[75,4,1]{2,1,0:T(4,128)S(1)}, f32[75,4,1]{2,1,0:T(4,128)S(1)}, u32[]{:S(2)}, u32[]{:S(2)}) collective-permute-start(f32[75,4,1]{2,1,0:T(4,128)S(1)} %get-tuple-element.128), channel_id=1, source_target_pairs={{1,0},{2,1},{3,2},{4,3},{5,4},{6,5},{7,6},{8,7},{9,8},{10,9},{11,1... | collective-permute-start | bytes 3608 | tf_op jit(solution)/shard_map/ppermute | solution.py:23
  11.8 4.9 %collective-permute-start.3 = (f32[75,1,128]{2,1,0:T(1,128)S(1)}, f32[75,1,128]{2,1,0:T(1,128)S(1)}, u32[]{:S(2)}, u32[]{:S(2)}) collective-permute-start(f32[75,1,128]{2,1,0:T(1,128)S(1)} %get-tuple-element.133), channel_id=1, source_target_pairs={{0,16},{16,32},{32,48},{48,64},{64,80},{80,96},{96,112},{1,17},{17... | collective-permute-start | bytes 115208 | tf_op jit(solution)/shard_map/ppermute | solution.py:20
  18.3 1.9 fusion.69.x_ref
  20.2 2.3 shard_map.93
  24.4 2.1 collective-permute-start.4
  27.8 4.9 %collective-permute-start.7 = (f32[75,1,128]{2,1,0:T(1,128)S(1)}, f32[75,1,128]{2,1,0:T(1,128)S(1)}, u32[]{:S(2)}, u32[]{:S(2)}) collective-permute-start(f32[75,1,128]{2,1,0:T(1,128)S(1)} %get-tuple-element.127), channel_id=1, source_target_pairs={{0,16},{16,32},{32,48},{48,64},{64,80},{80,96},{96,112},{1,17},{17... | collective-permute-start | bytes 115208 | tf_op jit(solution)/shard_map/ppermute | solution.py:20
  32.8 2.1 copy.67
  37.2 2.2 shard_map.94
  41.3 2.7 collective-permute-start.8
  45.4 4.9 %collective-permute-start.11 = (f32[75,1,128]{2,1,0:T(1,128)S(1)}, f32[75,1,128]{2,1,0:T(1,128)S(1)}, u32[]{:S(2)}, u32[]{:S(2)}) collective-permute-start(f32[75,1,128]{2,1,0:T(1,128)S(1)} %get-tuple-element.121), channel_id=1, source_target_pairs={{0,16},{16,32},{32,48},{48,64},{64,80},{80,96},{96,112},{1,17},{17... | collective-permute-start | bytes 115208 | tf_op jit(solution)/shard_map/ppermute | solution.py:20
  55.3 4.3 %all-to-all-start = ((f32[16,1,512]{2,1,0:T(1,128)}), f32[16,1,512]{2,1,0:T(1,128)S(1)}, u32[]{:S(2)}, u32[]{:S(2)}) async-start(f32[16,1,512]{2,1,0:T(1,128)} %reshape.278), calls=%async_computation | async-start | bytes 65536 | tf_op jit(solution)/shard_map/all_to_all | solution.py:101
  59.6 2.2 shard_map.95
  63.7 2.9 %collective-permute-start.12 = (f32[75,4,1]{2,1,0:T(4,128)}, f32[75,4,1]{2,1,0:T(4,128)S(1)}, u32[]{:S(2)}, u32[]{:S(2)}) collective-permute-start(f32[75,4,1]{2,1,0:T(4,128)} %get-tuple-element.110), channel_id=1, source_target_pairs={{1,0},{2,1},{3,2},{4,3},{5,4},{6,5},{7,6},{8,7},{9,8},{10,9},{11,1... | collective-permute-start | bytes 3608 | tf_op jit(solution)/shard_map/ppermute | solution.py:23
  69.8 10.8 %all-to-all-start.1 = ((f32[8,1,1024]{2,1,0:T(1,128)}), f32[8,1,1024]{2,1,0:T(1,128)S(1)}, u32[]{:S(2)}, u32[]{:S(2)}) async-start(f32[8,1,1024]{2,1,0:T(1,128)} %reshape.280), calls=%async_computation.1 | async-start | bytes 65536 | tf_op jit(solution)/shard_map/all_to_all | solution.py:102
  81.9 4.6 %collective-permute-start.15 = (f32[75,1,128]{2,1,0:T(1,128)S(1)}, f32[75,1,128]{2,1,0:T(1,128)S(1)}, u32[]{:S(2)}, u32[]{:S(2)}) collective-permute-start(f32[75,1,128]{2,1,0:T(1,128)S(1)} %get-tuple-element.115), channel_id=1, source_target_pairs={{0,16},{16,32},{32,48},{48,64},{64,80},{80,96},{96,112},{1,17},{17... | collective-permute-start | bytes 115208 | tf_op jit(solution)/shard_map/ppermute | solution.py:20
  86.5 2.1 all-to-all-done.1
  100.2 2.2 shard_map.96
  106.7 4.7 %collective-permute-start.22 = (f32[75,1,128]{2,1,0:T(1,128)S(1)}, f32[75,1,128]{2,1,0:T(1,128)S(1)}, u32[]{:S(2)}, u32[]{:S(2)}) collective-permute-start(f32[75,1,128]{2,1,0:T(1,128)S(1)} %get-tuple-element.109), channel_id=1, source_target_pairs={{0,16},{16,32},{32,48},{48,64},{64,80},{80,96},{96,112},{1,17},{17... | collective-permute-start | bytes 115208 | tf_op jit(solution)/shard_map/ppermute | solution.py:20
  111.4 1.9 fusion.107
  114.3 1.9 fusion.43.x_ref
  116.2 4.4 %all-to-all-start.2 = ((f32[16,1,512]{2,1,0:T(1,128)}), f32[16,1,512]{2,1,0:T(1,128)S(1)}, u32[]{:S(2)}, u32[]{:S(2)}) async-start(f32[16,1,512]{2,1,0:T(1,128)} %reshape.282), calls=%async_computation.2 | async-start | bytes 65536 | tf_op jit(solution)/shard_map/all_to_all | solution.py:101
  120.6 2.2 shard_map.97
  124.7 2.9 %collective-permute-start.23 = (f32[75,4,1]{2,1,0:T(4,128)}, f32[75,4,1]{2,1,0:T(4,128)S(1)}, u32[]{:S(2)}, u32[]{:S(2)}) collective-permute-start(f32[75,4,1]{2,1,0:T(4,128)} %get-tuple-element.98), channel_id=1, source_target_pairs={{1,0},{2,1},{3,2},{4,3},{5,4},{6,5},{7,6},{8,7},{9,8},{10,9},{11,1... | collective-permute-start | bytes 3608 | tf_op jit(solution)/shard_map/ppermute | solution.py:23
  130.2 6.8 %all-to-all-start.3 = ((f32[8,1,1024]{2,1,0:T(1,128)}), f32[8,1,1024]{2,1,0:T(1,128)S(1)}, u32[]{:S(2)}, u32[]{:S(2)}) async-start(f32[8,1,1024]{2,1,0:T(1,128)} %reshape.284), calls=%async_computation.3 | async-start | bytes 65536 | tf_op jit(solution)/shard_map/all_to_all | solution.py:102
  138.3 4.6 %collective-permute-start.26 = (f32[75,1,128]{2,1,0:T(1,128)S(1)}, f32[75,1,128]{2,1,0:T(1,128)S(1)}, u32[]{:S(2)}, u32[]{:S(2)}) collective-permute-start(f32[75,1,128]{2,1,0:T(1,128)S(1)} %get-tuple-element.103), channel_id=1, source_target_pairs={{0,16},{16,32},{32,48},{48,64},{64,80},{80,96},{96,112},{1,17},{17... | collective-permute-start | bytes 115208 | tf_op jit(solution)/shard_map/ppermute | solution.py:20
  142.8 2.1 all-to-all-done.3
  156.6 2.2 shard_map.98
  163.1 4.5 %collective-permute-start.33 = (f32[75,1,128]{2,1,0:T(1,128)S(1)}, f32[75,1,128]{2,1,0:T(1,128)S(1)}, u32[]{:S(2)}, u32[]{:S(2)}) collective-permute-start(f32[75,1,128]{2,1,0:T(1,128)S(1)} %get-tuple-element.95), channel_id=1, source_target_pairs={{0,16},{16,32},{32,48},{48,64},{64,80},{80,96},{96,112},{1,17},{17... | collective-permute-start | bytes 115208 | tf_op jit(solution)/shard_map/ppermute | solution.py:20
  167.6 1.9 fusion.108
  170.5 1.9 fusion.31.x_ref
  172.4 4.4 %all-to-all-start.4 = ((f32[16,1,512]{2,1,0:T(1,128)}), f32[16,1,512]{2,1,0:T(1,128)S(1)}, u32[]{:S(2)}, u32[]{:S(2)}) async-start(f32[16,1,512]{2,1,0:T(1,128)} %reshape.286), calls=%async_computation.4 | async-start | bytes 65536 | tf_op jit(solution)/shard_map/all_to_all | solution.py:101
  176.8 2.2 shard_map.99
  180.9 2.9 %collective-permute-start.34 = (f32[75,4,1]{2,1,0:T(4,128)}, f32[75,4,1]{2,1,0:T(4,128)S(1)}, u32[]{:S(2)}, u32[]{:S(2)}) collective-permute-start(f32[75,4,1]{2,1,0:T(4,128)} %get-tuple-element.84), channel_id=1, source_target_pairs={{1,0},{2,1},{3,2},{4,3},{5,4},{6,5},{7,6},{8,7},{9,8},{10,9},{11,1... | collective-permute-start | bytes 3608 | tf_op jit(solution)/shard_map/ppermute | solution.py:23
  186.4 6.9 %all-to-all-start.5 = ((f32[8,1,1024]{2,1,0:T(1,128)}), f32[8,1,1024]{2,1,0:T(1,128)S(1)}, u32[]{:S(2)}, u32[]{:S(2)}) async-start(f32[8,1,1024]{2,1,0:T(1,128)} %reshape.288), calls=%async_computation.5 | async-start | bytes 65536 | tf_op jit(solution)/shard_map/all_to_all | solution.py:102
  194.7 4.6 %collective-permute-start.37 = (f32[75,1,128]{2,1,0:T(1,128)S(1)}, f32[75,1,128]{2,1,0:T(1,128)S(1)}, u32[]{:S(2)}, u32[]{:S(2)}) collective-permute-start(f32[75,1,128]{2,1,0:T(1,128)S(1)} %get-tuple-element.89), channel_id=1, source_target_pairs={{0,16},{16,32},{32,48},{48,64},{64,80},{80,96},{96,112},{1,17},{17... | collective-permute-start | bytes 115208 | tf_op jit(solution)/shard_map/ppermute | solution.py:20
  199.2 2.1 all-to-all-done.5
  213.0 2.2 shard_map.100
  218.9 4.8 %collective-permute-start.44 = (f32[75,1,128]{2,1,0:T(1,128)S(1)}, f32[75,1,128]{2,1,0:T(1,128)S(1)}, u32[]{:S(2)}, u32[]{:S(2)}) collective-permute-start(f32[75,1,128]{2,1,0:T(1,128)S(1)} %get-tuple-element.81), channel_id=1, source_target_pairs={{0,16},{16,32},{32,48},{48,64},{64,80},{80,96},{96,112},{1,17},{17... | collective-permute-start | bytes 115208 | tf_op jit(solution)/shard_map/ppermute | solution.py:20
  226.5 1.9 fusion.19.x_ref
  228.4 4.4 %all-to-all-start.6 = ((f32[16,1,512]{2,1,0:T(1,128)}), f32[16,1,512]{2,1,0:T(1,128)S(1)}, u32[]{:S(2)}, u32[]{:S(2)}) async-start(f32[16,1,512]{2,1,0:T(1,128)} %reshape.290), calls=%async_computation.6 | async-start | bytes 65536 | tf_op jit(solution)/shard_map/all_to_all | solution.py:101
  232.8 2.2 shard_map.101
  236.3 2.9 %collective-permute-start.45 = (f32[75,4,1]{2,1,0:T(4,128)S(1)}, f32[75,4,1]{2,1,0:T(4,128)S(1)}, u32[]{:S(2)}, u32[]{:S(2)}) collective-permute-start(f32[75,4,1]{2,1,0:T(4,128)S(1)} %get-tuple-element.70), channel_id=1, source_target_pairs={{1,0},{2,1},{3,2},{4,3},{5,4},{6,5},{7,6},{8,7},{9,8},{10,9},{11,1... | collective-permute-start | bytes 3608 | tf_op jit(solution)/shard_map/ppermute | solution.py:23
  242.4 6.7 %all-to-all-start.7 = ((f32[8,1,1024]{2,1,0:T(1,128)}), f32[8,1,1024]{2,1,0:T(1,128)S(1)}, u32[]{:S(2)}, u32[]{:S(2)}) async-start(f32[8,1,1024]{2,1,0:T(1,128)} %reshape.292), calls=%async_computation.7 | async-start | bytes 65536 | tf_op jit(solution)/shard_map/all_to_all | solution.py:102
  250.5 4.6 %collective-permute-start.48 = (f32[75,1,128]{2,1,0:T(1,128)S(1)}, f32[75,1,128]{2,1,0:T(1,128)S(1)}, u32[]{:S(2)}, u32[]{:S(2)}) collective-permute-start(f32[75,1,128]{2,1,0:T(1,128)S(1)} %get-tuple-element.75), channel_id=1, source_target_pairs={{0,16},{16,32},{32,48},{48,64},{64,80},{80,96},{96,112},{1,17},{17... | collective-permute-start | bytes 115208 | tf_op jit(solution)/shard_map/ppermute | solution.py:20
  255.1 2.1 all-to-all-done.7
  263.3 2.4 collective-permute-done.49
  (261 shorter events, 102.8 us)
Async XLA Ops:
  7.5 9.6 %collective-permute-start = (f32[75,4,1]{2,1,0:T(4,128)S(1)}, f32[75,4,1]{2,1,0:T(4,128)S(1)}, u32[]{:S(2)}, u32[]{:S(2)}) collective-permute-start(f32[75,4,1]{2,1,0:T(4,128)S(1)} %get-tuple-element.128), channel_id=1, source_target_pairs={{1,0},{2,1},{3,2},{4,3},{5,4},{6,5},{7,6},{8,7},{9,8},{10,9},{11,1... | collective-permute-start | bytes 3608 | tf_op jit(solution)/shard_map/ppermute | solution.py:23
  24.4 10.8 %collective-permute-start.4 = (f32[75,4,1]{2,1,0:T(4,128)}, f32[75,4,1]{2,1,0:T(4,128)S(1)}, u32[]{:S(2)}, u32[]{:S(2)}) collective-permute-start(f32[75,4,1]{2,1,0:T(4,128)} %get-tuple-element.122), channel_id=1, source_target_pairs={{1,0},{2,1},{3,2},{4,3},{5,4},{6,5},{7,6},{8,7},{9,8},{10,9},{11,1... | collective-permute-start | bytes 3608 | tf_op jit(solution)/shard_map/ppermute | solution.py:23
  26.5 8.7 %collective-permute-start.5 = (f32[75,4,1]{2,1,0:T(4,128)}, f32[75,4,1]{2,1,0:T(4,128)}, u32[]{:S(2)}, u32[]{:S(2)}) collective-permute-start(f32[75,4,1]{2,1,0:T(4,128)} %get-tuple-element.123), channel_id=1, source_target_pairs={{0,1},{1,2},{2,3},{3,4},{4,5},{5,6},{6,7},{7,8},{8,9},{9,10},{10,1... | collective-permute-start | bytes 3608 | tf_op jit(solution)/shard_map/ppermute | solution.py:20
  26.5 8.7 %collective-permute-start.6 = (f32[75,1,128]{2,1,0:T(1,128)S(1)}, f32[75,1,128]{2,1,0:T(1,128)S(1)}, u32[]{:S(2)}, u32[]{:S(2)}) collective-permute-start(f32[75,1,128]{2,1,0:T(1,128)S(1)} %get-tuple-element.126), channel_id=1, source_target_pairs={{16,0},{32,16},{48,32},{64,48},{80,64},{96,80},{112,96},{17,1},{33... | collective-permute-start | bytes 115208 | tf_op jit(solution)/shard_map/ppermute | solution.py:23
  27.8 7.4 %collective-permute-start.7 = (f32[75,1,128]{2,1,0:T(1,128)S(1)}, f32[75,1,128]{2,1,0:T(1,128)S(1)}, u32[]{:S(2)}, u32[]{:S(2)}) collective-permute-start(f32[75,1,128]{2,1,0:T(1,128)S(1)} %get-tuple-element.127), channel_id=1, source_target_pairs={{0,16},{16,32},{32,48},{48,64},{64,80},{80,96},{96,112},{1,17},{17... | collective-permute-start | bytes 115208 | tf_op jit(solution)/shard_map/ppermute | solution.py:20
  41.3 12.9 %collective-permute-start.8 = (f32[75,4,1]{2,1,0:T(4,128)}, f32[75,4,1]{2,1,0:T(4,128)S(1)}, u32[]{:S(2)}, u32[]{:S(2)}) collective-permute-start(f32[75,4,1]{2,1,0:T(4,128)} %get-tuple-element.116), channel_id=1, source_target_pairs={{1,0},{2,1},{3,2},{4,3},{5,4},{6,5},{7,6},{8,7},{9,8},{10,9},{11,1... | collective-permute-start | bytes 3608 | tf_op jit(solution)/shard_map/ppermute | solution.py:23
  44.0 10.3 %collective-permute-start.9 = (f32[75,4,1]{2,1,0:T(4,128)}, f32[75,4,1]{2,1,0:T(4,128)S(1)}, u32[]{:S(2)}, u32[]{:S(2)}) collective-permute-start(f32[75,4,1]{2,1,0:T(4,128)} %get-tuple-element.117), channel_id=1, source_target_pairs={{0,1},{1,2},{2,3},{3,4},{4,5},{5,6},{6,7},{7,8},{8,9},{9,10},{10,1... | collective-permute-start | bytes 3608 | tf_op jit(solution)/shard_map/ppermute | solution.py:20
  44.1 10.2 %collective-permute-start.10 = (f32[75,1,128]{2,1,0:T(1,128)S(1)}, f32[75,1,128]{2,1,0:T(1,128)S(1)}, u32[]{:S(2)}, u32[]{:S(2)}) collective-permute-start(f32[75,1,128]{2,1,0:T(1,128)S(1)} %get-tuple-element.120), channel_id=1, source_target_pairs={{16,0},{32,16},{48,32},{64,48},{80,64},{96,80},{112,96},{17,1},{33... | collective-permute-start | bytes 115208 | tf_op jit(solution)/shard_map/ppermute | solution.py:23
  45.4 8.9 %collective-permute-start.11 = (f32[75,1,128]{2,1,0:T(1,128)S(1)}, f32[75,1,128]{2,1,0:T(1,128)S(1)}, u32[]{:S(2)}, u32[]{:S(2)}) collective-permute-start(f32[75,1,128]{2,1,0:T(1,128)S(1)} %get-tuple-element.121), channel_id=1, source_target_pairs={{0,16},{16,32},{32,48},{48,64},{64,80},{80,96},{96,112},{1,17},{17... | collective-permute-start | bytes 115208 | tf_op jit(solution)/shard_map/ppermute | solution.py:20
  55.3 12.0 %all-to-all-start = ((f32[16,1,512]{2,1,0:T(1,128)}), f32[16,1,512]{2,1,0:T(1,128)S(1)}, u32[]{:S(2)}, u32[]{:S(2)}) async-start(f32[16,1,512]{2,1,0:T(1,128)} %reshape.278), calls=%async_computation | async-start | bytes 65536 | tf_op jit(solution)/shard_map/all_to_all | solution.py:101
  63.7 27.9 %collective-permute-start.12 = (f32[75,4,1]{2,1,0:T(4,128)}, f32[75,4,1]{2,1,0:T(4,128)S(1)}, u32[]{:S(2)}, u32[]{:S(2)}) collective-permute-start(f32[75,4,1]{2,1,0:T(4,128)} %get-tuple-element.110), channel_id=1, source_target_pairs={{1,0},{2,1},{3,2},{4,3},{5,4},{6,5},{7,6},{8,7},{9,8},{10,9},{11,1... | collective-permute-start | bytes 3608 | tf_op jit(solution)/shard_map/ppermute | solution.py:23
  66.6 26.4 %collective-permute-start.13 = (f32[75,4,1]{2,1,0:T(4,128)}, f32[75,4,1]{2,1,0:T(4,128)}, u32[]{:S(2)}, u32[]{:S(2)}) collective-permute-start(f32[75,4,1]{2,1,0:T(4,128)} %get-tuple-element.111), channel_id=1, source_target_pairs={{0,1},{1,2},{2,3},{3,4},{4,5},{5,6},{6,7},{7,8},{8,9},{9,10},{10,1... | collective-permute-start | bytes 3608 | tf_op jit(solution)/shard_map/ppermute | solution.py:20
  69.8 18.8 %all-to-all-start.1 = ((f32[8,1,1024]{2,1,0:T(1,128)}), f32[8,1,1024]{2,1,0:T(1,128)S(1)}, u32[]{:S(2)}, u32[]{:S(2)}) async-start(f32[8,1,1024]{2,1,0:T(1,128)} %reshape.280), calls=%async_computation.1 | async-start | bytes 65536 | tf_op jit(solution)/shard_map/all_to_all | solution.py:102
  80.6 13.7 %collective-permute-start.14 = (f32[75,1,128]{2,1,0:T(1,128)S(1)}, f32[75,1,128]{2,1,0:T(1,128)S(1)}, u32[]{:S(2)}, u32[]{:S(2)}) collective-permute-start(f32[75,1,128]{2,1,0:T(1,128)S(1)} %get-tuple-element.114), channel_id=1, source_target_pairs={{16,0},{32,16},{48,32},{64,48},{80,64},{96,80},{112,96},{17,1},{33... | collective-permute-start | bytes 115208 | tf_op jit(solution)/shard_map/ppermute | solution.py:23
  81.9 12.4 %collective-permute-start.15 = (f32[75,1,128]{2,1,0:T(1,128)S(1)}, f32[75,1,128]{2,1,0:T(1,128)S(1)}, u32[]{:S(2)}, u32[]{:S(2)}) collective-permute-start(f32[75,1,128]{2,1,0:T(1,128)S(1)} %get-tuple-element.115), channel_id=1, source_target_pairs={{0,16},{16,32},{32,48},{48,64},{64,80},{80,96},{96,112},{1,17},{17... | collective-permute-start | bytes 115208 | tf_op jit(solution)/shard_map/ppermute | solution.py:20
  91.7 7.0 %collective-permute-start.17 = (f32[16,32]{1,0:T(8,128)S(1)}, f32[16,32]{1,0:T(8,128)S(1)}, u32[]{:S(2)}, u32[]{:S(2)}) collective-permute-start(f32[16,32]{1,0:T(8,128)S(1)} %fusion.7), channel_id=1, source_target_pairs={{128,384},{129,385},{130,386},{131,387},{132,388},{133,389},{134,3... | collective-permute-start | bytes 6152 | tf_op jit(solution)/shard_map/ppermute | solution.py:113
  104.2 10.0 %collective-permute-start.19 = (f32[75,4,1]{2,1,0:T(4,128)}, f32[75,4,1]{2,1,0:T(4,128)S(1)}, u32[]{:S(2)}, u32[]{:S(2)}) collective-permute-start(f32[75,4,1]{2,1,0:T(4,128)} %get-tuple-element.104), channel_id=1, source_target_pairs={{1,0},{2,1},{3,2},{4,3},{5,4},{6,5},{7,6},{8,7},{9,8},{10,9},{11,1... | collective-permute-start | bytes 3608 | tf_op jit(solution)/shard_map/ppermute | solution.py:23
  104.2 10.0 %collective-permute-start.20 = (f32[75,4,1]{2,1,0:T(4,128)}, f32[75,4,1]{2,1,0:T(4,128)}, u32[]{:S(2)}, u32[]{:S(2)}) collective-permute-start(f32[75,4,1]{2,1,0:T(4,128)} %get-tuple-element.105), channel_id=1, source_target_pairs={{0,1},{1,2},{2,3},{3,4},{4,5},{5,6},{6,7},{7,8},{8,9},{9,10},{10,1... | collective-permute-start | bytes 3608 | tf_op jit(solution)/shard_map/ppermute | solution.py:20
  105.4 8.8 %collective-permute-start.21 = (f32[75,1,128]{2,1,0:T(1,128)}, f32[75,1,128]{2,1,0:T(1,128)S(1)}, u32[]{:S(2)}, u32[]{:S(2)}) collective-permute-start(f32[75,1,128]{2,1,0:T(1,128)} %get-tuple-element.108), channel_id=1, source_target_pairs={{16,0},{32,16},{48,32},{64,48},{80,64},{96,80},{112,96},{17,1},{33... | collective-permute-start | bytes 115208 | tf_op jit(solution)/shard_map/ppermute | solution.py:23
  106.7 7.6 %collective-permute-start.22 = (f32[75,1,128]{2,1,0:T(1,128)S(1)}, f32[75,1,128]{2,1,0:T(1,128)S(1)}, u32[]{:S(2)}, u32[]{:S(2)}) collective-permute-start(f32[75,1,128]{2,1,0:T(1,128)S(1)} %get-tuple-element.109), channel_id=1, source_target_pairs={{0,16},{16,32},{32,48},{48,64},{64,80},{80,96},{96,112},{1,17},{17... | collective-permute-start | bytes 115208 | tf_op jit(solution)/shard_map/ppermute | solution.py:20
  116.2 12.1 %all-to-all-start.2 = ((f32[16,1,512]{2,1,0:T(1,128)}), f32[16,1,512]{2,1,0:T(1,128)S(1)}, u32[]{:S(2)}, u32[]{:S(2)}) async-start(f32[16,1,512]{2,1,0:T(1,128)} %reshape.282), calls=%async_computation.2 | async-start | bytes 65536 | tf_op jit(solution)/shard_map/all_to_all | solution.py:101
  124.7 23.3 %collective-permute-start.23 = (f32[75,4,1]{2,1,0:T(4,128)}, f32[75,4,1]{2,1,0:T(4,128)S(1)}, u32[]{:S(2)}, u32[]{:S(2)}) collective-permute-start(f32[75,4,1]{2,1,0:T(4,128)} %get-tuple-element.98), channel_id=1, source_target_pairs={{1,0},{2,1},{3,2},{4,3},{5,4},{6,5},{7,6},{8,7},{9,8},{10,9},{11,1... | collective-permute-start | bytes 3608 | tf_op jit(solution)/shard_map/ppermute | solution.py:23
  127.6 21.7 %collective-permute-start.24 = (f32[75,4,1]{2,1,0:T(4,128)}, f32[75,4,1]{2,1,0:T(4,128)}, u32[]{:S(2)}, u32[]{:S(2)}) collective-permute-start(f32[75,4,1]{2,1,0:T(4,128)} %get-tuple-element.99), channel_id=1, source_target_pairs={{0,1},{1,2},{2,3},{3,4},{4,5},{5,6},{6,7},{7,8},{8,9},{9,10},{10,1... | collective-permute-start | bytes 3608 | tf_op jit(solution)/shard_map/ppermute | solution.py:20
  130.2 14.8 %all-to-all-start.3 = ((f32[8,1,1024]{2,1,0:T(1,128)}), f32[8,1,1024]{2,1,0:T(1,128)S(1)}, u32[]{:S(2)}, u32[]{:S(2)}) async-start(f32[8,1,1024]{2,1,0:T(1,128)} %reshape.284), calls=%async_computation.3 | async-start | bytes 65536 | tf_op jit(solution)/shard_map/all_to_all | solution.py:102
  137.0 13.7 %collective-permute-start.25 = (f32[75,1,128]{2,1,0:T(1,128)S(1)}, f32[75,1,128]{2,1,0:T(1,128)S(1)}, u32[]{:S(2)}, u32[]{:S(2)}) collective-permute-start(f32[75,1,128]{2,1,0:T(1,128)S(1)} %get-tuple-element.102), channel_id=1, source_target_pairs={{16,0},{32,16},{48,32},{64,48},{80,64},{96,80},{112,96},{17,1},{33... | collective-permute-start | bytes 115208 | tf_op jit(solution)/shard_map/ppermute | solution.py:23
  138.3 12.4 %collective-permute-start.26 = (f32[75,1,128]{2,1,0:T(1,128)S(1)}, f32[75,1,128]{2,1,0:T(1,128)S(1)}, u32[]{:S(2)}, u32[]{:S(2)}) collective-permute-start(f32[75,1,128]{2,1,0:T(1,128)S(1)} %get-tuple-element.103), channel_id=1, source_target_pairs={{0,16},{16,32},{32,48},{48,64},{64,80},{80,96},{96,112},{1,17},{17... | collective-permute-start | bytes 115208 | tf_op jit(solution)/shard_map/ppermute | solution.py:20
  148.0 7.0 %collective-permute-start.28 = (f32[16,32]{1,0:T(8,128)S(1)}, f32[16,32]{1,0:T(8,128)S(1)}, u32[]{:S(2)}, u32[]{:S(2)}) collective-permute-start(f32[16,32]{1,0:T(8,128)S(1)} %fusion.5), channel_id=1, source_target_pairs={{128,384},{129,385},{130,386},{131,387},{132,388},{133,389},{134,3... | collective-permute-start | bytes 6152 | tf_op jit(solution)/shard_map/ppermute | solution.py:113
  160.6 9.8 %collective-permute-start.30 = (f32[75,4,1]{2,1,0:T(4,128)}, f32[75,4,1]{2,1,0:T(4,128)S(1)}, u32[]{:S(2)}, u32[]{:S(2)}) collective-permute-start(f32[75,4,1]{2,1,0:T(4,128)} %get-tuple-element.90), channel_id=1, source_target_pairs={{1,0},{2,1},{3,2},{4,3},{5,4},{6,5},{7,6},{8,7},{9,8},{10,9},{11,1... | collective-permute-start | bytes 3608 | tf_op jit(solution)/shard_map/ppermute | solution.py:23
  160.6 9.8 %collective-permute-start.31 = (f32[75,4,1]{2,1,0:T(4,128)}, f32[75,4,1]{2,1,0:T(4,128)}, u32[]{:S(2)}, u32[]{:S(2)}) collective-permute-start(f32[75,4,1]{2,1,0:T(4,128)} %get-tuple-element.91), channel_id=1, source_target_pairs={{0,1},{1,2},{2,3},{3,4},{4,5},{5,6},{6,7},{7,8},{8,9},{9,10},{10,1... | collective-permute-start | bytes 3608 | tf_op jit(solution)/shard_map/ppermute | solution.py:20
  161.8 8.7 %collective-permute-start.32 = (f32[75,1,128]{2,1,0:T(1,128)}, f32[75,1,128]{2,1,0:T(1,128)S(1)}, u32[]{:S(2)}, u32[]{:S(2)}) collective-permute-start(f32[75,1,128]{2,1,0:T(1,128)} %get-tuple-element.94), channel_id=1, source_target_pairs={{16,0},{32,16},{48,32},{64,48},{80,64},{96,80},{112,96},{17,1},{33... | collective-permute-start | bytes 115208 | tf_op jit(solution)/shard_map/ppermute | solution.py:23
  163.1 7.4 %collective-permute-start.33 = (f32[75,1,128]{2,1,0:T(1,128)S(1)}, f32[75,1,128]{2,1,0:T(1,128)S(1)}, u32[]{:S(2)}, u32[]{:S(2)}) collective-permute-start(f32[75,1,128]{2,1,0:T(1,128)S(1)} %get-tuple-element.95), channel_id=1, source_target_pairs={{0,16},{16,32},{32,48},{48,64},{64,80},{80,96},{96,112},{1,17},{17... | collective-permute-start | bytes 115208 | tf_op jit(solution)/shard_map/ppermute | solution.py:20
  172.4 12.1 %all-to-all-start.4 = ((f32[16,1,512]{2,1,0:T(1,128)}), f32[16,1,512]{2,1,0:T(1,128)S(1)}, u32[]{:S(2)}, u32[]{:S(2)}) async-start(f32[16,1,512]{2,1,0:T(1,128)} %reshape.286), calls=%async_computation.4 | async-start | bytes 65536 | tf_op jit(solution)/shard_map/all_to_all | solution.py:101
  180.9 23.5 %collective-permute-start.34 = (f32[75,4,1]{2,1,0:T(4,128)}, f32[75,4,1]{2,1,0:T(4,128)S(1)}, u32[]{:S(2)}, u32[]{:S(2)}) collective-permute-start(f32[75,4,1]{2,1,0:T(4,128)} %get-tuple-element.84), channel_id=1, source_target_pairs={{1,0},{2,1},{3,2},{4,3},{5,4},{6,5},{7,6},{8,7},{9,8},{10,9},{11,1... | collective-permute-start | bytes 3608 | tf_op jit(solution)/shard_map/ppermute | solution.py:23
  183.8 21.9 %collective-permute-start.35 = (f32[75,4,1]{2,1,0:T(4,128)}, f32[75,4,1]{2,1,0:T(4,128)}, u32[]{:S(2)}, u32[]{:S(2)}) collective-permute-start(f32[75,4,1]{2,1,0:T(4,128)} %get-tuple-element.85), channel_id=1, source_target_pairs={{0,1},{1,2},{2,3},{3,4},{4,5},{5,6},{6,7},{7,8},{8,9},{9,10},{10,1... | collective-permute-start | bytes 3608 | tf_op jit(solution)/shard_map/ppermute | solution.py:20
  186.4 15.0 %all-to-all-start.5 = ((f32[8,1,1024]{2,1,0:T(1,128)}), f32[8,1,1024]{2,1,0:T(1,128)S(1)}, u32[]{:S(2)}, u32[]{:S(2)}) async-start(f32[8,1,1024]{2,1,0:T(1,128)} %reshape.288), calls=%async_computation.5 | async-start | bytes 65536 | tf_op jit(solution)/shard_map/all_to_all | solution.py:102
  193.4 13.7 %collective-permute-start.36 = (f32[75,1,128]{2,1,0:T(1,128)S(1)}, f32[75,1,128]{2,1,0:T(1,128)S(1)}, u32[]{:S(2)}, u32[]{:S(2)}) collective-permute-start(f32[75,1,128]{2,1,0:T(1,128)S(1)} %get-tuple-element.88), channel_id=1, source_target_pairs={{16,0},{32,16},{48,32},{64,48},{80,64},{96,80},{112,96},{17,1},{33... | collective-permute-start | bytes 115208 | tf_op jit(solution)/shard_map/ppermute | solution.py:23
  194.7 12.4 %collective-permute-start.37 = (f32[75,1,128]{2,1,0:T(1,128)S(1)}, f32[75,1,128]{2,1,0:T(1,128)S(1)}, u32[]{:S(2)}, u32[]{:S(2)}) collective-permute-start(f32[75,1,128]{2,1,0:T(1,128)S(1)} %get-tuple-element.89), channel_id=1, source_target_pairs={{0,16},{16,32},{32,48},{48,64},{64,80},{80,96},{96,112},{1,17},{17... | collective-permute-start | bytes 115208 | tf_op jit(solution)/shard_map/ppermute | solution.py:20
  204.4 7.0 %collective-permute-start.39 = (f32[16,32]{1,0:T(8,128)S(1)}, f32[16,32]{1,0:T(8,128)S(1)}, u32[]{:S(2)}, u32[]{:S(2)}) collective-permute-start(f32[16,32]{1,0:T(8,128)S(1)} %fusion.3), channel_id=1, source_target_pairs={{128,384},{129,385},{130,386},{131,387},{132,388},{133,389},{134,3... | collective-permute-start | bytes 6152 | tf_op jit(solution)/shard_map/ppermute | solution.py:113
  217.0 9.4 %collective-permute-start.41 = (f32[75,4,1]{2,1,0:T(4,128)}, f32[75,4,1]{2,1,0:T(4,128)S(1)}, u32[]{:S(2)}, u32[]{:S(2)}) collective-permute-start(f32[75,4,1]{2,1,0:T(4,128)} %get-tuple-element.76), channel_id=1, source_target_pairs={{1,0},{2,1},{3,2},{4,3},{5,4},{6,5},{7,6},{8,7},{9,8},{10,9},{11,1... | collective-permute-start | bytes 3608 | tf_op jit(solution)/shard_map/ppermute | solution.py:23
  217.0 9.4 %collective-permute-start.42 = (f32[75,4,1]{2,1,0:T(4,128)}, f32[75,4,1]{2,1,0:T(4,128)}, u32[]{:S(2)}, u32[]{:S(2)}) collective-permute-start(f32[75,4,1]{2,1,0:T(4,128)} %get-tuple-element.77), channel_id=1, source_target_pairs={{0,1},{1,2},{2,3},{3,4},{4,5},{5,6},{6,7},{7,8},{8,9},{9,10},{10,1... | collective-permute-start | bytes 3608 | tf_op jit(solution)/shard_map/ppermute | solution.py:20
  217.6 8.9 %collective-permute-start.43 = (f32[75,1,128]{2,1,0:T(1,128)S(1)}, f32[75,1,128]{2,1,0:T(1,128)S(1)}, u32[]{:S(2)}, u32[]{:S(2)}) collective-permute-start(f32[75,1,128]{2,1,0:T(1,128)S(1)} %get-tuple-element.80), channel_id=1, source_target_pairs={{16,0},{32,16},{48,32},{64,48},{80,64},{96,80},{112,96},{17,1},{33... | collective-permute-start | bytes 115208 | tf_op jit(solution)/shard_map/ppermute | solution.py:23
  218.9 7.6 %collective-permute-start.44 = (f32[75,1,128]{2,1,0:T(1,128)S(1)}, f32[75,1,128]{2,1,0:T(1,128)S(1)}, u32[]{:S(2)}, u32[]{:S(2)}) collective-permute-start(f32[75,1,128]{2,1,0:T(1,128)S(1)} %get-tuple-element.81), channel_id=1, source_target_pairs={{0,16},{16,32},{32,48},{48,64},{64,80},{80,96},{96,112},{1,17},{17... | collective-permute-start | bytes 115208 | tf_op jit(solution)/shard_map/ppermute | solution.py:20
  228.4 12.1 %all-to-all-start.6 = ((f32[16,1,512]{2,1,0:T(1,128)}), f32[16,1,512]{2,1,0:T(1,128)S(1)}, u32[]{:S(2)}, u32[]{:S(2)}) async-start(f32[16,1,512]{2,1,0:T(1,128)} %reshape.290), calls=%async_computation.6 | async-start | bytes 65536 | tf_op jit(solution)/shard_map/all_to_all | solution.py:101
  236.3 24.0 %collective-permute-start.45 = (f32[75,4,1]{2,1,0:T(4,128)S(1)}, f32[75,4,1]{2,1,0:T(4,128)S(1)}, u32[]{:S(2)}, u32[]{:S(2)}) collective-permute-start(f32[75,4,1]{2,1,0:T(4,128)S(1)} %get-tuple-element.70), channel_id=1, source_target_pairs={{1,0},{2,1},{3,2},{4,3},{5,4},{6,5},{7,6},{8,7},{9,8},{10,9},{11,1... | collective-permute-start | bytes 3608 | tf_op jit(solution)/shard_map/ppermute | solution.py:23
  239.2 22.4 %collective-permute-start.46 = (f32[75,4,1]{2,1,0:T(4,128)S(1)}, f32[75,4,1]{2,1,0:T(4,128)S(1)}, u32[]{:S(2)}, u32[]{:S(2)}) collective-permute-start(f32[75,4,1]{2,1,0:T(4,128)S(1)} %get-tuple-element.71), channel_id=1, source_target_pairs={{0,1},{1,2},{2,3},{3,4},{4,5},{5,6},{6,7},{7,8},{8,9},{9,10},{10,1... | collective-permute-start | bytes 3608 | tf_op jit(solution)/shard_map/ppermute | solution.py:20
  242.4 14.8 %all-to-all-start.7 = ((f32[8,1,1024]{2,1,0:T(1,128)}), f32[8,1,1024]{2,1,0:T(1,128)S(1)}, u32[]{:S(2)}, u32[]{:S(2)}) async-start(f32[8,1,1024]{2,1,0:T(1,128)} %reshape.292), calls=%async_computation.7 | async-start | bytes 65536 | tf_op jit(solution)/shard_map/all_to_all | solution.py:102
  249.2 13.7 %collective-permute-start.47 = (f32[75,1,128]{2,1,0:T(1,128)S(1)}, f32[75,1,128]{2,1,0:T(1,128)S(1)}, u32[]{:S(2)}, u32[]{:S(2)}) collective-permute-start(f32[75,1,128]{2,1,0:T(1,128)S(1)} %get-tuple-element.74), channel_id=1, source_target_pairs={{16,0},{32,16},{48,32},{64,48},{80,64},{96,80},{112,96},{17,1},{33... | collective-permute-start | bytes 115208 | tf_op jit(solution)/shard_map/ppermute | solution.py:23
  250.5 12.4 %collective-permute-start.48 = (f32[75,1,128]{2,1,0:T(1,128)S(1)}, f32[75,1,128]{2,1,0:T(1,128)S(1)}, u32[]{:S(2)}, u32[]{:S(2)}) collective-permute-start(f32[75,1,128]{2,1,0:T(1,128)S(1)} %get-tuple-element.75), channel_id=1, source_target_pairs={{0,16},{16,32},{32,48},{48,64},{64,80},{80,96},{96,112},{1,17},{17... | collective-permute-start | bytes 115208 | tf_op jit(solution)/shard_map/ppermute | solution.py:20
  (35 other events, 404.0 us)

commit v4 on v3

--- a/solution.py
+++ b/solution.py
@@ -7,7 +7,7 @@
 
 NCPL = 4
 NSUB = 2
-SKEW = 2
+SKEW = 1
 
 
 def extended(block, sides, width, periodic):

time: 270 us -> 281 us (1.041)
  waiting for transfers between devices: 26.6 us -> 63 us
  starting transfers between devices: 145 us -> 130 us
  other arithmetic: 33.4 us -> 24.1 us
    all_to_all x4, waiting for transfers between devices: 8.4 us -> 27.8 us  [couple(): lax.all_to_all(staged, 'lat', split_axis=1, concat_axis=1, tiled=True)]
    ppermute x20 -> x18, waiting for transfers between devices: 1.27 us -> 10.7 us  [extended(): lax.ppermute(lax.slice_in_dim(block, block.shape[dim] - width, None, axis...]
    all_to_all x4, starting transfers between devices: 31.2 us -> 23.9 us  [couple(): lax.all_to_all(staged, 'lat', split_axis=1, concat_axis=1, tiled=True)]
    ppermute x20 -> x18, waiting for transfers between devices: 0.05 us -> 6.72 us  [extended(): lax.ppermute(lax.slice_in_dim(block, 0, width, axis=dim), axis, backward)]
    ppermute x20 -> x18, starting transfers between devices: 48.5 us -> 43.5 us  [extended(): lax.ppermute(lax.slice_in_dim(block, block.shape[dim] - width, None, axis...]
    mul x10 -> x9, other arithmetic: 10.3 us -> 5.36 us  [advect(): east_flux = east_speed * mixed_adj]
    ppermute x12, waiting for transfers between devices: 13.4 us -> 17.8 us  [reduce_forcing(): lax.ppermute(accumulated, 'sec', [(s, section_count - 1)])]
    unnamed x69 -> x64, local copies, waits for them, and re-layouts: 9.47 us -> 13.4 us
  transfers between devices with their start and end apart: 60 -> 56, of which waited for: 17 -> 19; matrix products, arithmetic and copies ran while one was open for 16% -> 7% of each run, Pallas kernels for 3% -> 0%
where the time goes in v4:
time: 281 us; the launch traced here: 280 us
  starting transfers between devices  130 us (46%)
  waiting for transfers between devices  63 us (22%)
  local copies, waits for them, and re-layouts  29.1 us (10%)
  other arithmetic  24.1 us (9%)
  Pallas kernels  22.5 us (8%)
  matrix products  9.65 us (3%)
    ppermute x18, starting transfers between devices, extended(): lax.ppermute(lax.slice_in_dim(block, block.shape[dim] - width, None, axis...  43.5 us
    ppermute x18, starting transfers between devices, extended(): lax.ppermute(lax.slice_in_dim(block, 0, width, axis=dim), axis, backward)  28.1 us
    all_to_all x4, waiting for transfers between devices, couple(): lax.all_to_all(staged, 'lat', split_axis=1, concat_axis=1, tiled=True)  27.8 us
    all_to_all x4, starting transfers between devices, couple(): lax.all_to_all(staged, 'lat', split_axis=1, concat_axis=1, tiled=True)  23.9 us
    pallas_call x9, Pallas kernels, column_solve(): pl.pallas_call(_solve_kernel, out_shape=jax.ShapeDtypeStruct(right.shape,...  20.1 us
    all_to_all x4, starting transfers between devices, couple(): lax.all_to_all(staged, 'lon', split_axis=2, concat_axis=2, tiled=True)  18.9 us
    ppermute x12, waiting for transfers between devices, reduce_forcing(): lax.ppermute(accumulated, 'sec', [(s, section_count - 1)])  17.8 us
    ppermute x12, starting transfers between devices, reduce_forcing(): lax.ppermute(accumulated, 'sec', [(s, section_count - 1)])  15.6 us
  transfers between devices with their start and end apart: 56, of which 19 were waited for; matrix products, arithmetic and copies ran while one was open for 7% of the time, Pallas kernels for 0%

profile of v4, /device:TPU:6, one launch (start us, length us, event | category | flops | bytes accessed | tf_op | source)
XLA Modules:
  0.0 279.6 jit_solution(5355275314404132036)
XLA Ops:
  1.6 2.3 shard_map.91
  4.0 2.3 shard_map.92
  7.5 2.9 %collective-permute-start = (f32[75,4,1]{2,1,0:T(4,128)S(1)}, f32[75,4,1]{2,1,0:T(4,128)S(1)}, u32[]{:S(2)}, u32[]{:S(2)}) collective-permute-start(f32[75,4,1]{2,1,0:T(4,128)S(1)} %get-tuple-element.116), channel_id=1, source_target_pairs={{1,0},{2,1},{3,2},{4,3},{5,4},{6,5},{7,6},{8,7},{9,8},{10,9},{11,1... | collective-permute-start | bytes 3608 | tf_op jit(solution)/shard_map/ppermute | solution.py:23
  11.8 4.9 %collective-permute-start.3 = (f32[75,1,128]{2,1,0:T(1,128)S(1)}, f32[75,1,128]{2,1,0:T(1,128)S(1)}, u32[]{:S(2)}, u32[]{:S(2)}) collective-permute-start(f32[75,1,128]{2,1,0:T(1,128)S(1)} %get-tuple-element.121), channel_id=1, source_target_pairs={{0,16},{16,32},{32,48},{48,64},{64,80},{80,96},{96,112},{1,17},{17... | collective-permute-start | bytes 115208 | tf_op jit(solution)/shard_map/ppermute | solution.py:20
  20.2 2.2 shard_map.93
  24.4 2.1 collective-permute-start.4
  27.9 4.9 %collective-permute-start.7 = (f32[75,1,128]{2,1,0:T(1,128)S(1)}, f32[75,1,128]{2,1,0:T(1,128)S(1)}, u32[]{:S(2)}, u32[]{:S(2)}) collective-permute-start(f32[75,1,128]{2,1,0:T(1,128)S(1)} %get-tuple-element.115), channel_id=1, source_target_pairs={{0,16},{16,32},{32,48},{48,64},{64,80},{80,96},{96,112},{1,17},{17... | collective-permute-start | bytes 115208 | tf_op jit(solution)/shard_map/ppermute | solution.py:20
  32.8 2.1 copy.67
  36.3 2.2 shard_map.94
  42.6 4.3 %all-to-all-start = ((f32[16,1,512]{2,1,0:T(1,128)}), f32[16,1,512]{2,1,0:T(1,128)S(1)}, u32[]{:S(2)}, u32[]{:S(2)}) async-start(f32[16,1,512]{2,1,0:T(1,128)} %reshape.278), calls=%async_computation | async-start | bytes 65536 | tf_op jit(solution)/shard_map/all_to_all | solution.py:101
  47.9 2.9 %collective-permute-start.8 = (f32[75,4,1]{2,1,0:T(4,128)}, f32[75,4,1]{2,1,0:T(4,128)S(1)}, u32[]{:S(2)}, u32[]{:S(2)}) collective-permute-start(f32[75,4,1]{2,1,0:T(4,128)} %get-tuple-element.104), channel_id=1, source_target_pairs={{1,0},{2,1},{3,2},{4,3},{5,4},{6,5},{7,6},{8,7},{9,8},{10,9},{11,1... | collective-permute-start | bytes 3608 | tf_op jit(solution)/shard_map/ppermute | solution.py:23
  52.7 4.9 %collective-permute-start.11 = (f32[75,1,128]{2,1,0:T(1,128)S(1)}, f32[75,1,128]{2,1,0:T(1,128)S(1)}, u32[]{:S(2)}, u32[]{:S(2)}) collective-permute-start(f32[75,1,128]{2,1,0:T(1,128)S(1)} %get-tuple-element.109), channel_id=1, source_target_pairs={{0,16},{16,32},{32,48},{48,64},{64,80},{80,96},{96,112},{1,17},{17... | collective-permute-start | bytes 115208 | tf_op jit(solution)/shard_map/ppermute | solution.py:20
  59.9 11.4 %all-to-all-start.1 = ((f32[8,1,1024]{2,1,0:T(1,128)}), f32[8,1,1024]{2,1,0:T(1,128)S(1)}, u32[]{:S(2)}, u32[]{:S(2)}) async-start(f32[8,1,1024]{2,1,0:T(1,128)} %reshape.280), calls=%async_computation.1 | async-start | bytes 65536 | tf_op jit(solution)/shard_map/all_to_all | solution.py:102
  72.6 6.7 %all-to-all-done.1 = f32[8,1,1024]{2,1,0:T(1,128)S(1)} async-done(((f32[8,1,1024]{2,1,0:T(1,128)}), f32[8,1,1024]{2,1,0:T(1,128)S(1)}, u32[]{:S(2)}, u32[]{:S(2)}) %all-to-all-start.1) | async-done | bytes 32800 | tf_op jit(solution)/shard_map/all_to_all | solution.py:102
  85.0 2.9 %collective-permute-done.12 = f32[16,32]{1,0:T(8,128)S(1)} collective-permute-done((f32[16,32]{1,0:T(8,128)S(1)}, f32[16,32]{1,0:T(8,128)S(1)}, u32[]{:S(2)}, u32[]{:S(2)}) %collective-permute-start.12) | collective-permute-done | bytes 2080 | tf_op jit(solution)/shard_map/ppermute | solution.py:113
  90.3 2.2 shard_map.95
  94.9 4.5 %collective-permute-start.18 = (f32[75,1,128]{2,1,0:T(1,128)S(1)}, f32[75,1,128]{2,1,0:T(1,128)S(1)}, u32[]{:S(2)}, u32[]{:S(2)}) collective-permute-start(f32[75,1,128]{2,1,0:T(1,128)S(1)} %get-tuple-element.103), channel_id=1, source_target_pairs={{0,16},{16,32},{32,48},{48,64},{64,80},{80,96},{96,112},{1,17},{17... | collective-permute-start | bytes 115208 | tf_op jit(solution)/shard_map/ppermute | solution.py:20
  100.1 2.2 collective-permute-done.15
  102.3 3.1 %collective-permute-done.16 = f32[75,4,1]{2,1,0:T(4,128)S(1)} collective-permute-done((f32[75,4,1]{2,1,0:T(4,128)S(1)}, f32[75,4,1]{2,1,0:T(4,128)S(1)}, u32[]{:S(2)}, u32[]{:S(2)}) %collective-permute-start.16) | collective-permute-done | bytes 1232 | tf_op jit(solution)/shard_map/ppermute | solution.py:20
  107.4 2.2 shard_map.96
  113.7 4.9 %all-to-all-start.2 = ((f32[16,1,512]{2,1,0:T(1,128)}), f32[16,1,512]{2,1,0:T(1,128)S(1)}, u32[]{:S(2)}, u32[]{:S(2)}) async-start(f32[16,1,512]{2,1,0:T(1,128)} %reshape.282), calls=%async_computation.2 | async-start | bytes 65536 | tf_op jit(solution)/shard_map/all_to_all | solution.py:101
  119.5 2.9 %collective-permute-start.19 = (f32[75,4,1]{2,1,0:T(4,128)}, f32[75,4,1]{2,1,0:T(4,128)S(1)}, u32[]{:S(2)}, u32[]{:S(2)}) collective-permute-start(f32[75,4,1]{2,1,0:T(4,128)} %get-tuple-element.92), channel_id=1, source_target_pairs={{1,0},{2,1},{3,2},{4,3},{5,4},{6,5},{7,6},{8,7},{9,8},{10,9},{11,1... | collective-permute-start | bytes 3608 | tf_op jit(solution)/shard_map/ppermute | solution.py:23
  124.3 4.5 %collective-permute-start.22 = (f32[75,1,128]{2,1,0:T(1,128)S(1)}, f32[75,1,128]{2,1,0:T(1,128)S(1)}, u32[]{:S(2)}, u32[]{:S(2)}) collective-permute-start(f32[75,1,128]{2,1,0:T(1,128)S(1)} %get-tuple-element.97), channel_id=1, source_target_pairs={{0,16},{16,32},{32,48},{48,64},{64,80},{80,96},{96,112},{1,17},{17... | collective-permute-start | bytes 115208 | tf_op jit(solution)/shard_map/ppermute | solution.py:20
  130.7 4.2 %all-to-all-start.3 = ((f32[8,1,1024]{2,1,0:T(1,128)}), f32[8,1,1024]{2,1,0:T(1,128)S(1)}, u32[]{:S(2)}, u32[]{:S(2)}) async-start(f32[8,1,1024]{2,1,0:T(1,128)} %reshape.284), calls=%async_computation.3 | async-start | bytes 65536 | tf_op jit(solution)/shard_map/all_to_all | solution.py:102
  136.1 6.7 %all-to-all-done.3 = f32[8,1,1024]{2,1,0:T(1,128)S(1)} async-done(((f32[8,1,1024]{2,1,0:T(1,128)}), f32[8,1,1024]{2,1,0:T(1,128)S(1)}, u32[]{:S(2)}, u32[]{:S(2)}) %all-to-all-start.3) | async-done | bytes 32800 | tf_op jit(solution)/shard_map/all_to_all | solution.py:102
  148.5 2.9 %collective-permute-done.23 = f32[16,32]{1,0:T(8,128)S(1)} collective-permute-done((f32[16,32]{1,0:T(8,128)S(1)}, f32[16,32]{1,0:T(8,128)S(1)}, u32[]{:S(2)}, u32[]{:S(2)}) %collective-permute-start.23) | collective-permute-done | bytes 2080 | tf_op jit(solution)/shard_map/ppermute | solution.py:113
  153.8 2.2 shard_map.97
  158.4 4.5 %collective-permute-start.29 = (f32[75,1,128]{2,1,0:T(1,128)S(1)}, f32[75,1,128]{2,1,0:T(1,128)S(1)}, u32[]{:S(2)}, u32[]{:S(2)}) collective-permute-start(f32[75,1,128]{2,1,0:T(1,128)S(1)} %get-tuple-element.91), channel_id=1, source_target_pairs={{0,16},{16,32},{32,48},{48,64},{64,80},{80,96},{96,112},{1,17},{17... | collective-permute-start | bytes 115208 | tf_op jit(solution)/shard_map/ppermute | solution.py:20
  163.6 2.2 collective-permute-done.26
  165.8 3.1 %collective-permute-done.27 = f32[75,4,1]{2,1,0:T(4,128)S(1)} collective-permute-done((f32[75,4,1]{2,1,0:T(4,128)S(1)}, f32[75,4,1]{2,1,0:T(4,128)S(1)}, u32[]{:S(2)}, u32[]{:S(2)}) %collective-permute-start.27) | collective-permute-done | bytes 1232 | tf_op jit(solution)/shard_map/ppermute | solution.py:20
  170.9 2.2 shard_map.98
  177.2 4.9 %all-to-all-start.4 = ((f32[16,1,512]{2,1,0:T(1,128)}), f32[16,1,512]{2,1,0:T(1,128)S(1)}, u32[]{:S(2)}, u32[]{:S(2)}) async-start(f32[16,1,512]{2,1,0:T(1,128)} %reshape.286), calls=%async_computation.4 | async-start | bytes 65536 | tf_op jit(solution)/shard_map/all_to_all | solution.py:101
  183.0 2.9 %collective-permute-start.30 = (f32[75,4,1]{2,1,0:T(4,128)}, f32[75,4,1]{2,1,0:T(4,128)S(1)}, u32[]{:S(2)}, u32[]{:S(2)}) collective-permute-start(f32[75,4,1]{2,1,0:T(4,128)} %get-tuple-element.80), channel_id=1, source_target_pairs={{1,0},{2,1},{3,2},{4,3},{5,4},{6,5},{7,6},{8,7},{9,8},{10,9},{11,1... | collective-permute-start | bytes 3608 | tf_op jit(solution)/shard_map/ppermute | solution.py:23
  187.8 4.5 %collective-permute-start.33 = (f32[75,1,128]{2,1,0:T(1,128)S(1)}, f32[75,1,128]{2,1,0:T(1,128)S(1)}, u32[]{:S(2)}, u32[]{:S(2)}) collective-permute-start(f32[75,1,128]{2,1,0:T(1,128)S(1)} %get-tuple-element.85), channel_id=1, source_target_pairs={{0,16},{16,32},{32,48},{48,64},{64,80},{80,96},{96,112},{1,17},{17... | collective-permute-start | bytes 115208 | tf_op jit(solution)/shard_map/ppermute | solution.py:20
  194.2 4.2 %all-to-all-start.5 = ((f32[8,1,1024]{2,1,0:T(1,128)}), f32[8,1,1024]{2,1,0:T(1,128)S(1)}, u32[]{:S(2)}, u32[]{:S(2)}) async-start(f32[8,1,1024]{2,1,0:T(1,128)} %reshape.288), calls=%async_computation.5 | async-start | bytes 65536 | tf_op jit(solution)/shard_map/all_to_all | solution.py:102
  199.7 6.7 %all-to-all-done.5 = f32[8,1,1024]{2,1,0:T(1,128)S(1)} async-done(((f32[8,1,1024]{2,1,0:T(1,128)}), f32[8,1,1024]{2,1,0:T(1,128)S(1)}, u32[]{:S(2)}, u32[]{:S(2)}) %all-to-all-start.5) | async-done | bytes 32800 | tf_op jit(solution)/shard_map/all_to_all | solution.py:102
  212.0 2.9 %collective-permute-done.34 = f32[16,32]{1,0:T(8,128)S(1)} collective-permute-done((f32[16,32]{1,0:T(8,128)S(1)}, f32[16,32]{1,0:T(8,128)S(1)}, u32[]{:S(2)}, u32[]{:S(2)}) %collective-permute-start.34) | collective-permute-done | bytes 2080 | tf_op jit(solution)/shard_map/ppermute | solution.py:113
  217.3 2.2 shard_map.99
  221.9 4.5 %collective-permute-start.40 = (f32[75,1,128]{2,1,0:T(1,128)S(1)}, f32[75,1,128]{2,1,0:T(1,128)S(1)}, u32[]{:S(2)}, u32[]{:S(2)}) collective-permute-start(f32[75,1,128]{2,1,0:T(1,128)S(1)} %get-tuple-element.79), channel_id=1, source_target_pairs={{0,16},{16,32},{32,48},{48,64},{64,80},{80,96},{96,112},{1,17},{17... | collective-permute-start | bytes 115208 | tf_op jit(solution)/shard_map/ppermute | solution.py:20
  227.1 2.2 collective-permute-done.37
  229.4 3.1 %collective-permute-done.38 = f32[75,4,1]{2,1,0:T(4,128)S(1)} collective-permute-done((f32[75,4,1]{2,1,0:T(4,128)S(1)}, f32[75,4,1]{2,1,0:T(4,128)S(1)}, u32[]{:S(2)}, u32[]{:S(2)}) %collective-permute-start.38) | collective-permute-done | bytes 1232 | tf_op jit(solution)/shard_map/ppermute | solution.py:20
  234.4 2.2 shard_map.100
  240.7 4.9 %all-to-all-start.6 = ((f32[16,1,512]{2,1,0:T(1,128)}), f32[16,1,512]{2,1,0:T(1,128)S(1)}, u32[]{:S(2)}, u32[]{:S(2)}) async-start(f32[16,1,512]{2,1,0:T(1,128)} %reshape.290), calls=%async_computation.6 | async-start | bytes 65536 | tf_op jit(solution)/shard_map/all_to_all | solution.py:101
  245.8 2.9 %collective-permute-start.41 = (f32[75,4,1]{2,1,0:T(4,128)S(1)}, f32[75,4,1]{2,1,0:T(4,128)S(1)}, u32[]{:S(2)}, u32[]{:S(2)}) collective-permute-start(f32[75,4,1]{2,1,0:T(4,128)S(1)} %get-tuple-element.68), channel_id=1, source_target_pairs={{1,0},{2,1},{3,2},{4,3},{5,4},{6,5},{7,6},{8,7},{9,8},{10,9},{11,1... | collective-permute-start | bytes 3608 | tf_op jit(solution)/shard_map/ppermute | solution.py:23
  250.1 4.5 %collective-permute-start.44 = (f32[75,1,128]{2,1,0:T(1,128)S(1)}, f32[75,1,128]{2,1,0:T(1,128)S(1)}, u32[]{:S(2)}, u32[]{:S(2)}) collective-permute-start(f32[75,1,128]{2,1,0:T(1,128)S(1)} %get-tuple-element.73), channel_id=1, source_target_pairs={{0,16},{16,32},{32,48},{48,64},{64,80},{80,96},{96,112},{1,17},{17... | collective-permute-start | bytes 115208 | tf_op jit(solution)/shard_map/ppermute | solution.py:20
  256.5 4.2 %all-to-all-start.7 = ((f32[8,1,1024]{2,1,0:T(1,128)}), f32[8,1,1024]{2,1,0:T(1,128)S(1)}, u32[]{:S(2)}, u32[]{:S(2)}) async-start(f32[8,1,1024]{2,1,0:T(1,128)} %reshape.292), calls=%async_computation.7 | async-start | bytes 65536 | tf_op jit(solution)/shard_map/all_to_all | solution.py:102
  261.0 7.6 %all-to-all-done.7 = f32[8,1,1024]{2,1,0:T(1,128)S(1)} async-done(((f32[8,1,1024]{2,1,0:T(1,128)}), f32[8,1,1024]{2,1,0:T(1,128)S(1)}, u32[]{:S(2)}, u32[]{:S(2)}) %all-to-all-start.7) | async-done | bytes 32800 | tf_op jit(solution)/shard_map/all_to_all | solution.py:102
  274.3 2.9 %collective-permute-done.45 = f32[16,32]{1,0:T(8,128)S(1)} collective-permute-done((f32[16,32]{1,0:T(8,128)S(1)}, f32[16,32]{1,0:T(8,128)S(1)}, u32[]{:S(2)}, u32[]{:S(2)}) %collective-permute-start.45) | collective-permute-done | bytes 2080 | tf_op jit(solution)/shard_map/ppermute | solution.py:113
  (246 shorter events, 97.2 us)
Async XLA Ops:
  7.5 9.6 %collective-permute-start = (f32[75,4,1]{2,1,0:T(4,128)S(1)}, f32[75,4,1]{2,1,0:T(4,128)S(1)}, u32[]{:S(2)}, u32[]{:S(2)}) collective-permute-start(f32[75,4,1]{2,1,0:T(4,128)S(1)} %get-tuple-element.116), channel_id=1, source_target_pairs={{1,0},{2,1},{3,2},{4,3},{5,4},{6,5},{7,6},{8,7},{9,8},{10,9},{11,1... | collective-permute-start | bytes 3608 | tf_op jit(solution)/shard_map/ppermute | solution.py:23
  10.4 6.7 %collective-permute-start.1 = (f32[75,4,1]{2,1,0:T(4,128)S(1)}, f32[75,4,1]{2,1,0:T(4,128)S(1)}, u32[]{:S(2)}, u32[]{:S(2)}) collective-permute-start(f32[75,4,1]{2,1,0:T(4,128)S(1)} %get-tuple-element.117), channel_id=1, source_target_pairs={{0,1},{1,2},{2,3},{3,4},{4,5},{5,6},{6,7},{7,8},{8,9},{9,10},{10,1... | collective-permute-start | bytes 3608 | tf_op jit(solution)/shard_map/ppermute | solution.py:20
  10.5 6.6 %collective-permute-start.2 = (f32[75,1,128]{2,1,0:T(1,128)S(1)}, f32[75,1,128]{2,1,0:T(1,128)S(1)}, u32[]{:S(2)}, u32[]{:S(2)}) collective-permute-start(f32[75,1,128]{2,1,0:T(1,128)S(1)} %get-tuple-element.120), channel_id=1, source_target_pairs={{16,0},{32,16},{48,32},{64,48},{80,64},{96,80},{112,96},{17,1},{33... | collective-permute-start | bytes 115208 | tf_op jit(solution)/shard_map/ppermute | solution.py:23
  11.8 6.5 %collective-permute-start.3 = (f32[75,1,128]{2,1,0:T(1,128)S(1)}, f32[75,1,128]{2,1,0:T(1,128)S(1)}, u32[]{:S(2)}, u32[]{:S(2)}) collective-permute-start(f32[75,1,128]{2,1,0:T(1,128)S(1)} %get-tuple-element.121), channel_id=1, source_target_pairs={{0,16},{16,32},{32,48},{48,64},{64,80},{80,96},{96,112},{1,17},{17... | collective-permute-start | bytes 115208 | tf_op jit(solution)/shard_map/ppermute | solution.py:20
  24.4 10.8 %collective-permute-start.4 = (f32[75,4,1]{2,1,0:T(4,128)}, f32[75,4,1]{2,1,0:T(4,128)S(1)}, u32[]{:S(2)}, u32[]{:S(2)}) collective-permute-start(f32[75,4,1]{2,1,0:T(4,128)} %get-tuple-element.110), channel_id=1, source_target_pairs={{1,0},{2,1},{3,2},{4,3},{5,4},{6,5},{7,6},{8,7},{9,8},{10,9},{11,1... | collective-permute-start | bytes 3608 | tf_op jit(solution)/shard_map/ppermute | solution.py:23
  26.5 8.7 %collective-permute-start.5 = (f32[75,4,1]{2,1,0:T(4,128)}, f32[75,4,1]{2,1,0:T(4,128)S(1)}, u32[]{:S(2)}, u32[]{:S(2)}) collective-permute-start(f32[75,4,1]{2,1,0:T(4,128)} %get-tuple-element.111), channel_id=1, source_target_pairs={{0,1},{1,2},{2,3},{3,4},{4,5},{5,6},{6,7},{7,8},{8,9},{9,10},{10,1... | collective-permute-start | bytes 3608 | tf_op jit(solution)/shard_map/ppermute | solution.py:20
  26.6 8.7 %collective-permute-start.6 = (f32[75,1,128]{2,1,0:T(1,128)S(1)}, f32[75,1,128]{2,1,0:T(1,128)S(1)}, u32[]{:S(2)}, u32[]{:S(2)}) collective-permute-start(f32[75,1,128]{2,1,0:T(1,128)S(1)} %get-tuple-element.114), channel_id=1, source_target_pairs={{16,0},{32,16},{48,32},{64,48},{80,64},{96,80},{112,96},{17,1},{33... | collective-permute-start | bytes 115208 | tf_op jit(solution)/shard_map/ppermute | solution.py:23
  27.9 7.4 %collective-permute-start.7 = (f32[75,1,128]{2,1,0:T(1,128)S(1)}, f32[75,1,128]{2,1,0:T(1,128)S(1)}, u32[]{:S(2)}, u32[]{:S(2)}) collective-permute-start(f32[75,1,128]{2,1,0:T(1,128)S(1)} %get-tuple-element.115), channel_id=1, source_target_pairs={{0,16},{16,32},{32,48},{48,64},{64,80},{80,96},{96,112},{1,17},{17... | collective-permute-start | bytes 115208 | tf_op jit(solution)/shard_map/ppermute | solution.py:20
  42.6 15.0 %all-to-all-start = ((f32[16,1,512]{2,1,0:T(1,128)}), f32[16,1,512]{2,1,0:T(1,128)S(1)}, u32[]{:S(2)}, u32[]{:S(2)}) async-start(f32[16,1,512]{2,1,0:T(1,128)} %reshape.278), calls=%async_computation | async-start | bytes 65536 | tf_op jit(solution)/shard_map/all_to_all | solution.py:101
  47.9 23.5 %collective-permute-start.8 = (f32[75,4,1]{2,1,0:T(4,128)}, f32[75,4,1]{2,1,0:T(4,128)S(1)}, u32[]{:S(2)}, u32[]{:S(2)}) collective-permute-start(f32[75,4,1]{2,1,0:T(4,128)} %get-tuple-element.104), channel_id=1, source_target_pairs={{1,0},{2,1},{3,2},{4,3},{5,4},{6,5},{7,6},{8,7},{9,8},{10,9},{11,1... | collective-permute-start | bytes 3608 | tf_op jit(solution)/shard_map/ppermute | solution.py:23
  50.7 20.6 %collective-permute-start.9 = (f32[75,4,1]{2,1,0:T(4,128)}, f32[75,4,1]{2,1,0:T(4,128)}, u32[]{:S(2)}, u32[]{:S(2)}) collective-permute-start(f32[75,4,1]{2,1,0:T(4,128)} %get-tuple-element.105), channel_id=1, source_target_pairs={{0,1},{1,2},{2,3},{3,4},{4,5},{5,6},{6,7},{7,8},{8,9},{9,10},{10,1... | collective-permute-start | bytes 3608 | tf_op jit(solution)/shard_map/ppermute | solution.py:20
  51.4 19.9 %collective-permute-start.10 = (f32[75,1,128]{2,1,0:T(1,128)}, f32[75,1,128]{2,1,0:T(1,128)S(1)}, u32[]{:S(2)}, u32[]{:S(2)}) collective-permute-start(f32[75,1,128]{2,1,0:T(1,128)} %get-tuple-element.108), channel_id=1, source_target_pairs={{16,0},{32,16},{48,32},{64,48},{80,64},{96,80},{112,96},{17,1},{33... | collective-permute-start | bytes 115208 | tf_op jit(solution)/shard_map/ppermute | solution.py:23
  52.7 18.7 %collective-permute-start.11 = (f32[75,1,128]{2,1,0:T(1,128)S(1)}, f32[75,1,128]{2,1,0:T(1,128)S(1)}, u32[]{:S(2)}, u32[]{:S(2)}) collective-permute-start(f32[75,1,128]{2,1,0:T(1,128)S(1)} %get-tuple-element.109), channel_id=1, source_target_pairs={{0,16},{16,32},{32,48},{48,64},{64,80},{80,96},{96,112},{1,17},{17... | collective-permute-start | bytes 115208 | tf_op jit(solution)/shard_map/ppermute | solution.py:20
  59.9 19.4 %all-to-all-start.1 = ((f32[8,1,1024]{2,1,0:T(1,128)}), f32[8,1,1024]{2,1,0:T(1,128)S(1)}, u32[]{:S(2)}, u32[]{:S(2)}) async-start(f32[8,1,1024]{2,1,0:T(1,128)} %reshape.280), calls=%async_computation.1 | async-start | bytes 65536 | tf_op jit(solution)/shard_map/all_to_all | solution.py:102
  81.1 6.8 %collective-permute-start.12 = (f32[16,32]{1,0:T(8,128)S(1)}, f32[16,32]{1,0:T(8,128)S(1)}, u32[]{:S(2)}, u32[]{:S(2)}) collective-permute-start(f32[16,32]{1,0:T(8,128)S(1)} %fusion.7), channel_id=1, source_target_pairs={{0,384},{1,385},{2,386},{3,387},{4,388},{5,389},{6,390},{7,391},{8... | collective-permute-start | bytes 6152 | tf_op jit(solution)/shard_map/ppermute | solution.py:113
  82.4 7.0 %collective-permute-start.13 = (f32[16,32]{1,0:T(8,128)S(1)}, f32[16,32]{1,0:T(8,128)S(1)}, u32[]{:S(2)}, u32[]{:S(2)}) collective-permute-start(f32[16,32]{1,0:T(8,128)S(1)} %fusion.7), channel_id=1, source_target_pairs={{128,384},{129,385},{130,386},{131,387},{132,388},{133,389},{134,3... | collective-permute-start | bytes 6152 | tf_op jit(solution)/shard_map/ppermute | solution.py:113
  93.6 11.9 %collective-permute-start.17 = (f32[75,1,128]{2,1,0:T(1,128)S(1)}, f32[75,1,128]{2,1,0:T(1,128)S(1)}, u32[]{:S(2)}, u32[]{:S(2)}) collective-permute-start(f32[75,1,128]{2,1,0:T(1,128)S(1)} %get-tuple-element.102), channel_id=1, source_target_pairs={{16,0},{32,16},{48,32},{64,48},{80,64},{96,80},{112,96},{17,1},{33... | collective-permute-start | bytes 115208 | tf_op jit(solution)/shard_map/ppermute | solution.py:23
  94.9 10.6 %collective-permute-start.18 = (f32[75,1,128]{2,1,0:T(1,128)S(1)}, f32[75,1,128]{2,1,0:T(1,128)S(1)}, u32[]{:S(2)}, u32[]{:S(2)}) collective-permute-start(f32[75,1,128]{2,1,0:T(1,128)S(1)} %get-tuple-element.103), channel_id=1, source_target_pairs={{0,16},{16,32},{32,48},{48,64},{64,80},{80,96},{96,112},{1,17},{17... | collective-permute-start | bytes 115208 | tf_op jit(solution)/shard_map/ppermute | solution.py:20
  99.6 5.9 %collective-permute-start.16 = (f32[75,4,1]{2,1,0:T(4,128)S(1)}, f32[75,4,1]{2,1,0:T(4,128)S(1)}, u32[]{:S(2)}, u32[]{:S(2)}) collective-permute-start(f32[75,4,1]{2,1,0:T(4,128)S(1)} %get-tuple-element.99), channel_id=1, source_target_pairs={{0,1},{1,2},{2,3},{3,4},{4,5},{5,6},{6,7},{7,8},{8,9},{9,10},{10,1... | collective-permute-start | bytes 3608 | tf_op jit(solution)/shard_map/ppermute | solution.py:20
  113.7 15.2 %all-to-all-start.2 = ((f32[16,1,512]{2,1,0:T(1,128)}), f32[16,1,512]{2,1,0:T(1,128)S(1)}, u32[]{:S(2)}, u32[]{:S(2)}) async-start(f32[16,1,512]{2,1,0:T(1,128)} %reshape.282), calls=%async_computation.2 | async-start | bytes 65536 | tf_op jit(solution)/shard_map/all_to_all | solution.py:101
  119.5 15.4 %collective-permute-start.19 = (f32[75,4,1]{2,1,0:T(4,128)}, f32[75,4,1]{2,1,0:T(4,128)S(1)}, u32[]{:S(2)}, u32[]{:S(2)}) collective-permute-start(f32[75,4,1]{2,1,0:T(4,128)} %get-tuple-element.92), channel_id=1, source_target_pairs={{1,0},{2,1},{3,2},{4,3},{5,4},{6,5},{7,6},{8,7},{9,8},{10,9},{11,1... | collective-permute-start | bytes 3608 | tf_op jit(solution)/shard_map/ppermute | solution.py:23
  122.3 12.5 %collective-permute-start.20 = (f32[75,4,1]{2,1,0:T(4,128)}, f32[75,4,1]{2,1,0:T(4,128)}, u32[]{:S(2)}, u32[]{:S(2)}) collective-permute-start(f32[75,4,1]{2,1,0:T(4,128)} %get-tuple-element.93), channel_id=1, source_target_pairs={{0,1},{1,2},{2,3},{3,4},{4,5},{5,6},{6,7},{7,8},{8,9},{9,10},{10,1... | collective-permute-start | bytes 3608 | tf_op jit(solution)/shard_map/ppermute | solution.py:20
  123.0 11.9 %collective-permute-start.21 = (f32[75,1,128]{2,1,0:T(1,128)}, f32[75,1,128]{2,1,0:T(1,128)S(1)}, u32[]{:S(2)}, u32[]{:S(2)}) collective-permute-start(f32[75,1,128]{2,1,0:T(1,128)} %get-tuple-element.96), channel_id=1, source_target_pairs={{16,0},{32,16},{48,32},{64,48},{80,64},{96,80},{112,96},{17,1},{33... | collective-permute-start | bytes 115208 | tf_op jit(solution)/shard_map/ppermute | solution.py:23
  124.3 10.6 %collective-permute-start.22 = (f32[75,1,128]{2,1,0:T(1,128)S(1)}, f32[75,1,128]{2,1,0:T(1,128)S(1)}, u32[]{:S(2)}, u32[]{:S(2)}) collective-permute-start(f32[75,1,128]{2,1,0:T(1,128)S(1)} %get-tuple-element.97), channel_id=1, source_target_pairs={{0,16},{16,32},{32,48},{48,64},{64,80},{80,96},{96,112},{1,17},{17... | collective-permute-start | bytes 115208 | tf_op jit(solution)/shard_map/ppermute | solution.py:20
  130.7 12.2 %all-to-all-start.3 = ((f32[8,1,1024]{2,1,0:T(1,128)}), f32[8,1,1024]{2,1,0:T(1,128)S(1)}, u32[]{:S(2)}, u32[]{:S(2)}) async-start(f32[8,1,1024]{2,1,0:T(1,128)} %reshape.284), calls=%async_computation.3 | async-start | bytes 65536 | tf_op jit(solution)/shard_map/all_to_all | solution.py:102
  144.6 6.8 %collective-permute-start.23 = (f32[16,32]{1,0:T(8,128)S(1)}, f32[16,32]{1,0:T(8,128)S(1)}, u32[]{:S(2)}, u32[]{:S(2)}) collective-permute-start(f32[16,32]{1,0:T(8,128)S(1)} %fusion.5), channel_id=1, source_target_pairs={{0,384},{1,385},{2,386},{3,387},{4,388},{5,389},{6,390},{7,391},{8... | collective-permute-start | bytes 6152 | tf_op jit(solution)/shard_map/ppermute | solution.py:113
  145.9 7.0 %collective-permute-start.24 = (f32[16,32]{1,0:T(8,128)S(1)}, f32[16,32]{1,0:T(8,128)S(1)}, u32[]{:S(2)}, u32[]{:S(2)}) collective-permute-start(f32[16,32]{1,0:T(8,128)S(1)} %fusion.5), channel_id=1, source_target_pairs={{128,384},{129,385},{130,386},{131,387},{132,388},{133,389},{134,3... | collective-permute-start | bytes 6152 | tf_op jit(solution)/shard_map/ppermute | solution.py:113
  157.1 11.9 %collective-permute-start.28 = (f32[75,1,128]{2,1,0:T(1,128)S(1)}, f32[75,1,128]{2,1,0:T(1,128)S(1)}, u32[]{:S(2)}, u32[]{:S(2)}) collective-permute-start(f32[75,1,128]{2,1,0:T(1,128)S(1)} %get-tuple-element.90), channel_id=1, source_target_pairs={{16,0},{32,16},{48,32},{64,48},{80,64},{96,80},{112,96},{17,1},{33... | collective-permute-start | bytes 115208 | tf_op jit(solution)/shard_map/ppermute | solution.py:23
  158.4 10.6 %collective-permute-start.29 = (f32[75,1,128]{2,1,0:T(1,128)S(1)}, f32[75,1,128]{2,1,0:T(1,128)S(1)}, u32[]{:S(2)}, u32[]{:S(2)}) collective-permute-start(f32[75,1,128]{2,1,0:T(1,128)S(1)} %get-tuple-element.91), channel_id=1, source_target_pairs={{0,16},{16,32},{32,48},{48,64},{64,80},{80,96},{96,112},{1,17},{17... | collective-permute-start | bytes 115208 | tf_op jit(solution)/shard_map/ppermute | solution.py:20
  177.2 15.2 %all-to-all-start.4 = ((f32[16,1,512]{2,1,0:T(1,128)}), f32[16,1,512]{2,1,0:T(1,128)S(1)}, u32[]{:S(2)}, u32[]{:S(2)}) async-start(f32[16,1,512]{2,1,0:T(1,128)} %reshape.286), calls=%async_computation.4 | async-start | bytes 65536 | tf_op jit(solution)/shard_map/all_to_all | solution.py:101
  183.0 15.4 %collective-permute-start.30 = (f32[75,4,1]{2,1,0:T(4,128)}, f32[75,4,1]{2,1,0:T(4,128)S(1)}, u32[]{:S(2)}, u32[]{:S(2)}) collective-permute-start(f32[75,4,1]{2,1,0:T(4,128)} %get-tuple-element.80), channel_id=1, source_target_pairs={{1,0},{2,1},{3,2},{4,3},{5,4},{6,5},{7,6},{8,7},{9,8},{10,9},{11,1... | collective-permute-start | bytes 3608 | tf_op jit(solution)/shard_map/ppermute | solution.py:23
  185.8 12.5 %collective-permute-start.31 = (f32[75,4,1]{2,1,0:T(4,128)}, f32[75,4,1]{2,1,0:T(4,128)}, u32[]{:S(2)}, u32[]{:S(2)}) collective-permute-start(f32[75,4,1]{2,1,0:T(4,128)} %get-tuple-element.81), channel_id=1, source_target_pairs={{0,1},{1,2},{2,3},{3,4},{4,5},{5,6},{6,7},{7,8},{8,9},{9,10},{10,1... | collective-permute-start | bytes 3608 | tf_op jit(solution)/shard_map/ppermute | solution.py:20
  186.5 11.9 %collective-permute-start.32 = (f32[75,1,128]{2,1,0:T(1,128)}, f32[75,1,128]{2,1,0:T(1,128)S(1)}, u32[]{:S(2)}, u32[]{:S(2)}) collective-permute-start(f32[75,1,128]{2,1,0:T(1,128)} %get-tuple-element.84), channel_id=1, source_target_pairs={{16,0},{32,16},{48,32},{64,48},{80,64},{96,80},{112,96},{17,1},{33... | collective-permute-start | bytes 115208 | tf_op jit(solution)/shard_map/ppermute | solution.py:23
  187.8 10.6 %collective-permute-start.33 = (f32[75,1,128]{2,1,0:T(1,128)S(1)}, f32[75,1,128]{2,1,0:T(1,128)S(1)}, u32[]{:S(2)}, u32[]{:S(2)}) collective-permute-start(f32[75,1,128]{2,1,0:T(1,128)S(1)} %get-tuple-element.85), channel_id=1, source_target_pairs={{0,16},{16,32},{32,48},{48,64},{64,80},{80,96},{96,112},{1,17},{17... | collective-permute-start | bytes 115208 | tf_op jit(solution)/shard_map/ppermute | solution.py:20
  194.2 12.2 %all-to-all-start.5 = ((f32[8,1,1024]{2,1,0:T(1,128)}), f32[8,1,1024]{2,1,0:T(1,128)S(1)}, u32[]{:S(2)}, u32[]{:S(2)}) async-start(f32[8,1,1024]{2,1,0:T(1,128)} %reshape.288), calls=%async_computation.5 | async-start | bytes 65536 | tf_op jit(solution)/shard_map/all_to_all | solution.py:102
  208.1 6.8 %collective-permute-start.34 = (f32[16,32]{1,0:T(8,128)S(1)}, f32[16,32]{1,0:T(8,128)S(1)}, u32[]{:S(2)}, u32[]{:S(2)}) collective-permute-start(f32[16,32]{1,0:T(8,128)S(1)} %fusion.3), channel_id=1, source_target_pairs={{0,384},{1,385},{2,386},{3,387},{4,388},{5,389},{6,390},{7,391},{8... | collective-permute-start | bytes 6152 | tf_op jit(solution)/shard_map/ppermute | solution.py:113
  209.4 7.0 %collective-permute-start.35 = (f32[16,32]{1,0:T(8,128)S(1)}, f32[16,32]{1,0:T(8,128)S(1)}, u32[]{:S(2)}, u32[]{:S(2)}) collective-permute-start(f32[16,32]{1,0:T(8,128)S(1)} %fusion.3), channel_id=1, source_target_pairs={{128,384},{129,385},{130,386},{131,387},{132,388},{133,389},{134,3... | collective-permute-start | bytes 6152 | tf_op jit(solution)/shard_map/ppermute | solution.py:113
  220.6 11.9 %collective-permute-start.39 = (f32[75,1,128]{2,1,0:T(1,128)S(1)}, f32[75,1,128]{2,1,0:T(1,128)S(1)}, u32[]{:S(2)}, u32[]{:S(2)}) collective-permute-start(f32[75,1,128]{2,1,0:T(1,128)S(1)} %get-tuple-element.78), channel_id=1, source_target_pairs={{16,0},{32,16},{48,32},{64,48},{80,64},{96,80},{112,96},{17,1},{33... | collective-permute-start | bytes 115208 | tf_op jit(solution)/shard_map/ppermute | solution.py:23
  221.9 10.6 %collective-permute-start.40 = (f32[75,1,128]{2,1,0:T(1,128)S(1)}, f32[75,1,128]{2,1,0:T(1,128)S(1)}, u32[]{:S(2)}, u32[]{:S(2)}) collective-permute-start(f32[75,1,128]{2,1,0:T(1,128)S(1)} %get-tuple-element.79), channel_id=1, source_target_pairs={{0,16},{16,32},{32,48},{48,64},{64,80},{80,96},{96,112},{1,17},{17... | collective-permute-start | bytes 115208 | tf_op jit(solution)/shard_map/ppermute | solution.py:20
  226.6 5.9 %collective-permute-start.38 = (f32[75,4,1]{2,1,0:T(4,128)S(1)}, f32[75,4,1]{2,1,0:T(4,128)S(1)}, u32[]{:S(2)}, u32[]{:S(2)}) collective-permute-start(f32[75,4,1]{2,1,0:T(4,128)S(1)} %get-tuple-element.75), channel_id=1, source_target_pairs={{0,1},{1,2},{2,3},{3,4},{4,5},{5,6},{6,7},{7,8},{8,9},{9,10},{10,1... | collective-permute-start | bytes 3608 | tf_op jit(solution)/shard_map/ppermute | solution.py:20
  240.7 13.9 %all-to-all-start.6 = ((f32[16,1,512]{2,1,0:T(1,128)}), f32[16,1,512]{2,1,0:T(1,128)S(1)}, u32[]{:S(2)}, u32[]{:S(2)}) async-start(f32[16,1,512]{2,1,0:T(1,128)} %reshape.290), calls=%async_computation.6 | async-start | bytes 65536 | tf_op jit(solution)/shard_map/all_to_all | solution.py:101
  245.8 14.8 %collective-permute-start.41 = (f32[75,4,1]{2,1,0:T(4,128)S(1)}, f32[75,4,1]{2,1,0:T(4,128)S(1)}, u32[]{:S(2)}, u32[]{:S(2)}) collective-permute-start(f32[75,4,1]{2,1,0:T(4,128)S(1)} %get-tuple-element.68), channel_id=1, source_target_pairs={{1,0},{2,1},{3,2},{4,3},{5,4},{6,5},{7,6},{8,7},{9,8},{10,9},{11,1... | collective-permute-start | bytes 3608 | tf_op jit(solution)/shard_map/ppermute | solution.py:23
  248.7 11.9 %collective-permute-start.42 = (f32[75,4,1]{2,1,0:T(4,128)S(1)}, f32[75,4,1]{2,1,0:T(4,128)S(1)}, u32[]{:S(2)}, u32[]{:S(2)}) collective-permute-start(f32[75,4,1]{2,1,0:T(4,128)S(1)} %get-tuple-element.69), channel_id=1, source_target_pairs={{0,1},{1,2},{2,3},{3,4},{4,5},{5,6},{6,7},{7,8},{8,9},{9,10},{10,1... | collective-permute-start | bytes 3608 | tf_op jit(solution)/shard_map/ppermute | solution.py:20
  248.8 11.9 %collective-permute-start.43 = (f32[75,1,128]{2,1,0:T(1,128)S(1)}, f32[75,1,128]{2,1,0:T(1,128)S(1)}, u32[]{:S(2)}, u32[]{:S(2)}) collective-permute-start(f32[75,1,128]{2,1,0:T(1,128)S(1)} %get-tuple-element.72), channel_id=1, source_target_pairs={{16,0},{32,16},{48,32},{64,48},{80,64},{96,80},{112,96},{17,1},{33... | collective-permute-start | bytes 115208 | tf_op jit(solution)/shard_map/ppermute | solution.py:23
  250.1 10.6 %collective-permute-start.44 = (f32[75,1,128]{2,1,0:T(1,128)S(1)}, f32[75,1,128]{2,1,0:T(1,128)S(1)}, u32[]{:S(2)}, u32[]{:S(2)}) collective-permute-start(f32[75,1,128]{2,1,0:T(1,128)S(1)} %get-tuple-element.73), channel_id=1, source_target_pairs={{0,16},{16,32},{32,48},{48,64},{64,80},{80,96},{96,112},{1,17},{17... | collective-permute-start | bytes 115208 | tf_op jit(solution)/shard_map/ppermute | solution.py:20
  256.5 12.2 %all-to-all-start.7 = ((f32[8,1,1024]{2,1,0:T(1,128)}), f32[8,1,1024]{2,1,0:T(1,128)S(1)}, u32[]{:S(2)}, u32[]{:S(2)}) async-start(f32[8,1,1024]{2,1,0:T(1,128)} %reshape.292), calls=%async_computation.7 | async-start | bytes 65536 | tf_op jit(solution)/shard_map/all_to_all | solution.py:102
  270.4 6.8 %collective-permute-start.45 = (f32[16,32]{1,0:T(8,128)S(1)}, f32[16,32]{1,0:T(8,128)S(1)}, u32[]{:S(2)}, u32[]{:S(2)}) collective-permute-start(f32[16,32]{1,0:T(8,128)S(1)} %fusion.1), channel_id=1, source_target_pairs={{0,384},{1,385},{2,386},{3,387},{4,388},{5,389},{6,390},{7,391},{8... | collective-permute-start | bytes 6152 | tf_op jit(solution)/shard_map/ppermute | solution.py:113
  271.7 7.0 %collective-permute-start.46 = (f32[16,32]{1,0:T(8,128)S(1)}, f32[16,32]{1,0:T(8,128)S(1)}, u32[]{:S(2)}, u32[]{:S(2)}) collective-permute-start(f32[16,32]{1,0:T(8,128)S(1)} %fusion.1), channel_id=1, source_target_pairs={{128,384},{129,385},{130,386},{131,387},{132,388},{133,389},{134,3... | collective-permute-start | bytes 6152 | tf_op jit(solution)/shard_map/ppermute | solution.py:113
  (29 other events, 264.6 us)

commit v5 on v3

--- a/solution.py
+++ b/solution.py
@@ -42,7 +42,7 @@
         prior_c = factor
 
 
-def _solve_kernel(x_ref, inv_ref, b_ref, c_ref, o_ref):
+def _solve_kernel(x_ref, inv_ref, b_ref, c_ref, east_ref, north_ref, o_ref, e_ref, n_ref):
     lev = x_ref.shape[0]
 
     def down(k, z):
@@ -54,6 +54,8 @@
         k = lev - 1 - i
         x = o_ref[k] - c_ref[k] * x
         o_ref[k] = x
+        e_ref[k] = east_ref[k] * x
+        n_ref[k] = north_ref[k] * x
         return x
 
     zero = jnp.zeros(x_ref.shape[1:], jnp.float32)
@@ -71,18 +73,17 @@
     )(coeff)
 
 
-def column_solve(right, inv, lower, factor):
+def column_solve(right, inv, lower, factor, east_speed, north_speed):
     size = right.size
+    shape = jax.ShapeDtypeStruct(right.shape, jnp.float32)
     return pl.pallas_call(
         _solve_kernel,
-        out_shape=jax.ShapeDtypeStruct(right.shape, jnp.float32),
-        cost_estimate=pl.CostEstimate(flops=6 * size, bytes_accessed=20 * size, transcendentals=0),
-    )(right, inv, lower, factor)
+        out_shape=(shape, shape, shape),
+        cost_estimate=pl.CostEstimate(flops=8 * size, bytes_accessed=36 * size, transcendentals=0),
+    )(right, inv, lower, factor, east_speed, north_speed)
 
 
-def advect(mixed_adj, east_speed, north_speed):
-    east_flux = east_speed * mixed_adj
-    north_flux = north_speed * mixed_adj
+def advect(mixed_adj, east_flux, north_flux):
     east_rim = extended(east_flux, (("lon", 2),), 1, True)
     north_rim = extended(north_flux, (("lat", 1),), 1, False)
     east_diff = east_rim[:, :, 2:] - east_rim[:, :, :-2]
@@ -143,8 +144,8 @@
     one_hot = jnp.logical_and(matches, live_slot[:, None]).astype(jnp.float32)
 
     def substep(x):
-        mixed_adj = column_solve(x, inv, lower, factor)
-        return advect(mixed_adj, east_part, north_part) * keep_factor
+        mixed_adj, east_flux, north_flux = column_solve(x, inv, lower, factor, east_part, north_part)
+        return advect(mixed_adj, east_flux, north_flux) * keep_factor
 
     total_steps = NCPL * NSUB
     peer_count = record_counts.shape[-1]

time: 270 us -> 286 us (1.059)
  local copies, waits for them, and re-layouts: 27.5 us -> 47.6 us
  other arithmetic: 33.4 us -> 23.2 us
  starting transfers between devices: 145 us -> 150 us
  waiting for transfers between devices: 26.6 us -> 23.1 us
  Pallas kernels: 24.8 us -> 28.1 us
    slice x20, local copies, waits for them, and re-layouts: 8.7 us -> 28.6 us  [extended(): lax.slice_in_dim(block, 0, width, axis=dim)]
    mul x18 -> x8, other arithmetic: 21.1 us -> 9.46 us  [substep(): return advect(mixed_adj, east_flux, north_flux) * keep_factor]
    all_to_all x4, waiting for transfers between devices: 8.4 us -> 4.42 us  [couple(): lax.all_to_all(staged, 'lat', split_axis=1, concat_axis=1, tiled=True)]
    pallas_call x10, Pallas kernels: 22.5 us -> 25.7 us  [column_solve(): pl.pallas_call(_solve_kernel, out_shape=(shape, shape, shape), cost_estim...]
    unnamed x69 -> x101, local copies, waits for them, and re-layouts: 9.47 us -> 9.63 us
  transfers between devices with their start and end apart: 60 -> 60, of which waited for: 17 -> 17; matrix products, arithmetic and copies ran while one was open for 16% -> 19% of each run, Pallas kernels for 3% -> 4%
where the time goes in v5:
time: 286 us; the launch traced here: 283 us
  starting transfers between devices  150 us (52%)
  local copies, waits for them, and re-layouts  47.6 us (17%)
  Pallas kernels  28.1 us (10%)
  other arithmetic  23.2 us (8%)
  waiting for transfers between devices  23.1 us (8%)
  matrix products  9.54 us (3%)
    ppermute x20, starting transfers between devices, extended(): lax.ppermute(lax.slice_in_dim(block, block.shape[dim] - width, None, axis...  50.5 us
    all_to_all x4, starting transfers between devices, couple(): lax.all_to_all(staged, 'lat', split_axis=1, concat_axis=1, tiled=True)  33.4 us
    ppermute x20, starting transfers between devices, extended(): lax.ppermute(lax.slice_in_dim(block, 0, width, axis=dim), axis, backward)  32.4 us
    slice x20, local copies, waits for them, and re-layouts, extended(): lax.slice_in_dim(block, 0, width, axis=dim)  28.6 us
    pallas_call x10, Pallas kernels, column_solve(): pl.pallas_call(_solve_kernel, out_shape=(shape, shape, shape), cost_estim...  25.7 us
    all_to_all x4, starting transfers between devices, couple(): lax.all_to_all(staged, 'lon', split_axis=2, concat_axis=2, tiled=True)  18.6 us
    ppermute x12, starting transfers between devices, reduce_forcing(): lax.ppermute(accumulated, 'sec', [(s, section_count - 1)])  15.6 us
    ppermute x12, waiting for transfers between devices, reduce_forcing(): lax.ppermute(accumulated, 'sec', [(s, section_count - 1)])  15.2 us
  transfers between devices with their start and end apart: 60, of which 17 were waited for; matrix products, arithmetic and copies ran while one was open for 19% of the time, Pallas kernels for 4%

profile of v5, /device:TPU:6, one launch (start us, length us, event | category | flops | bytes accessed | tf_op | source)
XLA Modules:
  0.0 283.1 jit_solution(11012383750672711668)
XLA Ops:
  1.6 2.4 shard_map.91
  5.7 2.6 shard_map.92
  9.4 2.9 %collective-permute-start = (f32[75,4,1]{2,1,0:T(4,128)S(1)}, f32[75,4,1]{2,1,0:T(4,128)S(1)}, u32[]{:S(2)}, u32[]{:S(2)}) collective-permute-start(f32[75,4,1]{2,1,0:T(4,128)S(1)} %get-tuple-element.170), channel_id=1, source_target_pairs={{1,0},{2,1},{3,2},{4,3},{5,4},{6,5},{7,6},{8,7},{9,8},{10,9},{11,1... | collective-permute-start | bytes 3608 | tf_op jit(solution)/shard_map/ppermute | solution.py:23
  14.7 4.9 %collective-permute-start.3 = (f32[75,1,128]{2,1,0:T(1,128)S(1)}, f32[75,1,128]{2,1,0:T(1,128)S(1)}, u32[]{:S(2)}, u32[]{:S(2)}) collective-permute-start(f32[75,1,128]{2,1,0:T(1,128)S(1)} %get-tuple-element.173), channel_id=1, source_target_pairs={{0,16},{16,32},{32,48},{48,64},{64,80},{80,96},{96,112},{1,17},{17... | collective-permute-start | bytes 115208 | tf_op jit(solution)/shard_map/ppermute | solution.py:20
  21.2 2.2 fusion.69.x_ref
  23.5 2.6 shard_map.93
  27.9 2.1 collective-permute-start.4
  32.9 5.5 %collective-permute-start.7 = (f32[75,1,128]{2,1,0:T(1,128)}, f32[75,1,128]{2,1,0:T(1,128)}, u32[]{:S(2)}, u32[]{:S(2)}) collective-permute-start(f32[75,1,128]{2,1,0:T(1,128)} %get-tuple-element.169), channel_id=1, source_target_pairs={{0,16},{16,32},{32,48},{48,64},{64,80},{80,96},{96,112},{1,17},{17... | collective-permute-start | bytes 115208 | tf_op jit(solution)/shard_map/ppermute | solution.py:20
  38.5 2.1 copy.67
  42.8 2.6 shard_map.94
  46.6 2.7 collective-permute-start.8
  52.2 5.2 %collective-permute-start.11 = (f32[75,1,128]{2,1,0:T(1,128)}, f32[75,1,128]{2,1,0:T(1,128)}, u32[]{:S(2)}, u32[]{:S(2)}) collective-permute-start(f32[75,1,128]{2,1,0:T(1,128)} %get-tuple-element.165), channel_id=1, source_target_pairs={{0,16},{16,32},{32,48},{48,64},{64,80},{80,96},{96,112},{1,17},{17... | collective-permute-start | bytes 115208 | tf_op jit(solution)/shard_map/ppermute | solution.py:20
  58.6 1.9 fusion.106
  63.2 4.3 %all-to-all-start = ((f32[16,1,512]{2,1,0:T(1,128)}), f32[16,1,512]{2,1,0:T(1,128)S(1)}, u32[]{:S(2)}, u32[]{:S(2)}) async-start(f32[16,1,512]{2,1,0:T(1,128)} %reshape.278), calls=%async_computation | async-start | bytes 65536 | tf_op jit(solution)/shard_map/all_to_all | solution.py:102
  67.5 2.6 shard_map.95
  70.1 1.9 fusion.98
  72.0 2.9 %collective-permute-start.12 = (f32[75,4,1]{2,1,0:T(4,128)}, f32[75,4,1]{2,1,0:T(4,128)S(1)}, u32[]{:S(2)}, u32[]{:S(2)}) collective-permute-start(f32[75,4,1]{2,1,0:T(4,128)} %get-tuple-element.158), channel_id=1, source_target_pairs={{1,0},{2,1},{3,2},{4,3},{5,4},{6,5},{7,6},{8,7},{9,8},{10,9},{11,1... | collective-permute-start | bytes 3608 | tf_op jit(solution)/shard_map/ppermute | solution.py:23
  77.6 10.3 %all-to-all-start.1 = ((f32[8,1,1024]{2,1,0:T(1,128)}), f32[8,1,1024]{2,1,0:T(1,128)S(1)}, u32[]{:S(2)}, u32[]{:S(2)}) async-start(f32[8,1,1024]{2,1,0:T(1,128)} %reshape.280), calls=%async_computation.1 | async-start | bytes 65536 | tf_op jit(solution)/shard_map/all_to_all | solution.py:103
  90.2 4.6 %collective-permute-start.15 = (f32[75,1,128]{2,1,0:T(1,128)S(1)}, f32[75,1,128]{2,1,0:T(1,128)S(1)}, u32[]{:S(2)}, u32[]{:S(2)}) collective-permute-start(f32[75,1,128]{2,1,0:T(1,128)S(1)} %get-tuple-element.161), channel_id=1, source_target_pairs={{0,16},{16,32},{32,48},{48,64},{64,80},{80,96},{96,112},{1,17},{17... | collective-permute-start | bytes 115208 | tf_op jit(solution)/shard_map/ppermute | solution.py:20
  102.0 2.4 collective-permute-done.16
  107.5 2.6 shard_map.96
  114.7 5.2 %collective-permute-start.22 = (f32[75,1,128]{2,1,0:T(1,128)}, f32[75,1,128]{2,1,0:T(1,128)}, u32[]{:S(2)}, u32[]{:S(2)}) collective-permute-start(f32[75,1,128]{2,1,0:T(1,128)} %get-tuple-element.157), channel_id=1, source_target_pairs={{0,16},{16,32},{32,48},{48,64},{64,80},{80,96},{96,112},{1,17},{17... | collective-permute-start | bytes 115208 | tf_op jit(solution)/shard_map/ppermute | solution.py:20
  119.8 1.9 fusion.107
  124.5 4.8 %all-to-all-start.2 = ((f32[16,1,512]{2,1,0:T(1,128)}), f32[16,1,512]{2,1,0:T(1,128)S(1)}, u32[]{:S(2)}, u32[]{:S(2)}) async-start(f32[16,1,512]{2,1,0:T(1,128)} %reshape.282), calls=%async_computation.2 | async-start | bytes 65536 | tf_op jit(solution)/shard_map/all_to_all | solution.py:102
  129.2 2.6 shard_map.97
  131.8 1.9 fusion.94
  133.7 2.9 %collective-permute-start.23 = (f32[75,4,1]{2,1,0:T(4,128)}, f32[75,4,1]{2,1,0:T(4,128)S(1)}, u32[]{:S(2)}, u32[]{:S(2)}) collective-permute-start(f32[75,4,1]{2,1,0:T(4,128)} %get-tuple-element.150), channel_id=1, source_target_pairs={{1,0},{2,1},{3,2},{4,3},{5,4},{6,5},{7,6},{8,7},{9,8},{10,9},{11,1... | collective-permute-start | bytes 3608 | tf_op jit(solution)/shard_map/ppermute | solution.py:23
  138.7 7.7 %all-to-all-start.3 = ((f32[8,1,1024]{2,1,0:T(1,128)}), f32[8,1,1024]{2,1,0:T(1,128)S(1)}, u32[]{:S(2)}, u32[]{:S(2)}) async-start(f32[8,1,1024]{2,1,0:T(1,128)} %reshape.284), calls=%async_computation.3 | async-start | bytes 65536 | tf_op jit(solution)/shard_map/all_to_all | solution.py:103
  148.8 4.6 %collective-permute-start.26 = (f32[75,1,128]{2,1,0:T(1,128)S(1)}, f32[75,1,128]{2,1,0:T(1,128)S(1)}, u32[]{:S(2)}, u32[]{:S(2)}) collective-permute-start(f32[75,1,128]{2,1,0:T(1,128)S(1)} %get-tuple-element.153), channel_id=1, source_target_pairs={{0,16},{16,32},{32,48},{48,64},{64,80},{80,96},{96,112},{1,17},{17... | collective-permute-start | bytes 115208 | tf_op jit(solution)/shard_map/ppermute | solution.py:20
  160.5 2.4 collective-permute-done.27
  166.0 2.6 shard_map.98
  173.2 5.2 %collective-permute-start.33 = (f32[75,1,128]{2,1,0:T(1,128)}, f32[75,1,128]{2,1,0:T(1,128)}, u32[]{:S(2)}, u32[]{:S(2)}) collective-permute-start(f32[75,1,128]{2,1,0:T(1,128)} %get-tuple-element.147), channel_id=1, source_target_pairs={{0,16},{16,32},{32,48},{48,64},{64,80},{80,96},{96,112},{1,17},{17... | collective-permute-start | bytes 115208 | tf_op jit(solution)/shard_map/ppermute | solution.py:20
  178.4 1.9 fusion.108
  183.0 4.8 %all-to-all-start.4 = ((f32[16,1,512]{2,1,0:T(1,128)}), f32[16,1,512]{2,1,0:T(1,128)S(1)}, u32[]{:S(2)}, u32[]{:S(2)}) async-start(f32[16,1,512]{2,1,0:T(1,128)} %reshape.286), calls=%async_computation.4 | async-start | bytes 65536 | tf_op jit(solution)/shard_map/all_to_all | solution.py:102
  187.8 2.6 shard_map.99
  190.3 1.9 fusion.89
  192.2 2.9 %collective-permute-start.34 = (f32[75,4,1]{2,1,0:T(4,128)}, f32[75,4,1]{2,1,0:T(4,128)S(1)}, u32[]{:S(2)}, u32[]{:S(2)}) collective-permute-start(f32[75,4,1]{2,1,0:T(4,128)} %get-tuple-element.140), channel_id=1, source_target_pairs={{1,0},{2,1},{3,2},{4,3},{5,4},{6,5},{7,6},{8,7},{9,8},{10,9},{11,1... | collective-permute-start | bytes 3608 | tf_op jit(solution)/shard_map/ppermute | solution.py:23
  197.3 7.7 %all-to-all-start.5 = ((f32[8,1,1024]{2,1,0:T(1,128)}), f32[8,1,1024]{2,1,0:T(1,128)S(1)}, u32[]{:S(2)}, u32[]{:S(2)}) async-start(f32[8,1,1024]{2,1,0:T(1,128)} %reshape.288), calls=%async_computation.5 | async-start | bytes 65536 | tf_op jit(solution)/shard_map/all_to_all | solution.py:103
  207.3 4.6 %collective-permute-start.37 = (f32[75,1,128]{2,1,0:T(1,128)S(1)}, f32[75,1,128]{2,1,0:T(1,128)S(1)}, u32[]{:S(2)}, u32[]{:S(2)}) collective-permute-start(f32[75,1,128]{2,1,0:T(1,128)S(1)} %get-tuple-element.143), channel_id=1, source_target_pairs={{0,16},{16,32},{32,48},{48,64},{64,80},{80,96},{96,112},{1,17},{17... | collective-permute-start | bytes 115208 | tf_op jit(solution)/shard_map/ppermute | solution.py:20
  224.6 2.6 shard_map.100
  232.3 5.2 %collective-permute-start.44 = (f32[75,1,128]{2,1,0:T(1,128)}, f32[75,1,128]{2,1,0:T(1,128)}, u32[]{:S(2)}, u32[]{:S(2)}) collective-permute-start(f32[75,1,128]{2,1,0:T(1,128)} %get-tuple-element.137), channel_id=1, source_target_pairs={{0,16},{16,32},{32,48},{48,64},{64,80},{80,96},{96,112},{1,17},{17... | collective-permute-start | bytes 115208 | tf_op jit(solution)/shard_map/ppermute | solution.py:20
  237.5 1.9 fusion.109
  242.1 4.8 %all-to-all-start.6 = ((f32[16,1,512]{2,1,0:T(1,128)}), f32[16,1,512]{2,1,0:T(1,128)S(1)}, u32[]{:S(2)}, u32[]{:S(2)}) async-start(f32[16,1,512]{2,1,0:T(1,128)} %reshape.290), calls=%async_computation.6 | async-start | bytes 65536 | tf_op jit(solution)/shard_map/all_to_all | solution.py:102
  246.9 2.6 shard_map.101
  250.6 2.9 %collective-permute-start.45 = (f32[75,4,1]{2,1,0:T(4,128)S(1)}, f32[75,4,1]{2,1,0:T(4,128)S(1)}, u32[]{:S(2)}, u32[]{:S(2)}) collective-permute-start(f32[75,4,1]{2,1,0:T(4,128)S(1)} %get-tuple-element.130), channel_id=1, source_target_pairs={{1,0},{2,1},{3,2},{4,3},{5,4},{6,5},{7,6},{8,7},{9,8},{10,9},{11,1... | collective-permute-start | bytes 3608 | tf_op jit(solution)/shard_map/ppermute | solution.py:23
  256.4 7.7 %all-to-all-start.7 = ((f32[8,1,1024]{2,1,0:T(1,128)}), f32[8,1,1024]{2,1,0:T(1,128)S(1)}, u32[]{:S(2)}, u32[]{:S(2)}) async-start(f32[8,1,1024]{2,1,0:T(1,128)} %reshape.292), calls=%async_computation.7 | async-start | bytes 65536 | tf_op jit(solution)/shard_map/all_to_all | solution.py:103
  266.4 4.6 %collective-permute-start.48 = (f32[75,1,128]{2,1,0:T(1,128)S(1)}, f32[75,1,128]{2,1,0:T(1,128)S(1)}, u32[]{:S(2)}, u32[]{:S(2)}) collective-permute-start(f32[75,1,128]{2,1,0:T(1,128)S(1)} %get-tuple-element.133), channel_id=1, source_target_pairs={{0,16},{16,32},{32,48},{48,64},{64,80},{80,96},{96,112},{1,17},{17... | collective-permute-start | bytes 115208 | tf_op jit(solution)/shard_map/ppermute | solution.py:20
  278.2 2.4 collective-permute-done.49
  (284 shorter events, 108.7 us)
Async XLA Ops:
  9.4 10.6 %collective-permute-start = (f32[75,4,1]{2,1,0:T(4,128)S(1)}, f32[75,4,1]{2,1,0:T(4,128)S(1)}, u32[]{:S(2)}, u32[]{:S(2)}) collective-permute-start(f32[75,4,1]{2,1,0:T(4,128)S(1)} %get-tuple-element.170), channel_id=1, source_target_pairs={{1,0},{2,1},{3,2},{4,3},{5,4},{6,5},{7,6},{8,7},{9,8},{10,9},{11,1... | collective-permute-start | bytes 3608 | tf_op jit(solution)/shard_map/ppermute | solution.py:23
  12.3 7.7 %collective-permute-start.1 = (f32[75,4,1]{2,1,0:T(4,128)S(1)}, f32[75,4,1]{2,1,0:T(4,128)S(1)}, u32[]{:S(2)}, u32[]{:S(2)}) collective-permute-start(f32[75,4,1]{2,1,0:T(4,128)S(1)} %get-tuple-element.171), channel_id=1, source_target_pairs={{0,1},{1,2},{2,3},{3,4},{4,5},{5,6},{6,7},{7,8},{8,9},{9,10},{10,1... | collective-permute-start | bytes 3608 | tf_op jit(solution)/shard_map/ppermute | solution.py:20
  27.9 13.0 %collective-permute-start.4 = (f32[75,4,1]{2,1,0:T(4,128)}, f32[75,4,1]{2,1,0:T(4,128)S(1)}, u32[]{:S(2)}, u32[]{:S(2)}) collective-permute-start(f32[75,4,1]{2,1,0:T(4,128)} %get-tuple-element.166), channel_id=1, source_target_pairs={{1,0},{2,1},{3,2},{4,3},{5,4},{6,5},{7,6},{8,7},{9,8},{10,9},{11,1... | collective-permute-start | bytes 3608 | tf_op jit(solution)/shard_map/ppermute | solution.py:23
  30.0 10.9 %collective-permute-start.5 = (f32[75,4,1]{2,1,0:T(4,128)S(1)}, f32[75,4,1]{2,1,0:T(4,128)S(1)}, u32[]{:S(2)}, u32[]{:S(2)}) collective-permute-start(f32[75,4,1]{2,1,0:T(4,128)S(1)} %get-tuple-element.167), channel_id=1, source_target_pairs={{0,1},{1,2},{2,3},{3,4},{4,5},{5,6},{6,7},{7,8},{8,9},{9,10},{10,1... | collective-permute-start | bytes 3608 | tf_op jit(solution)/shard_map/ppermute | solution.py:20
  31.7 9.3 %collective-permute-start.6 = (f32[75,1,128]{2,1,0:T(1,128)}, f32[75,1,128]{2,1,0:T(1,128)S(1)}, u32[]{:S(2)}, u32[]{:S(2)}) collective-permute-start(f32[75,1,128]{2,1,0:T(1,128)} %get-tuple-element.168), channel_id=1, source_target_pairs={{16,0},{32,16},{48,32},{64,48},{80,64},{96,80},{112,96},{17,1},{33... | collective-permute-start | bytes 115208 | tf_op jit(solution)/shard_map/ppermute | solution.py:23
  32.9 8.0 %collective-permute-start.7 = (f32[75,1,128]{2,1,0:T(1,128)}, f32[75,1,128]{2,1,0:T(1,128)}, u32[]{:S(2)}, u32[]{:S(2)}) collective-permute-start(f32[75,1,128]{2,1,0:T(1,128)} %get-tuple-element.169), channel_id=1, source_target_pairs={{0,16},{16,32},{32,48},{48,64},{64,80},{80,96},{96,112},{1,17},{17... | collective-permute-start | bytes 115208 | tf_op jit(solution)/shard_map/ppermute | solution.py:20
  46.6 14.8 %collective-permute-start.8 = (f32[75,4,1]{2,1,0:T(4,128)S(1)}, f32[75,4,1]{2,1,0:T(4,128)S(1)}, u32[]{:S(2)}, u32[]{:S(2)}) collective-permute-start(f32[75,4,1]{2,1,0:T(4,128)S(1)} %get-tuple-element.162), channel_id=1, source_target_pairs={{1,0},{2,1},{3,2},{4,3},{5,4},{6,5},{7,6},{8,7},{9,8},{10,9},{11,1... | collective-permute-start | bytes 3608 | tf_op jit(solution)/shard_map/ppermute | solution.py:23
  49.2 12.1 %collective-permute-start.9 = (f32[75,4,1]{2,1,0:T(4,128)S(1)}, f32[75,4,1]{2,1,0:T(4,128)S(1)}, u32[]{:S(2)}, u32[]{:S(2)}) collective-permute-start(f32[75,4,1]{2,1,0:T(4,128)S(1)} %get-tuple-element.163), channel_id=1, source_target_pairs={{0,1},{1,2},{2,3},{3,4},{4,5},{5,6},{6,7},{7,8},{8,9},{9,10},{10,1... | collective-permute-start | bytes 3608 | tf_op jit(solution)/shard_map/ppermute | solution.py:20
  50.9 10.4 %collective-permute-start.10 = (f32[75,1,128]{2,1,0:T(1,128)}, f32[75,1,128]{2,1,0:T(1,128)S(1)}, u32[]{:S(2)}, u32[]{:S(2)}) collective-permute-start(f32[75,1,128]{2,1,0:T(1,128)} %get-tuple-element.164), channel_id=1, source_target_pairs={{16,0},{32,16},{48,32},{64,48},{80,64},{96,80},{112,96},{17,1},{33... | collective-permute-start | bytes 115208 | tf_op jit(solution)/shard_map/ppermute | solution.py:23
  52.2 9.1 %collective-permute-start.11 = (f32[75,1,128]{2,1,0:T(1,128)}, f32[75,1,128]{2,1,0:T(1,128)}, u32[]{:S(2)}, u32[]{:S(2)}) collective-permute-start(f32[75,1,128]{2,1,0:T(1,128)} %get-tuple-element.165), channel_id=1, source_target_pairs={{0,16},{16,32},{32,48},{48,64},{64,80},{80,96},{96,112},{1,17},{17... | collective-permute-start | bytes 115208 | tf_op jit(solution)/shard_map/ppermute | solution.py:20
  63.2 12.0 %all-to-all-start = ((f32[16,1,512]{2,1,0:T(1,128)}), f32[16,1,512]{2,1,0:T(1,128)S(1)}, u32[]{:S(2)}, u32[]{:S(2)}) async-start(f32[16,1,512]{2,1,0:T(1,128)} %reshape.278), calls=%async_computation | async-start | bytes 65536 | tf_op jit(solution)/shard_map/all_to_all | solution.py:102
  72.0 27.0 %collective-permute-start.12 = (f32[75,4,1]{2,1,0:T(4,128)}, f32[75,4,1]{2,1,0:T(4,128)S(1)}, u32[]{:S(2)}, u32[]{:S(2)}) collective-permute-start(f32[75,4,1]{2,1,0:T(4,128)} %get-tuple-element.158), channel_id=1, source_target_pairs={{1,0},{2,1},{3,2},{4,3},{5,4},{6,5},{7,6},{8,7},{9,8},{10,9},{11,1... | collective-permute-start | bytes 3608 | tf_op jit(solution)/shard_map/ppermute | solution.py:23
  74.8 25.4 %collective-permute-start.13 = (f32[75,4,1]{2,1,0:T(4,128)}, f32[75,4,1]{2,1,0:T(4,128)S(1)}, u32[]{:S(2)}, u32[]{:S(2)}) collective-permute-start(f32[75,4,1]{2,1,0:T(4,128)} %get-tuple-element.159), channel_id=1, source_target_pairs={{0,1},{1,2},{2,3},{3,4},{4,5},{5,6},{6,7},{7,8},{8,9},{9,10},{10,1... | collective-permute-start | bytes 3608 | tf_op jit(solution)/shard_map/ppermute | solution.py:20
  77.6 18.3 %all-to-all-start.1 = ((f32[8,1,1024]{2,1,0:T(1,128)}), f32[8,1,1024]{2,1,0:T(1,128)S(1)}, u32[]{:S(2)}, u32[]{:S(2)}) async-start(f32[8,1,1024]{2,1,0:T(1,128)} %reshape.280), calls=%async_computation.1 | async-start | bytes 65536 | tf_op jit(solution)/shard_map/all_to_all | solution.py:103
  88.9 12.6 %collective-permute-start.14 = (f32[75,1,128]{2,1,0:T(1,128)S(1)}, f32[75,1,128]{2,1,0:T(1,128)S(1)}, u32[]{:S(2)}, u32[]{:S(2)}) collective-permute-start(f32[75,1,128]{2,1,0:T(1,128)S(1)} %get-tuple-element.160), channel_id=1, source_target_pairs={{16,0},{32,16},{48,32},{64,48},{80,64},{96,80},{112,96},{17,1},{33... | collective-permute-start | bytes 115208 | tf_op jit(solution)/shard_map/ppermute | solution.py:23
  90.2 11.3 %collective-permute-start.15 = (f32[75,1,128]{2,1,0:T(1,128)S(1)}, f32[75,1,128]{2,1,0:T(1,128)S(1)}, u32[]{:S(2)}, u32[]{:S(2)}) collective-permute-start(f32[75,1,128]{2,1,0:T(1,128)S(1)} %get-tuple-element.161), channel_id=1, source_target_pairs={{0,16},{16,32},{32,48},{48,64},{64,80},{80,96},{96,112},{1,17},{17... | collective-permute-start | bytes 115208 | tf_op jit(solution)/shard_map/ppermute | solution.py:20
  111.2 11.4 %collective-permute-start.19 = (f32[75,4,1]{2,1,0:T(4,128)S(1)}, f32[75,4,1]{2,1,0:T(4,128)S(1)}, u32[]{:S(2)}, u32[]{:S(2)}) collective-permute-start(f32[75,4,1]{2,1,0:T(4,128)S(1)} %get-tuple-element.154), channel_id=1, source_target_pairs={{1,0},{2,1},{3,2},{4,3},{5,4},{6,5},{7,6},{8,7},{9,8},{10,9},{11,1... | collective-permute-start | bytes 3608 | tf_op jit(solution)/shard_map/ppermute | solution.py:23
  111.3 11.3 %collective-permute-start.20 = (f32[75,4,1]{2,1,0:T(4,128)S(1)}, f32[75,4,1]{2,1,0:T(4,128)S(1)}, u32[]{:S(2)}, u32[]{:S(2)}) collective-permute-start(f32[75,4,1]{2,1,0:T(4,128)S(1)} %get-tuple-element.155), channel_id=1, source_target_pairs={{0,1},{1,2},{2,3},{3,4},{4,5},{5,6},{6,7},{7,8},{8,9},{9,10},{10,1... | collective-permute-start | bytes 3608 | tf_op jit(solution)/shard_map/ppermute | solution.py:20
  113.4 9.2 %collective-permute-start.21 = (f32[75,1,128]{2,1,0:T(1,128)}, f32[75,1,128]{2,1,0:T(1,128)S(1)}, u32[]{:S(2)}, u32[]{:S(2)}) collective-permute-start(f32[75,1,128]{2,1,0:T(1,128)} %get-tuple-element.156), channel_id=1, source_target_pairs={{16,0},{32,16},{48,32},{64,48},{80,64},{96,80},{112,96},{17,1},{33... | collective-permute-start | bytes 115208 | tf_op jit(solution)/shard_map/ppermute | solution.py:23
  114.7 7.9 %collective-permute-start.22 = (f32[75,1,128]{2,1,0:T(1,128)}, f32[75,1,128]{2,1,0:T(1,128)}, u32[]{:S(2)}, u32[]{:S(2)}) collective-permute-start(f32[75,1,128]{2,1,0:T(1,128)} %get-tuple-element.157), channel_id=1, source_target_pairs={{0,16},{16,32},{32,48},{48,64},{64,80},{80,96},{96,112},{1,17},{17... | collective-permute-start | bytes 115208 | tf_op jit(solution)/shard_map/ppermute | solution.py:20
  124.5 12.4 %all-to-all-start.2 = ((f32[16,1,512]{2,1,0:T(1,128)}), f32[16,1,512]{2,1,0:T(1,128)S(1)}, u32[]{:S(2)}, u32[]{:S(2)}) async-start(f32[16,1,512]{2,1,0:T(1,128)} %reshape.282), calls=%async_computation.2 | async-start | bytes 65536 | tf_op jit(solution)/shard_map/all_to_all | solution.py:102
  133.7 23.8 %collective-permute-start.23 = (f32[75,4,1]{2,1,0:T(4,128)}, f32[75,4,1]{2,1,0:T(4,128)S(1)}, u32[]{:S(2)}, u32[]{:S(2)}) collective-permute-start(f32[75,4,1]{2,1,0:T(4,128)} %get-tuple-element.150), channel_id=1, source_target_pairs={{1,0},{2,1},{3,2},{4,3},{5,4},{6,5},{7,6},{8,7},{9,8},{10,9},{11,1... | collective-permute-start | bytes 3608 | tf_op jit(solution)/shard_map/ppermute | solution.py:23
  136.5 22.3 %collective-permute-start.24 = (f32[75,4,1]{2,1,0:T(4,128)}, f32[75,4,1]{2,1,0:T(4,128)S(1)}, u32[]{:S(2)}, u32[]{:S(2)}) collective-permute-start(f32[75,4,1]{2,1,0:T(4,128)} %get-tuple-element.151), channel_id=1, source_target_pairs={{0,1},{1,2},{2,3},{3,4},{4,5},{5,6},{6,7},{7,8},{8,9},{9,10},{10,1... | collective-permute-start | bytes 3608 | tf_op jit(solution)/shard_map/ppermute | solution.py:20
  138.7 15.7 %all-to-all-start.3 = ((f32[8,1,1024]{2,1,0:T(1,128)}), f32[8,1,1024]{2,1,0:T(1,128)S(1)}, u32[]{:S(2)}, u32[]{:S(2)}) async-start(f32[8,1,1024]{2,1,0:T(1,128)} %reshape.284), calls=%async_computation.3 | async-start | bytes 65536 | tf_op jit(solution)/shard_map/all_to_all | solution.py:103
  147.5 12.6 %collective-permute-start.25 = (f32[75,1,128]{2,1,0:T(1,128)S(1)}, f32[75,1,128]{2,1,0:T(1,128)S(1)}, u32[]{:S(2)}, u32[]{:S(2)}) collective-permute-start(f32[75,1,128]{2,1,0:T(1,128)S(1)} %get-tuple-element.152), channel_id=1, source_target_pairs={{16,0},{32,16},{48,32},{64,48},{80,64},{96,80},{112,96},{17,1},{33... | collective-permute-start | bytes 115208 | tf_op jit(solution)/shard_map/ppermute | solution.py:23
  148.8 11.3 %collective-permute-start.26 = (f32[75,1,128]{2,1,0:T(1,128)S(1)}, f32[75,1,128]{2,1,0:T(1,128)S(1)}, u32[]{:S(2)}, u32[]{:S(2)}) collective-permute-start(f32[75,1,128]{2,1,0:T(1,128)S(1)} %get-tuple-element.153), channel_id=1, source_target_pairs={{0,16},{16,32},{32,48},{48,64},{64,80},{80,96},{96,112},{1,17},{17... | collective-permute-start | bytes 115208 | tf_op jit(solution)/shard_map/ppermute | solution.py:20
  169.7 11.4 %collective-permute-start.30 = (f32[75,4,1]{2,1,0:T(4,128)S(1)}, f32[75,4,1]{2,1,0:T(4,128)S(1)}, u32[]{:S(2)}, u32[]{:S(2)}) collective-permute-start(f32[75,4,1]{2,1,0:T(4,128)S(1)} %get-tuple-element.144), channel_id=1, source_target_pairs={{1,0},{2,1},{3,2},{4,3},{5,4},{6,5},{7,6},{8,7},{9,8},{10,9},{11,1... | collective-permute-start | bytes 3608 | tf_op jit(solution)/shard_map/ppermute | solution.py:23
  169.9 11.3 %collective-permute-start.31 = (f32[75,4,1]{2,1,0:T(4,128)S(1)}, f32[75,4,1]{2,1,0:T(4,128)S(1)}, u32[]{:S(2)}, u32[]{:S(2)}) collective-permute-start(f32[75,4,1]{2,1,0:T(4,128)S(1)} %get-tuple-element.145), channel_id=1, source_target_pairs={{0,1},{1,2},{2,3},{3,4},{4,5},{5,6},{6,7},{7,8},{8,9},{9,10},{10,1... | collective-permute-start | bytes 3608 | tf_op jit(solution)/shard_map/ppermute | solution.py:20
  172.0 9.2 %collective-permute-start.32 = (f32[75,1,128]{2,1,0:T(1,128)}, f32[75,1,128]{2,1,0:T(1,128)S(1)}, u32[]{:S(2)}, u32[]{:S(2)}) collective-permute-start(f32[75,1,128]{2,1,0:T(1,128)} %get-tuple-element.146), channel_id=1, source_target_pairs={{16,0},{32,16},{48,32},{64,48},{80,64},{96,80},{112,96},{17,1},{33... | collective-permute-start | bytes 115208 | tf_op jit(solution)/shard_map/ppermute | solution.py:23
  173.2 7.9 %collective-permute-start.33 = (f32[75,1,128]{2,1,0:T(1,128)}, f32[75,1,128]{2,1,0:T(1,128)}, u32[]{:S(2)}, u32[]{:S(2)}) collective-permute-start(f32[75,1,128]{2,1,0:T(1,128)} %get-tuple-element.147), channel_id=1, source_target_pairs={{0,16},{16,32},{32,48},{48,64},{64,80},{80,96},{96,112},{1,17},{17... | collective-permute-start | bytes 115208 | tf_op jit(solution)/shard_map/ppermute | solution.py:20
  183.0 12.5 %all-to-all-start.4 = ((f32[16,1,512]{2,1,0:T(1,128)}), f32[16,1,512]{2,1,0:T(1,128)S(1)}, u32[]{:S(2)}, u32[]{:S(2)}) async-start(f32[16,1,512]{2,1,0:T(1,128)} %reshape.286), calls=%async_computation.4 | async-start | bytes 65536 | tf_op jit(solution)/shard_map/all_to_all | solution.py:102
  192.2 23.8 %collective-permute-start.34 = (f32[75,4,1]{2,1,0:T(4,128)}, f32[75,4,1]{2,1,0:T(4,128)S(1)}, u32[]{:S(2)}, u32[]{:S(2)}) collective-permute-start(f32[75,4,1]{2,1,0:T(4,128)} %get-tuple-element.140), channel_id=1, source_target_pairs={{1,0},{2,1},{3,2},{4,3},{5,4},{6,5},{7,6},{8,7},{9,8},{10,9},{11,1... | collective-permute-start | bytes 3608 | tf_op jit(solution)/shard_map/ppermute | solution.py:23
  195.1 22.3 %collective-permute-start.35 = (f32[75,4,1]{2,1,0:T(4,128)}, f32[75,4,1]{2,1,0:T(4,128)S(1)}, u32[]{:S(2)}, u32[]{:S(2)}) collective-permute-start(f32[75,4,1]{2,1,0:T(4,128)} %get-tuple-element.141), channel_id=1, source_target_pairs={{0,1},{1,2},{2,3},{3,4},{4,5},{5,6},{6,7},{7,8},{8,9},{9,10},{10,1... | collective-permute-start | bytes 3608 | tf_op jit(solution)/shard_map/ppermute | solution.py:20
  197.3 15.7 %all-to-all-start.5 = ((f32[8,1,1024]{2,1,0:T(1,128)}), f32[8,1,1024]{2,1,0:T(1,128)S(1)}, u32[]{:S(2)}, u32[]{:S(2)}) async-start(f32[8,1,1024]{2,1,0:T(1,128)} %reshape.288), calls=%async_computation.5 | async-start | bytes 65536 | tf_op jit(solution)/shard_map/all_to_all | solution.py:103
  206.0 12.6 %collective-permute-start.36 = (f32[75,1,128]{2,1,0:T(1,128)S(1)}, f32[75,1,128]{2,1,0:T(1,128)S(1)}, u32[]{:S(2)}, u32[]{:S(2)}) collective-permute-start(f32[75,1,128]{2,1,0:T(1,128)S(1)} %get-tuple-element.142), channel_id=1, source_target_pairs={{16,0},{32,16},{48,32},{64,48},{80,64},{96,80},{112,96},{17,1},{33... | collective-permute-start | bytes 115208 | tf_op jit(solution)/shard_map/ppermute | solution.py:23
  207.3 11.4 %collective-permute-start.37 = (f32[75,1,128]{2,1,0:T(1,128)S(1)}, f32[75,1,128]{2,1,0:T(1,128)S(1)}, u32[]{:S(2)}, u32[]{:S(2)}) collective-permute-start(f32[75,1,128]{2,1,0:T(1,128)S(1)} %get-tuple-element.143), channel_id=1, source_target_pairs={{0,16},{16,32},{32,48},{48,64},{64,80},{80,96},{96,112},{1,17},{17... | collective-permute-start | bytes 115208 | tf_op jit(solution)/shard_map/ppermute | solution.py:20
  216.1 7.0 %collective-permute-start.39 = (f32[16,32]{1,0:T(8,128)S(1)}, f32[16,32]{1,0:T(8,128)S(1)}, u32[]{:S(2)}, u32[]{:S(2)}) collective-permute-start(f32[16,32]{1,0:T(8,128)S(1)} %fusion.3), channel_id=1, source_target_pairs={{128,384},{129,385},{130,386},{131,387},{132,388},{133,389},{134,3... | collective-permute-start | bytes 6152 | tf_op jit(solution)/shard_map/ppermute | solution.py:114
  228.9 11.4 %collective-permute-start.41 = (f32[75,4,1]{2,1,0:T(4,128)}, f32[75,4,1]{2,1,0:T(4,128)S(1)}, u32[]{:S(2)}, u32[]{:S(2)}) collective-permute-start(f32[75,4,1]{2,1,0:T(4,128)} %get-tuple-element.134), channel_id=1, source_target_pairs={{1,0},{2,1},{3,2},{4,3},{5,4},{6,5},{7,6},{8,7},{9,8},{10,9},{11,1... | collective-permute-start | bytes 3608 | tf_op jit(solution)/shard_map/ppermute | solution.py:23
  229.0 11.3 %collective-permute-start.42 = (f32[75,4,1]{2,1,0:T(4,128)S(1)}, f32[75,4,1]{2,1,0:T(4,128)S(1)}, u32[]{:S(2)}, u32[]{:S(2)}) collective-permute-start(f32[75,4,1]{2,1,0:T(4,128)S(1)} %get-tuple-element.135), channel_id=1, source_target_pairs={{0,1},{1,2},{2,3},{3,4},{4,5},{5,6},{6,7},{7,8},{8,9},{9,10},{10,1... | collective-permute-start | bytes 3608 | tf_op jit(solution)/shard_map/ppermute | solution.py:20
  231.1 9.2 %collective-permute-start.43 = (f32[75,1,128]{2,1,0:T(1,128)}, f32[75,1,128]{2,1,0:T(1,128)S(1)}, u32[]{:S(2)}, u32[]{:S(2)}) collective-permute-start(f32[75,1,128]{2,1,0:T(1,128)} %get-tuple-element.136), channel_id=1, source_target_pairs={{16,0},{32,16},{48,32},{64,48},{80,64},{96,80},{112,96},{17,1},{33... | collective-permute-start | bytes 115208 | tf_op jit(solution)/shard_map/ppermute | solution.py:23
  232.3 7.9 %collective-permute-start.44 = (f32[75,1,128]{2,1,0:T(1,128)}, f32[75,1,128]{2,1,0:T(1,128)}, u32[]{:S(2)}, u32[]{:S(2)}) collective-permute-start(f32[75,1,128]{2,1,0:T(1,128)} %get-tuple-element.137), channel_id=1, source_target_pairs={{0,16},{16,32},{32,48},{48,64},{64,80},{80,96},{96,112},{1,17},{17... | collective-permute-start | bytes 115208 | tf_op jit(solution)/shard_map/ppermute | solution.py:20
  242.1 12.4 %all-to-all-start.6 = ((f32[16,1,512]{2,1,0:T(1,128)}), f32[16,1,512]{2,1,0:T(1,128)S(1)}, u32[]{:S(2)}, u32[]{:S(2)}) async-start(f32[16,1,512]{2,1,0:T(1,128)} %reshape.290), calls=%async_computation.6 | async-start | bytes 65536 | tf_op jit(solution)/shard_map/all_to_all | solution.py:102
  250.6 24.5 %collective-permute-start.45 = (f32[75,4,1]{2,1,0:T(4,128)S(1)}, f32[75,4,1]{2,1,0:T(4,128)S(1)}, u32[]{:S(2)}, u32[]{:S(2)}) collective-permute-start(f32[75,4,1]{2,1,0:T(4,128)S(1)} %get-tuple-element.130), channel_id=1, source_target_pairs={{1,0},{2,1},{3,2},{4,3},{5,4},{6,5},{7,6},{8,7},{9,8},{10,9},{11,1... | collective-permute-start | bytes 3608 | tf_op jit(solution)/shard_map/ppermute | solution.py:23
  253.5 23.0 %collective-permute-start.46 = (f32[75,4,1]{2,1,0:T(4,128)S(1)}, f32[75,4,1]{2,1,0:T(4,128)S(1)}, u32[]{:S(2)}, u32[]{:S(2)}) collective-permute-start(f32[75,4,1]{2,1,0:T(4,128)S(1)} %get-tuple-element.131), channel_id=1, source_target_pairs={{0,1},{1,2},{2,3},{3,4},{4,5},{5,6},{6,7},{7,8},{8,9},{9,10},{10,1... | collective-permute-start | bytes 3608 | tf_op jit(solution)/shard_map/ppermute | solution.py:20
  256.4 15.7 %all-to-all-start.7 = ((f32[8,1,1024]{2,1,0:T(1,128)}), f32[8,1,1024]{2,1,0:T(1,128)S(1)}, u32[]{:S(2)}, u32[]{:S(2)}) async-start(f32[8,1,1024]{2,1,0:T(1,128)} %reshape.292), calls=%async_computation.7 | async-start | bytes 65536 | tf_op jit(solution)/shard_map/all_to_all | solution.py:103
  265.1 12.6 %collective-permute-start.47 = (f32[75,1,128]{2,1,0:T(1,128)S(1)}, f32[75,1,128]{2,1,0:T(1,128)S(1)}, u32[]{:S(2)}, u32[]{:S(2)}) collective-permute-start(f32[75,1,128]{2,1,0:T(1,128)S(1)} %get-tuple-element.132), channel_id=1, source_target_pairs={{16,0},{32,16},{48,32},{64,48},{80,64},{96,80},{112,96},{17,1},{33... | collective-permute-start | bytes 115208 | tf_op jit(solution)/shard_map/ppermute | solution.py:23
  266.4 11.3 %collective-permute-start.48 = (f32[75,1,128]{2,1,0:T(1,128)S(1)}, f32[75,1,128]{2,1,0:T(1,128)S(1)}, u32[]{:S(2)}, u32[]{:S(2)}) collective-permute-start(f32[75,1,128]{2,1,0:T(1,128)S(1)} %get-tuple-element.133), channel_id=1, source_target_pairs={{0,16},{16,32},{32,48},{48,64},{64,80},{80,96},{96,112},{1,17},{17... | collective-permute-start | bytes 115208 | tf_op jit(solution)/shard_map/ppermute | solution.py:20
  275.2 7.0 %collective-permute-start.50 = (f32[16,32]{1,0:T(8,128)S(1)}, f32[16,32]{1,0:T(8,128)S(1)}, u32[]{:S(2)}, u32[]{:S(2)}) collective-permute-start(f32[16,32]{1,0:T(8,128)S(1)} %fusion.1), channel_id=1, source_target_pairs={{128,384},{129,385},{130,386},{131,387},{132,388},{133,389},{134,3... | collective-permute-start | bytes 6152 | tf_op jit(solution)/shard_map/ppermute | solution.py:114
  (51 other events, 735.1 us)

commit v6 on v1

--- a/solution.py
+++ b/solution.py
@@ -90,27 +90,32 @@
     return mixed_adj + 0.5 * (east_diff + north_diff)
 
 
-def couple(field_part, weight_table, source_block, peer_count):
+def section_exchange(values, axis):
+    lat_count, lon_count = lax.axis_size("lat"), lax.axis_size("lon")
+    shape = values.shape
+    staged = values.reshape(shape[:axis] + (lat_count, lon_count) + shape[axis + 1 :])
+    staged = lax.all_to_all(staged, "lon", split_axis=axis + 1, concat_axis=axis + 1, tiled=True)
+    staged = lax.all_to_all(staged, "lat", split_axis=axis, concat_axis=axis, tiled=True)
+    return staged.reshape(shape)
+
+
+def couple(field_part, weight_table, source_block, one_hot_out):
     block_cells = weight_table.shape[0]
-    capacity = source_block.shape[-1]
+    peer_count, capacity = one_hot_out.shape[:2]
     surface = field_part[-1].reshape(-1, block_cells)
     gathered = jnp.take(surface, source_block.reshape(-1), axis=0)
     contribution = jnp.einsum("diz,zi->dz", weight_table, gathered, precision=lax.Precision.HIGHEST)
-    return lax.all_to_all(
+    partial = jnp.einsum(
+        "drj,rjb->rdb",
         contribution.reshape(block_cells, peer_count, capacity),
-        ("lat", "lon"),
-        split_axis=1,
-        concat_axis=1,
-        tiled=True,
+        one_hot_out,
+        precision=lax.Precision.HIGHEST,
     )
+    return lax.psum_scatter(partial, ("lat", "lon"), scatter_dimension=0, tiled=True)
 
 
 def reduce_forcing(received, one_hot):
-    block_cells = received.shape[0]
-    arrived = received.reshape(block_cells, -1)
-    accumulated = jnp.dot(
-        arrived, one_hot, precision=lax.Precision.HIGHEST, preferred_element_type=jnp.float32
-    )
+    accumulated = received[0]
     section_count = lax.axis_size("sec")
     return [lax.ppermute(accumulated, "sec", [(s, section_count - 1)]) for s in range(section_count - 1)]
 
@@ -138,11 +143,12 @@
     weight_table = weights[0, 0, 0].astype(jnp.float32)
     block_count = field_part.shape[1] * field_part.shape[2] // weight_table.shape[0]
     capacity = source_block.shape[-1]
-    live_slot = (
-        jnp.arange(capacity, dtype=jnp.int32)[None, :] < record_counts[0, 0, 0][:, None]
-    ).reshape(-1)
-    matches = dest_block.reshape(-1)[:, None] == jnp.arange(block_count, dtype=jnp.int32)[None, :]
-    one_hot = jnp.logical_and(matches, live_slot[:, None]).astype(jnp.float32)
+    live_slot = jnp.arange(capacity, dtype=jnp.int32)[None, :] < record_counts[0, 0, 0][:, None]
+    dest_out = section_exchange(jnp.where(live_slot, dest_block[0, 0, 0], -1), 0)
+    one_hot_out = (
+        dest_out[:, :, None] == jnp.arange(block_count, dtype=jnp.int32)[None, None, :]
+    ).astype(jnp.float32)
+    one_hot = None
 
     def substep(x):
         mixed_adj = column_solve(x, inv, lower, factor)
@@ -166,7 +172,7 @@
         air_done = step + 1
         if air_done <= total_steps and air_done % NSUB == 0:
             in_flight[air_done // NSUB - 1] = (
-                0, couple(field_part, weight_table, source_block, peer_count))
+                0, couple(field_part, weight_table, source_block, one_hot_out))
         if step == total_steps - 1:
             saved = field_part
         ocean_done = step - SKEW + 1

time: 283 us -> 980 us (3.46)
  waiting for transfers between devices: 58.4 us -> 774 us
  starting transfers between devices: 141 us -> 104 us
  between operations: 0.85 us -> 14.1 us
    reduce_scatter x0 -> x4, waiting for transfers between devices: none -> 753 us  [couple(): lax.psum_scatter(partial, ('lat', 'lon'), scatter_dimension=0, tiled=True)]
    all_to_all x4 -> x2, starting transfers between devices: 58.6 us -> 14.9 us  [the longest x1 9.67 us: section_exchange(): lax.all_to_all(staged, 'lat', split_axis=axis, concat_axis=axis, tiled=True)]
    all_to_all x4 -> x2, waiting for transfers between devices: 28.3 us -> 7.4 us  [the longest x1 7.4 us: section_exchange(): lax.all_to_all(staged, 'lon', split_axis=axis + 1, concat_axis=axis + 1,...]
    ppermute x20, starting transfers between devices: 35.8 us -> 49.9 us  [extended(): lax.ppermute(lax.slice_in_dim(block, block.shape[dim] - width, None, axis...]
  transfers between devices with their start and end apart: 56 -> 58, of which waited for: 22 -> 13; matrix products, arithmetic and copies ran while one was open for 11% -> 3% of each run, Pallas kernels for 3% -> 1%
where the time goes in v6:
time: 980 us; the launch traced here: 978 us
  waiting for transfers between devices  774 us (79%)
  starting transfers between devices  104 us (11%)
  other arithmetic  27.4 us (3%)
  Pallas kernels  24.8 us (3%)
  local copies, waits for them, and re-layouts  17.2 us (2%)
  matrix products  16.3 us (2%)
  between operations  14.1 us (1%)
    reduce_scatter x4, waiting for transfers between devices, couple(): lax.psum_scatter(partial, ('lat', 'lon'), scatter_dimension=0, tiled=True)  753 us
    ppermute x20, starting transfers between devices, extended(): lax.ppermute(lax.slice_in_dim(block, block.shape[dim] - width, None, axis...  49.9 us
    ppermute x20, starting transfers between devices, extended(): lax.ppermute(lax.slice_in_dim(block, 0, width, axis=dim), axis, backward)  23.8 us
    pallas_call x10, Pallas kernels, column_solve(): pl.pallas_call(_solve_kernel, out_shape=jax.ShapeDtypeStruct(right.shape,...  22.4 us
  transfers between devices with their start and end apart: 58, of which 13 were waited for; matrix products, arithmetic and copies ran while one was open for 3% of the time, Pallas kernels for 1%

profile of v6, /device:TPU:6, one launch (start us, length us, event | category | flops | bytes accessed | tf_op | source)
XLA Modules:
  0.0 978.0 jit_solution(4985434131924059160)
XLA Ops:
  8.2 2.4 shard_map.91
  10.5 2.3 shard_map.92
  14.0 2.9 collective-permute-start
  18.3 4.9 collective-permute-start.3
  25.4 5.2 all-to-all-start
  30.9 7.4 all-to-all-done
  39.0 1.9 fusion.64.x_ref
  40.9 9.7 all-to-all-start.1
  50.6 2.2 shard_map.93
  57.2 5.2 collective-permute-start.7
  62.4 2.1 copy.38
  66.5 2.2 shard_map.94
  70.5 2.1 collective-permute-start.8
  74.6 4.5 collective-permute-start.11
  80.3 1.9 fusion.98
  82.2 2.2 fusion.3
  85.5 2.2 shard_map.95
  90.1 4.5 collective-permute-start.15
  94.8 1.8 collective-permute-start.12
  96.6 186.5 %reduce-scatter.5.cloned.1.call-done = f32[1,16,32]{2,1,0:T(8,128)} async-done(((f32[128,16,32]{2,1,0:T(8,128)}), f32[1,16,32]{2,1,0:T(8,128)}) %reduce-scatter.5.cloned.1.call-update) | async-done | bytes 2064 | tf_op jit(solution)/shard_map/reduce_scatter | solution.py:114
  288.3 1.8 collective-permute-done.16
  290.1 1.6 collective-permute-done.17
  293.1 1.9 fusion.99
  295.0 2.2 shard_map.96
  301.5 5.2 collective-permute-start.22
  306.7 2.2 fusion.2
  308.9 1.8 fusion.38.x_ref
  310.8 2.2 shard_map.97
  315.3 4.5 collective-permute-start.26
  321.4 188.7 %reduce-scatter.7.cloned.1.call-done = f32[1,16,32]{2,1,0:T(8,128)} async-done(((f32[128,16,32]{2,1,0:T(8,128)}), f32[1,16,32]{2,1,0:T(8,128)}) %reduce-scatter.7.cloned.1.call-update) | async-done | bytes 2064 | tf_op jit(solution)/shard_map/reduce_scatter | solution.py:114
  515.3 1.8 collective-permute-done.27
  520.1 1.9 fusion.100
  522.1 2.2 shard_map.98
  528.5 5.2 collective-permute-start.33
  533.7 2.2 fusion.1
  535.9 1.8 fusion.26.x_ref
  537.8 2.2 shard_map.99
  542.4 4.5 collective-permute-start.37
  548.4 188.7 %reduce-scatter.9.cloned.1.call-done = f32[1,16,32]{2,1,0:T(8,128)} async-done(((f32[128,16,32]{2,1,0:T(8,128)}), f32[1,16,32]{2,1,0:T(8,128)}) %reduce-scatter.9.cloned.1.call-update) | async-done | bytes 2064 | tf_op jit(solution)/shard_map/reduce_scatter | solution.py:114
  742.3 1.8 collective-permute-done.38
  747.1 1.9 fusion.101
  749.1 2.2 shard_map.100
  754.4 4.8 collective-permute-start.44
  759.2 2.2 fusion
  762.4 2.2 shard_map.101
  767.0 4.5 collective-permute-start.48
  773.1 188.9 %reduce-scatter.11.cloned.1.call-done = f32[1,16,32]{2,1,0:T(8,128)} async-done(((f32[128,16,32]{2,1,0:T(8,128)}), f32[1,16,32]{2,1,0:T(8,128)}) %reduce-scatter.11.cloned.1.call-update) | async-done | bytes 2064 | tf_op jit(solution)/shard_map/reduce_scatter | solution.py:114
  967.2 1.8 collective-permute-done.49
  (214 shorter events, 76.7 us)
Async XLA Ops:
  14.0 24.9 %collective-permute-start = (f32[75,4,1]{2,1,0:T(4,128)S(1)}, f32[75,4,1]{2,1,0:T(4,128)S(1)}, u32[]{:S(2)}, u32[]{:S(2)}) collective-permute-start(f32[75,4,1]{2,1,0:T(4,128)S(1)} %get-tuple-element.128), channel_id=1, source_target_pairs={{1,0},{2,1},{3,2},{4,3},{5,4},{6,5},{7,6},{8,7},{9,8},{10,9},{11,1... | collective-permute-start | bytes 3608 | tf_op jit(solution)/shard_map/ppermute | solution.py:23
  17.0 22.0 %collective-permute-start.1 = (f32[75,4,1]{2,1,0:T(4,128)S(1)}, f32[75,4,1]{2,1,0:T(4,128)S(1)}, u32[]{:S(2)}, u32[]{:S(2)}) collective-permute-start(f32[75,4,1]{2,1,0:T(4,128)S(1)} %get-tuple-element.129), channel_id=1, source_target_pairs={{0,1},{1,2},{2,3},{3,4},{4,5},{5,6},{6,7},{7,8},{8,9},{9,10},{10,1... | collective-permute-start | bytes 3608 | tf_op jit(solution)/shard_map/ppermute | solution.py:20
  17.0 21.9 %collective-permute-start.2 = (f32[75,1,128]{2,1,0:T(1,128)S(1)}, f32[75,1,128]{2,1,0:T(1,128)S(1)}, u32[]{:S(2)}, u32[]{:S(2)}) collective-permute-start(f32[75,1,128]{2,1,0:T(1,128)S(1)} %get-tuple-element.132), channel_id=1, source_target_pairs={{16,0},{32,16},{48,32},{64,48},{80,64},{96,80},{112,96},{17,1},{33... | collective-permute-start | bytes 115208 | tf_op jit(solution)/shard_map/ppermute | solution.py:23
  18.3 20.6 %collective-permute-start.3 = (f32[75,1,128]{2,1,0:T(1,128)S(1)}, f32[75,1,128]{2,1,0:T(1,128)S(1)}, u32[]{:S(2)}, u32[]{:S(2)}) collective-permute-start(f32[75,1,128]{2,1,0:T(1,128)S(1)} %get-tuple-element.133), channel_id=1, source_target_pairs={{0,16},{16,32},{32,48},{48,64},{64,80},{80,96},{96,112},{1,17},{17... | collective-permute-start | bytes 115208 | tf_op jit(solution)/shard_map/ppermute | solution.py:20
  25.4 12.9 %all-to-all-start = ((s32[8,16,4]{0,2,1:T(4,128)}), s32[8,16,4]{0,2,1:T(4,128)S(1)}, u32[]{:S(2)}, u32[]{:S(2)}) async-start(s32[8,16,4]{0,2,1:T(4,128)} %copy.29), calls=%async_computation | async-start | bytes 65536 | tf_op jit(solution)/shard_map/all_to_all | solution.py:97
  40.9 23.6 %all-to-all-start.1 = ((s32[8,16,4]{1,2,0:T(4,128)}), s32[8,16,4]{1,2,0:T(4,128)S(1)}, u32[]{:S(2)}, u32[]{:S(2)}) async-start(s32[8,16,4]{1,2,0:T(4,128)} %copy.30), calls=%async_computation.1 | async-start | bytes 32768 | tf_op jit(solution)/shard_map/all_to_all | solution.py:98
  50.6 232.5 %reduce-scatter.5.cloned.1.call-start = ((), (), s32[]{:S(2)}) async-start(), calls=%async_computation.6 | async-start | bytes 1056768 | tf_op jit(solution)/shard_map/reduce_scatter | solution.py:114
  54.8 9.9 %collective-permute-start.4 = (f32[75,4,1]{2,1,0:T(4,128)}, f32[75,4,1]{2,1,0:T(4,128)S(1)}, u32[]{:S(2)}, u32[]{:S(2)}) collective-permute-start(f32[75,4,1]{2,1,0:T(4,128)} %get-tuple-element.122), channel_id=1, source_target_pairs={{1,0},{2,1},{3,2},{4,3},{5,4},{6,5},{7,6},{8,7},{9,8},{10,9},{11,1... | collective-permute-start | bytes 3608 | tf_op jit(solution)/shard_map/ppermute | solution.py:23
  54.8 9.9 %collective-permute-start.5 = (f32[75,4,1]{2,1,0:T(4,128)}, f32[75,4,1]{2,1,0:T(4,128)S(1)}, u32[]{:S(2)}, u32[]{:S(2)}) collective-permute-start(f32[75,4,1]{2,1,0:T(4,128)} %get-tuple-element.123), channel_id=1, source_target_pairs={{0,1},{1,2},{2,3},{3,4},{4,5},{5,6},{6,7},{7,8},{8,9},{9,10},{10,1... | collective-permute-start | bytes 3608 | tf_op jit(solution)/shard_map/ppermute | solution.py:20
  56.0 8.7 collective-permute-start.6
  57.2 7.4 collective-permute-start.7
  70.5 13.9 %collective-permute-start.8 = (f32[75,4,1]{2,1,0:T(4,128)}, f32[75,4,1]{2,1,0:T(4,128)S(1)}, u32[]{:S(2)}, u32[]{:S(2)}) collective-permute-start(f32[75,4,1]{2,1,0:T(4,128)} %get-tuple-element.116), channel_id=1, source_target_pairs={{1,0},{2,1},{3,2},{4,3},{5,4},{6,5},{7,6},{8,7},{9,8},{10,9},{11,1... | collective-permute-start | bytes 3608 | tf_op jit(solution)/shard_map/ppermute | solution.py:23
  72.6 11.8 %collective-permute-start.9 = (f32[75,4,1]{2,1,0:T(4,128)S(1)}, f32[75,4,1]{2,1,0:T(4,128)S(1)}, u32[]{:S(2)}, u32[]{:S(2)}) collective-permute-start(f32[75,4,1]{2,1,0:T(4,128)S(1)} %get-tuple-element.117), channel_id=1, source_target_pairs={{0,1},{1,2},{2,3},{3,4},{4,5},{5,6},{6,7},{7,8},{8,9},{9,10},{10,1... | collective-permute-start | bytes 3608 | tf_op jit(solution)/shard_map/ppermute | solution.py:20
  73.3 11.1 %collective-permute-start.10 = (f32[75,1,128]{2,1,0:T(1,128)}, f32[75,1,128]{2,1,0:T(1,128)S(1)}, u32[]{:S(2)}, u32[]{:S(2)}) collective-permute-start(f32[75,1,128]{2,1,0:T(1,128)} %get-tuple-element.120), channel_id=1, source_target_pairs={{16,0},{32,16},{48,32},{64,48},{80,64},{96,80},{112,96},{17,1},{33... | collective-permute-start | bytes 115208 | tf_op jit(solution)/shard_map/ppermute | solution.py:23
  74.6 9.9 %collective-permute-start.11 = (f32[75,1,128]{2,1,0:T(1,128)S(1)}, f32[75,1,128]{2,1,0:T(1,128)S(1)}, u32[]{:S(2)}, u32[]{:S(2)}) collective-permute-start(f32[75,1,128]{2,1,0:T(1,128)S(1)} %get-tuple-element.121), channel_id=1, source_target_pairs={{0,16},{16,32},{32,48},{48,64},{64,80},{80,96},{96,112},{1,17},{17... | collective-permute-start | bytes 115208 | tf_op jit(solution)/shard_map/ppermute | solution.py:20
  85.5 424.7 %reduce-scatter.7.cloned.1.call-start = ((), (), s32[]{:S(2)}) async-start(), calls=%async_computation.7 | async-start | bytes 1056768 | tf_op jit(solution)/shard_map/reduce_scatter | solution.py:114
  88.8 198.2 %collective-permute-start.14 = (f32[75,1,128]{2,1,0:T(1,128)S(1)}, f32[75,1,128]{2,1,0:T(1,128)S(1)}, u32[]{:S(2)}, u32[]{:S(2)}) collective-permute-start(f32[75,1,128]{2,1,0:T(1,128)S(1)} %get-tuple-element.114), channel_id=1, source_target_pairs={{16,0},{32,16},{48,32},{64,48},{80,64},{96,80},{112,96},{17,1},{33... | collective-permute-start | bytes 115208 | tf_op jit(solution)/shard_map/ppermute | solution.py:23
  90.1 197.0 %collective-permute-start.15 = (f32[75,1,128]{2,1,0:T(1,128)S(1)}, f32[75,1,128]{2,1,0:T(1,128)S(1)}, u32[]{:S(2)}, u32[]{:S(2)}) collective-permute-start(f32[75,1,128]{2,1,0:T(1,128)S(1)} %get-tuple-element.115), channel_id=1, source_target_pairs={{0,16},{16,32},{32,48},{48,64},{64,80},{80,96},{96,112},{1,17},{17... | collective-permute-start | bytes 115208 | tf_op jit(solution)/shard_map/ppermute | solution.py:20
  94.8 189.6 %collective-permute-start.12 = (f32[75,4,1]{2,1,0:T(4,128)S(1)}, f32[75,4,1]{2,1,0:T(4,128)S(1)}, u32[]{:S(2)}, u32[]{:S(2)}) collective-permute-start(f32[75,4,1]{2,1,0:T(4,128)S(1)} %get-tuple-element.110), channel_id=1, source_target_pairs={{1,0},{2,1},{3,2},{4,3},{5,4},{6,5},{7,6},{8,7},{9,8},{10,9},{11,1... | collective-permute-start | bytes 3608 | tf_op jit(solution)/shard_map/ppermute | solution.py:23
  96.6 189.1 %collective-permute-start.13 = (f32[75,4,1]{2,1,0:T(4,128)S(1)}, f32[75,4,1]{2,1,0:T(4,128)S(1)}, u32[]{:S(2)}, u32[]{:S(2)}) collective-permute-start(f32[75,4,1]{2,1,0:T(4,128)S(1)} %get-tuple-element.111), channel_id=1, source_target_pairs={{0,1},{1,2},{2,3},{3,4},{4,5},{5,6},{6,7},{7,8},{8,9},{9,10},{10,1... | collective-permute-start | bytes 3608 | tf_op jit(solution)/shard_map/ppermute | solution.py:20
  284.4 7.3 collective-permute-start.17
  299.0 9.8 %collective-permute-start.19 = (f32[75,4,1]{2,1,0:T(4,128)}, f32[75,4,1]{2,1,0:T(4,128)S(1)}, u32[]{:S(2)}, u32[]{:S(2)}) collective-permute-start(f32[75,4,1]{2,1,0:T(4,128)} %get-tuple-element.104), channel_id=1, source_target_pairs={{1,0},{2,1},{3,2},{4,3},{5,4},{6,5},{7,6},{8,7},{9,8},{10,9},{11,1... | collective-permute-start | bytes 3608 | tf_op jit(solution)/shard_map/ppermute | solution.py:23
  299.0 9.8 %collective-permute-start.20 = (f32[75,4,1]{2,1,0:T(4,128)S(1)}, f32[75,4,1]{2,1,0:T(4,128)S(1)}, u32[]{:S(2)}, u32[]{:S(2)}) collective-permute-start(f32[75,4,1]{2,1,0:T(4,128)S(1)} %get-tuple-element.105), channel_id=1, source_target_pairs={{0,1},{1,2},{2,3},{3,4},{4,5},{5,6},{6,7},{7,8},{8,9},{9,10},{10,1... | collective-permute-start | bytes 3608 | tf_op jit(solution)/shard_map/ppermute | solution.py:20
  300.2 8.6 collective-permute-start.21
  301.5 7.4 collective-permute-start.22
  310.7 426.4 %reduce-scatter.9.cloned.1.call-start = ((), (), s32[]{:S(2)}) async-start(), calls=%async_computation.8 | async-start | bytes 1056768 | tf_op jit(solution)/shard_map/reduce_scatter | solution.py:114
  314.0 200.0 %collective-permute-start.25 = (f32[75,1,128]{2,1,0:T(1,128)S(1)}, f32[75,1,128]{2,1,0:T(1,128)S(1)}, u32[]{:S(2)}, u32[]{:S(2)}) collective-permute-start(f32[75,1,128]{2,1,0:T(1,128)S(1)} %get-tuple-element.102), channel_id=1, source_target_pairs={{16,0},{32,16},{48,32},{64,48},{80,64},{96,80},{112,96},{17,1},{33... | collective-permute-start | bytes 115208 | tf_op jit(solution)/shard_map/ppermute | solution.py:23
  315.3 198.7 %collective-permute-start.26 = (f32[75,1,128]{2,1,0:T(1,128)S(1)}, f32[75,1,128]{2,1,0:T(1,128)S(1)}, u32[]{:S(2)}, u32[]{:S(2)}) collective-permute-start(f32[75,1,128]{2,1,0:T(1,128)S(1)} %get-tuple-element.103), channel_id=1, source_target_pairs={{0,16},{16,32},{32,48},{48,64},{64,80},{80,96},{96,112},{1,17},{17... | collective-permute-start | bytes 115208 | tf_op jit(solution)/shard_map/ppermute | solution.py:20
  320.1 191.4 %collective-permute-start.23 = (f32[75,4,1]{2,1,0:T(4,128)S(1)}, f32[75,4,1]{2,1,0:T(4,128)S(1)}, u32[]{:S(2)}, u32[]{:S(2)}) collective-permute-start(f32[75,4,1]{2,1,0:T(4,128)S(1)} %get-tuple-element.98), channel_id=1, source_target_pairs={{1,0},{2,1},{3,2},{4,3},{5,4},{6,5},{7,6},{8,7},{9,8},{10,9},{11,1... | collective-permute-start | bytes 3608 | tf_op jit(solution)/shard_map/ppermute | solution.py:23
  321.4 191.3 %collective-permute-start.24 = (f32[75,4,1]{2,1,0:T(4,128)S(1)}, f32[75,4,1]{2,1,0:T(4,128)S(1)}, u32[]{:S(2)}, u32[]{:S(2)}) collective-permute-start(f32[75,4,1]{2,1,0:T(4,128)S(1)} %get-tuple-element.99), channel_id=1, source_target_pairs={{0,1},{1,2},{2,3},{3,4},{4,5},{5,6},{6,7},{7,8},{8,9},{9,10},{10,1... | collective-permute-start | bytes 3608 | tf_op jit(solution)/shard_map/ppermute | solution.py:20
  511.4 7.3 collective-permute-start.28
  526.1 9.8 %collective-permute-start.30 = (f32[75,4,1]{2,1,0:T(4,128)}, f32[75,4,1]{2,1,0:T(4,128)S(1)}, u32[]{:S(2)}, u32[]{:S(2)}) collective-permute-start(f32[75,4,1]{2,1,0:T(4,128)} %get-tuple-element.90), channel_id=1, source_target_pairs={{1,0},{2,1},{3,2},{4,3},{5,4},{6,5},{7,6},{8,7},{9,8},{10,9},{11,1... | collective-permute-start | bytes 3608 | tf_op jit(solution)/shard_map/ppermute | solution.py:23
  526.1 9.8 %collective-permute-start.31 = (f32[75,4,1]{2,1,0:T(4,128)S(1)}, f32[75,4,1]{2,1,0:T(4,128)S(1)}, u32[]{:S(2)}, u32[]{:S(2)}) collective-permute-start(f32[75,4,1]{2,1,0:T(4,128)S(1)} %get-tuple-element.91), channel_id=1, source_target_pairs={{0,1},{1,2},{2,3},{3,4},{4,5},{5,6},{6,7},{7,8},{8,9},{9,10},{10,1... | collective-permute-start | bytes 3608 | tf_op jit(solution)/shard_map/ppermute | solution.py:20
  527.3 8.6 collective-permute-start.32
  528.5 7.4 collective-permute-start.33
  537.7 424.2 %reduce-scatter.11.cloned.1.call-start = ((), (), s32[]{:S(2)}) async-start(), calls=%async_computation.9 | async-start | bytes 1056768 | tf_op jit(solution)/shard_map/reduce_scatter | solution.py:114
  541.1 200.0 %collective-permute-start.36 = (f32[75,1,128]{2,1,0:T(1,128)S(1)}, f32[75,1,128]{2,1,0:T(1,128)S(1)}, u32[]{:S(2)}, u32[]{:S(2)}) collective-permute-start(f32[75,1,128]{2,1,0:T(1,128)S(1)} %get-tuple-element.88), channel_id=1, source_target_pairs={{16,0},{32,16},{48,32},{64,48},{80,64},{96,80},{112,96},{17,1},{33... | collective-permute-start | bytes 115208 | tf_op jit(solution)/shard_map/ppermute | solution.py:23
  542.4 198.7 %collective-permute-start.37 = (f32[75,1,128]{2,1,0:T(1,128)S(1)}, f32[75,1,128]{2,1,0:T(1,128)S(1)}, u32[]{:S(2)}, u32[]{:S(2)}) collective-permute-start(f32[75,1,128]{2,1,0:T(1,128)S(1)} %get-tuple-element.89), channel_id=1, source_target_pairs={{0,16},{16,32},{32,48},{48,64},{64,80},{80,96},{96,112},{1,17},{17... | collective-permute-start | bytes 115208 | tf_op jit(solution)/shard_map/ppermute | solution.py:20
  547.1 191.3 %collective-permute-start.34 = (f32[75,4,1]{2,1,0:T(4,128)S(1)}, f32[75,4,1]{2,1,0:T(4,128)S(1)}, u32[]{:S(2)}, u32[]{:S(2)}) collective-permute-start(f32[75,4,1]{2,1,0:T(4,128)S(1)} %get-tuple-element.84), channel_id=1, source_target_pairs={{1,0},{2,1},{3,2},{4,3},{5,4},{6,5},{7,6},{8,7},{9,8},{10,9},{11,1... | collective-permute-start | bytes 3608 | tf_op jit(solution)/shard_map/ppermute | solution.py:23
  548.4 191.3 %collective-permute-start.35 = (f32[75,4,1]{2,1,0:T(4,128)S(1)}, f32[75,4,1]{2,1,0:T(4,128)S(1)}, u32[]{:S(2)}, u32[]{:S(2)}) collective-permute-start(f32[75,4,1]{2,1,0:T(4,128)S(1)} %get-tuple-element.85), channel_id=1, source_target_pairs={{0,1},{1,2},{2,3},{3,4},{4,5},{5,6},{6,7},{7,8},{8,9},{9,10},{10,1... | collective-permute-start | bytes 3608 | tf_op jit(solution)/shard_map/ppermute | solution.py:20
  752.5 8.8 collective-permute-start.41
  752.5 8.8 collective-permute-start.42
  753.1 8.3 collective-permute-start.43
  765.7 200.2 %collective-permute-start.47 = (f32[75,1,128]{2,1,0:T(1,128)S(1)}, f32[75,1,128]{2,1,0:T(1,128)S(1)}, u32[]{:S(2)}, u32[]{:S(2)}) collective-permute-start(f32[75,1,128]{2,1,0:T(1,128)S(1)} %get-tuple-element.74), channel_id=1, source_target_pairs={{16,0},{32,16},{48,32},{64,48},{80,64},{96,80},{112,96},{17,1},{33... | collective-permute-start | bytes 115208 | tf_op jit(solution)/shard_map/ppermute | solution.py:23
  767.0 198.9 %collective-permute-start.48 = (f32[75,1,128]{2,1,0:T(1,128)S(1)}, f32[75,1,128]{2,1,0:T(1,128)S(1)}, u32[]{:S(2)}, u32[]{:S(2)}) collective-permute-start(f32[75,1,128]{2,1,0:T(1,128)S(1)} %get-tuple-element.75), channel_id=1, source_target_pairs={{0,16},{16,32},{32,48},{48,64},{64,80},{80,96},{96,112},{1,17},{17... | collective-permute-start | bytes 115208 | tf_op jit(solution)/shard_map/ppermute | solution.py:20
  771.7 191.6 %collective-permute-start.45 = (f32[75,4,1]{2,1,0:T(4,128)S(1)}, f32[75,4,1]{2,1,0:T(4,128)S(1)}, u32[]{:S(2)}, u32[]{:S(2)}) collective-permute-start(f32[75,4,1]{2,1,0:T(4,128)S(1)} %get-tuple-element.70), channel_id=1, source_target_pairs={{1,0},{2,1},{3,2},{4,3},{5,4},{6,5},{7,6},{8,7},{9,8},{10,9},{11,1... | collective-permute-start | bytes 3608 | tf_op jit(solution)/shard_map/ppermute | solution.py:23
  773.1 191.5 %collective-permute-start.46 = (f32[75,4,1]{2,1,0:T(4,128)S(1)}, f32[75,4,1]{2,1,0:T(4,128)S(1)}, u32[]{:S(2)}, u32[]{:S(2)}) collective-permute-start(f32[75,4,1]{2,1,0:T(4,128)S(1)} %get-tuple-element.71), channel_id=1, source_target_pairs={{0,1},{1,2},{2,3},{3,4},{4,5},{5,6},{6,7},{7,8},{8,9},{9,10},{10,1... | collective-permute-start | bytes 3608 | tf_op jit(solution)/shard_map/ppermute | solution.py:20
  963.3 7.3 collective-permute-start.50
  (28 other events, 384.9 us)
Sparse Core Ops, SparseCore 0:
  85.6 197.4 reduce-scatter.4
  310.8 199.2 reduce-scatter.6
  537.9 199.2 reduce-scatter.8
  762.5 199.4 reduce-scatter.10

commit v7 on v3

--- a/solution.py
+++ b/solution.py
@@ -98,8 +98,8 @@
     contribution = jnp.einsum("diz,zi->dz", weight_table, gathered, precision=lax.Precision.HIGHEST)
     lat_count, lon_count = lax.axis_size("lat"), lax.axis_size("lon")
     staged = contribution.reshape(block_cells, lat_count, lon_count, capacity)
+    staged = lax.all_to_all(staged, "lat", split_axis=1, concat_axis=1, tiled=True)
     staged = lax.all_to_all(staged, "lon", split_axis=2, concat_axis=2, tiled=True)
-    staged = lax.all_to_all(staged, "lat", split_axis=1, concat_axis=1, tiled=True)
     return staged.reshape(block_cells, peer_count, capacity)
 
 

time: 270 us -> 275 us (1.019)
  local copies, waits for them, and re-layouts: 27.5 us -> 30.8 us
  waiting for transfers between devices: 26.6 us -> 29.6 us
    all_to_all x4, starting transfers between devices: 17.6 us -> 23.7 us  [couple(): lax.all_to_all(staged, 'lon', split_axis=2, concat_axis=2, tiled=True)]
    ppermute x20, starting transfers between devices: 32 us -> 27.3 us  [extended(): lax.ppermute(lax.slice_in_dim(block, 0, width, axis=dim), axis, backward)]
  transfers between devices with their start and end apart: 60 -> 60, of which waited for: 17 -> 17; matrix products, arithmetic and copies ran while one was open for 16% -> 17% of each run, Pallas kernels for 3% -> 3%
where the time goes in v7:
time: 275 us; the launch traced here: 273 us
  starting transfers between devices  144 us (52%)
  other arithmetic  32.5 us (12%)
  local copies, waits for them, and re-layouts  30.8 us (11%)
  waiting for transfers between devices  29.6 us (11%)
  Pallas kernels  24.8 us (9%)
  matrix products  9.64 us (4%)
    ppermute x20, starting transfers between devices, extended(): lax.ppermute(lax.slice_in_dim(block, block.shape[dim] - width, None, axis...  48 us
    all_to_all x4, starting transfers between devices, couple(): lax.all_to_all(staged, 'lat', split_axis=1, concat_axis=1, tiled=True)  29.5 us
    ppermute x20, starting transfers between devices, extended(): lax.ppermute(lax.slice_in_dim(block, 0, width, axis=dim), axis, backward)  27.3 us
    all_to_all x4, starting transfers between devices, couple(): lax.all_to_all(staged, 'lon', split_axis=2, concat_axis=2, tiled=True)  23.7 us
    pallas_call x10, Pallas kernels, column_solve(): pl.pallas_call(_solve_kernel, out_shape=jax.ShapeDtypeStruct(right.shape,...  22.5 us
    ppermute x12, starting transfers between devices, reduce_forcing(): lax.ppermute(accumulated, 'sec', [(s, section_count - 1)])  15.8 us
    ppermute x12, waiting for transfers between devices, reduce_forcing(): lax.ppermute(accumulated, 'sec', [(s, section_count - 1)])  13.2 us
    slice x20, local copies, waits for them, and re-layouts, extended(): lax.slice_in_dim(block, 0, width, axis=dim)  11.3 us
  transfers between devices with their start and end apart: 60, of which 17 were waited for; matrix products, arithmetic and copies ran while one was open for 17% of the time, Pallas kernels for 3%

profile of v7, /device:TPU:6, one launch (start us, length us, event | category | flops | bytes accessed | tf_op | source)
XLA Modules:
  0.0 272.8 jit_solution(3440684548266257088)
XLA Ops:
  1.6 2.3 shard_map.91
  4.0 2.3 shard_map.92
  7.5 2.9 %collective-permute-start = (f32[75,4,1]{2,1,0:T(4,128)S(1)}, f32[75,4,1]{2,1,0:T(4,128)S(1)}, u32[]{:S(2)}, u32[]{:S(2)}) collective-permute-start(f32[75,4,1]{2,1,0:T(4,128)S(1)} %get-tuple-element.128), channel_id=1, source_target_pairs={{1,0},{2,1},{3,2},{4,3},{5,4},{6,5},{7,6},{8,7},{9,8},{10,9},{11,1... | collective-permute-start | bytes 3608 | tf_op jit(solution)/shard_map/ppermute | solution.py:23
  11.8 4.9 %collective-permute-start.3 = (f32[75,1,128]{2,1,0:T(1,128)S(1)}, f32[75,1,128]{2,1,0:T(1,128)S(1)}, u32[]{:S(2)}, u32[]{:S(2)}) collective-permute-start(f32[75,1,128]{2,1,0:T(1,128)S(1)} %get-tuple-element.133), channel_id=1, source_target_pairs={{0,16},{16,32},{32,48},{48,64},{64,80},{80,96},{96,112},{1,17},{17... | collective-permute-start | bytes 115208 | tf_op jit(solution)/shard_map/ppermute | solution.py:20
  18.3 1.9 fusion.69.x_ref
  20.2 2.3 shard_map.93
  24.4 2.1 collective-permute-start.4
  27.8 4.9 %collective-permute-start.7 = (f32[75,1,128]{2,1,0:T(1,128)S(1)}, f32[75,1,128]{2,1,0:T(1,128)S(1)}, u32[]{:S(2)}, u32[]{:S(2)}) collective-permute-start(f32[75,1,128]{2,1,0:T(1,128)S(1)} %get-tuple-element.127), channel_id=1, source_target_pairs={{0,16},{16,32},{32,48},{48,64},{64,80},{80,96},{96,112},{1,17},{17... | collective-permute-start | bytes 115208 | tf_op jit(solution)/shard_map/ppermute | solution.py:20
  32.8 2.1 copy.45
  37.2 2.2 shard_map.94
  41.3 2.7 collective-permute-start.8
  45.4 4.9 %collective-permute-start.11 = (f32[75,1,128]{2,1,0:T(1,128)S(1)}, f32[75,1,128]{2,1,0:T(1,128)S(1)}, u32[]{:S(2)}, u32[]{:S(2)}) collective-permute-start(f32[75,1,128]{2,1,0:T(1,128)S(1)} %get-tuple-element.121), channel_id=1, source_target_pairs={{0,16},{16,32},{32,48},{48,64},{64,80},{80,96},{96,112},{1,17},{17... | collective-permute-start | bytes 115208 | tf_op jit(solution)/shard_map/ppermute | solution.py:20
  51.5 1.9 fusion.106
  55.2 10.9 %all-to-all-start = ((f32[8,1,1024]{2,1,0:T(1,128)}), f32[8,1,1024]{2,1,0:T(1,128)S(1)}, u32[]{:S(2)}, u32[]{:S(2)}) async-start(f32[8,1,1024]{2,1,0:T(1,128)} %reshape.278), calls=%async_computation | async-start | bytes 65536 | tf_op jit(solution)/shard_map/all_to_all | solution.py:101
  66.1 2.2 shard_map.95
  71.7 2.4 all-to-all-done
  76.3 4.3 %all-to-all-start.1 = ((f32[16,1,512]{2,1,0:T(1,128)}), f32[16,1,512]{2,1,0:T(1,128)S(1)}, u32[]{:S(2)}, u32[]{:S(2)}) async-start(f32[16,1,512]{2,1,0:T(1,128)} %reshape.280), calls=%async_computation.1 | async-start | bytes 65536 | tf_op jit(solution)/shard_map/all_to_all | solution.py:102
  82.7 4.5 %collective-permute-start.15 = (f32[75,1,128]{2,1,0:T(1,128)}, f32[75,1,128]{2,1,0:T(1,128)S(1)}, u32[]{:S(2)}, u32[]{:S(2)}) collective-permute-start(f32[75,1,128]{2,1,0:T(1,128)} %get-tuple-element.115), channel_id=1, source_target_pairs={{0,16},{16,32},{32,48},{48,64},{64,80},{80,96},{96,112},{1,17},{17... | collective-permute-start | bytes 115208 | tf_op jit(solution)/shard_map/ppermute | solution.py:20
  100.1 2.2 shard_map.96
  106.7 4.7 %collective-permute-start.22 = (f32[75,1,128]{2,1,0:T(1,128)}, f32[75,1,128]{2,1,0:T(1,128)S(1)}, u32[]{:S(2)}, u32[]{:S(2)}) collective-permute-start(f32[75,1,128]{2,1,0:T(1,128)} %get-tuple-element.109), channel_id=1, source_target_pairs={{0,16},{16,32},{32,48},{48,64},{64,80},{80,96},{96,112},{1,17},{17... | collective-permute-start | bytes 115208 | tf_op jit(solution)/shard_map/ppermute | solution.py:20
  111.4 1.9 fusion.107
  114.2 1.9 fusion.43.x_ref
  116.1 6.6 %all-to-all-start.2 = ((f32[8,1,1024]{2,1,0:T(1,128)}), f32[8,1,1024]{2,1,0:T(1,128)S(1)}, u32[]{:S(2)}, u32[]{:S(2)}) async-start(f32[8,1,1024]{2,1,0:T(1,128)} %reshape.282), calls=%async_computation.2 | async-start | bytes 65536 | tf_op jit(solution)/shard_map/all_to_all | solution.py:101
  122.6 2.2 shard_map.97
  128.4 2.2 all-to-all-done.2
  132.4 6.5 %all-to-all-start.3 = ((f32[16,1,512]{2,1,0:T(1,128)}), f32[16,1,512]{2,1,0:T(1,128)S(1)}, u32[]{:S(2)}, u32[]{:S(2)}) async-start(f32[16,1,512]{2,1,0:T(1,128)} %reshape.284), calls=%async_computation.3 | async-start | bytes 65536 | tf_op jit(solution)/shard_map/all_to_all | solution.py:102
  140.9 4.5 %collective-permute-start.26 = (f32[75,1,128]{2,1,0:T(1,128)}, f32[75,1,128]{2,1,0:T(1,128)S(1)}, u32[]{:S(2)}, u32[]{:S(2)}) collective-permute-start(f32[75,1,128]{2,1,0:T(1,128)} %get-tuple-element.103), channel_id=1, source_target_pairs={{0,16},{16,32},{32,48},{48,64},{64,80},{80,96},{96,112},{1,17},{17... | collective-permute-start | bytes 115208 | tf_op jit(solution)/shard_map/ppermute | solution.py:20
  158.3 2.2 shard_map.98
  164.9 4.5 %collective-permute-start.33 = (f32[75,1,128]{2,1,0:T(1,128)}, f32[75,1,128]{2,1,0:T(1,128)S(1)}, u32[]{:S(2)}, u32[]{:S(2)}) collective-permute-start(f32[75,1,128]{2,1,0:T(1,128)} %get-tuple-element.95), channel_id=1, source_target_pairs={{0,16},{16,32},{32,48},{48,64},{64,80},{80,96},{96,112},{1,17},{17... | collective-permute-start | bytes 115208 | tf_op jit(solution)/shard_map/ppermute | solution.py:20
  169.4 1.9 fusion.108
  172.2 1.9 fusion.31.x_ref
  174.1 6.0 %all-to-all-start.4 = ((f32[8,1,1024]{2,1,0:T(1,128)}), f32[8,1,1024]{2,1,0:T(1,128)S(1)}, u32[]{:S(2)}, u32[]{:S(2)}) async-start(f32[8,1,1024]{2,1,0:T(1,128)} %reshape.286), calls=%async_computation.4 | async-start | bytes 65536 | tf_op jit(solution)/shard_map/all_to_all | solution.py:101
  180.1 2.2 shard_map.99
  185.9 2.2 all-to-all-done.4
  189.9 6.5 %all-to-all-start.5 = ((f32[16,1,512]{2,1,0:T(1,128)}), f32[16,1,512]{2,1,0:T(1,128)S(1)}, u32[]{:S(2)}, u32[]{:S(2)}) async-start(f32[16,1,512]{2,1,0:T(1,128)} %reshape.288), calls=%async_computation.5 | async-start | bytes 65536 | tf_op jit(solution)/shard_map/all_to_all | solution.py:102
  198.4 4.5 %collective-permute-start.37 = (f32[75,1,128]{2,1,0:T(1,128)}, f32[75,1,128]{2,1,0:T(1,128)S(1)}, u32[]{:S(2)}, u32[]{:S(2)}) collective-permute-start(f32[75,1,128]{2,1,0:T(1,128)} %get-tuple-element.89), channel_id=1, source_target_pairs={{0,16},{16,32},{32,48},{48,64},{64,80},{80,96},{96,112},{1,17},{17... | collective-permute-start | bytes 115208 | tf_op jit(solution)/shard_map/ppermute | solution.py:20
  215.8 2.2 shard_map.100
  222.4 4.5 %collective-permute-start.44 = (f32[75,1,128]{2,1,0:T(1,128)}, f32[75,1,128]{2,1,0:T(1,128)S(1)}, u32[]{:S(2)}, u32[]{:S(2)}) collective-permute-start(f32[75,1,128]{2,1,0:T(1,128)} %get-tuple-element.81), channel_id=1, source_target_pairs={{0,16},{16,32},{32,48},{48,64},{64,80},{80,96},{96,112},{1,17},{17... | collective-permute-start | bytes 115208 | tf_op jit(solution)/shard_map/ppermute | solution.py:20
  226.9 1.9 fusion.109
  229.7 2.0 fusion.19.x_ref
  231.6 6.0 %all-to-all-start.6 = ((f32[8,1,1024]{2,1,0:T(1,128)}), f32[8,1,1024]{2,1,0:T(1,128)S(1)}, u32[]{:S(2)}, u32[]{:S(2)}) async-start(f32[8,1,1024]{2,1,0:T(1,128)} %reshape.290), calls=%async_computation.6 | async-start | bytes 65536 | tf_op jit(solution)/shard_map/all_to_all | solution.py:101
  237.7 2.2 shard_map.101
  241.1 1.6 collective-permute-start.45
  242.8 2.9 %all-to-all-done.6 = f32[8,1,1024]{2,1,0:T(1,128)S(1)} async-done(((f32[8,1,1024]{2,1,0:T(1,128)}), f32[8,1,1024]{2,1,0:T(1,128)S(1)}, u32[]{:S(2)}, u32[]{:S(2)}) %all-to-all-start.6) | async-done | bytes 32800 | tf_op jit(solution)/shard_map/all_to_all | solution.py:101
  247.5 6.5 %all-to-all-start.7 = ((f32[16,1,512]{2,1,0:T(1,128)}), f32[16,1,512]{2,1,0:T(1,128)S(1)}, u32[]{:S(2)}, u32[]{:S(2)}) async-start(f32[16,1,512]{2,1,0:T(1,128)} %reshape.292), calls=%async_computation.7 | async-start | bytes 65536 | tf_op jit(solution)/shard_map/all_to_all | solution.py:102
  255.3 4.5 %collective-permute-start.48 = (f32[75,1,128]{2,1,0:T(1,128)S(1)}, f32[75,1,128]{2,1,0:T(1,128)S(1)}, u32[]{:S(2)}, u32[]{:S(2)}) collective-permute-start(f32[75,1,128]{2,1,0:T(1,128)S(1)} %get-tuple-element.75), channel_id=1, source_target_pairs={{0,16},{16,32},{32,48},{48,64},{64,80},{80,96},{96,112},{1,17},{17... | collective-permute-start | bytes 115208 | tf_op jit(solution)/shard_map/ppermute | solution.py:20
  259.9 1.8 all-to-all-done.7
  267.9 2.4 collective-permute-done.49
  (261 shorter events, 106.1 us)
Async XLA Ops:
  7.5 9.6 %collective-permute-start = (f32[75,4,1]{2,1,0:T(4,128)S(1)}, f32[75,4,1]{2,1,0:T(4,128)S(1)}, u32[]{:S(2)}, u32[]{:S(2)}) collective-permute-start(f32[75,4,1]{2,1,0:T(4,128)S(1)} %get-tuple-element.128), channel_id=1, source_target_pairs={{1,0},{2,1},{3,2},{4,3},{5,4},{6,5},{7,6},{8,7},{9,8},{10,9},{11,1... | collective-permute-start | bytes 3608 | tf_op jit(solution)/shard_map/ppermute | solution.py:23
  24.4 10.8 %collective-permute-start.4 = (f32[75,4,1]{2,1,0:T(4,128)}, f32[75,4,1]{2,1,0:T(4,128)S(1)}, u32[]{:S(2)}, u32[]{:S(2)}) collective-permute-start(f32[75,4,1]{2,1,0:T(4,128)} %get-tuple-element.122), channel_id=1, source_target_pairs={{1,0},{2,1},{3,2},{4,3},{5,4},{6,5},{7,6},{8,7},{9,8},{10,9},{11,1... | collective-permute-start | bytes 3608 | tf_op jit(solution)/shard_map/ppermute | solution.py:23
  26.5 8.7 %collective-permute-start.5 = (f32[75,4,1]{2,1,0:T(4,128)}, f32[75,4,1]{2,1,0:T(4,128)}, u32[]{:S(2)}, u32[]{:S(2)}) collective-permute-start(f32[75,4,1]{2,1,0:T(4,128)} %get-tuple-element.123), channel_id=1, source_target_pairs={{0,1},{1,2},{2,3},{3,4},{4,5},{5,6},{6,7},{7,8},{8,9},{9,10},{10,1... | collective-permute-start | bytes 3608 | tf_op jit(solution)/shard_map/ppermute | solution.py:20
  26.5 8.7 %collective-permute-start.6 = (f32[75,1,128]{2,1,0:T(1,128)S(1)}, f32[75,1,128]{2,1,0:T(1,128)S(1)}, u32[]{:S(2)}, u32[]{:S(2)}) collective-permute-start(f32[75,1,128]{2,1,0:T(1,128)S(1)} %get-tuple-element.126), channel_id=1, source_target_pairs={{16,0},{32,16},{48,32},{64,48},{80,64},{96,80},{112,96},{17,1},{33... | collective-permute-start | bytes 115208 | tf_op jit(solution)/shard_map/ppermute | solution.py:23
  27.8 7.4 %collective-permute-start.7 = (f32[75,1,128]{2,1,0:T(1,128)S(1)}, f32[75,1,128]{2,1,0:T(1,128)S(1)}, u32[]{:S(2)}, u32[]{:S(2)}) collective-permute-start(f32[75,1,128]{2,1,0:T(1,128)S(1)} %get-tuple-element.127), channel_id=1, source_target_pairs={{0,16},{16,32},{32,48},{48,64},{64,80},{80,96},{96,112},{1,17},{17... | collective-permute-start | bytes 115208 | tf_op jit(solution)/shard_map/ppermute | solution.py:20
  41.3 12.9 %collective-permute-start.8 = (f32[75,4,1]{2,1,0:T(4,128)}, f32[75,4,1]{2,1,0:T(4,128)S(1)}, u32[]{:S(2)}, u32[]{:S(2)}) collective-permute-start(f32[75,4,1]{2,1,0:T(4,128)} %get-tuple-element.116), channel_id=1, source_target_pairs={{1,0},{2,1},{3,2},{4,3},{5,4},{6,5},{7,6},{8,7},{9,8},{10,9},{11,1... | collective-permute-start | bytes 3608 | tf_op jit(solution)/shard_map/ppermute | solution.py:23
  44.0 10.2 %collective-permute-start.9 = (f32[75,4,1]{2,1,0:T(4,128)}, f32[75,4,1]{2,1,0:T(4,128)S(1)}, u32[]{:S(2)}, u32[]{:S(2)}) collective-permute-start(f32[75,4,1]{2,1,0:T(4,128)} %get-tuple-element.117), channel_id=1, source_target_pairs={{0,1},{1,2},{2,3},{3,4},{4,5},{5,6},{6,7},{7,8},{8,9},{9,10},{10,1... | collective-permute-start | bytes 3608 | tf_op jit(solution)/shard_map/ppermute | solution.py:20
  44.1 10.1 %collective-permute-start.10 = (f32[75,1,128]{2,1,0:T(1,128)S(1)}, f32[75,1,128]{2,1,0:T(1,128)S(1)}, u32[]{:S(2)}, u32[]{:S(2)}) collective-permute-start(f32[75,1,128]{2,1,0:T(1,128)S(1)} %get-tuple-element.120), channel_id=1, source_target_pairs={{16,0},{32,16},{48,32},{64,48},{80,64},{96,80},{112,96},{17,1},{33... | collective-permute-start | bytes 115208 | tf_op jit(solution)/shard_map/ppermute | solution.py:23
  45.4 8.8 %collective-permute-start.11 = (f32[75,1,128]{2,1,0:T(1,128)S(1)}, f32[75,1,128]{2,1,0:T(1,128)S(1)}, u32[]{:S(2)}, u32[]{:S(2)}) collective-permute-start(f32[75,1,128]{2,1,0:T(1,128)S(1)} %get-tuple-element.121), channel_id=1, source_target_pairs={{0,16},{16,32},{32,48},{48,64},{64,80},{80,96},{96,112},{1,17},{17... | collective-permute-start | bytes 115208 | tf_op jit(solution)/shard_map/ppermute | solution.py:20
  55.2 18.9 %all-to-all-start = ((f32[8,1,1024]{2,1,0:T(1,128)}), f32[8,1,1024]{2,1,0:T(1,128)S(1)}, u32[]{:S(2)}, u32[]{:S(2)}) async-start(f32[8,1,1024]{2,1,0:T(1,128)} %reshape.278), calls=%async_computation | async-start | bytes 65536 | tf_op jit(solution)/shard_map/all_to_all | solution.py:101
  70.2 21.4 %collective-permute-start.12 = (f32[75,4,1]{2,1,0:T(4,128)}, f32[75,4,1]{2,1,0:T(4,128)S(1)}, u32[]{:S(2)}, u32[]{:S(2)}) collective-permute-start(f32[75,4,1]{2,1,0:T(4,128)} %get-tuple-element.110), channel_id=1, source_target_pairs={{1,0},{2,1},{3,2},{4,3},{5,4},{6,5},{7,6},{8,7},{9,8},{10,9},{11,1... | collective-permute-start | bytes 3608 | tf_op jit(solution)/shard_map/ppermute | solution.py:23
  71.7 21.2 %collective-permute-start.13 = (f32[75,4,1]{2,1,0:T(4,128)}, f32[75,4,1]{2,1,0:T(4,128)}, u32[]{:S(2)}, u32[]{:S(2)}) collective-permute-start(f32[75,4,1]{2,1,0:T(4,128)} %get-tuple-element.111), channel_id=1, source_target_pairs={{0,1},{1,2},{2,3},{3,4},{4,5},{5,6},{6,7},{7,8},{8,9},{9,10},{10,1... | collective-permute-start | bytes 3608 | tf_op jit(solution)/shard_map/ppermute | solution.py:20
  76.3 12.0 %all-to-all-start.1 = ((f32[16,1,512]{2,1,0:T(1,128)}), f32[16,1,512]{2,1,0:T(1,128)S(1)}, u32[]{:S(2)}, u32[]{:S(2)}) async-start(f32[16,1,512]{2,1,0:T(1,128)} %reshape.280), calls=%async_computation.1 | async-start | bytes 65536 | tf_op jit(solution)/shard_map/all_to_all | solution.py:102
  81.4 12.8 %collective-permute-start.14 = (f32[75,1,128]{2,1,0:T(1,128)}, f32[75,1,128]{2,1,0:T(1,128)S(1)}, u32[]{:S(2)}, u32[]{:S(2)}) collective-permute-start(f32[75,1,128]{2,1,0:T(1,128)} %get-tuple-element.114), channel_id=1, source_target_pairs={{16,0},{32,16},{48,32},{64,48},{80,64},{96,80},{112,96},{17,1},{33... | collective-permute-start | bytes 115208 | tf_op jit(solution)/shard_map/ppermute | solution.py:23
  82.7 11.6 %collective-permute-start.15 = (f32[75,1,128]{2,1,0:T(1,128)}, f32[75,1,128]{2,1,0:T(1,128)S(1)}, u32[]{:S(2)}, u32[]{:S(2)}) collective-permute-start(f32[75,1,128]{2,1,0:T(1,128)} %get-tuple-element.115), channel_id=1, source_target_pairs={{0,16},{16,32},{32,48},{48,64},{64,80},{80,96},{96,112},{1,17},{17... | collective-permute-start | bytes 115208 | tf_op jit(solution)/shard_map/ppermute | solution.py:20
  91.6 7.0 %collective-permute-start.17 = (f32[16,32]{1,0:T(8,128)S(1)}, f32[16,32]{1,0:T(8,128)S(1)}, u32[]{:S(2)}, u32[]{:S(2)}) collective-permute-start(f32[16,32]{1,0:T(8,128)S(1)} %fusion.7), channel_id=1, source_target_pairs={{128,384},{129,385},{130,386},{131,387},{132,388},{133,389},{134,3... | collective-permute-start | bytes 6152 | tf_op jit(solution)/shard_map/ppermute | solution.py:113
  104.2 9.9 %collective-permute-start.19 = (f32[75,4,1]{2,1,0:T(4,128)}, f32[75,4,1]{2,1,0:T(4,128)S(1)}, u32[]{:S(2)}, u32[]{:S(2)}) collective-permute-start(f32[75,4,1]{2,1,0:T(4,128)} %get-tuple-element.104), channel_id=1, source_target_pairs={{1,0},{2,1},{3,2},{4,3},{5,4},{6,5},{7,6},{8,7},{9,8},{10,9},{11,1... | collective-permute-start | bytes 3608 | tf_op jit(solution)/shard_map/ppermute | solution.py:23
  104.3 9.8 %collective-permute-start.20 = (f32[75,4,1]{2,1,0:T(4,128)}, f32[75,4,1]{2,1,0:T(4,128)}, u32[]{:S(2)}, u32[]{:S(2)}) collective-permute-start(f32[75,4,1]{2,1,0:T(4,128)} %get-tuple-element.105), channel_id=1, source_target_pairs={{0,1},{1,2},{2,3},{3,4},{4,5},{5,6},{6,7},{7,8},{8,9},{9,10},{10,1... | collective-permute-start | bytes 3608 | tf_op jit(solution)/shard_map/ppermute | solution.py:20
  105.4 8.8 %collective-permute-start.21 = (f32[75,1,128]{2,1,0:T(1,128)}, f32[75,1,128]{2,1,0:T(1,128)S(1)}, u32[]{:S(2)}, u32[]{:S(2)}) collective-permute-start(f32[75,1,128]{2,1,0:T(1,128)} %get-tuple-element.108), channel_id=1, source_target_pairs={{16,0},{32,16},{48,32},{64,48},{80,64},{96,80},{112,96},{17,1},{33... | collective-permute-start | bytes 115208 | tf_op jit(solution)/shard_map/ppermute | solution.py:23
  106.7 7.5 %collective-permute-start.22 = (f32[75,1,128]{2,1,0:T(1,128)}, f32[75,1,128]{2,1,0:T(1,128)S(1)}, u32[]{:S(2)}, u32[]{:S(2)}) collective-permute-start(f32[75,1,128]{2,1,0:T(1,128)} %get-tuple-element.109), channel_id=1, source_target_pairs={{0,16},{16,32},{32,48},{48,64},{64,80},{80,96},{96,112},{1,17},{17... | collective-permute-start | bytes 115208 | tf_op jit(solution)/shard_map/ppermute | solution.py:20
  116.1 14.6 %all-to-all-start.2 = ((f32[8,1,1024]{2,1,0:T(1,128)}), f32[8,1,1024]{2,1,0:T(1,128)S(1)}, u32[]{:S(2)}, u32[]{:S(2)}) async-start(f32[8,1,1024]{2,1,0:T(1,128)} %reshape.282), calls=%async_computation.2 | async-start | bytes 65536 | tf_op jit(solution)/shard_map/all_to_all | solution.py:101
  126.8 23.1 %collective-permute-start.23 = (f32[75,4,1]{2,1,0:T(4,128)}, f32[75,4,1]{2,1,0:T(4,128)S(1)}, u32[]{:S(2)}, u32[]{:S(2)}) collective-permute-start(f32[75,4,1]{2,1,0:T(4,128)} %get-tuple-element.98), channel_id=1, source_target_pairs={{1,0},{2,1},{3,2},{4,3},{5,4},{6,5},{7,6},{8,7},{9,8},{10,9},{11,1... | collective-permute-start | bytes 3608 | tf_op jit(solution)/shard_map/ppermute | solution.py:23
  128.4 22.7 %collective-permute-start.24 = (f32[75,4,1]{2,1,0:T(4,128)}, f32[75,4,1]{2,1,0:T(4,128)}, u32[]{:S(2)}, u32[]{:S(2)}) collective-permute-start(f32[75,4,1]{2,1,0:T(4,128)} %get-tuple-element.99), channel_id=1, source_target_pairs={{0,1},{1,2},{2,3},{3,4},{4,5},{5,6},{6,7},{7,8},{8,9},{9,10},{10,1... | collective-permute-start | bytes 3608 | tf_op jit(solution)/shard_map/ppermute | solution.py:20
  132.4 14.2 %all-to-all-start.3 = ((f32[16,1,512]{2,1,0:T(1,128)}), f32[16,1,512]{2,1,0:T(1,128)S(1)}, u32[]{:S(2)}, u32[]{:S(2)}) async-start(f32[16,1,512]{2,1,0:T(1,128)} %reshape.284), calls=%async_computation.3 | async-start | bytes 65536 | tf_op jit(solution)/shard_map/all_to_all | solution.py:102
  139.6 12.8 %collective-permute-start.25 = (f32[75,1,128]{2,1,0:T(1,128)}, f32[75,1,128]{2,1,0:T(1,128)S(1)}, u32[]{:S(2)}, u32[]{:S(2)}) collective-permute-start(f32[75,1,128]{2,1,0:T(1,128)} %get-tuple-element.102), channel_id=1, source_target_pairs={{16,0},{32,16},{48,32},{64,48},{80,64},{96,80},{112,96},{17,1},{33... | collective-permute-start | bytes 115208 | tf_op jit(solution)/shard_map/ppermute | solution.py:23
  140.9 11.6 %collective-permute-start.26 = (f32[75,1,128]{2,1,0:T(1,128)}, f32[75,1,128]{2,1,0:T(1,128)S(1)}, u32[]{:S(2)}, u32[]{:S(2)}) collective-permute-start(f32[75,1,128]{2,1,0:T(1,128)} %get-tuple-element.103), channel_id=1, source_target_pairs={{0,16},{16,32},{32,48},{48,64},{64,80},{80,96},{96,112},{1,17},{17... | collective-permute-start | bytes 115208 | tf_op jit(solution)/shard_map/ppermute | solution.py:20
  149.8 7.0 %collective-permute-start.28 = (f32[16,32]{1,0:T(8,128)S(1)}, f32[16,32]{1,0:T(8,128)S(1)}, u32[]{:S(2)}, u32[]{:S(2)}) collective-permute-start(f32[16,32]{1,0:T(8,128)S(1)} %fusion.5), channel_id=1, source_target_pairs={{128,384},{129,385},{130,386},{131,387},{132,388},{133,389},{134,3... | collective-permute-start | bytes 6152 | tf_op jit(solution)/shard_map/ppermute | solution.py:113
  162.4 9.8 %collective-permute-start.30 = (f32[75,4,1]{2,1,0:T(4,128)}, f32[75,4,1]{2,1,0:T(4,128)S(1)}, u32[]{:S(2)}, u32[]{:S(2)}) collective-permute-start(f32[75,4,1]{2,1,0:T(4,128)} %get-tuple-element.90), channel_id=1, source_target_pairs={{1,0},{2,1},{3,2},{4,3},{5,4},{6,5},{7,6},{8,7},{9,8},{10,9},{11,1... | collective-permute-start | bytes 3608 | tf_op jit(solution)/shard_map/ppermute | solution.py:23
  162.5 9.7 %collective-permute-start.31 = (f32[75,4,1]{2,1,0:T(4,128)}, f32[75,4,1]{2,1,0:T(4,128)}, u32[]{:S(2)}, u32[]{:S(2)}) collective-permute-start(f32[75,4,1]{2,1,0:T(4,128)} %get-tuple-element.91), channel_id=1, source_target_pairs={{0,1},{1,2},{2,3},{3,4},{4,5},{5,6},{6,7},{7,8},{8,9},{9,10},{10,1... | collective-permute-start | bytes 3608 | tf_op jit(solution)/shard_map/ppermute | solution.py:20
  163.6 8.6 %collective-permute-start.32 = (f32[75,1,128]{2,1,0:T(1,128)}, f32[75,1,128]{2,1,0:T(1,128)S(1)}, u32[]{:S(2)}, u32[]{:S(2)}) collective-permute-start(f32[75,1,128]{2,1,0:T(1,128)} %get-tuple-element.94), channel_id=1, source_target_pairs={{16,0},{32,16},{48,32},{64,48},{80,64},{96,80},{112,96},{17,1},{33... | collective-permute-start | bytes 115208 | tf_op jit(solution)/shard_map/ppermute | solution.py:23
  164.9 7.3 %collective-permute-start.33 = (f32[75,1,128]{2,1,0:T(1,128)}, f32[75,1,128]{2,1,0:T(1,128)S(1)}, u32[]{:S(2)}, u32[]{:S(2)}) collective-permute-start(f32[75,1,128]{2,1,0:T(1,128)} %get-tuple-element.95), channel_id=1, source_target_pairs={{0,16},{16,32},{32,48},{48,64},{64,80},{80,96},{96,112},{1,17},{17... | collective-permute-start | bytes 115208 | tf_op jit(solution)/shard_map/ppermute | solution.py:20
  174.1 14.1 %all-to-all-start.4 = ((f32[8,1,1024]{2,1,0:T(1,128)}), f32[8,1,1024]{2,1,0:T(1,128)S(1)}, u32[]{:S(2)}, u32[]{:S(2)}) async-start(f32[8,1,1024]{2,1,0:T(1,128)} %reshape.286), calls=%async_computation.4 | async-start | bytes 65536 | tf_op jit(solution)/shard_map/all_to_all | solution.py:101
  184.3 23.0 %collective-permute-start.34 = (f32[75,4,1]{2,1,0:T(4,128)}, f32[75,4,1]{2,1,0:T(4,128)S(1)}, u32[]{:S(2)}, u32[]{:S(2)}) collective-permute-start(f32[75,4,1]{2,1,0:T(4,128)} %get-tuple-element.84), channel_id=1, source_target_pairs={{1,0},{2,1},{3,2},{4,3},{5,4},{6,5},{7,6},{8,7},{9,8},{10,9},{11,1... | collective-permute-start | bytes 3608 | tf_op jit(solution)/shard_map/ppermute | solution.py:23
  185.9 22.7 %collective-permute-start.35 = (f32[75,4,1]{2,1,0:T(4,128)}, f32[75,4,1]{2,1,0:T(4,128)}, u32[]{:S(2)}, u32[]{:S(2)}) collective-permute-start(f32[75,4,1]{2,1,0:T(4,128)} %get-tuple-element.85), channel_id=1, source_target_pairs={{0,1},{1,2},{2,3},{3,4},{4,5},{5,6},{6,7},{7,8},{8,9},{9,10},{10,1... | collective-permute-start | bytes 3608 | tf_op jit(solution)/shard_map/ppermute | solution.py:20
  189.9 14.2 %all-to-all-start.5 = ((f32[16,1,512]{2,1,0:T(1,128)}), f32[16,1,512]{2,1,0:T(1,128)S(1)}, u32[]{:S(2)}, u32[]{:S(2)}) async-start(f32[16,1,512]{2,1,0:T(1,128)} %reshape.288), calls=%async_computation.5 | async-start | bytes 65536 | tf_op jit(solution)/shard_map/all_to_all | solution.py:102
  197.1 13.1 %collective-permute-start.36 = (f32[75,1,128]{2,1,0:T(1,128)}, f32[75,1,128]{2,1,0:T(1,128)S(1)}, u32[]{:S(2)}, u32[]{:S(2)}) collective-permute-start(f32[75,1,128]{2,1,0:T(1,128)} %get-tuple-element.88), channel_id=1, source_target_pairs={{16,0},{32,16},{48,32},{64,48},{80,64},{96,80},{112,96},{17,1},{33... | collective-permute-start | bytes 115208 | tf_op jit(solution)/shard_map/ppermute | solution.py:23
  198.4 11.8 %collective-permute-start.37 = (f32[75,1,128]{2,1,0:T(1,128)}, f32[75,1,128]{2,1,0:T(1,128)S(1)}, u32[]{:S(2)}, u32[]{:S(2)}) collective-permute-start(f32[75,1,128]{2,1,0:T(1,128)} %get-tuple-element.89), channel_id=1, source_target_pairs={{0,16},{16,32},{32,48},{48,64},{64,80},{80,96},{96,112},{1,17},{17... | collective-permute-start | bytes 115208 | tf_op jit(solution)/shard_map/ppermute | solution.py:20
  207.3 7.0 %collective-permute-start.39 = (f32[16,32]{1,0:T(8,128)S(1)}, f32[16,32]{1,0:T(8,128)S(1)}, u32[]{:S(2)}, u32[]{:S(2)}) collective-permute-start(f32[16,32]{1,0:T(8,128)S(1)} %fusion.3), channel_id=1, source_target_pairs={{128,384},{129,385},{130,386},{131,387},{132,388},{133,389},{134,3... | collective-permute-start | bytes 6152 | tf_op jit(solution)/shard_map/ppermute | solution.py:113
  219.9 9.8 %collective-permute-start.41 = (f32[75,4,1]{2,1,0:T(4,128)}, f32[75,4,1]{2,1,0:T(4,128)}, u32[]{:S(2)}, u32[]{:S(2)}) collective-permute-start(f32[75,4,1]{2,1,0:T(4,128)} %get-tuple-element.76), channel_id=1, source_target_pairs={{1,0},{2,1},{3,2},{4,3},{5,4},{6,5},{7,6},{8,7},{9,8},{10,9},{11,1... | collective-permute-start | bytes 3608 | tf_op jit(solution)/shard_map/ppermute | solution.py:23
  220.0 9.7 %collective-permute-start.42 = (f32[75,4,1]{2,1,0:T(4,128)}, f32[75,4,1]{2,1,0:T(4,128)}, u32[]{:S(2)}, u32[]{:S(2)}) collective-permute-start(f32[75,4,1]{2,1,0:T(4,128)} %get-tuple-element.77), channel_id=1, source_target_pairs={{0,1},{1,2},{2,3},{3,4},{4,5},{5,6},{6,7},{7,8},{8,9},{9,10},{10,1... | collective-permute-start | bytes 3608 | tf_op jit(solution)/shard_map/ppermute | solution.py:20
  221.1 8.6 %collective-permute-start.43 = (f32[75,1,128]{2,1,0:T(1,128)}, f32[75,1,128]{2,1,0:T(1,128)S(1)}, u32[]{:S(2)}, u32[]{:S(2)}) collective-permute-start(f32[75,1,128]{2,1,0:T(1,128)} %get-tuple-element.80), channel_id=1, source_target_pairs={{16,0},{32,16},{48,32},{64,48},{80,64},{96,80},{112,96},{17,1},{33... | collective-permute-start | bytes 115208 | tf_op jit(solution)/shard_map/ppermute | solution.py:23
  222.4 7.3 %collective-permute-start.44 = (f32[75,1,128]{2,1,0:T(1,128)}, f32[75,1,128]{2,1,0:T(1,128)S(1)}, u32[]{:S(2)}, u32[]{:S(2)}) collective-permute-start(f32[75,1,128]{2,1,0:T(1,128)} %get-tuple-element.81), channel_id=1, source_target_pairs={{0,16},{16,32},{32,48},{48,64},{64,80},{80,96},{96,112},{1,17},{17... | collective-permute-start | bytes 115208 | tf_op jit(solution)/shard_map/ppermute | solution.py:20
  231.6 14.1 %all-to-all-start.6 = ((f32[8,1,1024]{2,1,0:T(1,128)}), f32[8,1,1024]{2,1,0:T(1,128)S(1)}, u32[]{:S(2)}, u32[]{:S(2)}) async-start(f32[8,1,1024]{2,1,0:T(1,128)} %reshape.290), calls=%async_computation.6 | async-start | bytes 65536 | tf_op jit(solution)/shard_map/all_to_all | solution.py:101
  241.1 23.8 %collective-permute-start.45 = (f32[75,4,1]{2,1,0:T(4,128)S(1)}, f32[75,4,1]{2,1,0:T(4,128)S(1)}, u32[]{:S(2)}, u32[]{:S(2)}) collective-permute-start(f32[75,4,1]{2,1,0:T(4,128)S(1)} %get-tuple-element.70), channel_id=1, source_target_pairs={{1,0},{2,1},{3,2},{4,3},{5,4},{6,5},{7,6},{8,7},{9,8},{10,9},{11,1... | collective-permute-start | bytes 3608 | tf_op jit(solution)/shard_map/ppermute | solution.py:23
  242.8 23.4 %collective-permute-start.46 = (f32[75,4,1]{2,1,0:T(4,128)S(1)}, f32[75,4,1]{2,1,0:T(4,128)S(1)}, u32[]{:S(2)}, u32[]{:S(2)}) collective-permute-start(f32[75,4,1]{2,1,0:T(4,128)S(1)} %get-tuple-element.71), channel_id=1, source_target_pairs={{0,1},{1,2},{2,3},{3,4},{4,5},{5,6},{6,7},{7,8},{8,9},{9,10},{10,1... | collective-permute-start | bytes 3608 | tf_op jit(solution)/shard_map/ppermute | solution.py:20
  247.5 14.2 %all-to-all-start.7 = ((f32[16,1,512]{2,1,0:T(1,128)}), f32[16,1,512]{2,1,0:T(1,128)S(1)}, u32[]{:S(2)}, u32[]{:S(2)}) async-start(f32[16,1,512]{2,1,0:T(1,128)} %reshape.292), calls=%async_computation.7 | async-start | bytes 65536 | tf_op jit(solution)/shard_map/all_to_all | solution.py:102
  254.0 13.5 %collective-permute-start.47 = (f32[75,1,128]{2,1,0:T(1,128)S(1)}, f32[75,1,128]{2,1,0:T(1,128)S(1)}, u32[]{:S(2)}, u32[]{:S(2)}) collective-permute-start(f32[75,1,128]{2,1,0:T(1,128)S(1)} %get-tuple-element.74), channel_id=1, source_target_pairs={{16,0},{32,16},{48,32},{64,48},{80,64},{96,80},{112,96},{17,1},{33... | collective-permute-start | bytes 115208 | tf_op jit(solution)/shard_map/ppermute | solution.py:23
  255.3 12.2 %collective-permute-start.48 = (f32[75,1,128]{2,1,0:T(1,128)S(1)}, f32[75,1,128]{2,1,0:T(1,128)S(1)}, u32[]{:S(2)}, u32[]{:S(2)}) collective-permute-start(f32[75,1,128]{2,1,0:T(1,128)S(1)} %get-tuple-element.75), channel_id=1, source_target_pairs={{0,16},{16,32},{32,48},{48,64},{64,80},{80,96},{96,112},{1,17},{17... | collective-permute-start | bytes 115208 | tf_op jit(solution)/shard_map/ppermute | solution.py:20
  (35 other events, 399.7 us)

commit v8 on v3

--- a/solution.py
+++ b/solution.py
@@ -27,11 +27,11 @@
 
 def _factor_kernel(a_ref, inv_ref, b_ref, c_ref):
     lev = a_ref.shape[0]
-    prior_c = jnp.zeros(a_ref.shape[1:], jnp.float32)
     zero = jnp.zeros(a_ref.shape[1:], jnp.float32)
-    for k in range(lev):
-        lower = a_ref[k] if k >= 1 else zero
-        upper = a_ref[k + 1] if k + 1 < lev else zero
+
+    def level(k, prior_c):
+        lower = jnp.where(k >= 1, a_ref[k], zero)
+        upper = jnp.where(k + 1 < lev, a_ref[jnp.minimum(k + 1, lev - 1)], zero)
         centre = 1.0 + lower + upper
         pivot = centre + lower * prior_c
         inv = 1.0 / pivot
@@ -39,7 +39,9 @@
         inv_ref[k] = inv
         b_ref[k] = lower * inv
         c_ref[k] = factor
-        prior_c = factor
+        return factor
+
+    lax.fori_loop(0, lev, level, zero, unroll=5)
 
 
 def _solve_kernel(x_ref, inv_ref, b_ref, c_ref, o_ref):
@@ -57,8 +59,8 @@
         return x
 
     zero = jnp.zeros(x_ref.shape[1:], jnp.float32)
-    lax.fori_loop(0, lev, down, zero, unroll=5)
-    lax.fori_loop(0, lev, up, zero, unroll=5)
+    lax.fori_loop(0, lev, down, zero, unroll=15)
+    lax.fori_loop(0, lev, up, zero, unroll=15)
 
 
 def factorise(coeff):

time: 270 us -> 270 us (level)
  no operation moved by 1% of the time
where the time goes in v8:
time: 270 us; the launch traced here: 268 us
  starting transfers between devices  145 us (54%)
  other arithmetic  33.4 us (12%)
  local copies, waits for them, and re-layouts  27.5 us (10%)
  waiting for transfers between devices  26.8 us (10%)
  Pallas kernels  24.3 us (9%)
  matrix products  9.64 us (4%)
    ppermute x20, starting transfers between devices, extended(): lax.ppermute(lax.slice_in_dim(block, block.shape[dim] - width, None, axis...  48.5 us
    ppermute x20, starting transfers between devices, extended(): lax.ppermute(lax.slice_in_dim(block, 0, width, axis=dim), axis, backward)  32 us
    all_to_all x4, starting transfers between devices, couple(): lax.all_to_all(staged, 'lat', split_axis=1, concat_axis=1, tiled=True)  31.4 us
    pallas_call x10, Pallas kernels, column_solve(): pl.pallas_call(_solve_kernel, out_shape=jax.ShapeDtypeStruct(right.shape,...  21.9 us
    all_to_all x4, starting transfers between devices, couple(): lax.all_to_all(staged, 'lon', split_axis=2, concat_axis=2, tiled=True)  17.4 us
    ppermute x12, starting transfers between devices, reduce_forcing(): lax.ppermute(accumulated, 'sec', [(s, section_count - 1)])  15.6 us
    ppermute x12, waiting for transfers between devices, reduce_forcing(): lax.ppermute(accumulated, 'sec', [(s, section_count - 1)])  13.4 us
    mul x8, other arithmetic, substep(): return advect(mixed_adj, east_part, north_part) * keep_factor  10.9 us
  transfers between devices with their start and end apart: 60, of which 17 were waited for; matrix products, arithmetic and copies ran while one was open for 16% of the time, Pallas kernels for 3%

profile of v8, /device:TPU:6, one launch (start us, length us, event | category | flops | bytes accessed | tf_op | source)
XLA Modules:
  0.0 268.0 jit_solution(2538211676390857434)
XLA Ops:
  1.6 2.4 shard_map.91
  4.0 2.2 shard_map.92
  7.5 2.9 %collective-permute-start = (f32[75,4,1]{2,1,0:T(4,128)S(1)}, f32[75,4,1]{2,1,0:T(4,128)S(1)}, u32[]{:S(2)}, u32[]{:S(2)}) collective-permute-start(f32[75,4,1]{2,1,0:T(4,128)S(1)} %get-tuple-element.128), channel_id=1, source_target_pairs={{1,0},{2,1},{3,2},{4,3},{5,4},{6,5},{7,6},{8,7},{9,8},{10,9},{11,1... | collective-permute-start | bytes 3608 | tf_op jit(solution)/shard_map/ppermute | solution.py:23
  11.8 4.9 %collective-permute-start.3 = (f32[75,1,128]{2,1,0:T(1,128)S(1)}, f32[75,1,128]{2,1,0:T(1,128)S(1)}, u32[]{:S(2)}, u32[]{:S(2)}) collective-permute-start(f32[75,1,128]{2,1,0:T(1,128)S(1)} %get-tuple-element.133), channel_id=1, source_target_pairs={{0,16},{16,32},{32,48},{48,64},{64,80},{80,96},{96,112},{1,17},{17... | collective-permute-start | bytes 115208 | tf_op jit(solution)/shard_map/ppermute | solution.py:20
  18.3 1.9 fusion.69.x_ref
  20.3 2.2 shard_map.93
  24.3 2.1 collective-permute-start.4
  27.8 4.9 %collective-permute-start.7 = (f32[75,1,128]{2,1,0:T(1,128)S(1)}, f32[75,1,128]{2,1,0:T(1,128)S(1)}, u32[]{:S(2)}, u32[]{:S(2)}) collective-permute-start(f32[75,1,128]{2,1,0:T(1,128)S(1)} %get-tuple-element.127), channel_id=1, source_target_pairs={{0,16},{16,32},{32,48},{48,64},{64,80},{80,96},{96,112},{1,17},{17... | collective-permute-start | bytes 115208 | tf_op jit(solution)/shard_map/ppermute | solution.py:20
  32.7 2.1 copy.67
  37.2 2.2 shard_map.94
  41.2 2.7 collective-permute-start.8
  45.3 4.9 %collective-permute-start.11 = (f32[75,1,128]{2,1,0:T(1,128)S(1)}, f32[75,1,128]{2,1,0:T(1,128)S(1)}, u32[]{:S(2)}, u32[]{:S(2)}) collective-permute-start(f32[75,1,128]{2,1,0:T(1,128)S(1)} %get-tuple-element.121), channel_id=1, source_target_pairs={{0,16},{16,32},{32,48},{48,64},{64,80},{80,96},{96,112},{1,17},{17... | collective-permute-start | bytes 115208 | tf_op jit(solution)/shard_map/ppermute | solution.py:20
  55.2 4.3 %all-to-all-start = ((f32[16,1,512]{2,1,0:T(1,128)}), f32[16,1,512]{2,1,0:T(1,128)S(1)}, u32[]{:S(2)}, u32[]{:S(2)}) async-start(f32[16,1,512]{2,1,0:T(1,128)} %reshape.278), calls=%async_computation | async-start | bytes 65536 | tf_op jit(solution)/shard_map/all_to_all | solution.py:103
  59.5 2.2 shard_map.95
  63.6 2.9 %collective-permute-start.12 = (f32[75,4,1]{2,1,0:T(4,128)}, f32[75,4,1]{2,1,0:T(4,128)S(1)}, u32[]{:S(2)}, u32[]{:S(2)}) collective-permute-start(f32[75,4,1]{2,1,0:T(4,128)} %get-tuple-element.110), channel_id=1, source_target_pairs={{1,0},{2,1},{3,2},{4,3},{5,4},{6,5},{7,6},{8,7},{9,8},{10,9},{11,1... | collective-permute-start | bytes 3608 | tf_op jit(solution)/shard_map/ppermute | solution.py:23
  69.7 10.8 %all-to-all-start.1 = ((f32[8,1,1024]{2,1,0:T(1,128)}), f32[8,1,1024]{2,1,0:T(1,128)S(1)}, u32[]{:S(2)}, u32[]{:S(2)}) async-start(f32[8,1,1024]{2,1,0:T(1,128)} %reshape.280), calls=%async_computation.1 | async-start | bytes 65536 | tf_op jit(solution)/shard_map/all_to_all | solution.py:104
  81.8 4.6 %collective-permute-start.15 = (f32[75,1,128]{2,1,0:T(1,128)S(1)}, f32[75,1,128]{2,1,0:T(1,128)S(1)}, u32[]{:S(2)}, u32[]{:S(2)}) collective-permute-start(f32[75,1,128]{2,1,0:T(1,128)S(1)} %get-tuple-element.115), channel_id=1, source_target_pairs={{0,16},{16,32},{32,48},{48,64},{64,80},{80,96},{96,112},{1,17},{17... | collective-permute-start | bytes 115208 | tf_op jit(solution)/shard_map/ppermute | solution.py:20
  86.4 2.1 all-to-all-done.1
  100.1 2.2 shard_map.96
  106.5 4.7 %collective-permute-start.22 = (f32[75,1,128]{2,1,0:T(1,128)S(1)}, f32[75,1,128]{2,1,0:T(1,128)S(1)}, u32[]{:S(2)}, u32[]{:S(2)}) collective-permute-start(f32[75,1,128]{2,1,0:T(1,128)S(1)} %get-tuple-element.109), channel_id=1, source_target_pairs={{0,16},{16,32},{32,48},{48,64},{64,80},{80,96},{96,112},{1,17},{17... | collective-permute-start | bytes 115208 | tf_op jit(solution)/shard_map/ppermute | solution.py:20
  111.3 1.9 fusion.107
  114.1 1.9 fusion.43.x_ref
  116.0 4.4 %all-to-all-start.2 = ((f32[16,1,512]{2,1,0:T(1,128)}), f32[16,1,512]{2,1,0:T(1,128)S(1)}, u32[]{:S(2)}, u32[]{:S(2)}) async-start(f32[16,1,512]{2,1,0:T(1,128)} %reshape.282), calls=%async_computation.2 | async-start | bytes 65536 | tf_op jit(solution)/shard_map/all_to_all | solution.py:103
  120.4 2.2 shard_map.97
  124.5 2.9 %collective-permute-start.23 = (f32[75,4,1]{2,1,0:T(4,128)}, f32[75,4,1]{2,1,0:T(4,128)S(1)}, u32[]{:S(2)}, u32[]{:S(2)}) collective-permute-start(f32[75,4,1]{2,1,0:T(4,128)} %get-tuple-element.98), channel_id=1, source_target_pairs={{1,0},{2,1},{3,2},{4,3},{5,4},{6,5},{7,6},{8,7},{9,8},{10,9},{11,1... | collective-permute-start | bytes 3608 | tf_op jit(solution)/shard_map/ppermute | solution.py:23
  129.9 6.8 %all-to-all-start.3 = ((f32[8,1,1024]{2,1,0:T(1,128)}), f32[8,1,1024]{2,1,0:T(1,128)S(1)}, u32[]{:S(2)}, u32[]{:S(2)}) async-start(f32[8,1,1024]{2,1,0:T(1,128)} %reshape.284), calls=%async_computation.3 | async-start | bytes 65536 | tf_op jit(solution)/shard_map/all_to_all | solution.py:104
  138.1 4.6 %collective-permute-start.26 = (f32[75,1,128]{2,1,0:T(1,128)S(1)}, f32[75,1,128]{2,1,0:T(1,128)S(1)}, u32[]{:S(2)}, u32[]{:S(2)}) collective-permute-start(f32[75,1,128]{2,1,0:T(1,128)S(1)} %get-tuple-element.103), channel_id=1, source_target_pairs={{0,16},{16,32},{32,48},{48,64},{64,80},{80,96},{96,112},{1,17},{17... | collective-permute-start | bytes 115208 | tf_op jit(solution)/shard_map/ppermute | solution.py:20
  142.6 2.1 all-to-all-done.3
  156.3 2.2 shard_map.98
  162.8 4.5 %collective-permute-start.33 = (f32[75,1,128]{2,1,0:T(1,128)S(1)}, f32[75,1,128]{2,1,0:T(1,128)S(1)}, u32[]{:S(2)}, u32[]{:S(2)}) collective-permute-start(f32[75,1,128]{2,1,0:T(1,128)S(1)} %get-tuple-element.95), channel_id=1, source_target_pairs={{0,16},{16,32},{32,48},{48,64},{64,80},{80,96},{96,112},{1,17},{17... | collective-permute-start | bytes 115208 | tf_op jit(solution)/shard_map/ppermute | solution.py:20
  167.4 1.9 fusion.108
  170.2 1.9 fusion.31.x_ref
  172.1 4.4 %all-to-all-start.4 = ((f32[16,1,512]{2,1,0:T(1,128)}), f32[16,1,512]{2,1,0:T(1,128)S(1)}, u32[]{:S(2)}, u32[]{:S(2)}) async-start(f32[16,1,512]{2,1,0:T(1,128)} %reshape.286), calls=%async_computation.4 | async-start | bytes 65536 | tf_op jit(solution)/shard_map/all_to_all | solution.py:103
  176.5 2.2 shard_map.99
  180.6 2.9 %collective-permute-start.34 = (f32[75,4,1]{2,1,0:T(4,128)}, f32[75,4,1]{2,1,0:T(4,128)S(1)}, u32[]{:S(2)}, u32[]{:S(2)}) collective-permute-start(f32[75,4,1]{2,1,0:T(4,128)} %get-tuple-element.84), channel_id=1, source_target_pairs={{1,0},{2,1},{3,2},{4,3},{5,4},{6,5},{7,6},{8,7},{9,8},{10,9},{11,1... | collective-permute-start | bytes 3608 | tf_op jit(solution)/shard_map/ppermute | solution.py:23
  186.0 6.9 %all-to-all-start.5 = ((f32[8,1,1024]{2,1,0:T(1,128)}), f32[8,1,1024]{2,1,0:T(1,128)S(1)}, u32[]{:S(2)}, u32[]{:S(2)}) async-start(f32[8,1,1024]{2,1,0:T(1,128)} %reshape.288), calls=%async_computation.5 | async-start | bytes 65536 | tf_op jit(solution)/shard_map/all_to_all | solution.py:104
  194.3 4.6 %collective-permute-start.37 = (f32[75,1,128]{2,1,0:T(1,128)S(1)}, f32[75,1,128]{2,1,0:T(1,128)S(1)}, u32[]{:S(2)}, u32[]{:S(2)}) collective-permute-start(f32[75,1,128]{2,1,0:T(1,128)S(1)} %get-tuple-element.89), channel_id=1, source_target_pairs={{0,16},{16,32},{32,48},{48,64},{64,80},{80,96},{96,112},{1,17},{17... | collective-permute-start | bytes 115208 | tf_op jit(solution)/shard_map/ppermute | solution.py:20
  198.9 2.1 all-to-all-done.5
  212.6 2.2 shard_map.100
  218.5 4.8 %collective-permute-start.44 = (f32[75,1,128]{2,1,0:T(1,128)S(1)}, f32[75,1,128]{2,1,0:T(1,128)S(1)}, u32[]{:S(2)}, u32[]{:S(2)}) collective-permute-start(f32[75,1,128]{2,1,0:T(1,128)S(1)} %get-tuple-element.81), channel_id=1, source_target_pairs={{0,16},{16,32},{32,48},{48,64},{64,80},{80,96},{96,112},{1,17},{17... | collective-permute-start | bytes 115208 | tf_op jit(solution)/shard_map/ppermute | solution.py:20
  226.1 1.9 fusion.19.x_ref
  228.0 4.4 %all-to-all-start.6 = ((f32[16,1,512]{2,1,0:T(1,128)}), f32[16,1,512]{2,1,0:T(1,128)S(1)}, u32[]{:S(2)}, u32[]{:S(2)}) async-start(f32[16,1,512]{2,1,0:T(1,128)} %reshape.290), calls=%async_computation.6 | async-start | bytes 65536 | tf_op jit(solution)/shard_map/all_to_all | solution.py:103
  232.4 2.2 shard_map.101
  235.8 2.9 %collective-permute-start.45 = (f32[75,4,1]{2,1,0:T(4,128)S(1)}, f32[75,4,1]{2,1,0:T(4,128)S(1)}, u32[]{:S(2)}, u32[]{:S(2)}) collective-permute-start(f32[75,4,1]{2,1,0:T(4,128)S(1)} %get-tuple-element.70), channel_id=1, source_target_pairs={{1,0},{2,1},{3,2},{4,3},{5,4},{6,5},{7,6},{8,7},{9,8},{10,9},{11,1... | collective-permute-start | bytes 3608 | tf_op jit(solution)/shard_map/ppermute | solution.py:23
  242.0 7.0 %all-to-all-start.7 = ((f32[8,1,1024]{2,1,0:T(1,128)}), f32[8,1,1024]{2,1,0:T(1,128)S(1)}, u32[]{:S(2)}, u32[]{:S(2)}) async-start(f32[8,1,1024]{2,1,0:T(1,128)} %reshape.292), calls=%async_computation.7 | async-start | bytes 65536 | tf_op jit(solution)/shard_map/all_to_all | solution.py:104
  250.3 4.6 %collective-permute-start.48 = (f32[75,1,128]{2,1,0:T(1,128)S(1)}, f32[75,1,128]{2,1,0:T(1,128)S(1)}, u32[]{:S(2)}, u32[]{:S(2)}) collective-permute-start(f32[75,1,128]{2,1,0:T(1,128)S(1)} %get-tuple-element.75), channel_id=1, source_target_pairs={{0,16},{16,32},{32,48},{48,64},{64,80},{80,96},{96,112},{1,17},{17... | collective-permute-start | bytes 115208 | tf_op jit(solution)/shard_map/ppermute | solution.py:20
  254.8 2.1 all-to-all-done.7
  263.1 2.4 collective-permute-done.49
  (261 shorter events, 103.1 us)
Async XLA Ops:
  7.5 9.6 %collective-permute-start = (f32[75,4,1]{2,1,0:T(4,128)S(1)}, f32[75,4,1]{2,1,0:T(4,128)S(1)}, u32[]{:S(2)}, u32[]{:S(2)}) collective-permute-start(f32[75,4,1]{2,1,0:T(4,128)S(1)} %get-tuple-element.128), channel_id=1, source_target_pairs={{1,0},{2,1},{3,2},{4,3},{5,4},{6,5},{7,6},{8,7},{9,8},{10,9},{11,1... | collective-permute-start | bytes 3608 | tf_op jit(solution)/shard_map/ppermute | solution.py:23
  24.3 10.8 %collective-permute-start.4 = (f32[75,4,1]{2,1,0:T(4,128)}, f32[75,4,1]{2,1,0:T(4,128)S(1)}, u32[]{:S(2)}, u32[]{:S(2)}) collective-permute-start(f32[75,4,1]{2,1,0:T(4,128)} %get-tuple-element.122), channel_id=1, source_target_pairs={{1,0},{2,1},{3,2},{4,3},{5,4},{6,5},{7,6},{8,7},{9,8},{10,9},{11,1... | collective-permute-start | bytes 3608 | tf_op jit(solution)/shard_map/ppermute | solution.py:23
  26.4 8.7 %collective-permute-start.5 = (f32[75,4,1]{2,1,0:T(4,128)}, f32[75,4,1]{2,1,0:T(4,128)}, u32[]{:S(2)}, u32[]{:S(2)}) collective-permute-start(f32[75,4,1]{2,1,0:T(4,128)} %get-tuple-element.123), channel_id=1, source_target_pairs={{0,1},{1,2},{2,3},{3,4},{4,5},{5,6},{6,7},{7,8},{8,9},{9,10},{10,1... | collective-permute-start | bytes 3608 | tf_op jit(solution)/shard_map/ppermute | solution.py:20
  26.5 8.7 %collective-permute-start.6 = (f32[75,1,128]{2,1,0:T(1,128)S(1)}, f32[75,1,128]{2,1,0:T(1,128)S(1)}, u32[]{:S(2)}, u32[]{:S(2)}) collective-permute-start(f32[75,1,128]{2,1,0:T(1,128)S(1)} %get-tuple-element.126), channel_id=1, source_target_pairs={{16,0},{32,16},{48,32},{64,48},{80,64},{96,80},{112,96},{17,1},{33... | collective-permute-start | bytes 115208 | tf_op jit(solution)/shard_map/ppermute | solution.py:23
  27.8 7.4 %collective-permute-start.7 = (f32[75,1,128]{2,1,0:T(1,128)S(1)}, f32[75,1,128]{2,1,0:T(1,128)S(1)}, u32[]{:S(2)}, u32[]{:S(2)}) collective-permute-start(f32[75,1,128]{2,1,0:T(1,128)S(1)} %get-tuple-element.127), channel_id=1, source_target_pairs={{0,16},{16,32},{32,48},{48,64},{64,80},{80,96},{96,112},{1,17},{17... | collective-permute-start | bytes 115208 | tf_op jit(solution)/shard_map/ppermute | solution.py:20
  41.2 12.9 %collective-permute-start.8 = (f32[75,4,1]{2,1,0:T(4,128)}, f32[75,4,1]{2,1,0:T(4,128)S(1)}, u32[]{:S(2)}, u32[]{:S(2)}) collective-permute-start(f32[75,4,1]{2,1,0:T(4,128)} %get-tuple-element.116), channel_id=1, source_target_pairs={{1,0},{2,1},{3,2},{4,3},{5,4},{6,5},{7,6},{8,7},{9,8},{10,9},{11,1... | collective-permute-start | bytes 3608 | tf_op jit(solution)/shard_map/ppermute | solution.py:23
  43.9 10.3 %collective-permute-start.9 = (f32[75,4,1]{2,1,0:T(4,128)}, f32[75,4,1]{2,1,0:T(4,128)S(1)}, u32[]{:S(2)}, u32[]{:S(2)}) collective-permute-start(f32[75,4,1]{2,1,0:T(4,128)} %get-tuple-element.117), channel_id=1, source_target_pairs={{0,1},{1,2},{2,3},{3,4},{4,5},{5,6},{6,7},{7,8},{8,9},{9,10},{10,1... | collective-permute-start | bytes 3608 | tf_op jit(solution)/shard_map/ppermute | solution.py:20
  44.0 10.2 %collective-permute-start.10 = (f32[75,1,128]{2,1,0:T(1,128)S(1)}, f32[75,1,128]{2,1,0:T(1,128)S(1)}, u32[]{:S(2)}, u32[]{:S(2)}) collective-permute-start(f32[75,1,128]{2,1,0:T(1,128)S(1)} %get-tuple-element.120), channel_id=1, source_target_pairs={{16,0},{32,16},{48,32},{64,48},{80,64},{96,80},{112,96},{17,1},{33... | collective-permute-start | bytes 115208 | tf_op jit(solution)/shard_map/ppermute | solution.py:23
  45.3 8.9 %collective-permute-start.11 = (f32[75,1,128]{2,1,0:T(1,128)S(1)}, f32[75,1,128]{2,1,0:T(1,128)S(1)}, u32[]{:S(2)}, u32[]{:S(2)}) collective-permute-start(f32[75,1,128]{2,1,0:T(1,128)S(1)} %get-tuple-element.121), channel_id=1, source_target_pairs={{0,16},{16,32},{32,48},{48,64},{64,80},{80,96},{96,112},{1,17},{17... | collective-permute-start | bytes 115208 | tf_op jit(solution)/shard_map/ppermute | solution.py:20
  55.2 12.0 %all-to-all-start = ((f32[16,1,512]{2,1,0:T(1,128)}), f32[16,1,512]{2,1,0:T(1,128)S(1)}, u32[]{:S(2)}, u32[]{:S(2)}) async-start(f32[16,1,512]{2,1,0:T(1,128)} %reshape.278), calls=%async_computation | async-start | bytes 65536 | tf_op jit(solution)/shard_map/all_to_all | solution.py:103
  63.6 28.0 %collective-permute-start.12 = (f32[75,4,1]{2,1,0:T(4,128)}, f32[75,4,1]{2,1,0:T(4,128)S(1)}, u32[]{:S(2)}, u32[]{:S(2)}) collective-permute-start(f32[75,4,1]{2,1,0:T(4,128)} %get-tuple-element.110), channel_id=1, source_target_pairs={{1,0},{2,1},{3,2},{4,3},{5,4},{6,5},{7,6},{8,7},{9,8},{10,9},{11,1... | collective-permute-start | bytes 3608 | tf_op jit(solution)/shard_map/ppermute | solution.py:23
  66.4 26.4 %collective-permute-start.13 = (f32[75,4,1]{2,1,0:T(4,128)}, f32[75,4,1]{2,1,0:T(4,128)}, u32[]{:S(2)}, u32[]{:S(2)}) collective-permute-start(f32[75,4,1]{2,1,0:T(4,128)} %get-tuple-element.111), channel_id=1, source_target_pairs={{0,1},{1,2},{2,3},{3,4},{4,5},{5,6},{6,7},{7,8},{8,9},{9,10},{10,1... | collective-permute-start | bytes 3608 | tf_op jit(solution)/shard_map/ppermute | solution.py:20
  69.7 18.8 %all-to-all-start.1 = ((f32[8,1,1024]{2,1,0:T(1,128)}), f32[8,1,1024]{2,1,0:T(1,128)S(1)}, u32[]{:S(2)}, u32[]{:S(2)}) async-start(f32[8,1,1024]{2,1,0:T(1,128)} %reshape.280), calls=%async_computation.1 | async-start | bytes 65536 | tf_op jit(solution)/shard_map/all_to_all | solution.py:104
  80.5 13.7 %collective-permute-start.14 = (f32[75,1,128]{2,1,0:T(1,128)S(1)}, f32[75,1,128]{2,1,0:T(1,128)S(1)}, u32[]{:S(2)}, u32[]{:S(2)}) collective-permute-start(f32[75,1,128]{2,1,0:T(1,128)S(1)} %get-tuple-element.114), channel_id=1, source_target_pairs={{16,0},{32,16},{48,32},{64,48},{80,64},{96,80},{112,96},{17,1},{33... | collective-permute-start | bytes 115208 | tf_op jit(solution)/shard_map/ppermute | solution.py:23
  81.8 12.4 %collective-permute-start.15 = (f32[75,1,128]{2,1,0:T(1,128)S(1)}, f32[75,1,128]{2,1,0:T(1,128)S(1)}, u32[]{:S(2)}, u32[]{:S(2)}) collective-permute-start(f32[75,1,128]{2,1,0:T(1,128)S(1)} %get-tuple-element.115), channel_id=1, source_target_pairs={{0,16},{16,32},{32,48},{48,64},{64,80},{80,96},{96,112},{1,17},{17... | collective-permute-start | bytes 115208 | tf_op jit(solution)/shard_map/ppermute | solution.py:20
  91.6 7.0 %collective-permute-start.17 = (f32[16,32]{1,0:T(8,128)S(1)}, f32[16,32]{1,0:T(8,128)S(1)}, u32[]{:S(2)}, u32[]{:S(2)}) collective-permute-start(f32[16,32]{1,0:T(8,128)S(1)} %fusion.7), channel_id=1, source_target_pairs={{128,384},{129,385},{130,386},{131,387},{132,388},{133,389},{134,3... | collective-permute-start | bytes 6152 | tf_op jit(solution)/shard_map/ppermute | solution.py:115
  104.1 10.0 %collective-permute-start.19 = (f32[75,4,1]{2,1,0:T(4,128)}, f32[75,4,1]{2,1,0:T(4,128)S(1)}, u32[]{:S(2)}, u32[]{:S(2)}) collective-permute-start(f32[75,4,1]{2,1,0:T(4,128)} %get-tuple-element.104), channel_id=1, source_target_pairs={{1,0},{2,1},{3,2},{4,3},{5,4},{6,5},{7,6},{8,7},{9,8},{10,9},{11,1... | collective-permute-start | bytes 3608 | tf_op jit(solution)/shard_map/ppermute | solution.py:23
  104.1 10.0 %collective-permute-start.20 = (f32[75,4,1]{2,1,0:T(4,128)}, f32[75,4,1]{2,1,0:T(4,128)}, u32[]{:S(2)}, u32[]{:S(2)}) collective-permute-start(f32[75,4,1]{2,1,0:T(4,128)} %get-tuple-element.105), channel_id=1, source_target_pairs={{0,1},{1,2},{2,3},{3,4},{4,5},{5,6},{6,7},{7,8},{8,9},{9,10},{10,1... | collective-permute-start | bytes 3608 | tf_op jit(solution)/shard_map/ppermute | solution.py:20
  105.2 8.8 %collective-permute-start.21 = (f32[75,1,128]{2,1,0:T(1,128)}, f32[75,1,128]{2,1,0:T(1,128)S(1)}, u32[]{:S(2)}, u32[]{:S(2)}) collective-permute-start(f32[75,1,128]{2,1,0:T(1,128)} %get-tuple-element.108), channel_id=1, source_target_pairs={{16,0},{32,16},{48,32},{64,48},{80,64},{96,80},{112,96},{17,1},{33... | collective-permute-start | bytes 115208 | tf_op jit(solution)/shard_map/ppermute | solution.py:23
  106.5 7.6 %collective-permute-start.22 = (f32[75,1,128]{2,1,0:T(1,128)S(1)}, f32[75,1,128]{2,1,0:T(1,128)S(1)}, u32[]{:S(2)}, u32[]{:S(2)}) collective-permute-start(f32[75,1,128]{2,1,0:T(1,128)S(1)} %get-tuple-element.109), channel_id=1, source_target_pairs={{0,16},{16,32},{32,48},{48,64},{64,80},{80,96},{96,112},{1,17},{17... | collective-permute-start | bytes 115208 | tf_op jit(solution)/shard_map/ppermute | solution.py:20
  116.0 12.1 %all-to-all-start.2 = ((f32[16,1,512]{2,1,0:T(1,128)}), f32[16,1,512]{2,1,0:T(1,128)S(1)}, u32[]{:S(2)}, u32[]{:S(2)}) async-start(f32[16,1,512]{2,1,0:T(1,128)} %reshape.282), calls=%async_computation.2 | async-start | bytes 65536 | tf_op jit(solution)/shard_map/all_to_all | solution.py:103
  124.5 23.4 %collective-permute-start.23 = (f32[75,4,1]{2,1,0:T(4,128)}, f32[75,4,1]{2,1,0:T(4,128)S(1)}, u32[]{:S(2)}, u32[]{:S(2)}) collective-permute-start(f32[75,4,1]{2,1,0:T(4,128)} %get-tuple-element.98), channel_id=1, source_target_pairs={{1,0},{2,1},{3,2},{4,3},{5,4},{6,5},{7,6},{8,7},{9,8},{10,9},{11,1... | collective-permute-start | bytes 3608 | tf_op jit(solution)/shard_map/ppermute | solution.py:23
  127.3 21.8 %collective-permute-start.24 = (f32[75,4,1]{2,1,0:T(4,128)}, f32[75,4,1]{2,1,0:T(4,128)}, u32[]{:S(2)}, u32[]{:S(2)}) collective-permute-start(f32[75,4,1]{2,1,0:T(4,128)} %get-tuple-element.99), channel_id=1, source_target_pairs={{0,1},{1,2},{2,3},{3,4},{4,5},{5,6},{6,7},{7,8},{8,9},{9,10},{10,1... | collective-permute-start | bytes 3608 | tf_op jit(solution)/shard_map/ppermute | solution.py:20
  129.9 14.8 %all-to-all-start.3 = ((f32[8,1,1024]{2,1,0:T(1,128)}), f32[8,1,1024]{2,1,0:T(1,128)S(1)}, u32[]{:S(2)}, u32[]{:S(2)}) async-start(f32[8,1,1024]{2,1,0:T(1,128)} %reshape.284), calls=%async_computation.3 | async-start | bytes 65536 | tf_op jit(solution)/shard_map/all_to_all | solution.py:104
  136.8 13.7 %collective-permute-start.25 = (f32[75,1,128]{2,1,0:T(1,128)S(1)}, f32[75,1,128]{2,1,0:T(1,128)S(1)}, u32[]{:S(2)}, u32[]{:S(2)}) collective-permute-start(f32[75,1,128]{2,1,0:T(1,128)S(1)} %get-tuple-element.102), channel_id=1, source_target_pairs={{16,0},{32,16},{48,32},{64,48},{80,64},{96,80},{112,96},{17,1},{33... | collective-permute-start | bytes 115208 | tf_op jit(solution)/shard_map/ppermute | solution.py:23
  138.1 12.4 %collective-permute-start.26 = (f32[75,1,128]{2,1,0:T(1,128)S(1)}, f32[75,1,128]{2,1,0:T(1,128)S(1)}, u32[]{:S(2)}, u32[]{:S(2)}) collective-permute-start(f32[75,1,128]{2,1,0:T(1,128)S(1)} %get-tuple-element.103), channel_id=1, source_target_pairs={{0,16},{16,32},{32,48},{48,64},{64,80},{80,96},{96,112},{1,17},{17... | collective-permute-start | bytes 115208 | tf_op jit(solution)/shard_map/ppermute | solution.py:20
  147.8 7.0 %collective-permute-start.28 = (f32[16,32]{1,0:T(8,128)S(1)}, f32[16,32]{1,0:T(8,128)S(1)}, u32[]{:S(2)}, u32[]{:S(2)}) collective-permute-start(f32[16,32]{1,0:T(8,128)S(1)} %fusion.5), channel_id=1, source_target_pairs={{128,384},{129,385},{130,386},{131,387},{132,388},{133,389},{134,3... | collective-permute-start | bytes 6152 | tf_op jit(solution)/shard_map/ppermute | solution.py:115
  160.3 9.8 %collective-permute-start.30 = (f32[75,4,1]{2,1,0:T(4,128)}, f32[75,4,1]{2,1,0:T(4,128)S(1)}, u32[]{:S(2)}, u32[]{:S(2)}) collective-permute-start(f32[75,4,1]{2,1,0:T(4,128)} %get-tuple-element.90), channel_id=1, source_target_pairs={{1,0},{2,1},{3,2},{4,3},{5,4},{6,5},{7,6},{8,7},{9,8},{10,9},{11,1... | collective-permute-start | bytes 3608 | tf_op jit(solution)/shard_map/ppermute | solution.py:23
  160.4 9.8 %collective-permute-start.31 = (f32[75,4,1]{2,1,0:T(4,128)}, f32[75,4,1]{2,1,0:T(4,128)}, u32[]{:S(2)}, u32[]{:S(2)}) collective-permute-start(f32[75,4,1]{2,1,0:T(4,128)} %get-tuple-element.91), channel_id=1, source_target_pairs={{0,1},{1,2},{2,3},{3,4},{4,5},{5,6},{6,7},{7,8},{8,9},{9,10},{10,1... | collective-permute-start | bytes 3608 | tf_op jit(solution)/shard_map/ppermute | solution.py:20
  161.5 8.7 %collective-permute-start.32 = (f32[75,1,128]{2,1,0:T(1,128)}, f32[75,1,128]{2,1,0:T(1,128)S(1)}, u32[]{:S(2)}, u32[]{:S(2)}) collective-permute-start(f32[75,1,128]{2,1,0:T(1,128)} %get-tuple-element.94), channel_id=1, source_target_pairs={{16,0},{32,16},{48,32},{64,48},{80,64},{96,80},{112,96},{17,1},{33... | collective-permute-start | bytes 115208 | tf_op jit(solution)/shard_map/ppermute | solution.py:23
  162.8 7.4 %collective-permute-start.33 = (f32[75,1,128]{2,1,0:T(1,128)S(1)}, f32[75,1,128]{2,1,0:T(1,128)S(1)}, u32[]{:S(2)}, u32[]{:S(2)}) collective-permute-start(f32[75,1,128]{2,1,0:T(1,128)S(1)} %get-tuple-element.95), channel_id=1, source_target_pairs={{0,16},{16,32},{32,48},{48,64},{64,80},{80,96},{96,112},{1,17},{17... | collective-permute-start | bytes 115208 | tf_op jit(solution)/shard_map/ppermute | solution.py:20
  172.1 12.1 %all-to-all-start.4 = ((f32[16,1,512]{2,1,0:T(1,128)}), f32[16,1,512]{2,1,0:T(1,128)S(1)}, u32[]{:S(2)}, u32[]{:S(2)}) async-start(f32[16,1,512]{2,1,0:T(1,128)} %reshape.286), calls=%async_computation.4 | async-start | bytes 65536 | tf_op jit(solution)/shard_map/all_to_all | solution.py:103
  180.6 23.5 %collective-permute-start.34 = (f32[75,4,1]{2,1,0:T(4,128)}, f32[75,4,1]{2,1,0:T(4,128)S(1)}, u32[]{:S(2)}, u32[]{:S(2)}) collective-permute-start(f32[75,4,1]{2,1,0:T(4,128)} %get-tuple-element.84), channel_id=1, source_target_pairs={{1,0},{2,1},{3,2},{4,3},{5,4},{6,5},{7,6},{8,7},{9,8},{10,9},{11,1... | collective-permute-start | bytes 3608 | tf_op jit(solution)/shard_map/ppermute | solution.py:23
  183.4 22.0 %collective-permute-start.35 = (f32[75,4,1]{2,1,0:T(4,128)}, f32[75,4,1]{2,1,0:T(4,128)}, u32[]{:S(2)}, u32[]{:S(2)}) collective-permute-start(f32[75,4,1]{2,1,0:T(4,128)} %get-tuple-element.85), channel_id=1, source_target_pairs={{0,1},{1,2},{2,3},{3,4},{4,5},{5,6},{6,7},{7,8},{8,9},{9,10},{10,1... | collective-permute-start | bytes 3608 | tf_op jit(solution)/shard_map/ppermute | solution.py:20
  186.0 15.0 %all-to-all-start.5 = ((f32[8,1,1024]{2,1,0:T(1,128)}), f32[8,1,1024]{2,1,0:T(1,128)S(1)}, u32[]{:S(2)}, u32[]{:S(2)}) async-start(f32[8,1,1024]{2,1,0:T(1,128)} %reshape.288), calls=%async_computation.5 | async-start | bytes 65536 | tf_op jit(solution)/shard_map/all_to_all | solution.py:104
  193.0 13.7 %collective-permute-start.36 = (f32[75,1,128]{2,1,0:T(1,128)S(1)}, f32[75,1,128]{2,1,0:T(1,128)S(1)}, u32[]{:S(2)}, u32[]{:S(2)}) collective-permute-start(f32[75,1,128]{2,1,0:T(1,128)S(1)} %get-tuple-element.88), channel_id=1, source_target_pairs={{16,0},{32,16},{48,32},{64,48},{80,64},{96,80},{112,96},{17,1},{33... | collective-permute-start | bytes 115208 | tf_op jit(solution)/shard_map/ppermute | solution.py:23
  194.3 12.4 %collective-permute-start.37 = (f32[75,1,128]{2,1,0:T(1,128)S(1)}, f32[75,1,128]{2,1,0:T(1,128)S(1)}, u32[]{:S(2)}, u32[]{:S(2)}) collective-permute-start(f32[75,1,128]{2,1,0:T(1,128)S(1)} %get-tuple-element.89), channel_id=1, source_target_pairs={{0,16},{16,32},{32,48},{48,64},{64,80},{80,96},{96,112},{1,17},{17... | collective-permute-start | bytes 115208 | tf_op jit(solution)/shard_map/ppermute | solution.py:20
  204.1 7.0 %collective-permute-start.39 = (f32[16,32]{1,0:T(8,128)S(1)}, f32[16,32]{1,0:T(8,128)S(1)}, u32[]{:S(2)}, u32[]{:S(2)}) collective-permute-start(f32[16,32]{1,0:T(8,128)S(1)} %fusion.3), channel_id=1, source_target_pairs={{128,384},{129,385},{130,386},{131,387},{132,388},{133,389},{134,3... | collective-permute-start | bytes 6152 | tf_op jit(solution)/shard_map/ppermute | solution.py:115
  216.6 9.4 %collective-permute-start.41 = (f32[75,4,1]{2,1,0:T(4,128)}, f32[75,4,1]{2,1,0:T(4,128)S(1)}, u32[]{:S(2)}, u32[]{:S(2)}) collective-permute-start(f32[75,4,1]{2,1,0:T(4,128)} %get-tuple-element.76), channel_id=1, source_target_pairs={{1,0},{2,1},{3,2},{4,3},{5,4},{6,5},{7,6},{8,7},{9,8},{10,9},{11,1... | collective-permute-start | bytes 3608 | tf_op jit(solution)/shard_map/ppermute | solution.py:23
  216.6 9.4 %collective-permute-start.42 = (f32[75,4,1]{2,1,0:T(4,128)}, f32[75,4,1]{2,1,0:T(4,128)}, u32[]{:S(2)}, u32[]{:S(2)}) collective-permute-start(f32[75,4,1]{2,1,0:T(4,128)} %get-tuple-element.77), channel_id=1, source_target_pairs={{0,1},{1,2},{2,3},{3,4},{4,5},{5,6},{6,7},{7,8},{8,9},{9,10},{10,1... | collective-permute-start | bytes 3608 | tf_op jit(solution)/shard_map/ppermute | solution.py:20
  217.2 8.9 %collective-permute-start.43 = (f32[75,1,128]{2,1,0:T(1,128)S(1)}, f32[75,1,128]{2,1,0:T(1,128)S(1)}, u32[]{:S(2)}, u32[]{:S(2)}) collective-permute-start(f32[75,1,128]{2,1,0:T(1,128)S(1)} %get-tuple-element.80), channel_id=1, source_target_pairs={{16,0},{32,16},{48,32},{64,48},{80,64},{96,80},{112,96},{17,1},{33... | collective-permute-start | bytes 115208 | tf_op jit(solution)/shard_map/ppermute | solution.py:23
  218.5 7.6 %collective-permute-start.44 = (f32[75,1,128]{2,1,0:T(1,128)S(1)}, f32[75,1,128]{2,1,0:T(1,128)S(1)}, u32[]{:S(2)}, u32[]{:S(2)}) collective-permute-start(f32[75,1,128]{2,1,0:T(1,128)S(1)} %get-tuple-element.81), channel_id=1, source_target_pairs={{0,16},{16,32},{32,48},{48,64},{64,80},{80,96},{96,112},{1,17},{17... | collective-permute-start | bytes 115208 | tf_op jit(solution)/shard_map/ppermute | solution.py:20
  228.0 12.1 %all-to-all-start.6 = ((f32[16,1,512]{2,1,0:T(1,128)}), f32[16,1,512]{2,1,0:T(1,128)S(1)}, u32[]{:S(2)}, u32[]{:S(2)}) async-start(f32[16,1,512]{2,1,0:T(1,128)} %reshape.290), calls=%async_computation.6 | async-start | bytes 65536 | tf_op jit(solution)/shard_map/all_to_all | solution.py:103
  235.8 24.3 %collective-permute-start.45 = (f32[75,4,1]{2,1,0:T(4,128)S(1)}, f32[75,4,1]{2,1,0:T(4,128)S(1)}, u32[]{:S(2)}, u32[]{:S(2)}) collective-permute-start(f32[75,4,1]{2,1,0:T(4,128)S(1)} %get-tuple-element.70), channel_id=1, source_target_pairs={{1,0},{2,1},{3,2},{4,3},{5,4},{6,5},{7,6},{8,7},{9,8},{10,9},{11,1... | collective-permute-start | bytes 3608 | tf_op jit(solution)/shard_map/ppermute | solution.py:23
  238.6 22.7 %collective-permute-start.46 = (f32[75,4,1]{2,1,0:T(4,128)S(1)}, f32[75,4,1]{2,1,0:T(4,128)S(1)}, u32[]{:S(2)}, u32[]{:S(2)}) collective-permute-start(f32[75,4,1]{2,1,0:T(4,128)S(1)} %get-tuple-element.71), channel_id=1, source_target_pairs={{0,1},{1,2},{2,3},{3,4},{4,5},{5,6},{6,7},{7,8},{8,9},{9,10},{10,1... | collective-permute-start | bytes 3608 | tf_op jit(solution)/shard_map/ppermute | solution.py:20
  242.0 15.0 %all-to-all-start.7 = ((f32[8,1,1024]{2,1,0:T(1,128)}), f32[8,1,1024]{2,1,0:T(1,128)S(1)}, u32[]{:S(2)}, u32[]{:S(2)}) async-start(f32[8,1,1024]{2,1,0:T(1,128)} %reshape.292), calls=%async_computation.7 | async-start | bytes 65536 | tf_op jit(solution)/shard_map/all_to_all | solution.py:104
  249.0 13.7 %collective-permute-start.47 = (f32[75,1,128]{2,1,0:T(1,128)S(1)}, f32[75,1,128]{2,1,0:T(1,128)S(1)}, u32[]{:S(2)}, u32[]{:S(2)}) collective-permute-start(f32[75,1,128]{2,1,0:T(1,128)S(1)} %get-tuple-element.74), channel_id=1, source_target_pairs={{16,0},{32,16},{48,32},{64,48},{80,64},{96,80},{112,96},{17,1},{33... | collective-permute-start | bytes 115208 | tf_op jit(solution)/shard_map/ppermute | solution.py:23
  250.3 12.4 %collective-permute-start.48 = (f32[75,1,128]{2,1,0:T(1,128)S(1)}, f32[75,1,128]{2,1,0:T(1,128)S(1)}, u32[]{:S(2)}, u32[]{:S(2)}) collective-permute-start(f32[75,1,128]{2,1,0:T(1,128)S(1)} %get-tuple-element.75), channel_id=1, source_target_pairs={{0,16},{16,32},{32,48},{48,64},{64,80},{80,96},{96,112},{1,17},{17... | collective-permute-start | bytes 115208 | tf_op jit(solution)/shard_map/ppermute | solution.py:20
  (35 other events, 404.2 us)

commit v9 on v3

--- a/solution.py
+++ b/solution.py
@@ -110,7 +110,11 @@
         arrived, one_hot, precision=lax.Precision.HIGHEST, preferred_element_type=jnp.float32
     )
     section_count = lax.axis_size("sec")
-    return [lax.ppermute(accumulated, "sec", [(s, section_count - 1)]) for s in range(section_count - 1)]
+    if section_count != 4:
+        return [lax.ppermute(accumulated, "sec", [(s, section_count - 1)]) for s in range(section_count - 1)]
+    first = lax.ppermute(accumulated, "sec", [(0, 3), (1, 2)])
+    second = lax.ppermute(accumulated + first, "sec", [(2, 3)])
+    return [first, second]
 
 
 def forcing_field(parts, shape):

time: 270 us -> 283 us (1.048)
  waiting for transfers between devices: 26.6 us -> 61.5 us
  starting transfers between devices: 145 us -> 128 us
  other arithmetic: 33.4 us -> 29.7 us
    ppermute x12 -> x8, waiting for transfers between devices: 13.4 us -> 34.4 us  [the longest x4 19.1 us: reduce_forcing(): first = lax.ppermute(accumulated, 'sec', [(0, 3), (1, 2)])]
    all_to_all x4, waiting for transfers between devices: 3.43 us -> 17.4 us  [couple(): lax.all_to_all(staged, 'lon', split_axis=2, concat_axis=2, tiled=True)]
    ppermute x20, starting transfers between devices: 32 us -> 20.7 us  [extended(): lax.ppermute(lax.slice_in_dim(block, 0, width, axis=dim), axis, backward)]
    ppermute x12 -> x8, starting transfers between devices: 15.6 us -> 10.3 us  [the longest x4 5.21 us: reduce_forcing(): first = lax.ppermute(accumulated, 'sec', [(0, 3), (1, 2)])]
    all_to_all x4, starting transfers between devices: 17.6 us -> 14.8 us  [couple(): lax.all_to_all(staged, 'lon', split_axis=2, concat_axis=2, tiled=True)]
    unnamed x69 -> x67, local copies, waits for them, and re-layouts: 9.47 us -> 9.49 us
  transfers between devices with their start and end apart: 60 -> 56, of which waited for: 17 -> 17; matrix products, arithmetic and copies ran while one was open for 16% -> 11% of each run, Pallas kernels for 3% -> 3%
where the time goes in v9:
time: 283 us; the launch traced here: 281 us
  starting transfers between devices  128 us (45%)
  waiting for transfers between devices  61.5 us (22%)
  other arithmetic  29.7 us (10%)
  local copies, waits for them, and re-layouts  25.4 us (9%)
  Pallas kernels  25 us (9%)
  matrix products  9.65 us (3%)
    ppermute x20, starting transfers between devices, extended(): lax.ppermute(lax.slice_in_dim(block, block.shape[dim] - width, None, axis...  50.5 us
    all_to_all x4, starting transfers between devices, couple(): lax.all_to_all(staged, 'lat', split_axis=1, concat_axis=1, tiled=True)  32 us
    pallas_call x10, Pallas kernels, column_solve(): pl.pallas_call(_solve_kernel, out_shape=jax.ShapeDtypeStruct(right.shape,...  22.7 us
    ppermute x20, starting transfers between devices, extended(): lax.ppermute(lax.slice_in_dim(block, 0, width, axis=dim), axis, backward)  20.7 us
    ppermute x4, waiting for transfers between devices, reduce_forcing(): first = lax.ppermute(accumulated, 'sec', [(0, 3), (1, 2)])  19.1 us
    all_to_all x4, waiting for transfers between devices, couple(): lax.all_to_all(staged, 'lon', split_axis=2, concat_axis=2, tiled=True)  17.4 us
    ppermute x4, waiting for transfers between devices, reduce_forcing(): second = lax.ppermute(accumulated + first, 'sec', [(2, 3)])  15.3 us
    all_to_all x4, starting transfers between devices, couple(): lax.all_to_all(staged, 'lon', split_axis=2, concat_axis=2, tiled=True)  14.8 us
  transfers between devices with their start and end apart: 56, of which 17 were waited for; matrix products, arithmetic and copies ran while one was open for 11% of the time, Pallas kernels for 3%

profile of v9, /device:TPU:6, one launch (start us, length us, event | category | flops | bytes accessed | tf_op | source)
XLA Modules:
  0.0 280.7 jit_solution(10466600653903864587)
XLA Ops:
  1.6 2.4 shard_map.91
  4.0 2.3 shard_map.92
  7.5 2.9 %collective-permute-start = (f32[75,4,1]{2,1,0:T(4,128)S(1)}, f32[75,4,1]{2,1,0:T(4,128)S(1)}, u32[]{:S(2)}, u32[]{:S(2)}) collective-permute-start(f32[75,4,1]{2,1,0:T(4,128)S(1)} %get-tuple-element.128), channel_id=1, source_target_pairs={{1,0},{2,1},{3,2},{4,3},{5,4},{6,5},{7,6},{8,7},{9,8},{10,9},{11,1... | collective-permute-start | bytes 3608 | tf_op jit(solution)/shard_map/ppermute | solution.py:23
  11.8 4.9 %collective-permute-start.3 = (f32[75,1,128]{2,1,0:T(1,128)S(1)}, f32[75,1,128]{2,1,0:T(1,128)S(1)}, u32[]{:S(2)}, u32[]{:S(2)}) collective-permute-start(f32[75,1,128]{2,1,0:T(1,128)S(1)} %get-tuple-element.133), channel_id=1, source_target_pairs={{0,16},{16,32},{32,48},{48,64},{64,80},{80,96},{96,112},{1,17},{17... | collective-permute-start | bytes 115208 | tf_op jit(solution)/shard_map/ppermute | solution.py:20
  20.3 2.3 shard_map.93
  24.4 2.1 collective-permute-start.4
  27.9 4.9 %collective-permute-start.7 = (f32[75,1,128]{2,1,0:T(1,128)S(1)}, f32[75,1,128]{2,1,0:T(1,128)S(1)}, u32[]{:S(2)}, u32[]{:S(2)}) collective-permute-start(f32[75,1,128]{2,1,0:T(1,128)S(1)} %get-tuple-element.127), channel_id=1, source_target_pairs={{0,16},{16,32},{32,48},{48,64},{64,80},{80,96},{96,112},{1,17},{17... | collective-permute-start | bytes 115208 | tf_op jit(solution)/shard_map/ppermute | solution.py:20
  37.2 2.3 shard_map.94
  41.4 2.7 collective-permute-start.8
  45.4 4.9 %collective-permute-start.11 = (f32[75,1,128]{2,1,0:T(1,128)S(1)}, f32[75,1,128]{2,1,0:T(1,128)S(1)}, u32[]{:S(2)}, u32[]{:S(2)}) collective-permute-start(f32[75,1,128]{2,1,0:T(1,128)S(1)} %get-tuple-element.121), channel_id=1, source_target_pairs={{0,16},{16,32},{32,48},{48,64},{64,80},{80,96},{96,112},{1,17},{17... | collective-permute-start | bytes 115208 | tf_op jit(solution)/shard_map/ppermute | solution.py:20
  55.4 4.3 %all-to-all-start = ((f32[16,1,512]{2,1,0:T(1,128)}), f32[16,1,512]{2,1,0:T(1,128)S(1)}, u32[]{:S(2)}, u32[]{:S(2)}) async-start(f32[16,1,512]{2,1,0:T(1,128)} %reshape.278), calls=%async_computation | async-start | bytes 65536 | tf_op jit(solution)/shard_map/all_to_all | solution.py:101
  59.7 2.3 shard_map.95
  63.0 4.4 %all-to-all-done = f32[16,1,512]{2,1,0:T(1,128)S(1)} async-done(((f32[16,1,512]{2,1,0:T(1,128)}), f32[16,1,512]{2,1,0:T(1,128)S(1)}, u32[]{:S(2)}, u32[]{:S(2)}) %all-to-all-start) | async-done | bytes 32800 | tf_op jit(solution)/shard_map/all_to_all | solution.py:101
  69.6 10.8 %all-to-all-start.1 = ((f32[8,1,1024]{2,1,0:T(1,128)}), f32[8,1,1024]{2,1,0:T(1,128)S(1)}, u32[]{:S(2)}, u32[]{:S(2)}) async-start(f32[8,1,1024]{2,1,0:T(1,128)} %reshape.280), calls=%async_computation.1 | async-start | bytes 65536 | tf_op jit(solution)/shard_map/all_to_all | solution.py:102
  81.8 4.6 %collective-permute-start.15 = (f32[75,1,128]{2,1,0:T(1,128)S(1)}, f32[75,1,128]{2,1,0:T(1,128)S(1)}, u32[]{:S(2)}, u32[]{:S(2)}) collective-permute-start(f32[75,1,128]{2,1,0:T(1,128)S(1)} %get-tuple-element.115), channel_id=1, source_target_pairs={{0,16},{16,32},{32,48},{48,64},{64,80},{80,96},{96,112},{1,17},{17... | collective-permute-start | bytes 115208 | tf_op jit(solution)/shard_map/ppermute | solution.py:20
  86.3 2.1 all-to-all-done.1
  92.1 4.8 %collective-permute-done.16 = f32[16,32]{1,0:T(8,128)S(1)} collective-permute-done((f32[16,32]{1,0:T(8,128)S(1)}, f32[16,32]{1,0:T(8,128)S(1)}, u32[]{:S(2)}, u32[]{:S(2)}) %collective-permute-start.16) | collective-permute-done | bytes 2080 | tf_op jit(solution)/shard_map/ppermute | solution.py:115
  98.6 3.8 %collective-permute-done.17 = f32[16,32]{1,0:T(8,128)S(1)} collective-permute-done((f32[16,32]{1,0:T(8,128)S(1)}, f32[16,32]{1,0:T(8,128)S(1)}, u32[]{:S(2)}, u32[]{:S(2)}) %collective-permute-start.17) | collective-permute-done | bytes 2080 | tf_op jit(solution)/shard_map/ppermute | solution.py:116
  103.8 2.3 shard_map.96
  110.4 4.7 %collective-permute-start.21 = (f32[75,1,128]{2,1,0:T(1,128)S(1)}, f32[75,1,128]{2,1,0:T(1,128)S(1)}, u32[]{:S(2)}, u32[]{:S(2)}) collective-permute-start(f32[75,1,128]{2,1,0:T(1,128)S(1)} %get-tuple-element.109), channel_id=1, source_target_pairs={{0,16},{16,32},{32,48},{48,64},{64,80},{80,96},{96,112},{1,17},{17... | collective-permute-start | bytes 115208 | tf_op jit(solution)/shard_map/ppermute | solution.py:20
  119.8 3.5 %all-to-all-start.2 = ((f32[16,1,512]{2,1,0:T(1,128)}), f32[16,1,512]{2,1,0:T(1,128)S(1)}, u32[]{:S(2)}, u32[]{:S(2)}) async-start(f32[16,1,512]{2,1,0:T(1,128)} %reshape.282), calls=%async_computation.2 | async-start | bytes 65536 | tf_op jit(solution)/shard_map/all_to_all | solution.py:101
  123.3 2.3 shard_map.97
  126.7 4.3 %all-to-all-done.2 = f32[16,1,512]{2,1,0:T(1,128)S(1)} async-done(((f32[16,1,512]{2,1,0:T(1,128)}), f32[16,1,512]{2,1,0:T(1,128)S(1)}, u32[]{:S(2)}, u32[]{:S(2)}) %all-to-all-start.2) | async-done | bytes 32800 | tf_op jit(solution)/shard_map/all_to_all | solution.py:101
  132.7 7.0 %all-to-all-start.3 = ((f32[8,1,1024]{2,1,0:T(1,128)}), f32[8,1,1024]{2,1,0:T(1,128)S(1)}, u32[]{:S(2)}, u32[]{:S(2)}) async-start(f32[8,1,1024]{2,1,0:T(1,128)} %reshape.284), calls=%async_computation.3 | async-start | bytes 65536 | tf_op jit(solution)/shard_map/all_to_all | solution.py:102
  141.1 4.6 %collective-permute-start.25 = (f32[75,1,128]{2,1,0:T(1,128)S(1)}, f32[75,1,128]{2,1,0:T(1,128)S(1)}, u32[]{:S(2)}, u32[]{:S(2)}) collective-permute-start(f32[75,1,128]{2,1,0:T(1,128)S(1)} %get-tuple-element.103), channel_id=1, source_target_pairs={{0,16},{16,32},{32,48},{48,64},{64,80},{80,96},{96,112},{1,17},{17... | collective-permute-start | bytes 115208 | tf_op jit(solution)/shard_map/ppermute | solution.py:20
  145.7 2.1 all-to-all-done.3
  151.4 4.8 %collective-permute-done.26 = f32[16,32]{1,0:T(8,128)S(1)} collective-permute-done((f32[16,32]{1,0:T(8,128)S(1)}, f32[16,32]{1,0:T(8,128)S(1)}, u32[]{:S(2)}, u32[]{:S(2)}) %collective-permute-start.26) | collective-permute-done | bytes 2080 | tf_op jit(solution)/shard_map/ppermute | solution.py:115
  157.9 3.8 %collective-permute-done.27 = f32[16,32]{1,0:T(8,128)S(1)} collective-permute-done((f32[16,32]{1,0:T(8,128)S(1)}, f32[16,32]{1,0:T(8,128)S(1)}, u32[]{:S(2)}, u32[]{:S(2)}) %collective-permute-start.27) | collective-permute-done | bytes 2080 | tf_op jit(solution)/shard_map/ppermute | solution.py:116
  163.2 2.3 shard_map.98
  169.7 4.5 %collective-permute-start.31 = (f32[75,1,128]{2,1,0:T(1,128)S(1)}, f32[75,1,128]{2,1,0:T(1,128)S(1)}, u32[]{:S(2)}, u32[]{:S(2)}) collective-permute-start(f32[75,1,128]{2,1,0:T(1,128)S(1)} %get-tuple-element.95), channel_id=1, source_target_pairs={{0,16},{16,32},{32,48},{48,64},{64,80},{80,96},{96,112},{1,17},{17... | collective-permute-start | bytes 115208 | tf_op jit(solution)/shard_map/ppermute | solution.py:20
  179.0 3.5 %all-to-all-start.4 = ((f32[16,1,512]{2,1,0:T(1,128)}), f32[16,1,512]{2,1,0:T(1,128)S(1)}, u32[]{:S(2)}, u32[]{:S(2)}) async-start(f32[16,1,512]{2,1,0:T(1,128)} %reshape.286), calls=%async_computation.4 | async-start | bytes 65536 | tf_op jit(solution)/shard_map/all_to_all | solution.py:101
  182.5 2.3 shard_map.99
  185.8 4.3 %all-to-all-done.4 = f32[16,1,512]{2,1,0:T(1,128)S(1)} async-done(((f32[16,1,512]{2,1,0:T(1,128)}), f32[16,1,512]{2,1,0:T(1,128)S(1)}, u32[]{:S(2)}, u32[]{:S(2)}) %all-to-all-start.4) | async-done | bytes 32800 | tf_op jit(solution)/shard_map/all_to_all | solution.py:101
  191.9 7.2 %all-to-all-start.5 = ((f32[8,1,1024]{2,1,0:T(1,128)}), f32[8,1,1024]{2,1,0:T(1,128)S(1)}, u32[]{:S(2)}, u32[]{:S(2)}) async-start(f32[8,1,1024]{2,1,0:T(1,128)} %reshape.288), calls=%async_computation.5 | async-start | bytes 65536 | tf_op jit(solution)/shard_map/all_to_all | solution.py:102
  200.5 4.6 %collective-permute-start.35 = (f32[75,1,128]{2,1,0:T(1,128)S(1)}, f32[75,1,128]{2,1,0:T(1,128)S(1)}, u32[]{:S(2)}, u32[]{:S(2)}) collective-permute-start(f32[75,1,128]{2,1,0:T(1,128)S(1)} %get-tuple-element.89), channel_id=1, source_target_pairs={{0,16},{16,32},{32,48},{48,64},{64,80},{80,96},{96,112},{1,17},{17... | collective-permute-start | bytes 115208 | tf_op jit(solution)/shard_map/ppermute | solution.py:20
  205.0 2.1 all-to-all-done.5
  210.8 4.8 %collective-permute-done.36 = f32[16,32]{1,0:T(8,128)S(1)} collective-permute-done((f32[16,32]{1,0:T(8,128)S(1)}, f32[16,32]{1,0:T(8,128)S(1)}, u32[]{:S(2)}, u32[]{:S(2)}) %collective-permute-start.36) | collective-permute-done | bytes 2080 | tf_op jit(solution)/shard_map/ppermute | solution.py:115
  217.3 3.8 %collective-permute-done.37 = f32[16,32]{1,0:T(8,128)S(1)} collective-permute-done((f32[16,32]{1,0:T(8,128)S(1)}, f32[16,32]{1,0:T(8,128)S(1)}, u32[]{:S(2)}, u32[]{:S(2)}) %collective-permute-start.37) | collective-permute-done | bytes 2080 | tf_op jit(solution)/shard_map/ppermute | solution.py:116
  222.5 2.3 shard_map.100
  228.5 4.8 %collective-permute-start.41 = (f32[75,1,128]{2,1,0:T(1,128)S(1)}, f32[75,1,128]{2,1,0:T(1,128)S(1)}, u32[]{:S(2)}, u32[]{:S(2)}) collective-permute-start(f32[75,1,128]{2,1,0:T(1,128)S(1)} %get-tuple-element.81), channel_id=1, source_target_pairs={{0,16},{16,32},{32,48},{48,64},{64,80},{80,96},{96,112},{1,17},{17... | collective-permute-start | bytes 115208 | tf_op jit(solution)/shard_map/ppermute | solution.py:20
  238.0 3.5 %all-to-all-start.6 = ((f32[16,1,512]{2,1,0:T(1,128)}), f32[16,1,512]{2,1,0:T(1,128)S(1)}, u32[]{:S(2)}, u32[]{:S(2)}) async-start(f32[16,1,512]{2,1,0:T(1,128)} %reshape.290), calls=%async_computation.6 | async-start | bytes 65536 | tf_op jit(solution)/shard_map/all_to_all | solution.py:101
  241.5 2.3 shard_map.101
  244.8 4.3 %all-to-all-done.6 = f32[16,1,512]{2,1,0:T(1,128)S(1)} async-done(((f32[16,1,512]{2,1,0:T(1,128)}), f32[16,1,512]{2,1,0:T(1,128)S(1)}, u32[]{:S(2)}, u32[]{:S(2)}) %all-to-all-start.6) | async-done | bytes 32800 | tf_op jit(solution)/shard_map/all_to_all | solution.py:101
  250.9 7.0 %all-to-all-start.7 = ((f32[8,1,1024]{2,1,0:T(1,128)}), f32[8,1,1024]{2,1,0:T(1,128)S(1)}, u32[]{:S(2)}, u32[]{:S(2)}) async-start(f32[8,1,1024]{2,1,0:T(1,128)} %reshape.292), calls=%async_computation.7 | async-start | bytes 65536 | tf_op jit(solution)/shard_map/all_to_all | solution.py:102
  259.2 4.6 %collective-permute-start.45 = (f32[75,1,128]{2,1,0:T(1,128)S(1)}, f32[75,1,128]{2,1,0:T(1,128)S(1)}, u32[]{:S(2)}, u32[]{:S(2)}) collective-permute-start(f32[75,1,128]{2,1,0:T(1,128)S(1)} %get-tuple-element.75), channel_id=1, source_target_pairs={{0,16},{16,32},{32,48},{48,64},{64,80},{80,96},{96,112},{1,17},{17... | collective-permute-start | bytes 115208 | tf_op jit(solution)/shard_map/ppermute | solution.py:20
  263.8 2.1 all-to-all-done.7
  269.5 4.8 %collective-permute-done.46 = f32[16,32]{1,0:T(8,128)S(1)} collective-permute-done((f32[16,32]{1,0:T(8,128)S(1)}, f32[16,32]{1,0:T(8,128)S(1)}, u32[]{:S(2)}, u32[]{:S(2)}) %collective-permute-start.46) | collective-permute-done | bytes 2080 | tf_op jit(solution)/shard_map/ppermute | solution.py:115
  276.0 3.8 %collective-permute-done.47 = f32[16,32]{1,0:T(8,128)S(1)} collective-permute-done((f32[16,32]{1,0:T(8,128)S(1)}, f32[16,32]{1,0:T(8,128)S(1)}, u32[]{:S(2)}, u32[]{:S(2)}) %collective-permute-start.47) | collective-permute-done | bytes 2080 | tf_op jit(solution)/shard_map/ppermute | solution.py:116
  (255 shorter events, 92.9 us)
Async XLA Ops:
  7.5 9.6 %collective-permute-start = (f32[75,4,1]{2,1,0:T(4,128)S(1)}, f32[75,4,1]{2,1,0:T(4,128)S(1)}, u32[]{:S(2)}, u32[]{:S(2)}) collective-permute-start(f32[75,4,1]{2,1,0:T(4,128)S(1)} %get-tuple-element.128), channel_id=1, source_target_pairs={{1,0},{2,1},{3,2},{4,3},{5,4},{6,5},{7,6},{8,7},{9,8},{10,9},{11,1... | collective-permute-start | bytes 3608 | tf_op jit(solution)/shard_map/ppermute | solution.py:23
  10.4 6.7 %collective-permute-start.1 = (f32[75,4,1]{2,1,0:T(4,128)S(1)}, f32[75,4,1]{2,1,0:T(4,128)S(1)}, u32[]{:S(2)}, u32[]{:S(2)}) collective-permute-start(f32[75,4,1]{2,1,0:T(4,128)S(1)} %get-tuple-element.129), channel_id=1, source_target_pairs={{0,1},{1,2},{2,3},{3,4},{4,5},{5,6},{6,7},{7,8},{8,9},{9,10},{10,1... | collective-permute-start | bytes 3608 | tf_op jit(solution)/shard_map/ppermute | solution.py:20
  10.5 6.6 %collective-permute-start.2 = (f32[75,1,128]{2,1,0:T(1,128)S(1)}, f32[75,1,128]{2,1,0:T(1,128)S(1)}, u32[]{:S(2)}, u32[]{:S(2)}) collective-permute-start(f32[75,1,128]{2,1,0:T(1,128)S(1)} %get-tuple-element.132), channel_id=1, source_target_pairs={{16,0},{32,16},{48,32},{64,48},{80,64},{96,80},{112,96},{17,1},{33... | collective-permute-start | bytes 115208 | tf_op jit(solution)/shard_map/ppermute | solution.py:23
  24.4 10.8 %collective-permute-start.4 = (f32[75,4,1]{2,1,0:T(4,128)}, f32[75,4,1]{2,1,0:T(4,128)S(1)}, u32[]{:S(2)}, u32[]{:S(2)}) collective-permute-start(f32[75,4,1]{2,1,0:T(4,128)} %get-tuple-element.122), channel_id=1, source_target_pairs={{1,0},{2,1},{3,2},{4,3},{5,4},{6,5},{7,6},{8,7},{9,8},{10,9},{11,1... | collective-permute-start | bytes 3608 | tf_op jit(solution)/shard_map/ppermute | solution.py:23
  26.5 8.7 %collective-permute-start.5 = (f32[75,4,1]{2,1,0:T(4,128)}, f32[75,4,1]{2,1,0:T(4,128)}, u32[]{:S(2)}, u32[]{:S(2)}) collective-permute-start(f32[75,4,1]{2,1,0:T(4,128)} %get-tuple-element.123), channel_id=1, source_target_pairs={{0,1},{1,2},{2,3},{3,4},{4,5},{5,6},{6,7},{7,8},{8,9},{9,10},{10,1... | collective-permute-start | bytes 3608 | tf_op jit(solution)/shard_map/ppermute | solution.py:20
  26.6 8.7 %collective-permute-start.6 = (f32[75,1,128]{2,1,0:T(1,128)S(1)}, f32[75,1,128]{2,1,0:T(1,128)S(1)}, u32[]{:S(2)}, u32[]{:S(2)}) collective-permute-start(f32[75,1,128]{2,1,0:T(1,128)S(1)} %get-tuple-element.126), channel_id=1, source_target_pairs={{16,0},{32,16},{48,32},{64,48},{80,64},{96,80},{112,96},{17,1},{33... | collective-permute-start | bytes 115208 | tf_op jit(solution)/shard_map/ppermute | solution.py:23
  27.9 7.4 %collective-permute-start.7 = (f32[75,1,128]{2,1,0:T(1,128)S(1)}, f32[75,1,128]{2,1,0:T(1,128)S(1)}, u32[]{:S(2)}, u32[]{:S(2)}) collective-permute-start(f32[75,1,128]{2,1,0:T(1,128)S(1)} %get-tuple-element.127), channel_id=1, source_target_pairs={{0,16},{16,32},{32,48},{48,64},{64,80},{80,96},{96,112},{1,17},{17... | collective-permute-start | bytes 115208 | tf_op jit(solution)/shard_map/ppermute | solution.py:20
  41.4 12.9 %collective-permute-start.8 = (f32[75,4,1]{2,1,0:T(4,128)}, f32[75,4,1]{2,1,0:T(4,128)S(1)}, u32[]{:S(2)}, u32[]{:S(2)}) collective-permute-start(f32[75,4,1]{2,1,0:T(4,128)} %get-tuple-element.116), channel_id=1, source_target_pairs={{1,0},{2,1},{3,2},{4,3},{5,4},{6,5},{7,6},{8,7},{9,8},{10,9},{11,1... | collective-permute-start | bytes 3608 | tf_op jit(solution)/shard_map/ppermute | solution.py:23
  44.1 10.3 %collective-permute-start.9 = (f32[75,4,1]{2,1,0:T(4,128)}, f32[75,4,1]{2,1,0:T(4,128)S(1)}, u32[]{:S(2)}, u32[]{:S(2)}) collective-permute-start(f32[75,4,1]{2,1,0:T(4,128)} %get-tuple-element.117), channel_id=1, source_target_pairs={{0,1},{1,2},{2,3},{3,4},{4,5},{5,6},{6,7},{7,8},{8,9},{9,10},{10,1... | collective-permute-start | bytes 3608 | tf_op jit(solution)/shard_map/ppermute | solution.py:20
  44.1 10.2 %collective-permute-start.10 = (f32[75,1,128]{2,1,0:T(1,128)S(1)}, f32[75,1,128]{2,1,0:T(1,128)S(1)}, u32[]{:S(2)}, u32[]{:S(2)}) collective-permute-start(f32[75,1,128]{2,1,0:T(1,128)S(1)} %get-tuple-element.120), channel_id=1, source_target_pairs={{16,0},{32,16},{48,32},{64,48},{80,64},{96,80},{112,96},{17,1},{33... | collective-permute-start | bytes 115208 | tf_op jit(solution)/shard_map/ppermute | solution.py:23
  45.4 8.9 %collective-permute-start.11 = (f32[75,1,128]{2,1,0:T(1,128)S(1)}, f32[75,1,128]{2,1,0:T(1,128)S(1)}, u32[]{:S(2)}, u32[]{:S(2)}) collective-permute-start(f32[75,1,128]{2,1,0:T(1,128)S(1)} %get-tuple-element.121), channel_id=1, source_target_pairs={{0,16},{16,32},{32,48},{48,64},{64,80},{80,96},{96,112},{1,17},{17... | collective-permute-start | bytes 115208 | tf_op jit(solution)/shard_map/ppermute | solution.py:20
  55.4 12.0 %all-to-all-start = ((f32[16,1,512]{2,1,0:T(1,128)}), f32[16,1,512]{2,1,0:T(1,128)S(1)}, u32[]{:S(2)}, u32[]{:S(2)}) async-start(f32[16,1,512]{2,1,0:T(1,128)} %reshape.278), calls=%async_computation | async-start | bytes 65536 | tf_op jit(solution)/shard_map/all_to_all | solution.py:101
  69.6 18.8 %all-to-all-start.1 = ((f32[8,1,1024]{2,1,0:T(1,128)}), f32[8,1,1024]{2,1,0:T(1,128)S(1)}, u32[]{:S(2)}, u32[]{:S(2)}) async-start(f32[8,1,1024]{2,1,0:T(1,128)} %reshape.280), calls=%async_computation.1 | async-start | bytes 65536 | tf_op jit(solution)/shard_map/all_to_all | solution.py:102
  80.5 17.7 %collective-permute-start.14 = (f32[75,1,128]{2,1,0:T(1,128)S(1)}, f32[75,1,128]{2,1,0:T(1,128)S(1)}, u32[]{:S(2)}, u32[]{:S(2)}) collective-permute-start(f32[75,1,128]{2,1,0:T(1,128)S(1)} %get-tuple-element.114), channel_id=1, source_target_pairs={{16,0},{32,16},{48,32},{64,48},{80,64},{96,80},{112,96},{17,1},{33... | collective-permute-start | bytes 115208 | tf_op jit(solution)/shard_map/ppermute | solution.py:23
  81.8 16.4 %collective-permute-start.15 = (f32[75,1,128]{2,1,0:T(1,128)S(1)}, f32[75,1,128]{2,1,0:T(1,128)S(1)}, u32[]{:S(2)}, u32[]{:S(2)}) collective-permute-start(f32[75,1,128]{2,1,0:T(1,128)S(1)} %get-tuple-element.115), channel_id=1, source_target_pairs={{0,16},{16,32},{32,48},{48,64},{64,80},{80,96},{96,112},{1,17},{17... | collective-permute-start | bytes 115208 | tf_op jit(solution)/shard_map/ppermute | solution.py:20
  90.1 6.8 %collective-permute-start.16 = (f32[16,32]{1,0:T(8,128)S(1)}, f32[16,32]{1,0:T(8,128)S(1)}, u32[]{:S(2)}, u32[]{:S(2)}) collective-permute-start(f32[16,32]{1,0:T(8,128)S(1)} %fusion.7), channel_id=1, source_target_pairs={{0,384},{128,256},{1,385},{129,257},{2,386},{130,258},{3,387},{131... | collective-permute-start | bytes 6152 | tf_op jit(solution)/shard_map/ppermute | solution.py:115
  91.5 6.6 %collective-permute-start.12 = (f32[75,4,1]{2,1,0:T(4,128)S(1)}, f32[75,4,1]{2,1,0:T(4,128)S(1)}, u32[]{:S(2)}, u32[]{:S(2)}) collective-permute-start(f32[75,4,1]{2,1,0:T(4,128)S(1)} %get-tuple-element.110), channel_id=1, source_target_pairs={{1,0},{2,1},{3,2},{4,3},{5,4},{6,5},{7,6},{8,7},{9,8},{10,9},{11,1... | collective-permute-start | bytes 3608 | tf_op jit(solution)/shard_map/ppermute | solution.py:23
  91.6 6.6 %collective-permute-start.13 = (f32[75,4,1]{2,1,0:T(4,128)S(1)}, f32[75,4,1]{2,1,0:T(4,128)S(1)}, u32[]{:S(2)}, u32[]{:S(2)}) collective-permute-start(f32[75,4,1]{2,1,0:T(4,128)S(1)} %get-tuple-element.111), channel_id=1, source_target_pairs={{0,1},{1,2},{2,3},{3,4},{4,5},{5,6},{6,7},{7,8},{8,9},{9,10},{10,1... | collective-permute-start | bytes 3608 | tf_op jit(solution)/shard_map/ppermute | solution.py:20
  107.9 10.0 %collective-permute-start.18 = (f32[75,4,1]{2,1,0:T(4,128)}, f32[75,4,1]{2,1,0:T(4,128)S(1)}, u32[]{:S(2)}, u32[]{:S(2)}) collective-permute-start(f32[75,4,1]{2,1,0:T(4,128)} %get-tuple-element.104), channel_id=1, source_target_pairs={{1,0},{2,1},{3,2},{4,3},{5,4},{6,5},{7,6},{8,7},{9,8},{10,9},{11,1... | collective-permute-start | bytes 3608 | tf_op jit(solution)/shard_map/ppermute | solution.py:23
  107.9 10.0 %collective-permute-start.19 = (f32[75,4,1]{2,1,0:T(4,128)}, f32[75,4,1]{2,1,0:T(4,128)}, u32[]{:S(2)}, u32[]{:S(2)}) collective-permute-start(f32[75,4,1]{2,1,0:T(4,128)} %get-tuple-element.105), channel_id=1, source_target_pairs={{0,1},{1,2},{2,3},{3,4},{4,5},{5,6},{6,7},{7,8},{8,9},{9,10},{10,1... | collective-permute-start | bytes 3608 | tf_op jit(solution)/shard_map/ppermute | solution.py:20
  109.1 8.8 %collective-permute-start.20 = (f32[75,1,128]{2,1,0:T(1,128)}, f32[75,1,128]{2,1,0:T(1,128)S(1)}, u32[]{:S(2)}, u32[]{:S(2)}) collective-permute-start(f32[75,1,128]{2,1,0:T(1,128)} %get-tuple-element.108), channel_id=1, source_target_pairs={{16,0},{32,16},{48,32},{64,48},{80,64},{96,80},{112,96},{17,1},{33... | collective-permute-start | bytes 115208 | tf_op jit(solution)/shard_map/ppermute | solution.py:23
  110.4 7.5 %collective-permute-start.21 = (f32[75,1,128]{2,1,0:T(1,128)S(1)}, f32[75,1,128]{2,1,0:T(1,128)S(1)}, u32[]{:S(2)}, u32[]{:S(2)}) collective-permute-start(f32[75,1,128]{2,1,0:T(1,128)S(1)} %get-tuple-element.109), channel_id=1, source_target_pairs={{0,16},{16,32},{32,48},{48,64},{64,80},{80,96},{96,112},{1,17},{17... | collective-permute-start | bytes 115208 | tf_op jit(solution)/shard_map/ppermute | solution.py:20
  119.8 11.1 %all-to-all-start.2 = ((f32[16,1,512]{2,1,0:T(1,128)}), f32[16,1,512]{2,1,0:T(1,128)S(1)}, u32[]{:S(2)}, u32[]{:S(2)}) async-start(f32[16,1,512]{2,1,0:T(1,128)} %reshape.282), calls=%async_computation.2 | async-start | bytes 65536 | tf_op jit(solution)/shard_map/all_to_all | solution.py:101
  132.7 15.0 %all-to-all-start.3 = ((f32[8,1,1024]{2,1,0:T(1,128)}), f32[8,1,1024]{2,1,0:T(1,128)S(1)}, u32[]{:S(2)}, u32[]{:S(2)}) async-start(f32[8,1,1024]{2,1,0:T(1,128)} %reshape.284), calls=%async_computation.3 | async-start | bytes 65536 | tf_op jit(solution)/shard_map/all_to_all | solution.py:102
  139.8 17.7 %collective-permute-start.24 = (f32[75,1,128]{2,1,0:T(1,128)S(1)}, f32[75,1,128]{2,1,0:T(1,128)S(1)}, u32[]{:S(2)}, u32[]{:S(2)}) collective-permute-start(f32[75,1,128]{2,1,0:T(1,128)S(1)} %get-tuple-element.102), channel_id=1, source_target_pairs={{16,0},{32,16},{48,32},{64,48},{80,64},{96,80},{112,96},{17,1},{33... | collective-permute-start | bytes 115208 | tf_op jit(solution)/shard_map/ppermute | solution.py:23
  141.1 16.4 %collective-permute-start.25 = (f32[75,1,128]{2,1,0:T(1,128)S(1)}, f32[75,1,128]{2,1,0:T(1,128)S(1)}, u32[]{:S(2)}, u32[]{:S(2)}) collective-permute-start(f32[75,1,128]{2,1,0:T(1,128)S(1)} %get-tuple-element.103), channel_id=1, source_target_pairs={{0,16},{16,32},{32,48},{48,64},{64,80},{80,96},{96,112},{1,17},{17... | collective-permute-start | bytes 115208 | tf_op jit(solution)/shard_map/ppermute | solution.py:20
  149.4 6.8 %collective-permute-start.26 = (f32[16,32]{1,0:T(8,128)S(1)}, f32[16,32]{1,0:T(8,128)S(1)}, u32[]{:S(2)}, u32[]{:S(2)}) collective-permute-start(f32[16,32]{1,0:T(8,128)S(1)} %fusion.5), channel_id=1, source_target_pairs={{0,384},{128,256},{1,385},{129,257},{2,386},{130,258},{3,387},{131... | collective-permute-start | bytes 6152 | tf_op jit(solution)/shard_map/ppermute | solution.py:115
  150.9 6.6 %collective-permute-start.22 = (f32[75,4,1]{2,1,0:T(4,128)S(1)}, f32[75,4,1]{2,1,0:T(4,128)S(1)}, u32[]{:S(2)}, u32[]{:S(2)}) collective-permute-start(f32[75,4,1]{2,1,0:T(4,128)S(1)} %get-tuple-element.98), channel_id=1, source_target_pairs={{1,0},{2,1},{3,2},{4,3},{5,4},{6,5},{7,6},{8,7},{9,8},{10,9},{11,1... | collective-permute-start | bytes 3608 | tf_op jit(solution)/shard_map/ppermute | solution.py:23
  167.3 9.8 %collective-permute-start.28 = (f32[75,4,1]{2,1,0:T(4,128)}, f32[75,4,1]{2,1,0:T(4,128)S(1)}, u32[]{:S(2)}, u32[]{:S(2)}) collective-permute-start(f32[75,4,1]{2,1,0:T(4,128)} %get-tuple-element.90), channel_id=1, source_target_pairs={{1,0},{2,1},{3,2},{4,3},{5,4},{6,5},{7,6},{8,7},{9,8},{10,9},{11,1... | collective-permute-start | bytes 3608 | tf_op jit(solution)/shard_map/ppermute | solution.py:23
  167.3 9.8 %collective-permute-start.29 = (f32[75,4,1]{2,1,0:T(4,128)}, f32[75,4,1]{2,1,0:T(4,128)}, u32[]{:S(2)}, u32[]{:S(2)}) collective-permute-start(f32[75,4,1]{2,1,0:T(4,128)} %get-tuple-element.91), channel_id=1, source_target_pairs={{0,1},{1,2},{2,3},{3,4},{4,5},{5,6},{6,7},{7,8},{8,9},{9,10},{10,1... | collective-permute-start | bytes 3608 | tf_op jit(solution)/shard_map/ppermute | solution.py:20
  168.4 8.6 %collective-permute-start.30 = (f32[75,1,128]{2,1,0:T(1,128)}, f32[75,1,128]{2,1,0:T(1,128)S(1)}, u32[]{:S(2)}, u32[]{:S(2)}) collective-permute-start(f32[75,1,128]{2,1,0:T(1,128)} %get-tuple-element.94), channel_id=1, source_target_pairs={{16,0},{32,16},{48,32},{64,48},{80,64},{96,80},{112,96},{17,1},{33... | collective-permute-start | bytes 115208 | tf_op jit(solution)/shard_map/ppermute | solution.py:23
  169.7 7.4 %collective-permute-start.31 = (f32[75,1,128]{2,1,0:T(1,128)S(1)}, f32[75,1,128]{2,1,0:T(1,128)S(1)}, u32[]{:S(2)}, u32[]{:S(2)}) collective-permute-start(f32[75,1,128]{2,1,0:T(1,128)S(1)} %get-tuple-element.95), channel_id=1, source_target_pairs={{0,16},{16,32},{32,48},{48,64},{64,80},{80,96},{96,112},{1,17},{17... | collective-permute-start | bytes 115208 | tf_op jit(solution)/shard_map/ppermute | solution.py:20
  179.0 11.1 %all-to-all-start.4 = ((f32[16,1,512]{2,1,0:T(1,128)}), f32[16,1,512]{2,1,0:T(1,128)S(1)}, u32[]{:S(2)}, u32[]{:S(2)}) async-start(f32[16,1,512]{2,1,0:T(1,128)} %reshape.286), calls=%async_computation.4 | async-start | bytes 65536 | tf_op jit(solution)/shard_map/all_to_all | solution.py:101
  191.9 15.2 %all-to-all-start.5 = ((f32[8,1,1024]{2,1,0:T(1,128)}), f32[8,1,1024]{2,1,0:T(1,128)S(1)}, u32[]{:S(2)}, u32[]{:S(2)}) async-start(f32[8,1,1024]{2,1,0:T(1,128)} %reshape.288), calls=%async_computation.5 | async-start | bytes 65536 | tf_op jit(solution)/shard_map/all_to_all | solution.py:102
  199.2 17.7 %collective-permute-start.34 = (f32[75,1,128]{2,1,0:T(1,128)S(1)}, f32[75,1,128]{2,1,0:T(1,128)S(1)}, u32[]{:S(2)}, u32[]{:S(2)}) collective-permute-start(f32[75,1,128]{2,1,0:T(1,128)S(1)} %get-tuple-element.88), channel_id=1, source_target_pairs={{16,0},{32,16},{48,32},{64,48},{80,64},{96,80},{112,96},{17,1},{33... | collective-permute-start | bytes 115208 | tf_op jit(solution)/shard_map/ppermute | solution.py:23
  200.5 16.4 %collective-permute-start.35 = (f32[75,1,128]{2,1,0:T(1,128)S(1)}, f32[75,1,128]{2,1,0:T(1,128)S(1)}, u32[]{:S(2)}, u32[]{:S(2)}) collective-permute-start(f32[75,1,128]{2,1,0:T(1,128)S(1)} %get-tuple-element.89), channel_id=1, source_target_pairs={{0,16},{16,32},{32,48},{48,64},{64,80},{80,96},{96,112},{1,17},{17... | collective-permute-start | bytes 115208 | tf_op jit(solution)/shard_map/ppermute | solution.py:20
  208.8 6.8 %collective-permute-start.36 = (f32[16,32]{1,0:T(8,128)S(1)}, f32[16,32]{1,0:T(8,128)S(1)}, u32[]{:S(2)}, u32[]{:S(2)}) collective-permute-start(f32[16,32]{1,0:T(8,128)S(1)} %fusion.3), channel_id=1, source_target_pairs={{0,384},{128,256},{1,385},{129,257},{2,386},{130,258},{3,387},{131... | collective-permute-start | bytes 6152 | tf_op jit(solution)/shard_map/ppermute | solution.py:115
  210.2 6.6 %collective-permute-start.32 = (f32[75,4,1]{2,1,0:T(4,128)S(1)}, f32[75,4,1]{2,1,0:T(4,128)S(1)}, u32[]{:S(2)}, u32[]{:S(2)}) collective-permute-start(f32[75,4,1]{2,1,0:T(4,128)S(1)} %get-tuple-element.84), channel_id=1, source_target_pairs={{1,0},{2,1},{3,2},{4,3},{5,4},{6,5},{7,6},{8,7},{9,8},{10,9},{11,1... | collective-permute-start | bytes 3608 | tf_op jit(solution)/shard_map/ppermute | solution.py:23
  226.6 9.4 %collective-permute-start.38 = (f32[75,4,1]{2,1,0:T(4,128)}, f32[75,4,1]{2,1,0:T(4,128)S(1)}, u32[]{:S(2)}, u32[]{:S(2)}) collective-permute-start(f32[75,4,1]{2,1,0:T(4,128)} %get-tuple-element.76), channel_id=1, source_target_pairs={{1,0},{2,1},{3,2},{4,3},{5,4},{6,5},{7,6},{8,7},{9,8},{10,9},{11,1... | collective-permute-start | bytes 3608 | tf_op jit(solution)/shard_map/ppermute | solution.py:23
  226.6 9.4 %collective-permute-start.39 = (f32[75,4,1]{2,1,0:T(4,128)}, f32[75,4,1]{2,1,0:T(4,128)}, u32[]{:S(2)}, u32[]{:S(2)}) collective-permute-start(f32[75,4,1]{2,1,0:T(4,128)} %get-tuple-element.77), channel_id=1, source_target_pairs={{0,1},{1,2},{2,3},{3,4},{4,5},{5,6},{6,7},{7,8},{8,9},{9,10},{10,1... | collective-permute-start | bytes 3608 | tf_op jit(solution)/shard_map/ppermute | solution.py:20
  227.2 8.9 %collective-permute-start.40 = (f32[75,1,128]{2,1,0:T(1,128)S(1)}, f32[75,1,128]{2,1,0:T(1,128)S(1)}, u32[]{:S(2)}, u32[]{:S(2)}) collective-permute-start(f32[75,1,128]{2,1,0:T(1,128)S(1)} %get-tuple-element.80), channel_id=1, source_target_pairs={{16,0},{32,16},{48,32},{64,48},{80,64},{96,80},{112,96},{17,1},{33... | collective-permute-start | bytes 115208 | tf_op jit(solution)/shard_map/ppermute | solution.py:23
  228.5 7.6 %collective-permute-start.41 = (f32[75,1,128]{2,1,0:T(1,128)S(1)}, f32[75,1,128]{2,1,0:T(1,128)S(1)}, u32[]{:S(2)}, u32[]{:S(2)}) collective-permute-start(f32[75,1,128]{2,1,0:T(1,128)S(1)} %get-tuple-element.81), channel_id=1, source_target_pairs={{0,16},{16,32},{32,48},{48,64},{64,80},{80,96},{96,112},{1,17},{17... | collective-permute-start | bytes 115208 | tf_op jit(solution)/shard_map/ppermute | solution.py:20
  238.0 11.1 %all-to-all-start.6 = ((f32[16,1,512]{2,1,0:T(1,128)}), f32[16,1,512]{2,1,0:T(1,128)S(1)}, u32[]{:S(2)}, u32[]{:S(2)}) async-start(f32[16,1,512]{2,1,0:T(1,128)} %reshape.290), calls=%async_computation.6 | async-start | bytes 65536 | tf_op jit(solution)/shard_map/all_to_all | solution.py:101
  250.9 15.0 %all-to-all-start.7 = ((f32[8,1,1024]{2,1,0:T(1,128)}), f32[8,1,1024]{2,1,0:T(1,128)S(1)}, u32[]{:S(2)}, u32[]{:S(2)}) async-start(f32[8,1,1024]{2,1,0:T(1,128)} %reshape.292), calls=%async_computation.7 | async-start | bytes 65536 | tf_op jit(solution)/shard_map/all_to_all | solution.py:102
  257.9 17.7 %collective-permute-start.44 = (f32[75,1,128]{2,1,0:T(1,128)S(1)}, f32[75,1,128]{2,1,0:T(1,128)S(1)}, u32[]{:S(2)}, u32[]{:S(2)}) collective-permute-start(f32[75,1,128]{2,1,0:T(1,128)S(1)} %get-tuple-element.74), channel_id=1, source_target_pairs={{16,0},{32,16},{48,32},{64,48},{80,64},{96,80},{112,96},{17,1},{33... | collective-permute-start | bytes 115208 | tf_op jit(solution)/shard_map/ppermute | solution.py:23
  259.2 16.4 %collective-permute-start.45 = (f32[75,1,128]{2,1,0:T(1,128)S(1)}, f32[75,1,128]{2,1,0:T(1,128)S(1)}, u32[]{:S(2)}, u32[]{:S(2)}) collective-permute-start(f32[75,1,128]{2,1,0:T(1,128)S(1)} %get-tuple-element.75), channel_id=1, source_target_pairs={{0,16},{16,32},{32,48},{48,64},{64,80},{80,96},{96,112},{1,17},{17... | collective-permute-start | bytes 115208 | tf_op jit(solution)/shard_map/ppermute | solution.py:20
  267.5 6.8 %collective-permute-start.46 = (f32[16,32]{1,0:T(8,128)S(1)}, f32[16,32]{1,0:T(8,128)S(1)}, u32[]{:S(2)}, u32[]{:S(2)}) collective-permute-start(f32[16,32]{1,0:T(8,128)S(1)} %fusion.1), channel_id=1, source_target_pairs={{0,384},{128,256},{1,385},{129,257},{2,386},{130,258},{3,387},{131... | collective-permute-start | bytes 6152 | tf_op jit(solution)/shard_map/ppermute | solution.py:115
  269.0 6.6 %collective-permute-start.42 = (f32[75,4,1]{2,1,0:T(4,128)S(1)}, f32[75,4,1]{2,1,0:T(4,128)S(1)}, u32[]{:S(2)}, u32[]{:S(2)}) collective-permute-start(f32[75,4,1]{2,1,0:T(4,128)S(1)} %get-tuple-element.70), channel_id=1, source_target_pairs={{1,0},{2,1},{3,2},{4,3},{5,4},{6,5},{7,6},{8,7},{9,8},{10,9},{11,1... | collective-permute-start | bytes 3608 | tf_op jit(solution)/shard_map/ppermute | solution.py:23
  (30 other events, 389.1 us)
